TPU v7x, 32 devices: a whole 2x2x4 slice. The times are simulated.
32 devices in a mesh: groups: 2 (over y), seq: 4 (over z), head: 2 (over x), sub: 2 (over core).
Axes of the slice: x: 2, y: 2, z: 4, core: 2. Of those that a mesh axis runs over, the one named last changes fastest.
Arguments:
- queries: bfloat16 [64, 1024, 128], P(('head', 'sub'), ('groups', 'seq')), parts along dimension 1, may hold values from -6 to 6
- keys_values: bfloat16 [8, 1024, 256], P(('head', 'sub'), ('groups', 'seq')), parts along dimension 1, may hold values from -6 to 6
- student_x: bfloat16 [64, 1024, 128], P(('head', 'sub'), ('groups', 'seq')), parts along dimension 1, may hold values from -32 to 32
- state_maps: bfloat16 [8, 1024, 128], P(('head', 'sub'), ('groups', 'seq')), parts along dimension 1, may hold values from -0.75 to 0.75
- decay_logit: float32 [64, 1024], P(('head', 'sub'), ('groups', 'seq')), parts along dimension 1, may hold values from 0 to 16
- skip_gain: float32 [64], P(('head', 'sub')), may hold values from 0.5 to 2
- init_state: float32 [128, 64, 128], P(('groups', 'head', 'sub')), parts along dimension 0, may hold values from -6 to 6
Outputs:
- grad_x: bfloat16 [64, 1024, 128], P(('head', 'sub'), ('groups', 'seq')), parts along dimension 1
- grad_maps: bfloat16 [8, 1024, 128], P(('head', 'sub'), ('groups', 'seq')), parts along dimension 1
- grad_log_decay: float32 [64, 1024], P(('head', 'sub'), ('groups', 'seq')), parts along dimension 1
There are 2 independent parts, one for each index of `groups`. A program takes and returns all parts, laid end to end along the dimension named above; an argument that names none is the same for every part. Nothing has to cross between parts.
All inputs are finite; a program needn't handle non-finite values.
Results may differ from a plain program's by a relative error of at most 0.013.
Values may be sent and summed in bfloat16 or wider, within the bound.
No kernel may reach another device: no remote copies, remote signals or barrier semaphores. Data moves between devices by JAX's collectives and lax.ppermute only.
A program may use at most 64 MiB of HBM per device.

v0:
```python
import jax
import jax.numpy as jnp
from jax import lax
from jax.sharding import PartitionSpec as P

epsilon = 1e-05
highest = lax.Precision.HIGHEST


def split_three(values):
    top = lax.reduce_precision(values, exponent_bits=8, mantissa_bits=7)
    rest = values - top
    middle = lax.reduce_precision(rest, exponent_bits=8, mantissa_bits=7)
    low = rest - middle
    return jnp.stack([top, middle, low]).astype(jnp.bfloat16)


def join_three(parts):
    wide = parts.astype(jnp.float32)
    return wide[..., 0, :] + wide[..., 1, :] + wide[..., 2, :]


def pack_rows(big, smalls):
    rows = big.astype(jnp.bfloat16).reshape(-1, 128)
    vector = jnp.concatenate([v.reshape(-1) for v in smalls])
    padded = -(-vector.shape[0] // 128) * 128
    vector = jnp.pad(vector, (0, padded - vector.shape[0]))
    extra = split_three(vector).reshape(3 * padded // 128, 128)
    extra = jnp.pad(extra, ((0, (-extra.shape[0]) % 16), (0, 0)))
    return jnp.concatenate([rows, extra], axis=0)


def unpack_rows(received, big_shape, small_shapes):
    big_rows = 1
    for d in big_shape:
        big_rows *= d
    big_rows //= 128
    big = received[:big_rows].reshape(big_shape)
    sizes = []
    for shape in small_shapes:
        size = 1
        for d in shape:
            size *= d
        sizes.append(size)
    padded = -(-sum(sizes) // 128) * 128
    extra = received[big_rows : big_rows + 3 * padded // 128].reshape(3, padded)
    vector = join_three(extra)
    smalls = []
    offset = 0
    for shape, size in zip(small_shapes, sizes):
        smalls.append(vector[offset : offset + size].reshape(shape))
        offset += size
    return big, smalls


def shifted(x, step):
    seq_count = lax.axis_size("seq")
    seq_rank = lax.axis_index("seq")
    if seq_count <= 8:
        moved = []
        for distance in range(1, seq_count):
            if step > 0:
                pairs = [(j, j + distance) for j in range(seq_count - distance)]
            else:
                pairs = [(j + distance, j) for j in range(seq_count - distance)]
            moved.append(lax.ppermute(x, "seq", pairs))
        return moved
    gathered = lax.all_gather(x, "seq", axis=0)
    moved = []
    for distance in range(1, seq_count):
        source = seq_rank + step * distance
        valid = (source >= 0) & (source < seq_count)
        picked = lax.dynamic_index_in_dim(gathered, jnp.clip(source, 0, seq_count - 1), 0, False)
        moved.append(jnp.where(valid, picked, jnp.zeros_like(picked)))
    return moved


def teacher_rows(queries, kv_list, seq_rank):
    local_heads, tok_dev, head_width = queries.shape
    local_groups = kv_list[0].shape[0]
    per_group = local_heads // local_groups
    grouped = queries.reshape(local_groups, per_group, tok_dev, head_width)
    rows = jnp.arange(tok_dev)
    within = rows[:, None] >= rows[None, :]
    block_scores = []
    for distance, block in enumerate(kv_list):
        scores = jnp.einsum(
            "gptd,gkd->gptk", grouped, block[..., :head_width], preferred_element_type=jnp.float32
        )
        scores = scores * head_width ** (-0.5)
        if distance == 0:
            allowed = within
        else:
            allowed = distance <= seq_rank
        block_scores.append(jnp.where(allowed, scores, -jnp.inf))
    highest_score = block_scores[0].max(axis=3, keepdims=True)
    for scores in block_scores[1:]:
        highest_score = jnp.maximum(highest_score, scores.max(axis=3, keepdims=True))
    row_sums = None
    mixed = None
    for scores, block in zip(block_scores, kv_list):
        exponentials = jnp.exp(scores - highest_score)
        part_sum = jnp.sum(exponentials, axis=3, keepdims=True)
        part = jnp.einsum(
            "gptk,gkd->gptd",
            exponentials.astype(jnp.bfloat16),
            block[..., head_width:],
            preferred_element_type=jnp.float32,
        )
        row_sums = part_sum if row_sums is None else row_sums + part_sum
        mixed = part if mixed is None else mixed + part
    mixed = mixed / row_sums
    return mixed.astype(jnp.bfloat16).reshape(local_heads, tok_dev, head_width)


def body(queries, keys_values, student_x, state_maps, decay_logit, skip_gain, init_state):
    local_heads, tok_dev, head_width = student_x.shape
    local_groups = state_maps.shape[0]
    per_group = local_heads // local_groups
    state_size = state_maps.shape[2] // 2
    seq_count = lax.axis_size("seq")
    seq_rank = lax.axis_index("seq")

    kv_earlier = shifted(keys_values, 1)

    log_decay = jax.nn.log_sigmoid(decay_logit)
    cumulative = jnp.cumsum(log_decay, axis=1)
    totals = cumulative[:, -1]
    to_end = jnp.exp(totals[:, None] - cumulative)
    from_start = jnp.exp(cumulative)
    in_maps = state_maps[:, :, :state_size]
    out_maps = state_maps[:, :, state_size:]
    inputs_wide = student_x.astype(jnp.float32)
    in_heads = jnp.repeat(in_maps.astype(jnp.float32), per_group, axis=0)
    out_heads = jnp.repeat(out_maps.astype(jnp.float32), per_group, axis=0)
    weighted_in = in_heads * to_end[..., None]
    end_state = jnp.einsum("hsn,hsp->hnp", weighted_in, inputs_wide, precision=highest)

    state_earlier = shifted(pack_rows(end_state, [totals]), 1)
    ends_earlier = []
    prefix_state = jnp.zeros_like(end_state)
    gap = jnp.zeros_like(totals)
    for distance, received in enumerate(state_earlier, start=1):
        ends, (totals_there,) = unpack_rows(received, end_state.shape, [totals.shape])
        valid = distance <= seq_rank
        totals_there = jnp.where(valid, totals_there, 0.0)
        weight = jnp.where(valid, jnp.exp(gap), 0.0)
        ends_earlier.append(ends)
        prefix_state = prefix_state + weight[:, None, None] * ends.astype(jnp.float32)
        gap = gap + totals_there
    entering = prefix_state + jnp.exp(gap)[:, None, None] * init_state

    intersection = jnp.einsum("gtn,gsn->gts", out_maps, in_maps, preferred_element_type=jnp.float32)
    order_ids = jnp.arange(tok_dev)
    causal = (order_ids[:, None] >= order_ids[None, :])[None]
    gaps = cumulative[:, :, None] - cumulative[:, None, :]
    decayed = jnp.where(causal, jnp.exp(jnp.where(causal, gaps, 0.0)), 0.0)
    mixing = (
        decayed.reshape(local_groups, per_group, tok_dev, tok_dev) * intersection[:, None]
    ).reshape(local_heads, tok_dev, tok_dev)
    local_out = jnp.einsum("hts,hsp->htp", mixing, inputs_wide, precision=highest)

    teacher = teacher_rows(queries, [keys_values] + kv_earlier, seq_rank)
    teacher_wide = teacher.astype(jnp.float32)
    target = teacher_wide * lax.rsqrt(
        jnp.mean(teacher_wide * teacher_wide, axis=2, keepdims=True) + epsilon
    )

    state_out = local_out + from_start[..., None] * jnp.einsum(
        "htn,hnp->htp", out_heads, entering, precision=highest
    )
    outputs = state_out + skip_gain[:, None, None] * inputs_wide
    inverse = lax.rsqrt(jnp.mean(outputs * outputs, axis=2, keepdims=True) + epsilon)
    normed = outputs * inverse
    residual = normed - target
    grad_out = (residual - normed * jnp.mean(residual * normed, axis=2, keepdims=True)) * inverse
    forward_term = jnp.sum(grad_out * state_out, axis=2)
    flow = jnp.einsum(
        "htn,htp->hnp", out_heads * from_start[..., None], grad_out, precision=highest
    )
    local_dx = jnp.einsum("hts,htp->hsp", mixing, grad_out, precision=highest)
    closing = jnp.sum(forward_term - jnp.sum(inputs_wide * local_dx, axis=2), axis=1)
    if ends_earlier:
        ends_dot_flow = jnp.stack(
            [jnp.sum(ends.astype(jnp.float32) * flow, axis=(1, 2)) for ends in ends_earlier]
        )
    else:
        ends_dot_flow = jnp.zeros((1,) + totals.shape, jnp.float32)

    flow_later = shifted(pack_rows(flow, [totals, closing, ends_dot_flow]), -1)

    cross = jnp.einsum("htp,hsp->hts", grad_out, inputs_wide, precision=highest)
    paired = decayed * cross
    local_din = jnp.einsum("hts,htn->hsn", paired, out_heads, precision=highest)
    grad_output_maps = jnp.einsum("hts,hsn->htn", paired, in_heads, precision=highest)
    grad_output_maps = grad_output_maps + from_start[..., None] * jnp.einsum(
        "hnp,htp->htn", entering, grad_out, precision=highest
    )

    incoming = jnp.zeros_like(flow)
    later_sum = jnp.zeros_like(totals)
    gap = jnp.zeros_like(totals)
    through = []
    dots_there = []
    for distance, received in enumerate(flow_later, start=1):
        flows, (totals_there, closing_there, dots) = unpack_rows(
            received, flow.shape, [totals.shape, closing.shape, ends_dot_flow.shape]
        )
        valid = seq_rank + distance < seq_count
        totals_there = jnp.where(valid, totals_there, 0.0)
        weight = jnp.where(valid, jnp.exp(gap), 0.0)
        incoming = incoming + weight[:, None, None] * flows.astype(jnp.float32)
        later_sum = later_sum + jnp.where(valid, closing_there, 0.0)
        for early in range(1, distance):
            pair_gap = gap - through[early - 1]
            later_sum = later_sum - jnp.where(
                valid, jnp.exp(jnp.where(valid, pair_gap, 0.0)) * dots[distance - early - 1], 0.0
            )
        gap = gap + totals_there
        through.append(gap)

    state_dx = local_dx + jnp.einsum("hsn,hnp->hsp", weighted_in, incoming, precision=highest)
    terms = forward_term - jnp.sum(inputs_wide * state_dx, axis=2)
    grad_log_decay = later_sum[:, None] + lax.cumsum(terms, axis=1, reverse=True)
    grad_input_maps = (
        local_din
        + jnp.einsum("hnp,hsp->hsn", incoming, inputs_wide, precision=highest) * to_end[..., None]
    )
    grad_maps = jnp.concatenate([grad_input_maps, grad_output_maps], axis=2)
    grad_maps = grad_maps.reshape(local_groups, per_group, tok_dev, 2 * state_size).sum(axis=1)
    grad_x = state_dx + skip_gain[:, None, None] * grad_out
    return (grad_x.astype(jnp.bfloat16), grad_maps.astype(jnp.bfloat16), grad_log_decay)


def solution(mesh):
    in_specs = (
        P(("head", "sub"), ("groups", "seq"), None),
        P(("head", "sub"), ("groups", "seq"), None),
        P(("head", "sub"), ("groups", "seq"), None),
        P(("head", "sub"), ("groups", "seq"), None),
        P(("head", "sub"), ("groups", "seq")),
        P(("head", "sub")),
        P(("groups", "head", "sub"), None, None),
    )
    out_specs = (
        P(("head", "sub"), ("groups", "seq"), None),
        P(("head", "sub"), ("groups", "seq"), None),
        P(("head", "sub"), ("groups", "seq")),
    )
    return jax.shard_map(body, mesh=mesh, in_specs=in_specs, out_specs=out_specs, check_vma=False)
```

profile of v0, /device:TPU:8, one launch (start us, length us, event | category | flops | bytes accessed | tf_op | source)
XLA Modules:
  0.0 88.1 jit_solution(14832743780401299886)
XLA Ops:
  0.7 1.4 %collective-permute-start.5 = (bf16[2,128,256]{2,1,0:T(8,128)(2,1)}, bf16[2,128,256]{2,1,0:T(8,128)(2,1)}, u32[]{:S(2)}, u32[]{:S(2)}) collective-permute-start(bf16[2,128,256]{2,1,0:T(8,128)(2,1)} %param.8), channel_id=1, source_target_pairs={{0,12},{1,13},{2,14},{3,15},{16,28},{17,29},{18,30},{19,31}} | collective-permute-start | bytes 393224 | tf_op jit(solution)/shard_map/ppermute | solution.py:66
  2.1 3.5 %collective-permute-start.3 = (bf16[2,128,256]{2,1,0:T(8,128)(2,1)}, bf16[2,128,256]{2,1,0:T(8,128)(2,1)}, u32[]{:S(2)}, u32[]{:S(2)}) collective-permute-start(bf16[2,128,256]{2,1,0:T(8,128)(2,1)} %param.8), channel_id=1, source_target_pairs={{0,4},{4,8},{8,12},{1,5},{5,9},{9,13},{2,6},{6,10},{10,14},{3,7},{... | collective-permute-start | bytes 393224 | tf_op jit(solution)/shard_map/ppermute | solution.py:66
  5.6 3.0 %collective-permute-start.4 = (bf16[2,128,256]{2,1,0:T(8,128)(2,1)}, bf16[2,128,256]{2,1,0:T(8,128)(2,1)}, u32[]{:S(2)}, u32[]{:S(2)}) collective-permute-start(bf16[2,128,256]{2,1,0:T(8,128)(2,1)} %param.8), channel_id=1, source_target_pairs={{0,8},{4,12},{1,9},{5,13},{2,10},{6,14},{3,11},{7,15},{16,24},{20,... | collective-permute-start | bytes 393224 | tf_op jit(solution)/shard_map/ppermute | solution.py:66
  8.5 0.7 fusion.52
  10.1 0.5 convolution_convert_fusion
  10.7 0.7 pad_maximum_fusion.1
  11.4 1.3 %collective-permute-start.1 = (bf16[1040,128]{1,0:T(8,128)(2,1)}, bf16[1040,128]{1,0:T(8,128)(2,1)S(1)}, u32[]{:S(2)}, u32[]{:S(2)}) collective-permute-start(bf16[1040,128]{1,0:T(8,128)(2,1)} %pad_maximum_fusion.1), channel_id=1, source_target_pairs={{0,8},{4,12},{1,9},{5,13},{2,10},{6,14},{3,11},{7,15},{16,24},{20,... | collective-permute-start | bytes 798728 | tf_op jit(solution)/shard_map/ppermute | solution.py:66
  12.7 1.9 %collective-permute-start = (bf16[1040,128]{1,0:T(8,128)(2,1)}, bf16[1040,128]{1,0:T(8,128)(2,1)}, u32[]{:S(2)}, u32[]{:S(2)}) collective-permute-start(bf16[1040,128]{1,0:T(8,128)(2,1)} %pad_maximum_fusion.1), channel_id=1, source_target_pairs={{0,4},{4,8},{8,12},{1,5},{5,9},{9,13},{2,6},{6,10},{10,14},{3,7},{... | collective-permute-start | bytes 798728 | tf_op jit(solution)/shard_map/ppermute | solution.py:66
  15.0 0.4 bitcast_multiply_fusion.1
  15.4 2.3 %fusion.104 = f32[16,128,128]{1,2,0:T(8,128)} fusion(f32[16,128,128]{2,1,0:T(8,128)S(1)} %bitcast_multiply_fusion.1, bf16[16,128,128]{2,1,0:T(8,128)(2,1)S(1)} %copy-done.1), kind=kOutput, calls=%fused_computation.199 | convolution fusion | flops 402653184 | bytes 2621440 | tf_op jit(solution)/shard_map/hts,hsp->htp/dot_general | solution.py:161
  17.6 1.9 %fusion.102 = (f32[2,8,128]{2,1,0:T(8,128)}, f32[2,8,128,128]{2,3,1,0:T(8,128)}) fusion(bf16[2,8,128,128]{3,2,1,0:T(8,128)(2,1)S(1)} %bitcast.187, bf16[2,128,256]{2,1,0:T(8,128)(2,1)S(1)} %copy-done.21, pred[128,128]{0,1:T(8,128)(4,1)S(1)} %iota_compare_fusion), kind=kOutput, calls=%fused_computation.197 | convolution fusion | flops 67893248 | bytes 1662976 | tf_op jit(solution)/shard_map/gptd,gkd->gptk/dot_general | solution.py:87
  19.9 0.9 collective-permute-start.2
  20.8 1.1 %fusion.103 = (f32[2,8,128]{2,1,0:T(8,128)S(1)}, f32[2,8,128,128]{2,3,1,0:T(8,128)S(1)}) fusion(bf16[2,8,128,128]{3,2,1,0:T(8,128)(2,1)S(1)} %bitcast.188, bf16[2,128,256]{2,1,0:T(8,128)(2,1)} %collective-permute-done.3, pred[]{:T(512)S(6)} %ge.51), kind=kOutput, calls=%fused_computation.198 | convolution fusion | flops 67893248 | bytes 1646593 | tf_op jit(solution)/shard_map/gptd,gkd->gptk/dot_general | solution.py:87
  22.0 1.1 %fusion.100 = (f32[2,8,128]{2,1,0:T(8,128)S(1)}, f32[2,8,128,128]{2,3,1,0:T(8,128)S(1)}) fusion(bf16[2,8,128,128]{3,2,1,0:T(8,128)(2,1)S(1)} %bitcast.190, bf16[2,128,256]{2,1,0:T(8,128)(2,1)} %collective-permute-done.5, pred[]{:T(512)S(6)} %ge.53), kind=kOutput, calls=%fused_computation.195 | convolution fusion | flops 67893248 | bytes 1646593 | tf_op jit(solution)/shard_map/gptd,gkd->gptk/dot_general | solution.py:87
  23.5 1.2 %fusion.101 = (f32[2,8,128]{2,1,0:T(8,128)S(1)}, f32[2,8,128,128]{2,3,1,0:T(8,128)S(1)}) fusion(bf16[2,8,128,128]{3,2,1,0:T(8,128)(2,1)S(1)} %bitcast.189, bf16[2,128,256]{2,1,0:T(8,128)(2,1)} %collective-permute-done.4, pred[]{:T(512)S(6)} %ge.52), kind=kOutput, calls=%fused_computation.196 | convolution fusion | flops 67893248 | bytes 1646593 | tf_op jit(solution)/shard_map/gptd,gkd->gptk/dot_general | solution.py:87
  25.0 1.0 %fusion.17 = (f32[2,8,128]{2,1,0:T(8,128)S(1)}, f32[2,8,128]{2,1,0:T(8,128)S(1)}, f32[2,8,128]{2,1,0:T(8,128)S(1)}, f32[2,8,128]{2,1,0:T(8,128)S(1)}) fusion(f32[2,8,128,128]{2,3,1,0:T(8,128)S(1)} %get-tuple-element.48, f32[2,8,128]{2,1,0:T(8,128)S(1)} %maximum_maximum_fusion, f32[2,8,128,128]{2,3,1,0:T(8,128)S(1)} %copy-done.6, ...), kind=kLoop, calls=%fused_computation.49 | loop fusion | flops 2088960 | bytes 4235264 | tf_op jit(solution)/shard_map/reduce_sum | solution.py:103
  26.0 1.2 %fusion.29 = f32[2,8,128,128]{2,3,1,0:T(8,128)S(1)} fusion(f32[2,8,128,128]{2,3,1,0:T(8,128)S(1)} %get-tuple-element.42, f32[2,8,128]{2,1,0:T(8,128)S(1)} %maximum_maximum_fusion, bf16[2,128,256]{2,1,0:T(8,128)(2,1)} %collective-permute-done.5), kind=kOutput, calls=%fused_computation.67 | convolution fusion | flops 67633152 | bytes 2170880 | tf_op jit(solution)/shard_map/gptk,gkd->gptd/dot_general | solution.py:104
  27.2 1.2 %convolution_add_fusion.2 = f32[2,8,128,128]{2,3,1,0:T(8,128)S(1)} fusion(f32[2,8,128,128]{2,3,1,0:T(8,128)S(1)} %fusion.33, f32[2,8,128,128]{2,3,1,0:T(8,128)S(1)} %get-tuple-element.48, f32[2,8,128]{2,1,0:T(8,128)S(1)} %maximum_maximum_fusion, bf16[2,128,256]{2,1,0:T(8,128)(2,1)} %collective-permute-done.3), kind=kOutput, calls=%fused_computation.11 | convolution fusion | flops 67895296 | bytes 3219456 | tf_op jit(solution)/shard_map/gptk,gkd->gptd/dot_general | solution.py:104
  28.4 1.3 %multiply_reduce_fusion.2 = (f32[2,8,128]{2,1,0:T(8,128)S(1)}, f32[2,8,128,128]{2,3,1,0:T(8,128)S(1)}) fusion(f32[2,8,128]{2,1,0:T(8,128)S(1)} %add_add_fusion, f32[2,8,128,128]{2,3,1,0:T(8,128)S(1)} %fusion.29, f32[2,8,128,128]{2,3,1,0:T(8,128)S(1)} %convolution_add_fusion.2, bf16[2,128,256]{2,1,0:T(8,128)(2,1)} %collective-permute-done.4, ...), kind=kOutput, calls=%fused_computation.40 | convolution fusion | flops 69466112 | bytes 4284416 | tf_op jit(solution)/shard_map/gptk,gkd->gptd/dot_general | solution.py:104
  29.8 5.1 %collective-permute-done.1 = bf16[1040,128]{1,0:T(8,128)(2,1)S(1)} collective-permute-done((bf16[1040,128]{1,0:T(8,128)(2,1)}, bf16[1040,128]{1,0:T(8,128)(2,1)S(1)}, u32[]{:S(2)}, u32[]{:S(2)}) %collective-permute-start.1) | collective-permute-done | bytes 266272 | tf_op jit(solution)/shard_map/ppermute | solution.py:66
  34.9 5.0 %collective-permute-done = bf16[1040,128]{1,0:T(8,128)(2,1)} collective-permute-done((bf16[1040,128]{1,0:T(8,128)(2,1)}, bf16[1040,128]{1,0:T(8,128)(2,1)}, u32[]{:S(2)}, u32[]{:S(2)}) %collective-permute-start) | collective-permute-done | bytes 266272 | tf_op jit(solution)/shard_map/ppermute | solution.py:66
  39.9 0.7 slice_convert_fusion.5
  40.8 0.7 copy-done.24
  41.4 3.1 %multiply_reduce_fusion.3 = (f32[16,128]{1,0:T(8,128)S(1)}, f32[16,128,128]{1,2,0:T(8,128)S(1)}) fusion(bf16[16,128,128]{1,2,0:T(8,128)(2,1)S(1)} %copy.48, f32[16]{0:T(128)S(1)} %copy-done.24, f32[16,128,128]{1,2,0:T(8,128)S(1)} %copy-done.11, f32[16,128,64]{1,2,0:T(8,128)S(1)} %bitcast.191, f32[16,64,128]{2,1,0:T(8,128)S(1)} %copy-done.16, ...), kind=kOutput, calls=%fused_computation.45 | convolution fusion | flops 204470272 | bytes 4474884 | tf_op jit(solution)/shard_map/htn,hnp->htp/dot_general | solution.py:169
  44.5 0.4 multiply_reduce_fusion.1
  45.0 0.6 multiply_reduce_fusion
  45.5 0.6 copy-done.3
  46.2 2.1 %fusion.12 = (f32[16,128]{1,0:T(8,128)S(1)}, f32[16,128,128]{1,2,0:T(8,128)}) fusion(bf16[16,128,128]{1,2,0:T(8,128)(2,1)S(1)} %copy.48, f32[16,128,128]{2,1,0:T(8,128)S(1)} %copy-done.3, f32[16,128,128]{1,2,0:T(8,128)S(1)} %get-tuple-element.22), kind=kOutput, calls=%fused_computation.29 | convolution fusion | flops 403437568 | bytes 3678208 | tf_op jit(solution)/shard_map/hts,htp->hsp/dot_general | solution.py:181
  48.3 2.1 %fusion.37 = f32[16,64,128]{2,1,0:T(8,128)S(1)} fusion(f32[16,128,128]{1,2,0:T(8,128)S(1)} %get-tuple-element.22, f32[16,128,64]{1,2,0:T(8,128)S(1)} %bitcast.192, f32[16,128]{1,0:T(8,128)S(1)} %get-tuple-element.31), kind=kOutput, calls=%fused_computation.74 | convolution fusion | flops 201457664 | bytes 2105344 | tf_op jit(solution)/shard_map/htn,htp->hnp/dot_general | solution.py:178
  50.5 1.0 %slice.240 = bf16[1024,128]{1,0:T(8,128)(2,1)S(1)} slice(bf16[1040,128]{1,0:T(8,128)(2,1)} %collective-permute-done), slice={[0:1024], [0:128]} | slice | bytes 524288 | tf_op jit(solution)/shard_map/slice | solution.py:38
  51.5 0.9 %slice-done = bf16[1024,128]{1,0:T(8,128)(2,1)S(1)} async-done(((bf16[1040,128]{1,0:T(8,128)(2,1)}), bf16[1024,128]{1,0:T(8,128)(2,1)S(1)}, s32[]{:S(2)}) %slice-start) | async-done | bytes 262168 | tf_op jit(solution)/shard_map/slice | solution.py:38
  52.4 1.0 %fusion.26 = (f32[16]{0:T(128)S(1)}, f32[16]{0:T(128)S(1)}, f32[16]{0:T(128)S(1)}, bf16[16,64,128]{2,1,0:T(8,128)(2,1)}) fusion(f32[16,64,128]{2,1,0:T(8,128)S(1)} %fusion.37, bf16[16,64,128]{2,1,0:T(8,128)(2,1)S(1)} %bitcast.205, bf16[16,64,128]{2,1,0:T(8,128)(2,1)S(1)} %bitcast.206, bf16[16,64,128]{2,1,0:T(8,128)(2,1)S(1)} %bitcast.203), kind=kLoop, calls=%fused_computation.64 | loop fusion | flops 1310672 | bytes 1573056 | tf_op jit(solution)/shard_map/reduce_sum | solution.py:185
  53.7 1.0 %pad_maximum_fusion.2 = bf16[1040,128]{1,0:T(8,128)(2,1)S(1)} fusion(bf16[16,128]{1,0:T(8,128)(2,1)S(1)} %fusion.62, bf16[1024,128]{1,0:T(8,128)(2,1)} %bitcast.204), kind=kLoop, calls=%fused_computation.83 | loop fusion | flops 532480 | bytes 532480 | tf_op jit(solution)/shard_map/concatenate | solution.py:30
  54.7 0.8 collective-permute-start.8
  55.5 1.3 %collective-permute-start.7 = (bf16[1040,128]{1,0:T(8,128)(2,1)S(1)}, bf16[1040,128]{1,0:T(8,128)(2,1)S(1)}, u32[]{:S(2)}, u32[]{:S(2)}) collective-permute-start(bf16[1040,128]{1,0:T(8,128)(2,1)S(1)} %pad_maximum_fusion.2), channel_id=1, source_target_pairs={{8,0},{12,4},{9,1},{13,5},{10,2},{14,6},{11,3},{15,7},{24,16},{28,... | collective-permute-start | bytes 798728 | tf_op jit(solution)/shard_map/ppermute | solution.py:66
  56.8 2.1 %collective-permute-start.6 = (bf16[1040,128]{1,0:T(8,128)(2,1)S(1)}, bf16[1040,128]{1,0:T(8,128)(2,1)S(1)}, u32[]{:S(2)}, u32[]{:S(2)}) collective-permute-start(bf16[1040,128]{1,0:T(8,128)(2,1)S(1)} %pad_maximum_fusion.2), channel_id=1, source_target_pairs={{4,0},{8,4},{12,8},{5,1},{9,5},{13,9},{6,2},{10,6},{14,10},{7,3},{... | collective-permute-start | bytes 798728 | tf_op jit(solution)/shard_map/ppermute | solution.py:66
  59.0 1.2 %convolution_multiply_fusion = f32[16,128,128]{2,1,0:T(8,128)S(1)} fusion(f32[16,128,128]{1,2,0:T(8,128)S(1)} %get-tuple-element.22, bf16[16,128,128]{2,1,0:T(8,128)(2,1)S(1)} %copy-done.1, f32[16,128]{1,0:T(8,128)S(1)} %reduce_window_sum.21, pred[128,128]{1,0:T(8,128)(4,1)S(1)} %copy.44), kind=kOutput, calls=%fused_computation.3 | convolution fusion | flops 403701760 | bytes 2646016 | tf_op jit(solution)/shard_map/htp,hsp->hts/dot_general | solution.py:192
  60.2 2.3 %convolution_multiply_fusion.6 = f32[16,128,64]{1,2,0:T(8,128)S(1)} fusion(f32[16,128,128]{1,2,0:T(8,128)S(1)} %get-tuple-element.22, f32[16,128]{1,0:T(8,128)S(1)} %get-tuple-element.31, f32[16,64,128]{2,1,0:T(8,128)S(1)} %copy-done.17, f32[16]{0:T(128)S(1)} %fusion.90, f32[16]{0:T(128)S(1)} %get-tuple-element.23, f32[16]{0:T(128)S(1)} %get-tuple-element.37, ...), kind=kOutput, calls=%fused_computation.22 | convolution fusion | flops 202768384 | bytes 2893316 | tf_op jit(solution)/shard_map/hnp,htp->htn/dot_general | solution.py:196
  62.6 2.9 %convolution_add_fusion.3 = f32[16,128,64]{1,2,0:T(8,128)} fusion(f32[16,128,64]{1,2,0:T(8,128)S(1)} %convolution_multiply_fusion.6, f32[16,128,128]{2,1,0:T(8,128)S(1)} %convolution_multiply_fusion, f32[16,128,64]{1,2,0:T(8,128)S(1)} %bitcast.195), kind=kOutput, calls=%fused_computation.23 | convolution fusion | flops 201457664 | bytes 2621440 | tf_op jit(solution)/shard_map/hts,hsn->htn/dot_general | solution.py:195
  65.5 2.1 %collective-permute-done.7 = bf16[1040,128]{1,0:T(8,128)(2,1)S(1)} collective-permute-done((bf16[1040,128]{1,0:T(8,128)(2,1)S(1)}, bf16[1040,128]{1,0:T(8,128)(2,1)S(1)}, u32[]{:S(2)}, u32[]{:S(2)}) %collective-permute-start.7) | collective-permute-done | bytes 266272 | tf_op jit(solution)/shard_map/ppermute | solution.py:66
  67.7 9.1 %collective-permute-done.6 = bf16[1040,128]{1,0:T(8,128)(2,1)S(1)} collective-permute-done((bf16[1040,128]{1,0:T(8,128)(2,1)S(1)}, bf16[1040,128]{1,0:T(8,128)(2,1)S(1)}, u32[]{:S(2)}, u32[]{:S(2)}) %collective-permute-start.6) | collective-permute-done | bytes 266272 | tf_op jit(solution)/shard_map/ppermute | solution.py:66
  77.0 2.0 %fusion.10 = f32[16,128,64]{1,2,0:T(8,128)} fusion(bf16[16,128,128]{2,1,0:T(8,128)(2,1)S(1)} %copy-done.1, f32[16,128]{1,0:T(8,128)S(1)} %get-tuple-element.30, bf16[16,64,128]{2,1,0:T(8,128)(2,1)S(1)} %bitcast.201, f32[16,64,128]{2,1,0:T(8,128)S(1)} %bitcast.197, bf16[16,64,128]{2,1,0:T(8,128)(2,1)S(1)} %bitcast.199, f32[16]{0:T(128)S(1)} %get-tuple-element.33, ...), kind=kOutput, calls=%fused_computation.26 | convolution fusion | flops 202244096 | bytes 2105472 | tf_op jit(solution)/shard_map/hnp,hsp->hsn/dot_general | solution.py:227
  78.9 2.8 %fusion.13 = (f32[16,128]{1,0:T(8,128)S(1)}, bf16[16,128,128]{1,2,0:T(8,128)(2,1)}) fusion(bf16[16,128,128]{1,2,0:T(8,128)(2,1)S(1)} %copy.48, f32[16,128,128]{1,2,0:T(8,128)S(1)} %get-tuple-element.22, f32[16]{0:T(128)S(1)} %copy-done.24, f32[16,128,128]{1,2,0:T(8,128)S(1)} %copy-done.10, bf16[16,64,128]{2,1,0:T(8,128)(2,1)S(1)} %bitcast.202, ...), kind=kOutput, calls=%fused_computation.30 | convolution fusion | flops 204077056 | bytes 4735168 | tf_op jit(solution)/shard_map/hsn,hnp->hsp/dot_general | solution.py:222
  81.8 1.2 %reduce_window_sum.22 = f32[16,128]{1,0:T(8,128)S(1)} reduce-window(f32[16,128]{1,0:T(8,128)S(1)} %sub.118, f32[]{:T(128)} %constant.12.clone.1), window={size=1x128 pad=0_0x0_127}, to_apply=%region_20.21 | reduce-window | flops 260096 | bytes 16388 | tf_op jit(solution)/shard_map/body/reduce_window_sum | solution.py:224
  83.0 2.3 %convolution_add_fusion.4 = f32[16,128,64]{1,2,0:T(8,128)S(1)} fusion(f32[16,128,64]{1,2,0:T(8,128)} %fusion.10, f32[16,128,128]{2,1,0:T(8,128)S(1)} %copy-done.5, f32[16,128,64]{1,2,0:T(8,128)} %bitcast.193), kind=kOutput, calls=%fused_computation.24 | convolution fusion | flops 201457664 | bytes 2621440 | tf_op jit(solution)/shard_map/hts,htn->hsn/dot_general | solution.py:194
  85.4 0.7 copy.61
  86.4 1.0 %copy.60 = bf16[16,128,128]{2,1,0:T(8,128)(2,1)} copy(bf16[16,128,128]{1,2,0:T(8,128)(2,1)S(1)} %copy-done.19) | data formatting | bytes 1048576
  87.4 0.7 broadcast_add_fusion
  (100 shorter events, 3.3 us)
Async XLA Ops:
  0.6 17.0 %copy-start = (bf16[16,128,128]{2,1,0:T(8,128)(2,1)S(1)}, bf16[16,128,128]{2,1,0:T(8,128)(2,1)}, u32[]{:S(2)}) copy-start(bf16[16,128,128]{2,1,0:T(8,128)(2,1)} %param.7) | copy-start | bytes 1572868
  0.6 9.2 %copy-start.20 = (bf16[2,128,128]{2,1,0:T(8,128)(2,1)S(1)}, bf16[2,128,128]{2,1,0:T(8,128)(2,1)}, u32[]{:S(2)}) copy-start(bf16[2,128,128]{2,1,0:T(8,128)(2,1)} %param.10) | copy-start | bytes 196612
  0.7 9.5 %copy-start.1 = (bf16[16,128,128]{2,1,0:T(8,128)(2,1)S(1)}, bf16[16,128,128]{2,1,0:T(8,128)(2,1)}, u32[]{:S(2)}) copy-start(bf16[16,128,128]{2,1,0:T(8,128)(2,1)} %param.9) | copy-start | bytes 1572868
  0.7 21.3 %collective-permute-start.5 = (bf16[2,128,256]{2,1,0:T(8,128)(2,1)}, bf16[2,128,256]{2,1,0:T(8,128)(2,1)}, u32[]{:S(2)}, u32[]{:S(2)}) collective-permute-start(bf16[2,128,256]{2,1,0:T(8,128)(2,1)} %param.8), channel_id=1, source_target_pairs={{0,12},{1,13},{2,14},{3,15},{16,28},{17,29},{18,30},{19,31}} | collective-permute-start | bytes 393224 | tf_op jit(solution)/shard_map/ppermute | solution.py:66
  2.1 17.8 %collective-permute-start.3 = (bf16[2,128,256]{2,1,0:T(8,128)(2,1)}, bf16[2,128,256]{2,1,0:T(8,128)(2,1)}, u32[]{:S(2)}, u32[]{:S(2)}) collective-permute-start(bf16[2,128,256]{2,1,0:T(8,128)(2,1)} %param.8), channel_id=1, source_target_pairs={{0,4},{4,8},{8,12},{1,5},{5,9},{9,13},{2,6},{6,10},{10,14},{3,7},{... | collective-permute-start | bytes 393224 | tf_op jit(solution)/shard_map/ppermute | solution.py:66
  5.6 17.9 %collective-permute-start.4 = (bf16[2,128,256]{2,1,0:T(8,128)(2,1)}, bf16[2,128,256]{2,1,0:T(8,128)(2,1)}, u32[]{:S(2)}, u32[]{:S(2)}) collective-permute-start(bf16[2,128,256]{2,1,0:T(8,128)(2,1)} %param.8), channel_id=1, source_target_pairs={{0,8},{4,12},{1,9},{5,13},{2,10},{6,14},{3,11},{7,15},{16,24},{20,... | collective-permute-start | bytes 393224 | tf_op jit(solution)/shard_map/ppermute | solution.py:66
  10.1 52.5 %copy-start.8 = (f32[2,8,128,64]{2,3,1,0:T(8,128)}, f32[2,8,128,64]{2,3,1,0:T(8,128)S(1)}, u32[]{:S(2)}) copy-start(f32[2,8,128,64]{2,3,1,0:T(8,128)S(1)} %broadcast_in_dim.97) | copy-start | bytes 1572868
  11.4 23.5 %collective-permute-start.1 = (bf16[1040,128]{1,0:T(8,128)(2,1)}, bf16[1040,128]{1,0:T(8,128)(2,1)S(1)}, u32[]{:S(2)}, u32[]{:S(2)}) collective-permute-start(bf16[1040,128]{1,0:T(8,128)(2,1)} %pad_maximum_fusion.1), channel_id=1, source_target_pairs={{0,8},{4,12},{1,9},{5,13},{2,10},{6,14},{3,11},{7,15},{16,24},{20,... | collective-permute-start | bytes 798728 | tf_op jit(solution)/shard_map/ppermute | solution.py:66
  12.7 27.2 %collective-permute-start = (bf16[1040,128]{1,0:T(8,128)(2,1)}, bf16[1040,128]{1,0:T(8,128)(2,1)}, u32[]{:S(2)}, u32[]{:S(2)}) collective-permute-start(bf16[1040,128]{1,0:T(8,128)(2,1)} %pad_maximum_fusion.1), channel_id=1, source_target_pairs={{0,4},{4,8},{8,12},{1,5},{5,9},{9,13},{2,6},{6,10},{10,14},{3,7},{... | collective-permute-start | bytes 798728 | tf_op jit(solution)/shard_map/ppermute | solution.py:66
  15.3 2.3 %copy-start.2 = (f32[16,128,128]{2,1,0:T(8,128)}, f32[16,128,128]{2,1,0:T(8,128)S(1)}, u32[]{:S(2)}) copy-start(f32[16,128,128]{2,1,0:T(8,128)S(1)} %bitcast_multiply_fusion.1) | copy-start | bytes 3145732
  15.3 2.3 %copy-start.21 = (bf16[2,128,256]{2,1,0:T(8,128)(2,1)S(1)}, bf16[2,128,256]{2,1,0:T(8,128)(2,1)}, u32[]{:S(2)}) copy-start(bf16[2,128,256]{2,1,0:T(8,128)(2,1)} %param.8) | copy-start | bytes 393220
  19.9 20.6 %collective-permute-start.2 = (bf16[1040,128]{1,0:T(8,128)(2,1)}, bf16[1040,128]{1,0:T(8,128)(2,1)S(1)}, u32[]{:S(2)}, u32[]{:S(2)}) collective-permute-start(bf16[1040,128]{1,0:T(8,128)(2,1)} %pad_maximum_fusion.1), channel_id=1, source_target_pairs={{0,12},{1,13},{2,14},{3,15},{16,28},{17,29},{18,30},{19,31}} | collective-permute-start | bytes 798728 | tf_op jit(solution)/shard_map/ppermute | solution.py:66
  23.1 1.6 %copy-start.6 = (f32[2,8,128,128]{2,3,1,0:T(8,128)S(1)}, f32[2,8,128,128]{2,3,1,0:T(8,128)}, u32[]{:S(2)}) copy-start(f32[2,8,128,128]{2,3,1,0:T(8,128)} %get-tuple-element.46) | copy-start | bytes 3145732
  23.1 1.6 %copy-start.22 = (bf16[2,128,256]{2,1,0:T(8,128)(2,1)S(1)}, bf16[2,128,256]{2,1,0:T(8,128)(2,1)}, u32[]{:S(2)}) copy-start(bf16[2,128,256]{2,1,0:T(8,128)(2,1)} %param.8) | copy-start | bytes 393220
  23.5 1.2 %copy-start.23 = (f32[2,8,128]{2,1,0:T(8,128)S(1)}, f32[2,8,128]{2,1,0:T(8,128)}, u32[]{:S(2)}) copy-start(f32[2,8,128]{2,1,0:T(8,128)} %get-tuple-element.45) | copy-start | bytes 24580
  28.4 12.3 %copy-start.11 = (f32[16,128,128]{1,2,0:T(8,128)S(1)}, f32[16,128,128]{1,2,0:T(8,128)}, u32[]{:S(2)}) copy-start(f32[16,128,128]{1,2,0:T(8,128)} %fusion.104) | copy-start | bytes 3145732
  29.8 11.0 %copy-start.16 = (f32[16,64,128]{2,1,0:T(8,128)S(1)}, f32[16,64,128]{2,1,0:T(8,128)}, u32[]{:S(2)}) copy-start(f32[16,64,128]{2,1,0:T(8,128)} %param.13) | copy-start | bytes 1572868
  34.9 16.5 %copy-start.12 = (bf16[1040,128]{1,0:T(8,128)(2,1)}, bf16[1040,128]{1,0:T(8,128)(2,1)S(1)}, u32[]{:S(2)}) copy-start(bf16[1040,128]{1,0:T(8,128)(2,1)S(1)} %collective-permute-done.1) | copy-start | bytes 798724
  40.6 10.8 %copy-start.14 = (bf16[1040,128]{1,0:T(8,128)(2,1)}, bf16[1040,128]{1,0:T(8,128)(2,1)S(1)}, u32[]{:S(2)}) copy-start(bf16[1040,128]{1,0:T(8,128)(2,1)S(1)} %collective-permute-done.2) | copy-start | bytes 798724
  40.7 7.6 %copy-start.7 = (f32[2,8,128,64]{2,3,1,0:T(8,128)}, f32[2,8,128,64]{2,3,1,0:T(8,128)S(1)}, u32[]{:S(2)}) copy-start(f32[2,8,128,64]{2,3,1,0:T(8,128)S(1)} %broadcast_in_dim.100) | copy-start | bytes 1572868
  40.7 0.7 copy-start.24
  44.9 1.2 %copy-start.3 = (f32[16,128,128]{2,1,0:T(8,128)S(1)}, f32[16,128,128]{2,1,0:T(8,128)}, u32[]{:S(2)}) copy-start(f32[16,128,128]{2,1,0:T(8,128)} %copy-done.2) | copy-start | bytes 3145732
  51.4 1.0 %slice-start = ((bf16[1040,128]{1,0:T(8,128)(2,1)}), bf16[1024,128]{1,0:T(8,128)(2,1)S(1)}, s32[]{:S(2)}) async-start(bf16[1040,128]{1,0:T(8,128)(2,1)} %copy-done.12), calls=%async_computation | async-start | bytes 524288 | tf_op jit(solution)/shard_map/slice | solution.py:38
  54.7 5.5 %copy-start.13 = (bf16[1040,128]{1,0:T(8,128)(2,1)S(1)}, bf16[1040,128]{1,0:T(8,128)(2,1)}, u32[]{:S(2)}) copy-start(bf16[1040,128]{1,0:T(8,128)(2,1)} %copy-done.12) | copy-start | bytes 798724
  54.7 5.5 %copy-start.15 = (bf16[1040,128]{1,0:T(8,128)(2,1)S(1)}, bf16[1040,128]{1,0:T(8,128)(2,1)}, u32[]{:S(2)}) copy-start(bf16[1040,128]{1,0:T(8,128)(2,1)} %copy-done.14) | copy-start | bytes 798724
  54.7 5.5 %copy-start.17 = (f32[16,64,128]{2,1,0:T(8,128)S(1)}, f32[16,64,128]{2,1,0:T(8,128)}, u32[]{:S(2)}) copy-start(f32[16,64,128]{2,1,0:T(8,128)} %param.13) | copy-start | bytes 1572868
  54.7 10.8 %collective-permute-start.8 = (bf16[1040,128]{1,0:T(8,128)(2,1)S(1)}, bf16[1040,128]{1,0:T(8,128)(2,1)S(1)}, u32[]{:S(2)}, u32[]{:S(2)}) collective-permute-start(bf16[1040,128]{1,0:T(8,128)(2,1)S(1)} %pad_maximum_fusion.2), channel_id=1, source_target_pairs={{12,0},{13,1},{14,2},{15,3},{28,16},{29,17},{30,18},{31,19}} | collective-permute-start | bytes 798728 | tf_op jit(solution)/shard_map/ppermute | solution.py:66
  55.5 12.1 %collective-permute-start.7 = (bf16[1040,128]{1,0:T(8,128)(2,1)S(1)}, bf16[1040,128]{1,0:T(8,128)(2,1)S(1)}, u32[]{:S(2)}, u32[]{:S(2)}) collective-permute-start(bf16[1040,128]{1,0:T(8,128)(2,1)S(1)} %pad_maximum_fusion.2), channel_id=1, source_target_pairs={{8,0},{12,4},{9,1},{13,5},{10,2},{14,6},{11,3},{15,7},{24,16},{28,... | collective-permute-start | bytes 798728 | tf_op jit(solution)/shard_map/ppermute | solution.py:66
  56.8 19.9 %collective-permute-start.6 = (bf16[1040,128]{1,0:T(8,128)(2,1)S(1)}, bf16[1040,128]{1,0:T(8,128)(2,1)S(1)}, u32[]{:S(2)}, u32[]{:S(2)}) collective-permute-start(bf16[1040,128]{1,0:T(8,128)(2,1)S(1)} %pad_maximum_fusion.2), channel_id=1, source_target_pairs={{4,0},{8,4},{12,8},{5,1},{9,5},{13,9},{6,2},{10,6},{14,10},{7,3},{... | collective-permute-start | bytes 798728 | tf_op jit(solution)/shard_map/ppermute | solution.py:66
  60.2 2.4 %copy-start.4 = (f32[16,128,128]{2,1,0:T(8,128)}, f32[16,128,128]{2,1,0:T(8,128)S(1)}, u32[]{:S(2)}) copy-start(f32[16,128,128]{2,1,0:T(8,128)S(1)} %convolution_multiply_fusion) | copy-start | bytes 3145732
  77.0 2.0 %copy-start.9 = (f32[2,8,128,64]{2,3,1,0:T(8,128)S(1)}, f32[2,8,128,64]{2,3,1,0:T(8,128)}, u32[]{:S(2)}) copy-start(f32[2,8,128,64]{2,3,1,0:T(8,128)} %copy-done.8) | copy-start | bytes 1572868
  77.0 2.0 %copy-start.10 = (f32[16,128,128]{1,2,0:T(8,128)S(1)}, f32[16,128,128]{1,2,0:T(8,128)}, u32[]{:S(2)}) copy-start(f32[16,128,128]{1,2,0:T(8,128)} %get-tuple-element.54) | copy-start | bytes 3145732
  78.9 4.1 %copy-start.5 = (f32[16,128,128]{2,1,0:T(8,128)S(1)}, f32[16,128,128]{2,1,0:T(8,128)}, u32[]{:S(2)}) copy-start(f32[16,128,128]{2,1,0:T(8,128)} %copy-done.4) | copy-start | bytes 3145732
  83.0 2.3 %copy-start.18 = (f32[16,128,64]{1,2,0:T(8,128)S(1)}, f32[16,128,64]{1,2,0:T(8,128)}, u32[]{:S(2)}) copy-start(f32[16,128,64]{1,2,0:T(8,128)} %convolution_add_fusion.3) | copy-start | bytes 1572868
  85.3 1.0 %copy-start.19 = (bf16[16,128,128]{1,2,0:T(8,128)(2,1)S(1)}, bf16[16,128,128]{1,2,0:T(8,128)(2,1)}, u32[]{:S(2)}) copy-start(bf16[16,128,128]{1,2,0:T(8,128)(2,1)} %get-tuple-element.26) | copy-start | bytes 1572868
where the time goes:
time: 88.9 us; the launch traced here: 88.1 us
  matrix products  33.3 us (37%)
  waiting for transfers between devices  21.6 us (24%)
  starting transfers between devices  16.2 us (18%)
  other arithmetic  9.21 us (10%)
  local copies, waits for them, and re-layouts  6.37 us (7%)
  between operations  1.34 us (2%)
    ppermute x9, waiting for transfers between devices, shifted(): moved.append(lax.ppermute(x, 'seq', pairs))  21.6 us
    ppermute x9, starting transfers between devices, shifted(): moved.append(lax.ppermute(x, 'seq', pairs))  16.2 us
    dot_general x4, matrix products, teacher_rows(): jnp.einsum('gptd,gkd->gptk', grouped, block[..., :head_width], preferred_...  5.34 us
    dot_general x4, matrix products, teacher_rows(): jnp.einsum('gptk,gkd->gptd', exponentials.astype(jnp.bfloat16), block[......  4.05 us
    unnamed x56, local copies, waits for them, and re-layouts  3.95 us
    dot_general x1, matrix products, body(): jnp.einsum('htn,hnp->htp', out_heads, entering, precision=highest)  3.08 us
    dot_general x1, matrix products, body(): jnp.einsum('hts,hsn->htn', paired, in_heads, precision=highest)  2.93 us
    dot_general x1, matrix products, body(): jnp.einsum('hsn,hnp->hsp', weighted_in, incoming, precision=highest)  2.84 us
  transfers between devices with their start and end apart: 9, of which 5 were waited for; matrix products, arithmetic and copies ran while one was open for 27% of the time, Pallas kernels for 0%

commit v1 on v0

--- a/solution.py
+++ b/solution.py
@@ -20,8 +20,8 @@
     return wide[..., 0, :] + wide[..., 1, :] + wide[..., 2, :]
 
 
-def pack_rows(big, smalls):
-    rows = big.astype(jnp.bfloat16).reshape(-1, 128)
+def pack_rows(bigs, smalls):
+    rows = jnp.concatenate([b.astype(jnp.bfloat16).reshape(-1, 128) for b in bigs], axis=0)
     vector = jnp.concatenate([v.reshape(-1) for v in smalls])
     padded = -(-vector.shape[0] // 128) * 128
     vector = jnp.pad(vector, (0, padded - vector.shape[0]))
@@ -30,12 +30,16 @@
     return jnp.concatenate([rows, extra], axis=0)
 
 
-def unpack_rows(received, big_shape, small_shapes):
-    big_rows = 1
-    for d in big_shape:
-        big_rows *= d
-    big_rows //= 128
-    big = received[:big_rows].reshape(big_shape)
+def unpack_rows(received, big_shapes, small_shapes):
+    bigs = []
+    big_rows = 0
+    for shape in big_shapes:
+        count = 1
+        for d in shape:
+            count *= d
+        count //= 128
+        bigs.append(received[big_rows : big_rows + count].reshape(shape))
+        big_rows += count
     sizes = []
     for shape in small_shapes:
         size = 1
@@ -50,7 +54,7 @@
     for shape, size in zip(small_shapes, sizes):
         smalls.append(vector[offset : offset + size].reshape(shape))
         offset += size
-    return big, smalls
+    return bigs, smalls
 
 
 def shifted(x, step):
@@ -77,16 +81,14 @@
 
 def teacher_rows(queries, kv_list, seq_rank):
     local_heads, tok_dev, head_width = queries.shape
-    local_groups = kv_list[0].shape[0]
+    local_groups = kv_list[0][0].shape[0]
     per_group = local_heads // local_groups
     grouped = queries.reshape(local_groups, per_group, tok_dev, head_width)
     rows = jnp.arange(tok_dev)
     within = rows[:, None] >= rows[None, :]
     block_scores = []
-    for distance, block in enumerate(kv_list):
-        scores = jnp.einsum(
-            "gptd,gkd->gptk", grouped, block[..., :head_width], preferred_element_type=jnp.float32
-        )
+    for distance, (keys, _) in enumerate(kv_list):
+        scores = jnp.einsum("gptd,gkd->gptk", grouped, keys, preferred_element_type=jnp.float32)
         scores = scores * head_width ** (-0.5)
         if distance == 0:
             allowed = within
@@ -98,13 +100,13 @@
         highest_score = jnp.maximum(highest_score, scores.max(axis=3, keepdims=True))
     row_sums = None
     mixed = None
-    for scores, block in zip(block_scores, kv_list):
+    for scores, (_, values) in zip(block_scores, kv_list):
         exponentials = jnp.exp(scores - highest_score)
         part_sum = jnp.sum(exponentials, axis=3, keepdims=True)
         part = jnp.einsum(
             "gptk,gkd->gptd",
             exponentials.astype(jnp.bfloat16),
-            block[..., head_width:],
+            values,
             preferred_element_type=jnp.float32,
         )
         row_sums = part_sum if row_sums is None else row_sums + part_sum
@@ -120,8 +122,6 @@
     state_size = state_maps.shape[2] // 2
     seq_count = lax.axis_size("seq")
     seq_rank = lax.axis_index("seq")
-
-    kv_earlier = shifted(keys_values, 1)
 
     log_decay = jax.nn.log_sigmoid(decay_logit)
     cumulative = jnp.cumsum(log_decay, axis=1)
@@ -136,12 +136,18 @@
     weighted_in = in_heads * to_end[..., None]
     end_state = jnp.einsum("hsn,hsp->hnp", weighted_in, inputs_wide, precision=highest)
 
-    state_earlier = shifted(pack_rows(end_state, [totals]), 1)
+    own_keys = keys_values[..., :head_width]
+    own_values = keys_values[..., head_width:]
+    state_earlier = shifted(pack_rows([own_keys, own_values, end_state], [totals]), 1)
+    kv_earlier = []
     ends_earlier = []
     prefix_state = jnp.zeros_like(end_state)
     gap = jnp.zeros_like(totals)
     for distance, received in enumerate(state_earlier, start=1):
-        ends, (totals_there,) = unpack_rows(received, end_state.shape, [totals.shape])
+        (keys_there, values_there, ends), (totals_there,) = unpack_rows(
+            received, [own_keys.shape, own_values.shape, end_state.shape], [totals.shape]
+        )
+        kv_earlier.append((keys_there, values_there))
         valid = distance <= seq_rank
         totals_there = jnp.where(valid, totals_there, 0.0)
         weight = jnp.where(valid, jnp.exp(gap), 0.0)
@@ -160,7 +166,7 @@
     ).reshape(local_heads, tok_dev, tok_dev)
     local_out = jnp.einsum("hts,hsp->htp", mixing, inputs_wide, precision=highest)
 
-    teacher = teacher_rows(queries, [keys_values] + kv_earlier, seq_rank)
+    teacher = teacher_rows(queries, [(own_keys, own_values)] + kv_earlier, seq_rank)
     teacher_wide = teacher.astype(jnp.float32)
     target = teacher_wide * lax.rsqrt(
         jnp.mean(teacher_wide * teacher_wide, axis=2, keepdims=True) + epsilon
@@ -187,7 +193,7 @@
     else:
         ends_dot_flow = jnp.zeros((1,) + totals.shape, jnp.float32)
 
-    flow_later = shifted(pack_rows(flow, [totals, closing, ends_dot_flow]), -1)
+    flow_later = shifted(pack_rows([flow], [totals, closing, ends_dot_flow]), -1)
 
     cross = jnp.einsum("htp,hsp->hts", grad_out, inputs_wide, precision=highest)
     paired = decayed * cross
@@ -203,8 +209,8 @@
     through = []
     dots_there = []
     for distance, received in enumerate(flow_later, start=1):
-        flows, (totals_there, closing_there, dots) = unpack_rows(
-            received, flow.shape, [totals.shape, closing.shape, ends_dot_flow.shape]
+        (flows,), (totals_there, closing_there, dots) = unpack_rows(
+            received, [flow.shape], [totals.shape, closing.shape, ends_dot_flow.shape]
         )
         valid = seq_rank + distance < seq_count
         totals_there = jnp.where(valid, totals_there, 0.0)

time: 88.9 us -> 100 us (1.12)
  waiting for transfers between devices: 21.6 us -> 35.2 us
  local copies, waits for them, and re-layouts: 6.37 us -> 12 us
  matrix products: 33.3 us -> 27.7 us
  starting transfers between devices: 16.2 us -> 12 us
  other arithmetic: 9.21 us -> 11.2 us
    ppermute x9 -> x6, waiting for transfers between devices: 21.6 us -> 35.2 us  [shifted(): moved.append(lax.ppermute(x, 'seq', pairs))]
    dot_general x8, matrix products: 9.39 us -> 4.26 us  [the longest x4 2.8 us: teacher_rows(): jnp.einsum('gptd,gkd->gptk', grouped, keys, preferred_element_type=jnp.fl...]
    ppermute x9 -> x6, starting transfers between devices: 16.2 us -> 12 us  [shifted(): moved.append(lax.ppermute(x, 'seq', pairs))]
    unnamed x56 -> x84, local copies, waits for them, and re-layouts: 3.95 us -> 8.05 us
    dot_general x1, matrix products: 2.26 us -> 1.21 us  [body(): jnp.einsum('hts,hsp->htp', mixing, inputs_wide, precision=highest)]
    slice x6 -> x10, local copies, waits for them, and re-layouts: 1.94 us -> 2.87 us  [the longest x9 2.84 us: unpack_rows(): bigs.append(received[big_rows:big_rows + count].reshape(shape))]
  transfers between devices with their start and end apart: 9 -> 6, of which waited for: 5 -> 4; matrix products, arithmetic and copies ran while one was open for 27% -> 12% of each run, Pallas kernels for 0% -> 0%
where the time goes in v1:
time: 100 us; the launch traced here: 99.5 us
  waiting for transfers between devices  35.2 us (35%)
  matrix products  27.7 us (28%)
  local copies, waits for them, and re-layouts  12 us (12%)
  starting transfers between devices  12 us (12%)
  other arithmetic  11.2 us (11%)
  between operations  1.36 us (1%)
    ppermute x6, waiting for transfers between devices, shifted(): moved.append(lax.ppermute(x, 'seq', pairs))  35.2 us
    ppermute x6, starting transfers between devices, shifted(): moved.append(lax.ppermute(x, 'seq', pairs))  12 us
    unnamed x84, local copies, waits for them, and re-layouts  8.05 us
    dot_general x1, matrix products, body(): jnp.einsum('htn,hnp->htp', out_heads, entering, precision=highest)  3.1 us
    dot_general x1, matrix products, body(): jnp.einsum('hts,hsn->htn', paired, in_heads, precision=highest)  2.93 us
    slice x9, local copies, waits for them, and re-layouts, unpack_rows(): bigs.append(received[big_rows:big_rows + count].reshape(shape))  2.84 us
    dot_general x1, matrix products, body(): jnp.einsum('hsn,hnp->hsp', weighted_in, incoming, precision=highest)  2.84 us
    dot_general x4, matrix products, teacher_rows(): jnp.einsum('gptd,gkd->gptk', grouped, keys, preferred_element_type=jnp.fl...  2.8 us
  transfers between devices with their start and end apart: 6, of which 4 were waited for; matrix products, arithmetic and copies ran while one was open for 12% of the time, Pallas kernels for 0%

profile of v1, /device:TPU:8, one launch (start us, length us, event | category | flops | bytes accessed | tf_op | source)
XLA Modules:
  0.0 99.5 jit_solution(9098153848863729728)
XLA Ops:
  0.7 0.8 fusion.53
  1.9 0.6 copy-done.28
  2.5 0.6 subtract_exponential_fusion.4
  3.3 0.7 copy-done.17
  4.3 0.5 convolution_convert_fusion
  4.8 0.8 pad_maximum_fusion.1
  5.6 0.7 collective-permute-start.2
  6.3 3.5 %collective-permute-start = (bf16[1552,128]{1,0:T(8,128)(2,1)}, bf16[1552,128]{1,0:T(8,128)(2,1)S(1)}, u32[]{:S(2)}, u32[]{:S(2)}) collective-permute-start(bf16[1552,128]{1,0:T(8,128)(2,1)} %pad_maximum_fusion.1), channel_id=1, source_target_pairs={{0,4},{4,8},{8,12},{1,5},{5,9},{9,13},{2,6},{6,10},{10,14},{3,7},{... | collective-permute-start | bytes 1191944 | tf_op jit(solution)/shard_map/ppermute | solution.py:70
  9.8 3.7 %collective-permute-start.1 = (bf16[1552,128]{1,0:T(8,128)(2,1)}, bf16[1552,128]{1,0:T(8,128)(2,1)}, u32[]{:S(2)}, u32[]{:S(2)}) collective-permute-start(bf16[1552,128]{1,0:T(8,128)(2,1)} %pad_maximum_fusion.1), channel_id=1, source_target_pairs={{0,8},{4,12},{1,9},{5,13},{2,10},{6,14},{3,11},{7,15},{16,24},{20,... | collective-permute-start | bytes 1191944 | tf_op jit(solution)/shard_map/ppermute | solution.py:70
  13.5 1.9 %fusion.109 = (f32[2,8,128]{2,1,0:T(8,128)}, f32[2,8,128,128]{2,3,1,0:T(8,128)}) fusion(bf16[2,8,128,128]{3,2,1,0:T(8,128)(2,1)S(1)} %bitcast.193, bf16[2,128,256]{2,1,0:T(8,128)(2,1)S(1)} %copy-done.17, pred[128,128]{0,1:T(8,128)(4,1)S(1)} %iota_compare_fusion), kind=kOutput, calls=%fused_computation.198 | convolution fusion | flops 67893248 | bytes 1662976 | tf_op jit(solution)/shard_map/gptd,gkd->gptk/dot_general | solution.py:91
  16.0 0.7 copy.83
  17.0 1.2 %fusion.111 = f32[16,128,128]{1,2,0:T(8,128)S(1)} fusion(f32[16,128,128]{2,1,0:T(8,128)S(1)} %bitcast_multiply_fusion.1, bf16[16,128,128]{2,1,0:T(8,128)(2,1)S(1)} %copy-done.1), kind=kOutput, calls=%fused_computation.200 | convolution fusion | flops 402653184 | bytes 2621440 | tf_op jit(solution)/shard_map/hts,hsp->htp/dot_general | solution.py:167
  18.3 12.1 %collective-permute-done = bf16[1552,128]{1,0:T(8,128)(2,1)S(1)} collective-permute-done((bf16[1552,128]{1,0:T(8,128)(2,1)}, bf16[1552,128]{1,0:T(8,128)(2,1)S(1)}, u32[]{:S(2)}, u32[]{:S(2)}) %collective-permute-start) | collective-permute-done | bytes 397344 | tf_op jit(solution)/shard_map/ppermute | solution.py:70
  30.3 0.7 copy-done.9
  31.7 12.3 %collective-permute-done.1 = bf16[1552,128]{1,0:T(8,128)(2,1)} collective-permute-done((bf16[1552,128]{1,0:T(8,128)(2,1)}, bf16[1552,128]{1,0:T(8,128)(2,1)}, u32[]{:S(2)}, u32[]{:S(2)}) %collective-permute-start.1) | collective-permute-done | bytes 397344 | tf_op jit(solution)/shard_map/ppermute | solution.py:70
  44.1 0.9 fusion.102
  46.5 1.0 fusion.20
  47.9 0.4 multiply_reduce_fusion.2
  48.4 0.7 slice_convert_fusion.4
  49.3 0.4 copy-done.34
  50.0 3.1 %multiply_reduce_fusion.3 = (f32[16,128]{1,0:T(8,128)S(1)}, f32[16,128,128]{1,2,0:T(8,128)S(1)}) fusion(bf16[16,128,128]{1,2,0:T(8,128)(2,1)S(1)} %copy.48, f32[16]{0:T(128)S(1)} %copy-done.30, f32[16,128,128]{1,2,0:T(8,128)S(1)} %fusion.111, f32[16,128,64]{1,2,0:T(8,128)S(1)} %bitcast.197, f32[16,64,128]{2,1,0:T(8,128)S(1)} %copy-done.12, ...), kind=kOutput, calls=%fused_computation.48 | convolution fusion | flops 204470272 | bytes 4474884 | tf_op jit(solution)/shard_map/htn,hnp->htp/dot_general | solution.py:175
  53.1 0.4 multiply_reduce_fusion.1
  53.6 1.2 %multiply_reduce_fusion = (f32[16,128]{1,0:T(8,128)}, f32[16,128,128]{1,2,0:T(8,128)S(1)}) fusion(f32[16,128,128]{1,2,0:T(8,128)S(1)} %get-tuple-element.60, f32[16,128]{1,0:T(8,128)S(1)} %broadcast_multiply_fusion, f32[16,128]{1,0:T(8,128)S(1)} %rsqrt_bitcast_fusion, f32[2,8,128,128]{2,3,1,0:T(8,128)S(1)} %get-tuple-element.58, ...), kind=kLoop, calls=%fused_computation.40 | loop fusion | flops 2881536 | bytes 3702848 | tf_op jit(solution)/shard_map/reduce_sum | solution.py:183
  54.8 2.7 %fusion.15 = (f32[16,128]{1,0:T(8,128)}, f32[16,128,128]{1,2,0:T(8,128)}) fusion(bf16[16,128,128]{1,2,0:T(8,128)(2,1)S(1)} %copy.48, f32[16,128,128]{2,1,0:T(8,128)S(1)} %bitcast_multiply_fusion.1, f32[16,128,128]{1,2,0:T(8,128)S(1)} %get-tuple-element.22), kind=kOutput, calls=%fused_computation.32 | convolution fusion | flops 403437568 | bytes 3678208 | tf_op jit(solution)/shard_map/hts,htp->hsp/dot_general | solution.py:187
  57.5 2.1 %fusion.40 = f32[16,64,128]{2,1,0:T(8,128)S(1)} fusion(f32[16,128,128]{1,2,0:T(8,128)S(1)} %get-tuple-element.22, f32[16,128,64]{1,2,0:T(8,128)S(1)} %bitcast.198, f32[16,128]{1,0:T(8,128)S(1)} %copy-done.23), kind=kOutput, calls=%fused_computation.77 | convolution fusion | flops 201457664 | bytes 2105344 | tf_op jit(solution)/shard_map/htn,htp->hnp/dot_general | solution.py:184
  59.6 1.0 slice.242
  60.6 0.9 slice-done
  61.5 1.0 fusion.29
  62.5 0.7 reshape.257
  63.2 0.8 subtract_reduce_fusion
  64.2 1.0 pad_maximum_fusion.2
  65.2 0.8 collective-permute-start.5
  66.0 1.3 %collective-permute-start.4 = (bf16[1040,128]{1,0:T(8,128)(2,1)S(1)}, bf16[1040,128]{1,0:T(8,128)(2,1)S(1)}, u32[]{:S(2)}, u32[]{:S(2)}) collective-permute-start(bf16[1040,128]{1,0:T(8,128)(2,1)S(1)} %pad_maximum_fusion.2), channel_id=1, source_target_pairs={{8,0},{12,4},{9,1},{13,5},{10,2},{14,6},{11,3},{15,7},{24,16},{28,... | collective-permute-start | bytes 798728 | tf_op jit(solution)/shard_map/ppermute | solution.py:70
  67.3 2.1 %collective-permute-start.3 = (bf16[1040,128]{1,0:T(8,128)(2,1)S(1)}, bf16[1040,128]{1,0:T(8,128)(2,1)S(1)}, u32[]{:S(2)}, u32[]{:S(2)}) collective-permute-start(bf16[1040,128]{1,0:T(8,128)(2,1)S(1)} %pad_maximum_fusion.2), channel_id=1, source_target_pairs={{4,0},{8,4},{12,8},{5,1},{9,5},{13,9},{6,2},{10,6},{14,10},{7,3},{... | collective-permute-start | bytes 798728 | tf_op jit(solution)/shard_map/ppermute | solution.py:70
  69.4 1.2 %convolution_multiply_fusion = f32[16,128,128]{2,1,0:T(8,128)S(1)} fusion(f32[16,128,128]{1,2,0:T(8,128)S(1)} %get-tuple-element.22, bf16[16,128,128]{2,1,0:T(8,128)(2,1)S(1)} %copy-done.1, f32[16,128]{1,0:T(8,128)S(1)} %reduce_window_sum.21, pred[128,128]{1,0:T(8,128)(4,1)S(1)} %copy-done.20), kind=kOutput, calls=%fused_computation.3 | convolution fusion | flops 403701760 | bytes 2646016 | tf_op jit(solution)/shard_map/htp,hsp->hts/dot_general | solution.py:198
  70.7 2.3 %convolution_multiply_fusion.6 = f32[16,128,64]{1,2,0:T(8,128)S(1)} fusion(f32[16,128,128]{1,2,0:T(8,128)S(1)} %get-tuple-element.22, f32[16,128]{1,0:T(8,128)S(1)} %copy-done.24, f32[16,64,128]{2,1,0:T(8,128)S(1)} %copy-done.13, f32[16]{0:T(128)S(1)} %copy-done.33, f32[16]{0:T(128)S(1)} %copy-done.35, f32[16]{0:T(128)S(1)} %copy-done.37, ...), kind=kOutput, calls=%fused_computation.25 | convolution fusion | flops 202768384 | bytes 2893316 | tf_op jit(solution)/shard_map/hnp,htp->htn/dot_general | solution.py:202
  73.1 2.9 %convolution_add_fusion.3 = f32[16,128,64]{1,2,0:T(8,128)} fusion(f32[16,128,64]{1,2,0:T(8,128)S(1)} %convolution_multiply_fusion.6, f32[16,128,128]{2,1,0:T(8,128)S(1)} %convolution_multiply_fusion, f32[16,128,64]{1,2,0:T(8,128)S(1)} %bitcast.201), kind=kOutput, calls=%fused_computation.26 | convolution fusion | flops 201457664 | bytes 2621440 | tf_op jit(solution)/shard_map/hts,hsn->htn/dot_general | solution.py:201
  76.0 7.1 %collective-permute-done.4 = bf16[1040,128]{1,0:T(8,128)(2,1)S(1)} collective-permute-done((bf16[1040,128]{1,0:T(8,128)(2,1)S(1)}, bf16[1040,128]{1,0:T(8,128)(2,1)S(1)}, u32[]{:S(2)}, u32[]{:S(2)}) %collective-permute-start.4) | collective-permute-done | bytes 266272 | tf_op jit(solution)/shard_map/ppermute | solution.py:70
  83.1 3.8 %collective-permute-done.3 = bf16[1040,128]{1,0:T(8,128)(2,1)S(1)} collective-permute-done((bf16[1040,128]{1,0:T(8,128)(2,1)S(1)}, bf16[1040,128]{1,0:T(8,128)(2,1)S(1)}, u32[]{:S(2)}, u32[]{:S(2)}) %collective-permute-start.3) | collective-permute-done | bytes 266272 | tf_op jit(solution)/shard_map/ppermute | solution.py:70
  87.1 0.7 copy-done.22
  87.8 1.9 %fusion.13 = f32[16,128,64]{1,2,0:T(8,128)} fusion(bf16[16,128,128]{2,1,0:T(8,128)(2,1)S(1)} %copy-done.1, f32[16,128]{1,0:T(8,128)S(1)} %copy-done.22, bf16[16,64,128]{2,1,0:T(8,128)(2,1)S(1)} %bitcast.207, f32[16,64,128]{2,1,0:T(8,128)S(1)} %bitcast.203, bf16[16,64,128]{2,1,0:T(8,128)(2,1)S(1)} %bitcast.205, f32[16]{0:T(128)S(1)} %get-tuple-element.41, ...), kind=kOutput, calls=%fused_computation.29 | convolution fusion | flops 202244096 | bytes 2105472 | tf_op jit(solution)/shard_map/hnp,hsp->hsn/dot_general | solution.py:233
  89.8 0.6 copy-done.31
  90.4 2.8 %fusion.16 = (f32[16,128]{1,0:T(8,128)S(1)}, bf16[16,128,128]{1,2,0:T(8,128)(2,1)}) fusion(bf16[16,128,128]{1,2,0:T(8,128)(2,1)S(1)} %copy.48, f32[16,128,128]{1,2,0:T(8,128)S(1)} %get-tuple-element.22, f32[16]{0:T(128)S(1)} %copy-done.31, f32[16,128,128]{1,2,0:T(8,128)S(1)} %copy-done.8, bf16[16,64,128]{2,1,0:T(8,128)(2,1)S(1)} %bitcast.208, ...), kind=kOutput, calls=%fused_computation.33 | convolution fusion | flops 204077056 | bytes 4735168 | tf_op jit(solution)/shard_map/hsn,hnp->hsp/dot_general | solution.py:228
  93.3 1.2 %reduce_window_sum.22 = f32[16,128]{1,0:T(8,128)S(1)} reduce-window(f32[16,128]{1,0:T(8,128)S(1)} %sub.118, f32[]{:T(128)} %constant.12.clone.1), window={size=1x128 pad=0_0x0_127}, to_apply=%region_20.21 | reduce-window | flops 260096 | bytes 16388 | tf_op jit(solution)/shard_map/body/reduce_window_sum | solution.py:230
  94.5 2.3 %convolution_add_fusion.4 = f32[16,128,64]{1,2,0:T(8,128)S(1)} fusion(f32[16,128,64]{1,2,0:T(8,128)} %fusion.13, f32[16,128,128]{2,1,0:T(8,128)S(1)} %copy-done.4, f32[16,128,64]{1,2,0:T(8,128)} %bitcast.199), kind=kOutput, calls=%fused_computation.27 | convolution fusion | flops 201457664 | bytes 2621440 | tf_op jit(solution)/shard_map/hts,htn->hsn/dot_general | solution.py:200
  96.9 0.7 copy.60
  97.9 1.0 %copy.59 = bf16[16,128,128]{2,1,0:T(8,128)(2,1)} copy(bf16[16,128,128]{1,2,0:T(8,128)(2,1)S(1)} %copy-done.15) | data formatting | bytes 1048576
  98.9 0.7 broadcast_add_fusion
  (126 shorter events, 5.5 us)
Async XLA Ops:
  0.6 12.8 %copy-start = (bf16[16,128,128]{2,1,0:T(8,128)(2,1)S(1)}, bf16[16,128,128]{2,1,0:T(8,128)(2,1)}, u32[]{:S(2)}) copy-start(bf16[16,128,128]{2,1,0:T(8,128)(2,1)} %param.7) | copy-start | bytes 1572868
  0.6 2.5 %copy-start.16 = (bf16[2,128,128]{2,1,0:T(8,128)(2,1)S(1)}, bf16[2,128,128]{2,1,0:T(8,128)(2,1)}, u32[]{:S(2)}) copy-start(bf16[2,128,128]{2,1,0:T(8,128)(2,1)} %param.10) | copy-start | bytes 196612
  1.9 0.6 copy-start.28
  3.1 1.0 %copy-start.21 = (f32[16,128]{1,0:T(8,128)}, f32[16,128]{1,0:T(8,128)S(1)}, u32[]{:S(2)}) copy-start(f32[16,128]{1,0:T(8,128)S(1)} %get-tuple-element.38) | copy-start | bytes 24580
  3.1 0.9 copy-start.17
  3.2 1.1 %copy-start.1 = (bf16[16,128,128]{2,1,0:T(8,128)(2,1)S(1)}, bf16[16,128,128]{2,1,0:T(8,128)(2,1)}, u32[]{:S(2)}) copy-start(bf16[16,128,128]{2,1,0:T(8,128)(2,1)} %param.9) | copy-start | bytes 1572868
  4.1 68.9 %copy-start.6 = (f32[2,8,128,64]{2,3,1,0:T(8,128)}, f32[2,8,128,64]{2,3,1,0:T(8,128)S(1)}, u32[]{:S(2)}) copy-start(f32[2,8,128,64]{2,3,1,0:T(8,128)S(1)} %broadcast_in_dim.99) | copy-start | bytes 1572868
  5.6 25.8 %collective-permute-start.2 = (bf16[1552,128]{1,0:T(8,128)(2,1)}, bf16[1552,128]{1,0:T(8,128)(2,1)S(1)}, u32[]{:S(2)}, u32[]{:S(2)}) collective-permute-start(bf16[1552,128]{1,0:T(8,128)(2,1)} %pad_maximum_fusion.1), channel_id=1, source_target_pairs={{0,12},{1,13},{2,14},{3,15},{16,28},{17,29},{18,30},{19,31}} | collective-permute-start | bytes 1191944 | tf_op jit(solution)/shard_map/ppermute | solution.py:70
  6.3 24.0 %collective-permute-start = (bf16[1552,128]{1,0:T(8,128)(2,1)}, bf16[1552,128]{1,0:T(8,128)(2,1)S(1)}, u32[]{:S(2)}, u32[]{:S(2)}) collective-permute-start(bf16[1552,128]{1,0:T(8,128)(2,1)} %pad_maximum_fusion.1), channel_id=1, source_target_pairs={{0,4},{4,8},{8,12},{1,5},{5,9},{9,13},{2,6},{6,10},{10,14},{3,7},{... | collective-permute-start | bytes 1191944 | tf_op jit(solution)/shard_map/ppermute | solution.py:70
  9.8 34.3 %collective-permute-start.1 = (bf16[1552,128]{1,0:T(8,128)(2,1)}, bf16[1552,128]{1,0:T(8,128)(2,1)}, u32[]{:S(2)}, u32[]{:S(2)}) collective-permute-start(bf16[1552,128]{1,0:T(8,128)(2,1)} %pad_maximum_fusion.1), channel_id=1, source_target_pairs={{0,8},{4,12},{1,9},{5,13},{2,10},{6,14},{3,11},{7,15},{16,24},{20,... | collective-permute-start | bytes 1191944 | tf_op jit(solution)/shard_map/ppermute | solution.py:70
  15.7 1.0 %copy-start.19 = (pred[128,128]{1,0:T(8,128)(4,1)}, pred[128,128]{1,0:T(8,128)(4,1)S(1)}, u32[]{:S(2)}) copy-start(pred[128,128]{1,0:T(8,128)(4,1)S(1)} %copy.42) | copy-start | bytes 49156
  30.3 0.8 copy-start.9
  31.7 13.9 %copy-start.2 = (f32[2,8,128,128]{2,3,1,0:T(8,128)S(1)}, f32[2,8,128,128]{2,3,1,0:T(8,128)}, u32[]{:S(2)}) copy-start(f32[2,8,128,128]{2,3,1,0:T(8,128)} %get-tuple-element.54) | copy-start | bytes 3145732
  44.9 0.7 copy-start.27
  44.9 0.9 copy-start.18
  47.9 1.2 %copy-start.10 = (bf16[1552,128]{1,0:T(8,128)(2,1)S(1)}, bf16[1552,128]{1,0:T(8,128)(2,1)}, u32[]{:S(2)}) copy-start(bf16[1552,128]{1,0:T(8,128)(2,1)} %copy-done.9) | copy-start | bytes 1191940
  47.9 1.3 %copy-start.25 = (bf16[2,128,64]{1,2,0:T(8,128)(2,1)S(1)}, bf16[2,128,64]{1,2,0:T(8,128)(2,1)}, u32[]{:S(2)}) copy-start(bf16[2,128,64]{1,2,0:T(8,128)(2,1)} %copy.83) | copy-start | bytes 98308
  48.4 1.4 %copy-start.12 = (f32[16,64,128]{2,1,0:T(8,128)S(1)}, f32[16,64,128]{2,1,0:T(8,128)}, u32[]{:S(2)}) copy-start(f32[16,64,128]{2,1,0:T(8,128)} %param.13) | copy-start | bytes 1572868
  49.2 0.6 copy-start.34
  49.2 0.6 copy-start.36
  49.2 0.6 copy-start.32
  49.2 0.7 copy-start.23
  49.3 8.2 %copy-start.5 = (f32[2,8,128,64]{2,3,1,0:T(8,128)}, f32[2,8,128,64]{2,3,1,0:T(8,128)S(1)}, u32[]{:S(2)}) copy-start(f32[2,8,128,64]{2,3,1,0:T(8,128)S(1)} %broadcast_in_dim.102) | copy-start | bytes 1572868
  49.3 0.7 copy-start.30
  60.6 1.0 slice-start
  63.2 0.8 copy-start.29
  63.2 0.8 copy-start.38
  64.2 5.3 %copy-start.20 = (pred[128,128]{1,0:T(8,128)(4,1)S(1)}, pred[128,128]{1,0:T(8,128)(4,1)}, u32[]{:S(2)}) copy-start(pred[128,128]{1,0:T(8,128)(4,1)} %copy-done.19) | copy-start | bytes 49156
  65.1 5.5 %copy-start.11 = (bf16[1552,128]{1,0:T(8,128)(2,1)S(1)}, bf16[1552,128]{1,0:T(8,128)(2,1)}, u32[]{:S(2)}) copy-start(bf16[1552,128]{1,0:T(8,128)(2,1)} %copy-done.9) | copy-start | bytes 1191940
  65.2 5.5 %copy-start.13 = (f32[16,64,128]{2,1,0:T(8,128)S(1)}, f32[16,64,128]{2,1,0:T(8,128)}, u32[]{:S(2)}) copy-start(f32[16,64,128]{2,1,0:T(8,128)} %param.13) | copy-start | bytes 1572868
  65.2 5.5 %copy-start.24 = (f32[16,128]{1,0:T(8,128)S(1)}, f32[16,128]{1,0:T(8,128)}, u32[]{:S(2)}) copy-start(f32[16,128]{1,0:T(8,128)} %get-tuple-element.39) | copy-start | bytes 24580
  65.2 5.5 %copy-start.33 = (f32[16]{0:T(128)S(1)}, f32[16]{0:T(128)}, u32[]{:S(2)}) copy-start(f32[16]{0:T(128)} %copy-done.32) | copy-start | bytes 196
  65.2 5.5 %copy-start.35 = (f32[16]{0:T(128)S(1)}, f32[16]{0:T(128)}, u32[]{:S(2)}) copy-start(f32[16]{0:T(128)} %copy-done.34) | copy-start | bytes 196
  65.2 5.5 %copy-start.37 = (f32[16]{0:T(128)S(1)}, f32[16]{0:T(128)}, u32[]{:S(2)}) copy-start(f32[16]{0:T(128)} %copy-done.36) | copy-start | bytes 196
  65.2 10.8 %collective-permute-start.5 = (bf16[1040,128]{1,0:T(8,128)(2,1)S(1)}, bf16[1040,128]{1,0:T(8,128)(2,1)S(1)}, u32[]{:S(2)}, u32[]{:S(2)}) collective-permute-start(bf16[1040,128]{1,0:T(8,128)(2,1)S(1)} %pad_maximum_fusion.2), channel_id=1, source_target_pairs={{12,0},{13,1},{14,2},{15,3},{28,16},{29,17},{30,18},{31,19}} | collective-permute-start | bytes 798728 | tf_op jit(solution)/shard_map/ppermute | solution.py:70
  66.0 17.1 %collective-permute-start.4 = (bf16[1040,128]{1,0:T(8,128)(2,1)S(1)}, bf16[1040,128]{1,0:T(8,128)(2,1)S(1)}, u32[]{:S(2)}, u32[]{:S(2)}) collective-permute-start(bf16[1040,128]{1,0:T(8,128)(2,1)S(1)} %pad_maximum_fusion.2), channel_id=1, source_target_pairs={{8,0},{12,4},{9,1},{13,5},{10,2},{14,6},{11,3},{15,7},{24,16},{28,... | collective-permute-start | bytes 798728 | tf_op jit(solution)/shard_map/ppermute | solution.py:70
  67.3 19.6 %collective-permute-start.3 = (bf16[1040,128]{1,0:T(8,128)(2,1)S(1)}, bf16[1040,128]{1,0:T(8,128)(2,1)S(1)}, u32[]{:S(2)}, u32[]{:S(2)}) collective-permute-start(bf16[1040,128]{1,0:T(8,128)(2,1)S(1)} %pad_maximum_fusion.2), channel_id=1, source_target_pairs={{4,0},{8,4},{12,8},{5,1},{9,5},{13,9},{6,2},{10,6},{14,10},{7,3},{... | collective-permute-start | bytes 798728 | tf_op jit(solution)/shard_map/ppermute | solution.py:70
  70.7 2.4 %copy-start.3 = (f32[16,128,128]{2,1,0:T(8,128)}, f32[16,128,128]{2,1,0:T(8,128)S(1)}, u32[]{:S(2)}) copy-start(f32[16,128,128]{2,1,0:T(8,128)S(1)} %convolution_multiply_fusion) | copy-start | bytes 3145732
  87.1 0.7 copy-start.22
  87.8 2.0 %copy-start.7 = (f32[2,8,128,64]{2,3,1,0:T(8,128)S(1)}, f32[2,8,128,64]{2,3,1,0:T(8,128)}, u32[]{:S(2)}) copy-start(f32[2,8,128,64]{2,3,1,0:T(8,128)} %copy-done.6) | copy-start | bytes 1572868
  87.8 2.0 %copy-start.8 = (f32[16,128,128]{1,2,0:T(8,128)S(1)}, f32[16,128,128]{1,2,0:T(8,128)}, u32[]{:S(2)}) copy-start(f32[16,128,128]{1,2,0:T(8,128)} %get-tuple-element.62) | copy-start | bytes 3145732
  89.8 0.7 copy-start.31
  90.4 2.8 %copy-start.26 = (f32[16,128]{1,0:T(8,128)S(1)}, f32[16,128]{1,0:T(8,128)}, u32[]{:S(2)}) copy-start(f32[16,128]{1,0:T(8,128)} %get-tuple-element.21) | copy-start | bytes 24580
  90.4 4.1 %copy-start.4 = (f32[16,128,128]{2,1,0:T(8,128)S(1)}, f32[16,128,128]{2,1,0:T(8,128)}, u32[]{:S(2)}) copy-start(f32[16,128,128]{2,1,0:T(8,128)} %copy-done.3) | copy-start | bytes 3145732
  94.5 2.3 %copy-start.14 = (f32[16,128,64]{1,2,0:T(8,128)S(1)}, f32[16,128,64]{1,2,0:T(8,128)}, u32[]{:S(2)}) copy-start(f32[16,128,64]{1,2,0:T(8,128)} %convolution_add_fusion.3) | copy-start | bytes 1572868
  96.8 1.0 %copy-start.15 = (bf16[16,128,128]{1,2,0:T(8,128)(2,1)S(1)}, bf16[16,128,128]{1,2,0:T(8,128)(2,1)}, u32[]{:S(2)}) copy-start(bf16[16,128,128]{1,2,0:T(8,128)(2,1)} %get-tuple-element.26) | copy-start | bytes 1572868

commit v2 on v0

--- a/solution.py
+++ b/solution.py
@@ -113,7 +113,7 @@
     return mixed.astype(jnp.bfloat16).reshape(local_heads, tok_dev, head_width)
 
 
-def body(queries, keys_values, student_x, state_maps, decay_logit, skip_gain, init_state):
+def group_body(queries, keys_values, student_x, state_maps, decay_logit, skip_gain, init_state):
     local_heads, tok_dev, head_width = student_x.shape
     local_groups = state_maps.shape[0]
     per_group = local_heads // local_groups
@@ -232,6 +232,26 @@
     return (grad_x.astype(jnp.bfloat16), grad_maps.astype(jnp.bfloat16), grad_log_decay)
 
 
+def body(queries, keys_values, student_x, state_maps, decay_logit, skip_gain, init_state):
+    local_groups = state_maps.shape[0]
+    per_group = student_x.shape[0] // local_groups
+    results = []
+    for group in range(local_groups):
+        heads = slice(group * per_group, (group + 1) * per_group)
+        results.append(
+            group_body(
+                queries[heads],
+                keys_values[group : group + 1],
+                student_x[heads],
+                state_maps[group : group + 1],
+                decay_logit[heads],
+                skip_gain[heads],
+                init_state[heads],
+            )
+        )
+    return tuple(jnp.concatenate(parts, axis=0) for parts in zip(*results))
+
+
 def solution(mesh):
     in_specs = (
         P(("head", "sub"), ("groups", "seq"), None),

time: 88.9 us -> 127 us (1.43)
  the two profiles are of different devices: /device:TPU:8 before, /device:TPU:24 now
where the time goes in v2:
time: 127 us; the launch traced here: 125 us
  matrix products  36.8 us (29%)
  starting transfers between devices  28.2 us (22%)
  local copies, waits for them, and re-layouts  23.2 us (18%)
  other arithmetic  20.5 us (16%)
  waiting for transfers between devices  14.4 us (11%)
  between operations  2.12 us (2%)
    ppermute x18, starting transfers between devices, shifted(): moved.append(lax.ppermute(x, 'seq', pairs))  28.2 us
    unnamed x193, local copies, waits for them, and re-layouts  14.6 us
    ppermute x18, waiting for transfers between devices, shifted(): moved.append(lax.ppermute(x, 'seq', pairs))  14.4 us
    slice x15, local copies, waits for them, and re-layouts, unpack_rows(): big = received[:big_rows].reshape(big_shape)  5.62 us
    dot_general x8, matrix products, teacher_rows(): jnp.einsum('gptd,gkd->gptk', grouped, block[..., :head_width], preferred_...  5.37 us
    dot_general x8, matrix products, teacher_rows(): jnp.einsum('gptk,gkd->gptd', exponentials.astype(jnp.bfloat16), block[......  4.46 us
    dot_general x2, matrix products, group_body(): local_dx = jnp.einsum('hts,htp->hsp', mixing, grad_out, precision=highest)  4.1 us
    convert_element_type x12, other arithmetic, join_three(): wide = parts.astype(jnp.float32)  4.06 us
  transfers between devices with their start and end apart: 18, of which 3 were waited for; matrix products, arithmetic and copies ran while one was open for 36% of the time, Pallas kernels for 0%

profile of v2, /device:TPU:24, one launch (start us, length us, event | category | flops | bytes accessed | tf_op | source)
XLA Modules:
  0.0 125.2 jit_solution(12335863091864538559)
XLA Ops:
  0.7 1.6 %fusion.259 = (bf16[1,128,256]{2,1,0:T(8,128)(2,1)}, bf16[1,128,256]{2,1,0:T(8,128)(2,1)}) fusion(bf16[2,128,256]{2,1,0:T(8,128)(2,1)} %param.8), kind=kLoop, calls=%fused_computation.444 | loop fusion | bytes 262144 | tf_op jit(solution)/shard_map/slice | solution.py:244
  2.3 1.3 %collective-permute-start.5 = (bf16[1,128,256]{2,1,0:T(8,128)(2,1)}, bf16[1,128,256]{2,1,0:T(8,128)(2,1)}, u32[]{:S(2)}, u32[]{:S(2)}) collective-permute-start(bf16[1,128,256]{2,1,0:T(8,128)(2,1)} %get-tuple-element.46), channel_id=1, source_target_pairs={{0,12},{1,13},{2,14},{3,15},{16,28},{17,29},{18,30},{19,31}} | collective-permute-start | bytes 196616 | tf_op jit(solution)/shard_map/ppermute | solution.py:66
  3.6 1.3 %collective-permute-start.3 = (bf16[1,128,256]{2,1,0:T(8,128)(2,1)}, bf16[1,128,256]{2,1,0:T(8,128)(2,1)}, u32[]{:S(2)}, u32[]{:S(2)}) collective-permute-start(bf16[1,128,256]{2,1,0:T(8,128)(2,1)} %get-tuple-element.46), channel_id=1, source_target_pairs={{0,4},{4,8},{8,12},{1,5},{5,9},{9,13},{2,6},{6,10},{10,14},{3,7},{... | collective-permute-start | bytes 196616 | tf_op jit(solution)/shard_map/ppermute | solution.py:66
  4.9 1.3 %collective-permute-start.4 = (bf16[1,128,256]{2,1,0:T(8,128)(2,1)}, bf16[1,128,256]{2,1,0:T(8,128)(2,1)}, u32[]{:S(2)}, u32[]{:S(2)}) collective-permute-start(bf16[1,128,256]{2,1,0:T(8,128)(2,1)} %get-tuple-element.46), channel_id=1, source_target_pairs={{0,8},{4,12},{1,9},{5,13},{2,10},{6,14},{3,11},{7,15},{16,24},{20,... | collective-permute-start | bytes 196616 | tf_op jit(solution)/shard_map/ppermute | solution.py:66
  9.4 1.3 %collective-permute-start.1 = (bf16[528,128]{1,0:T(8,128)(2,1)}, bf16[528,128]{1,0:T(8,128)(2,1)S(1)}, u32[]{:S(2)}, u32[]{:S(2)}) collective-permute-start(bf16[528,128]{1,0:T(8,128)(2,1)} %pad_maximum_fusion.1), channel_id=1, source_target_pairs={{0,8},{4,12},{1,9},{5,13},{2,10},{6,14},{3,11},{7,15},{16,24},{20,... | collective-permute-start | bytes 405512 | tf_op jit(solution)/shard_map/ppermute | solution.py:66
  10.7 1.3 %collective-permute-start = (bf16[528,128]{1,0:T(8,128)(2,1)}, bf16[528,128]{1,0:T(8,128)(2,1)S(1)}, u32[]{:S(2)}, u32[]{:S(2)}) collective-permute-start(bf16[528,128]{1,0:T(8,128)(2,1)} %pad_maximum_fusion.1), channel_id=1, source_target_pairs={{0,4},{4,8},{8,12},{1,5},{5,9},{9,13},{2,6},{6,10},{10,14},{3,7},{... | collective-permute-start | bytes 405512 | tf_op jit(solution)/shard_map/ppermute | solution.py:66
  16.2 1.5 %fusion.38 = f32[8,128,128]{1,2,0:T(8,128)} fusion(f32[128,128]{0,1:T(8,128)S(1)} %fusion.147, f32[8,128]{1,0:T(8,128)S(1)} %reduce_window_sum.33, pred[128,128]{0,1:T(8,128)(4,1)S(1)} %iota_compare_fusion, bf16[16,128,128]{2,1,0:T(8,128)(2,1)S(1)} %copy-done.1), kind=kOutput, calls=%fused_computation.94 | convolution fusion | flops 201850880 | bytes 876544 | tf_op jit(solution)/shard_map/hts,hsp->htp/dot_general | solution.py:161
  19.9 1.4 %fusion.33 = f32[8,128,128]{1,2,0:T(8,128)} fusion(f32[128,128]{0,1:T(8,128)S(1)} %fusion.143, f32[8,128]{1,0:T(8,128)S(1)} %reduce_window_sum.34, pred[128,128]{0,1:T(8,128)(4,1)S(1)} %iota_compare_fusion, bf16[16,128,128]{2,1,0:T(8,128)(2,1)S(1)} %copy-done.1), kind=kOutput, calls=%fused_computation.79 | convolution fusion | flops 201850880 | bytes 876544 | tf_op jit(solution)/shard_map/hts,hsp->htp/dot_general | solution.py:161
  23.4 1.3 %collective-permute-start.2 = (bf16[528,128]{1,0:T(8,128)(2,1)}, bf16[528,128]{1,0:T(8,128)(2,1)S(1)}, u32[]{:S(2)}, u32[]{:S(2)}) collective-permute-start(bf16[528,128]{1,0:T(8,128)(2,1)} %pad_maximum_fusion.1), channel_id=1, source_target_pairs={{0,12},{1,13},{2,14},{3,15},{16,28},{17,29},{18,30},{19,31}} | collective-permute-start | bytes 405512 | tf_op jit(solution)/shard_map/ppermute | solution.py:66
  25.7 1.3 %collective-permute-start.14 = (bf16[1,128,256]{2,1,0:T(8,128)(2,1)S(1)}, bf16[1,128,256]{2,1,0:T(8,128)(2,1)S(1)}, u32[]{:S(2)}, u32[]{:S(2)}) collective-permute-start(bf16[1,128,256]{2,1,0:T(8,128)(2,1)S(1)} %copy-done.56), channel_id=1, source_target_pairs={{0,12},{1,13},{2,14},{3,15},{16,28},{17,29},{18,30},{19,31}} | collective-permute-start | bytes 196616 | tf_op jit(solution)/shard_map/ppermute | solution.py:66
  27.0 1.0 fusion.261
  28.0 1.4 %collective-permute-start.12 = (bf16[1,128,256]{2,1,0:T(8,128)(2,1)S(1)}, bf16[1,128,256]{2,1,0:T(8,128)(2,1)S(1)}, u32[]{:S(2)}, u32[]{:S(2)}) collective-permute-start(bf16[1,128,256]{2,1,0:T(8,128)(2,1)S(1)} %copy-done.56), channel_id=1, source_target_pairs={{0,4},{4,8},{8,12},{1,5},{5,9},{9,13},{2,6},{6,10},{10,14},{3,7},{... | collective-permute-start | bytes 196616 | tf_op jit(solution)/shard_map/ppermute | solution.py:66
  29.5 1.0 fusion.262
  31.4 1.0 fusion.78
  32.4 1.0 convolution_add_fusion.3
  33.8 2.2 %collective-permute-done.14 = bf16[1,128,256]{2,1,0:T(8,128)(2,1)S(1)} collective-permute-done((bf16[1,128,256]{2,1,0:T(8,128)(2,1)S(1)}, bf16[1,128,256]{2,1,0:T(8,128)(2,1)S(1)}, u32[]{:S(2)}, u32[]{:S(2)}) %collective-permute-start.14) | collective-permute-done | bytes 65568 | tf_op jit(solution)/shard_map/ppermute | solution.py:66
  36.0 1.3 %collective-permute-start.13 = (bf16[1,128,256]{2,1,0:T(8,128)(2,1)S(1)}, bf16[1,128,256]{2,1,0:T(8,128)(2,1)S(1)}, u32[]{:S(2)}, u32[]{:S(2)}) collective-permute-start(bf16[1,128,256]{2,1,0:T(8,128)(2,1)S(1)} %copy-done.56), channel_id=1, source_target_pairs={{0,8},{4,12},{1,9},{5,13},{2,10},{6,14},{3,11},{7,15},{16,24},{20,... | collective-permute-start | bytes 196616 | tf_op jit(solution)/shard_map/ppermute | solution.py:66
  37.6 1.3 %collective-permute-start.10 = (bf16[528,128]{1,0:T(8,128)(2,1)S(1)}, bf16[528,128]{1,0:T(8,128)(2,1)S(1)}, u32[]{:S(2)}, u32[]{:S(2)}) collective-permute-start(bf16[528,128]{1,0:T(8,128)(2,1)S(1)} %pad_maximum_fusion.3), channel_id=1, source_target_pairs={{0,8},{4,12},{1,9},{5,13},{2,10},{6,14},{3,11},{7,15},{16,24},{20,... | collective-permute-start | bytes 405512 | tf_op jit(solution)/shard_map/ppermute | solution.py:66
  39.1 1.1 multiply_reduce_fusion.6
  40.2 7.2 %collective-permute-done.13 = bf16[1,128,256]{2,1,0:T(8,128)(2,1)S(1)} collective-permute-done((bf16[1,128,256]{2,1,0:T(8,128)(2,1)S(1)}, bf16[1,128,256]{2,1,0:T(8,128)(2,1)S(1)}, u32[]{:S(2)}, u32[]{:S(2)}) %collective-permute-start.13) | collective-permute-done | bytes 65568 | tf_op jit(solution)/shard_map/ppermute | solution.py:66
  47.4 1.3 %collective-permute-start.9 = (bf16[528,128]{1,0:T(8,128)(2,1)S(1)}, bf16[528,128]{1,0:T(8,128)(2,1)S(1)}, u32[]{:S(2)}, u32[]{:S(2)}) collective-permute-start(bf16[528,128]{1,0:T(8,128)(2,1)S(1)} %pad_maximum_fusion.3), channel_id=1, source_target_pairs={{0,4},{4,8},{8,12},{1,5},{5,9},{9,13},{2,6},{6,10},{10,14},{3,7},{... | collective-permute-start | bytes 405512 | tf_op jit(solution)/shard_map/ppermute | solution.py:66
  51.2 1.5 %collective-permute-start.11 = (bf16[528,128]{1,0:T(8,128)(2,1)S(1)}, bf16[528,128]{1,0:T(8,128)(2,1)S(1)}, u32[]{:S(2)}, u32[]{:S(2)}) collective-permute-start(bf16[528,128]{1,0:T(8,128)(2,1)S(1)} %pad_maximum_fusion.3), channel_id=1, source_target_pairs={{0,12},{1,13},{2,14},{3,15},{16,28},{17,29},{18,30},{19,31}} | collective-permute-start | bytes 405512 | tf_op jit(solution)/shard_map/ppermute | solution.py:66
  53.4 1.1 multiply_reduce_fusion.7
  54.9 5.0 %collective-permute-done.11 = bf16[528,128]{1,0:T(8,128)(2,1)S(1)} collective-permute-done((bf16[528,128]{1,0:T(8,128)(2,1)S(1)}, bf16[528,128]{1,0:T(8,128)(2,1)S(1)}, u32[]{:S(2)}, u32[]{:S(2)}) %collective-permute-start.11) | collective-permute-done | bytes 135200 | tf_op jit(solution)/shard_map/ppermute | solution.py:66
  60.6 1.1 multiply_reduce_fusion.3
  62.0 1.2 multiply_reduce_fusion
  63.2 1.4 %fusion.25 = (f32[8,128]{1,0:T(8,128)S(1)}, f32[8,128,128]{1,2,0:T(8,128)S(1)}) fusion(bf16[8,128,128]{1,2,0:T(8,128)(2,1)S(1)} %copy.196, f32[8,128,128]{1,2,0:T(8,128)S(1)} %get-tuple-element.107, f32[128,128]{0,1:T(8,128)S(1)} %copy-done.46, f32[8,128]{1,0:T(8,128)S(1)} %reduce_window_sum.33, pred[128,128]{0,1:T(8,128)(4,1)S(1)} %copy-done.26), kind=kOutput, calls=%fused_computation.57 | convolution fusion | flops 202243072 | bytes 1400832 | tf_op jit(solution)/shard_map/hts,htp->hsp/dot_general | solution.py:181
  64.6 1.1 fusion.100
  68.4 1.6 %pad_maximum_fusion.2 = bf16[528,128]{1,0:T(8,128)(2,1)} fusion(bf16[16,128]{1,0:T(8,128)(2,1)S(1)} %fusion.173, bf16[512,128]{1,0:T(8,128)(2,1)} %bitcast.356), kind=kLoop, calls=%fused_computation.186 | loop fusion | flops 270336 | bytes 270336 | tf_op jit(solution)/shard_map/concatenate | solution.py:30
  70.0 2.2 %collective-permute-start.8 = (bf16[528,128]{1,0:T(8,128)(2,1)}, bf16[528,128]{1,0:T(8,128)(2,1)}, u32[]{:S(2)}, u32[]{:S(2)}) collective-permute-start(bf16[528,128]{1,0:T(8,128)(2,1)} %pad_maximum_fusion.2), channel_id=1, source_target_pairs={{12,0},{13,1},{14,2},{15,3},{28,16},{29,17},{30,18},{31,19}} | collective-permute-start | bytes 405512 | tf_op jit(solution)/shard_map/ppermute | solution.py:66
  72.1 2.0 %collective-permute-start.7 = (bf16[528,128]{1,0:T(8,128)(2,1)}, bf16[528,128]{1,0:T(8,128)(2,1)}, u32[]{:S(2)}, u32[]{:S(2)}) collective-permute-start(bf16[528,128]{1,0:T(8,128)(2,1)} %pad_maximum_fusion.2), channel_id=1, source_target_pairs={{8,0},{12,4},{9,1},{13,5},{10,2},{14,6},{11,3},{15,7},{24,16},{28,... | collective-permute-start | bytes 405512 | tf_op jit(solution)/shard_map/ppermute | solution.py:66
  74.1 2.5 %collective-permute-start.6 = (bf16[528,128]{1,0:T(8,128)(2,1)}, bf16[528,128]{1,0:T(8,128)(2,1)}, u32[]{:S(2)}, u32[]{:S(2)}) collective-permute-start(bf16[528,128]{1,0:T(8,128)(2,1)} %pad_maximum_fusion.2), channel_id=1, source_target_pairs={{4,0},{8,4},{12,8},{5,1},{9,5},{13,9},{6,2},{10,6},{14,10},{7,3},{... | collective-permute-start | bytes 405512 | tf_op jit(solution)/shard_map/ppermute | solution.py:66
  76.6 2.7 %fusion.28 = (f32[8,128]{1,0:T(8,128)}, f32[8,128,128]{1,2,0:T(8,128)}) fusion(bf16[8,128,128]{1,2,0:T(8,128)(2,1)S(1)} %copy.198, f32[8,128,128]{1,2,0:T(8,128)S(1)} %get-tuple-element.35, f32[128,128]{0,1:T(8,128)S(1)} %copy-done.44, f32[8,128]{1,0:T(8,128)S(1)} %reduce_window_sum.34, pred[128,128]{0,1:T(8,128)(4,1)S(1)} %copy-done.26), kind=kOutput, calls=%fused_computation.60 | convolution fusion | flops 202243072 | bytes 1400832 | tf_op jit(solution)/shard_map/hts,htp->hsp/dot_general | solution.py:181
  79.3 1.1 fusion.88
  83.7 1.6 %pad_maximum_fusion.4 = bf16[528,128]{1,0:T(8,128)(2,1)} fusion(bf16[16,128]{1,0:T(8,128)(2,1)S(1)} %fusion.177, bf16[512,128]{1,0:T(8,128)(2,1)} %bitcast.355), kind=kLoop, calls=%fused_computation.188 | loop fusion | flops 270336 | bytes 270336 | tf_op jit(solution)/shard_map/concatenate | solution.py:30
  85.3 1.9 %collective-permute-start.17 = (bf16[528,128]{1,0:T(8,128)(2,1)}, bf16[528,128]{1,0:T(8,128)(2,1)}, u32[]{:S(2)}, u32[]{:S(2)}) collective-permute-start(bf16[528,128]{1,0:T(8,128)(2,1)} %pad_maximum_fusion.4), channel_id=1, source_target_pairs={{12,0},{13,1},{14,2},{15,3},{28,16},{29,17},{30,18},{31,19}} | collective-permute-start | bytes 405512 | tf_op jit(solution)/shard_map/ppermute | solution.py:66
  87.2 1.9 %collective-permute-start.16 = (bf16[528,128]{1,0:T(8,128)(2,1)}, bf16[528,128]{1,0:T(8,128)(2,1)}, u32[]{:S(2)}, u32[]{:S(2)}) collective-permute-start(bf16[528,128]{1,0:T(8,128)(2,1)} %pad_maximum_fusion.4), channel_id=1, source_target_pairs={{8,0},{12,4},{9,1},{13,5},{10,2},{14,6},{11,3},{15,7},{24,16},{28,... | collective-permute-start | bytes 405512 | tf_op jit(solution)/shard_map/ppermute | solution.py:66
  90.4 1.8 %fusion.131 = f32[8,128,64]{1,2,0:T(8,128)} fusion(f32[8,128,128]{1,2,0:T(8,128)S(1)} %convolution_multiply_fusion.11, f32[128,64]{0,1:T(8,128)S(1)} %copy-done.42), kind=kOutput, calls=%fused_computation.200 | convolution fusion | flops 100663296 | bytes 819200 | tf_op jit(solution)/shard_map/hts,htn->hsn/dot_general | solution.py:194
  93.1 1.3 %convolution_add_fusion.7 = f32[8,128,64]{1,2,0:T(8,128)} fusion(f32[8,128,64]{1,2,0:T(8,128)S(1)} %convolution_multiply_fusion.14, f32[8,128,128]{1,2,0:T(8,128)S(1)} %convolution_multiply_fusion.11, f32[128,64]{0,1:T(8,128)S(1)} %copy-done.29), kind=kOutput, calls=%fused_computation.44 | convolution fusion | flops 100728832 | bytes 1081344 | tf_op jit(solution)/shard_map/hts,hsn->htn/dot_general | solution.py:195
  95.2 1.3 %convolution_add_fusion.6 = f32[8,128,64]{1,2,0:T(8,128)} fusion(f32[8,128,64]{1,2,0:T(8,128)S(1)} %convolution_multiply_fusion.12, f32[8,128,128]{1,2,0:T(8,128)S(1)} %convolution_multiply_fusion.10, f32[128,64]{0,1:T(8,128)S(1)} %copy-done.31), kind=kOutput, calls=%fused_computation.39 | convolution fusion | flops 100728832 | bytes 1081344 | tf_op jit(solution)/shard_map/hts,hsn->htn/dot_general | solution.py:195
  96.5 1.8 %fusion.121 = f32[8,128,64]{1,2,0:T(8,128)} fusion(f32[8,128,128]{1,2,0:T(8,128)S(1)} %convolution_multiply_fusion.10, f32[128,64]{0,1:T(8,128)S(1)} %copy-done.39), kind=kOutput, calls=%fused_computation.190 | convolution fusion | flops 100663296 | bytes 819200 | tf_op jit(solution)/shard_map/hts,htn->hsn/dot_general | solution.py:194
  98.3 1.9 %collective-permute-start.15 = (bf16[528,128]{1,0:T(8,128)(2,1)}, bf16[528,128]{1,0:T(8,128)(2,1)}, u32[]{:S(2)}, u32[]{:S(2)}) collective-permute-start(bf16[528,128]{1,0:T(8,128)(2,1)} %pad_maximum_fusion.4), channel_id=1, source_target_pairs={{4,0},{8,4},{12,8},{5,1},{9,5},{13,9},{6,2},{10,6},{14,10},{7,3},{... | collective-permute-start | bytes 405512 | tf_op jit(solution)/shard_map/ppermute | solution.py:66
  106.4 1.8 %fusion.26 = (f32[8,128]{1,0:T(8,128)S(1)}, bf16[8,128,128]{1,2,0:T(8,128)(2,1)}) fusion(bf16[8,128,128]{1,2,0:T(8,128)(2,1)S(1)} %copy.196, f32[8,128,128]{1,2,0:T(8,128)S(1)} %get-tuple-element.107, f32[8]{0:T(128)S(1)} %copy-done.67, f32[8,128,128]{1,2,0:T(8,128)S(1)} %get-tuple-element.105, bf16[8,64,128]{2,1,0:T(8,128)(2,1)S(1)} %bitcast.342, ...), kind=kOutput, calls=%fused_computation.58 | convolution fusion | flops 102038528 | bytes 2138208 | tf_op jit(solution)/shard_map/hsn,hnp->hsp/dot_general | solution.py:222
  108.2 1.2 reduce_window_sum.35
  115.0 1.8 %fusion.29 = (f32[8,128]{1,0:T(8,128)S(1)}, bf16[8,128,128]{1,2,0:T(8,128)(2,1)}) fusion(bf16[8,128,128]{1,2,0:T(8,128)(2,1)S(1)} %copy.198, f32[8,128,128]{1,2,0:T(8,128)S(1)} %get-tuple-element.35, f32[8]{0:T(128)S(1)} %copy-done.65, f32[8,128,128]{1,2,0:T(8,128)S(1)} %copy-done.2, bf16[8,64,128]{2,1,0:T(8,128)(2,1)S(1)} %bitcast.346, ...), kind=kOutput, calls=%fused_computation.61 | convolution fusion | flops 102038528 | bytes 2138208 | tf_op jit(solution)/shard_map/hsn,hnp->hsp/dot_general | solution.py:222
  116.9 1.2 reduce_window_sum.36
  118.1 1.6 %fusion.23 = f32[8,128,64]{1,2,0:T(8,128)S(1)} fusion(f32[8,128,64]{1,2,0:T(8,128)} %fusion.131, f32[8,128]{1,0:T(8,128)S(1)} %get-tuple-element.54, bf16[8,64,128]{2,1,0:T(8,128)(2,1)S(1)} %bitcast.343, f32[8,64,128]{2,1,0:T(8,128)S(1)} %bitcast.337, bf16[8,64,128]{2,1,0:T(8,128)(2,1)S(1)} %bitcast.341, f32[8]{0:T(128)S(1)} %copy-done.74, ...), kind=kOutput, calls=%fused_computation.47 | convolution fusion | flops 101187584 | bytes 1315840 | tf_op jit(solution)/shard_map/hnp,hsp->hsn/dot_general | solution.py:227
  122.8 1.0 copy.150
  (331 shorter events, 43.0 us)
Async XLA Ops:
  0.6 11.7 %copy-start = (bf16[16,128,128]{2,1,0:T(8,128)(2,1)S(1)}, bf16[16,128,128]{2,1,0:T(8,128)(2,1)}, u32[]{:S(2)}) copy-start(bf16[16,128,128]{2,1,0:T(8,128)(2,1)} %param.7) | copy-start | bytes 1572868
  0.6 5.5 %copy-start.72 = (f32[16,128]{1,0:T(8,128)S(1)}, f32[16,128]{1,0:T(8,128)}, u32[]{:S(2)}) copy-start(f32[16,128]{1,0:T(8,128)} %param.11) | copy-start | bytes 24580
  0.7 6.6 %copy-start.19 = (bf16[2,128,128]{2,1,0:T(8,128)(2,1)S(1)}, bf16[2,128,128]{2,1,0:T(8,128)(2,1)}, u32[]{:S(2)}) copy-start(bf16[2,128,128]{2,1,0:T(8,128)(2,1)} %param.10) | copy-start | bytes 196612
  0.7 7.5 %copy-start.1 = (bf16[16,128,128]{2,1,0:T(8,128)(2,1)S(1)}, bf16[16,128,128]{2,1,0:T(8,128)(2,1)}, u32[]{:S(2)}) copy-start(bf16[16,128,128]{2,1,0:T(8,128)(2,1)} %param.9) | copy-start | bytes 1572868
  2.3 23.4 %collective-permute-start.5 = (bf16[1,128,256]{2,1,0:T(8,128)(2,1)}, bf16[1,128,256]{2,1,0:T(8,128)(2,1)}, u32[]{:S(2)}, u32[]{:S(2)}) collective-permute-start(bf16[1,128,256]{2,1,0:T(8,128)(2,1)} %get-tuple-element.46), channel_id=1, source_target_pairs={{0,12},{1,13},{2,14},{3,15},{16,28},{17,29},{18,30},{19,31}} | collective-permute-start | bytes 196616 | tf_op jit(solution)/shard_map/ppermute | solution.py:66
  3.6 19.8 %collective-permute-start.3 = (bf16[1,128,256]{2,1,0:T(8,128)(2,1)}, bf16[1,128,256]{2,1,0:T(8,128)(2,1)}, u32[]{:S(2)}, u32[]{:S(2)}) collective-permute-start(bf16[1,128,256]{2,1,0:T(8,128)(2,1)} %get-tuple-element.46), channel_id=1, source_target_pairs={{0,4},{4,8},{8,12},{1,5},{5,9},{9,13},{2,6},{6,10},{10,14},{3,7},{... | collective-permute-start | bytes 196616 | tf_op jit(solution)/shard_map/ppermute | solution.py:66
  4.9 23.1 %collective-permute-start.4 = (bf16[1,128,256]{2,1,0:T(8,128)(2,1)}, bf16[1,128,256]{2,1,0:T(8,128)(2,1)}, u32[]{:S(2)}, u32[]{:S(2)}) collective-permute-start(bf16[1,128,256]{2,1,0:T(8,128)(2,1)} %get-tuple-element.46), channel_id=1, source_target_pairs={{0,8},{4,12},{1,9},{5,13},{2,10},{6,14},{3,11},{7,15},{16,24},{20,... | collective-permute-start | bytes 196616 | tf_op jit(solution)/shard_map/ppermute | solution.py:66
  7.3 45.6 %copy-start.51 = (f32[8,128]{1,0:T(8,128)}, f32[8,128]{1,0:T(8,128)S(1)}, u32[]{:S(2)}) copy-start(f32[8,128]{1,0:T(8,128)S(1)} %get-tuple-element.55) | copy-start | bytes 12292
  9.4 41.8 %collective-permute-start.1 = (bf16[528,128]{1,0:T(8,128)(2,1)}, bf16[528,128]{1,0:T(8,128)(2,1)S(1)}, u32[]{:S(2)}, u32[]{:S(2)}) collective-permute-start(bf16[528,128]{1,0:T(8,128)(2,1)} %pad_maximum_fusion.1), channel_id=1, source_target_pairs={{0,8},{4,12},{1,9},{5,13},{2,10},{6,14},{3,11},{7,15},{16,24},{20,... | collective-permute-start | bytes 405512 | tf_op jit(solution)/shard_map/ppermute | solution.py:66
  10.7 42.0 %collective-permute-start = (bf16[528,128]{1,0:T(8,128)(2,1)}, bf16[528,128]{1,0:T(8,128)(2,1)S(1)}, u32[]{:S(2)}, u32[]{:S(2)}) collective-permute-start(bf16[528,128]{1,0:T(8,128)(2,1)} %pad_maximum_fusion.1), channel_id=1, source_target_pairs={{0,4},{4,8},{8,12},{1,5},{5,9},{9,13},{2,6},{6,10},{10,14},{3,7},{... | collective-permute-start | bytes 405512 | tf_op jit(solution)/shard_map/ppermute | solution.py:66
  12.0 7.9 %copy-start.25 = (pred[128,128]{0,1:T(8,128)(4,1)}, pred[128,128]{0,1:T(8,128)(4,1)S(1)}, u32[]{:S(2)}) copy-start(pred[128,128]{0,1:T(8,128)(4,1)S(1)} %iota_compare_fusion) | copy-start | bytes 49156
  12.2 4.0 %copy-start.45 = (f32[128,128]{0,1:T(8,128)}, f32[128,128]{0,1:T(8,128)S(1)}, u32[]{:S(2)}) copy-start(f32[128,128]{0,1:T(8,128)S(1)} %fusion.147) | copy-start | bytes 196612
  16.0 6.3 %copy-start.49 = (f32[8,128]{1,0:T(8,128)}, f32[8,128]{1,0:T(8,128)S(1)}, u32[]{:S(2)}) copy-start(f32[8,128]{1,0:T(8,128)S(1)} %get-tuple-element.56) | copy-start | bytes 12292
  16.0 44.0 %copy-start.54 = (f32[8,128]{1,0:T(8,128)}, f32[8,128]{1,0:T(8,128)S(1)}, u32[]{:S(2)}) copy-start(f32[8,128]{1,0:T(8,128)S(1)} %get-tuple-element.57) | copy-start | bytes 12292
  16.2 3.7 %copy-start.43 = (f32[128,128]{0,1:T(8,128)}, f32[128,128]{0,1:T(8,128)S(1)}, u32[]{:S(2)}) copy-start(f32[128,128]{0,1:T(8,128)S(1)} %fusion.143) | copy-start | bytes 196612
  19.2 33.7 %copy-start.40 = (f32[128,64]{0,1:T(8,128)}, f32[128,64]{0,1:T(8,128)S(1)}, u32[]{:S(2)}) copy-start(f32[128,64]{0,1:T(8,128)S(1)} %copy.109) | copy-start | bytes 98308
  22.2 37.8 %copy-start.37 = (f32[128,64]{0,1:T(8,128)}, f32[128,64]{0,1:T(8,128)S(1)}, u32[]{:S(2)}) copy-start(f32[128,64]{0,1:T(8,128)S(1)} %copy.125) | copy-start | bytes 98308
  23.4 29.4 %collective-permute-start.2 = (bf16[528,128]{1,0:T(8,128)(2,1)}, bf16[528,128]{1,0:T(8,128)(2,1)S(1)}, u32[]{:S(2)}, u32[]{:S(2)}) collective-permute-start(bf16[528,128]{1,0:T(8,128)(2,1)} %pad_maximum_fusion.1), channel_id=1, source_target_pairs={{0,12},{1,13},{2,14},{3,15},{16,28},{17,29},{18,30},{19,31}} | collective-permute-start | bytes 405512 | tf_op jit(solution)/shard_map/ppermute | solution.py:66
  25.7 10.3 %collective-permute-start.14 = (bf16[1,128,256]{2,1,0:T(8,128)(2,1)S(1)}, bf16[1,128,256]{2,1,0:T(8,128)(2,1)S(1)}, u32[]{:S(2)}, u32[]{:S(2)}) collective-permute-start(bf16[1,128,256]{2,1,0:T(8,128)(2,1)S(1)} %copy-done.56), channel_id=1, source_target_pairs={{0,12},{1,13},{2,14},{3,15},{16,28},{17,29},{18,30},{19,31}} | collective-permute-start | bytes 196616 | tf_op jit(solution)/shard_map/ppermute | solution.py:66
  28.0 3.1 %copy-start.36 = (bf16[2,128,256]{2,1,0:T(8,128)(2,1)S(1)}, bf16[2,128,256]{2,1,0:T(8,128)(2,1)}, u32[]{:S(2)}) copy-start(bf16[2,128,256]{2,1,0:T(8,128)(2,1)} %param.8) | copy-start | bytes 393220
  28.0 9.5 %collective-permute-start.12 = (bf16[1,128,256]{2,1,0:T(8,128)(2,1)S(1)}, bf16[1,128,256]{2,1,0:T(8,128)(2,1)S(1)}, u32[]{:S(2)}, u32[]{:S(2)}) collective-permute-start(bf16[1,128,256]{2,1,0:T(8,128)(2,1)S(1)} %copy-done.56), channel_id=1, source_target_pairs={{0,4},{4,8},{8,12},{1,5},{5,9},{9,13},{2,6},{6,10},{10,14},{3,7},{... | collective-permute-start | bytes 196616 | tf_op jit(solution)/shard_map/ppermute | solution.py:66
  36.0 11.4 %collective-permute-start.13 = (bf16[1,128,256]{2,1,0:T(8,128)(2,1)S(1)}, bf16[1,128,256]{2,1,0:T(8,128)(2,1)S(1)}, u32[]{:S(2)}, u32[]{:S(2)}) collective-permute-start(bf16[1,128,256]{2,1,0:T(8,128)(2,1)S(1)} %copy-done.56), channel_id=1, source_target_pairs={{0,8},{4,12},{1,9},{5,13},{2,10},{6,14},{3,11},{7,15},{16,24},{20,... | collective-permute-start | bytes 196616 | tf_op jit(solution)/shard_map/ppermute | solution.py:66
  37.6 17.3 %collective-permute-start.10 = (bf16[528,128]{1,0:T(8,128)(2,1)S(1)}, bf16[528,128]{1,0:T(8,128)(2,1)S(1)}, u32[]{:S(2)}, u32[]{:S(2)}) collective-permute-start(bf16[528,128]{1,0:T(8,128)(2,1)S(1)} %pad_maximum_fusion.3), channel_id=1, source_target_pairs={{0,8},{4,12},{1,9},{5,13},{2,10},{6,14},{3,11},{7,15},{16,24},{20,... | collective-permute-start | bytes 405512 | tf_op jit(solution)/shard_map/ppermute | solution.py:66
  47.4 7.5 %collective-permute-start.9 = (bf16[528,128]{1,0:T(8,128)(2,1)S(1)}, bf16[528,128]{1,0:T(8,128)(2,1)S(1)}, u32[]{:S(2)}, u32[]{:S(2)}) collective-permute-start(bf16[528,128]{1,0:T(8,128)(2,1)S(1)} %pad_maximum_fusion.3), channel_id=1, source_target_pairs={{0,4},{4,8},{8,12},{1,5},{5,9},{9,13},{2,6},{6,10},{10,14},{3,7},{... | collective-permute-start | bytes 405512 | tf_op jit(solution)/shard_map/ppermute | solution.py:66
  50.8 2.5 %copy-start.3 = (f32[16,64,128]{2,1,0:T(8,128)S(1)}, f32[16,64,128]{2,1,0:T(8,128)}, u32[]{:S(2)}) copy-start(f32[16,64,128]{2,1,0:T(8,128)} %param.13) | copy-start | bytes 1572868
  51.2 14.6 %copy-start.7 = (bf16[528,128]{1,0:T(8,128)(2,1)}, bf16[528,128]{1,0:T(8,128)(2,1)S(1)}, u32[]{:S(2)}) copy-start(bf16[528,128]{1,0:T(8,128)(2,1)S(1)} %collective-permute-done.1) | copy-start | bytes 405508
  51.2 8.7 %collective-permute-start.11 = (bf16[528,128]{1,0:T(8,128)(2,1)S(1)}, bf16[528,128]{1,0:T(8,128)(2,1)S(1)}, u32[]{:S(2)}, u32[]{:S(2)}) collective-permute-start(bf16[528,128]{1,0:T(8,128)(2,1)S(1)} %pad_maximum_fusion.3), channel_id=1, source_target_pairs={{0,12},{1,13},{2,14},{3,15},{16,28},{17,29},{18,30},{19,31}} | collective-permute-start | bytes 405512 | tf_op jit(solution)/shard_map/ppermute | solution.py:66
  52.7 13.0 %copy-start.11 = (bf16[528,128]{1,0:T(8,128)(2,1)}, bf16[528,128]{1,0:T(8,128)(2,1)S(1)}, u32[]{:S(2)}) copy-start(bf16[528,128]{1,0:T(8,128)(2,1)S(1)} %collective-permute-done.2) | copy-start | bytes 405508
  54.6 5.9 %copy-start.33 = (f32[8,128,128]{1,2,0:T(8,128)S(1)}, f32[8,128,128]{1,2,0:T(8,128)}, u32[]{:S(2)}) copy-start(f32[8,128,128]{1,2,0:T(8,128)} %fusion.33) | copy-start | bytes 1572868
  54.9 6.9 %copy-start.13 = (bf16[528,128]{1,0:T(8,128)(2,1)}, bf16[528,128]{1,0:T(8,128)(2,1)S(1)}, u32[]{:S(2)}) copy-start(bf16[528,128]{1,0:T(8,128)(2,1)S(1)} %collective-permute-done.10) | copy-start | bytes 405508
  54.9 6.8 %copy-start.15 = (bf16[528,128]{1,0:T(8,128)(2,1)}, bf16[528,128]{1,0:T(8,128)(2,1)S(1)}, u32[]{:S(2)}) copy-start(bf16[528,128]{1,0:T(8,128)(2,1)S(1)} %collective-permute-done.9) | copy-start | bytes 405508
  63.2 4.4 %copy-start.59 = (f32[8,128]{1,0:T(8,128)}, f32[8,128]{1,0:T(8,128)S(1)}, u32[]{:S(2)}) copy-start(f32[8,128]{1,0:T(8,128)S(1)} %get-tuple-element.106) | copy-start | bytes 12292
  68.4 8.2 %copy-start.44 = (f32[128,128]{0,1:T(8,128)S(1)}, f32[128,128]{0,1:T(8,128)}, u32[]{:S(2)}) copy-start(f32[128,128]{0,1:T(8,128)} %copy-done.43) | copy-start | bytes 196612
  70.0 28.3 %collective-permute-start.8 = (bf16[528,128]{1,0:T(8,128)(2,1)}, bf16[528,128]{1,0:T(8,128)(2,1)}, u32[]{:S(2)}, u32[]{:S(2)}) collective-permute-start(bf16[528,128]{1,0:T(8,128)(2,1)} %pad_maximum_fusion.2), channel_id=1, source_target_pairs={{12,0},{13,1},{14,2},{15,3},{28,16},{29,17},{30,18},{31,19}} | collective-permute-start | bytes 405512 | tf_op jit(solution)/shard_map/ppermute | solution.py:66
  72.1 28.8 %collective-permute-start.7 = (bf16[528,128]{1,0:T(8,128)(2,1)}, bf16[528,128]{1,0:T(8,128)(2,1)}, u32[]{:S(2)}, u32[]{:S(2)}) collective-permute-start(bf16[528,128]{1,0:T(8,128)(2,1)} %pad_maximum_fusion.2), channel_id=1, source_target_pairs={{8,0},{12,4},{9,1},{13,5},{10,2},{14,6},{11,3},{15,7},{24,16},{28,... | collective-permute-start | bytes 405512 | tf_op jit(solution)/shard_map/ppermute | solution.py:66
  74.1 27.5 %collective-permute-start.6 = (bf16[528,128]{1,0:T(8,128)(2,1)}, bf16[528,128]{1,0:T(8,128)(2,1)}, u32[]{:S(2)}, u32[]{:S(2)}) collective-permute-start(bf16[528,128]{1,0:T(8,128)(2,1)} %pad_maximum_fusion.2), channel_id=1, source_target_pairs={{4,0},{8,4},{12,8},{5,1},{9,5},{13,9},{6,2},{10,6},{14,10},{7,3},{... | collective-permute-start | bytes 405512 | tf_op jit(solution)/shard_map/ppermute | solution.py:66
  76.6 2.7 %copy-start.38 = (f32[128,64]{0,1:T(8,128)S(1)}, f32[128,64]{0,1:T(8,128)}, u32[]{:S(2)}) copy-start(f32[128,64]{0,1:T(8,128)} %copy-done.37) | copy-start | bytes 98308
  76.6 2.7 %copy-start.55 = (f32[8,128]{1,0:T(8,128)S(1)}, f32[8,128]{1,0:T(8,128)}, u32[]{:S(2)}) copy-start(f32[8,128]{1,0:T(8,128)} %copy-done.54) | copy-start | bytes 12292
  83.7 5.5 %copy-start.27 = (pred[128,128]{0,1:T(8,128)(4,1)S(1)}, pred[128,128]{0,1:T(8,128)(4,1)}, u32[]{:S(2)}) copy-start(pred[128,128]{0,1:T(8,128)(4,1)} %copy-done.25) | copy-start | bytes 49156
  85.3 24.1 %collective-permute-start.17 = (bf16[528,128]{1,0:T(8,128)(2,1)}, bf16[528,128]{1,0:T(8,128)(2,1)}, u32[]{:S(2)}, u32[]{:S(2)}) collective-permute-start(bf16[528,128]{1,0:T(8,128)(2,1)} %pad_maximum_fusion.4), channel_id=1, source_target_pairs={{12,0},{13,1},{14,2},{15,3},{28,16},{29,17},{30,18},{31,19}} | collective-permute-start | bytes 405512 | tf_op jit(solution)/shard_map/ppermute | solution.py:66
  87.2 22.9 %collective-permute-start.16 = (bf16[528,128]{1,0:T(8,128)(2,1)}, bf16[528,128]{1,0:T(8,128)(2,1)}, u32[]{:S(2)}, u32[]{:S(2)}) collective-permute-start(bf16[528,128]{1,0:T(8,128)(2,1)} %pad_maximum_fusion.4), channel_id=1, source_target_pairs={{8,0},{12,4},{9,1},{13,5},{10,2},{14,6},{11,3},{15,7},{24,16},{28,... | collective-permute-start | bytes 405512 | tf_op jit(solution)/shard_map/ppermute | solution.py:66
  89.7 2.6 %copy-start.12 = (bf16[528,128]{1,0:T(8,128)(2,1)S(1)}, bf16[528,128]{1,0:T(8,128)(2,1)}, u32[]{:S(2)}) copy-start(bf16[528,128]{1,0:T(8,128)(2,1)} %copy-done.11) | copy-start | bytes 405508
  98.3 12.5 %collective-permute-start.15 = (bf16[528,128]{1,0:T(8,128)(2,1)}, bf16[528,128]{1,0:T(8,128)(2,1)}, u32[]{:S(2)}, u32[]{:S(2)}) collective-permute-start(bf16[528,128]{1,0:T(8,128)(2,1)} %pad_maximum_fusion.4), channel_id=1, source_target_pairs={{4,0},{8,4},{12,8},{5,1},{9,5},{13,9},{6,2},{10,6},{14,10},{7,3},{... | collective-permute-start | bytes 405512 | tf_op jit(solution)/shard_map/ppermute | solution.py:66
  102.9 2.8 %copy-start.73 = (f32[8]{0:T(128)}, f32[8]{0:T(128)S(1)}, u32[]{:S(2)}) copy-start(f32[8]{0:T(128)S(1)} %get-tuple-element.59) | copy-start | bytes 100
  102.9 2.8 %copy-start.75 = (f32[8]{0:T(128)}, f32[8]{0:T(128)S(1)}, u32[]{:S(2)}) copy-start(f32[8]{0:T(128)S(1)} %get-tuple-element.62) | copy-start | bytes 100
  108.2 6.2 %copy-start.2 = (f32[8,128,128]{1,2,0:T(8,128)S(1)}, f32[8,128,128]{1,2,0:T(8,128)}, u32[]{:S(2)}) copy-start(f32[8,128,128]{1,2,0:T(8,128)} %get-tuple-element.103) | copy-start | bytes 1572868
  111.6 2.8 %copy-start.32 = (f32[128,64]{0,1:T(8,128)S(1)}, f32[128,64]{0,1:T(8,128)}, u32[]{:S(2)}) copy-start(f32[128,64]{0,1:T(8,128)} %copy-done.30) | copy-start | bytes 98308
  115.0 3.1 %copy-start.6 = (bf16[512,128]{1,0:T(8,128)(2,1)S(1)}, bf16[512,128]{1,0:T(8,128)(2,1)}, u32[]{:S(2)}) copy-start(bf16[512,128]{1,0:T(8,128)(2,1)} %copy-done.5) | copy-start | bytes 393220
  (69 other events, 76.4 us)

commit v3 on v0

--- a/solution.py
+++ b/solution.py
@@ -178,8 +178,7 @@
     flow = jnp.einsum(
         "htn,htp->hnp", out_heads * from_start[..., None], grad_out, precision=highest
     )
-    local_dx = jnp.einsum("hts,htp->hsp", mixing, grad_out, precision=highest)
-    closing = jnp.sum(forward_term - jnp.sum(inputs_wide * local_dx, axis=2), axis=1)
+    closing = jnp.sum(flow * entering, axis=(1, 2))
     if ends_earlier:
         ends_dot_flow = jnp.stack(
             [jnp.sum(ends.astype(jnp.float32) * flow, axis=(1, 2)) for ends in ends_earlier]
@@ -188,6 +187,8 @@
         ends_dot_flow = jnp.zeros((1,) + totals.shape, jnp.float32)
 
     flow_later = shifted(pack_rows(flow, [totals, closing, ends_dot_flow]), -1)
+
+    local_dx = jnp.einsum("hts,htp->hsp", mixing, grad_out, precision=highest)
 
     cross = jnp.einsum("htp,hsp->hts", grad_out, inputs_wide, precision=highest)
     paired = decayed * cross

time: 88.9 us -> 82.4 us (0.927)
  matrix products: 33.3 us -> 29.7 us
  other arithmetic: 9.21 us -> 7.18 us
    dot_general x4, matrix products: 5.34 us -> 3.75 us  [teacher_rows(): jnp.einsum('gptd,gkd->gptk', grouped, block[..., :head_width], preferred_...]
    dot_general x1, matrix products: 2.34 us -> 1.04 us  [body(): jnp.einsum('hnp,htp->htn', entering, grad_out, precision=highest)]
    dot_general x1, matrix products: 3.08 us -> 2.02 us  [body(): jnp.einsum('htn,hnp->htp', out_heads, entering, precision=highest)]
    concatenate x2, other arithmetic: 1.69 us -> 0.78 us  [pack_rows(): return jnp.concatenate([rows, extra], axis=0)]
    slice x6 -> x7, local copies, waits for them, and re-layouts: 1.94 us -> 1.04 us  [unpack_rows(): big = received[:big_rows].reshape(big_shape)]
    unnamed x56 -> x40, local copies, waits for them, and re-layouts: 3.95 us -> 4.04 us
  transfers between devices with their start and end apart: 9 -> 9, of which waited for: 5 -> 5; matrix products, arithmetic and copies ran while one was open for 27% -> 28% of each run, Pallas kernels for 0% -> 0%
where the time goes in v3:
time: 82.4 us; the launch traced here: 81.6 us
  matrix products  29.7 us (36%)
  waiting for transfers between devices  22.1 us (27%)
  starting transfers between devices  15.8 us (19%)
  other arithmetic  7.18 us (9%)
  local copies, waits for them, and re-layouts  5.56 us (7%)
  between operations  1.28 us (2%)
    ppermute x9, waiting for transfers between devices, shifted(): moved.append(lax.ppermute(x, 'seq', pairs))  22.1 us
    ppermute x9, starting transfers between devices, shifted(): moved.append(lax.ppermute(x, 'seq', pairs))  15.8 us
    dot_general x4, matrix products, teacher_rows(): jnp.einsum('gptk,gkd->gptd', exponentials.astype(jnp.bfloat16), block[......  4.06 us
    unnamed x40, local copies, waits for them, and re-layouts  4.04 us
    dot_general x4, matrix products, teacher_rows(): jnp.einsum('gptd,gkd->gptk', grouped, block[..., :head_width], preferred_...  3.75 us
    dot_general x1, matrix products, body(): jnp.einsum('hts,hsn->htn', paired, in_heads, precision=highest)  2.94 us
    dot_general x1, matrix products, body(): jnp.einsum('hsn,hnp->hsp', weighted_in, incoming, precision=highest)  2.84 us
    dot_general x1, matrix products, body(): local_din = jnp.einsum('hts,htn->hsn', paired, out_heads, precision=highest)  2.44 us
  transfers between devices with their start and end apart: 9, of which 5 were waited for; matrix products, arithmetic and copies ran while one was open for 28% of the time, Pallas kernels for 0%

profile of v3, /device:TPU:8, one launch (start us, length us, event | category | flops | bytes accessed | tf_op | source)
XLA Modules:
  0.0 81.6 jit_solution(6475823142860286927)
XLA Ops:
  0.7 1.5 %collective-permute-start.5 = (bf16[2,128,256]{2,1,0:T(8,128)(2,1)}, bf16[2,128,256]{2,1,0:T(8,128)(2,1)}, u32[]{:S(2)}, u32[]{:S(2)}) collective-permute-start(bf16[2,128,256]{2,1,0:T(8,128)(2,1)} %param.8), channel_id=1, source_target_pairs={{0,12},{1,13},{2,14},{3,15},{16,28},{17,29},{18,30},{19,31}} | collective-permute-start | bytes 393224 | tf_op jit(solution)/shard_map/ppermute | solution.py:66
  2.1 3.5 %collective-permute-start.3 = (bf16[2,128,256]{2,1,0:T(8,128)(2,1)}, bf16[2,128,256]{2,1,0:T(8,128)(2,1)}, u32[]{:S(2)}, u32[]{:S(2)}) collective-permute-start(bf16[2,128,256]{2,1,0:T(8,128)(2,1)} %param.8), channel_id=1, source_target_pairs={{0,4},{4,8},{8,12},{1,5},{5,9},{9,13},{2,6},{6,10},{10,14},{3,7},{... | collective-permute-start | bytes 393224 | tf_op jit(solution)/shard_map/ppermute | solution.py:66
  5.6 2.9 %collective-permute-start.4 = (bf16[2,128,256]{2,1,0:T(8,128)(2,1)}, bf16[2,128,256]{2,1,0:T(8,128)(2,1)}, u32[]{:S(2)}, u32[]{:S(2)}) collective-permute-start(bf16[2,128,256]{2,1,0:T(8,128)(2,1)} %param.8), channel_id=1, source_target_pairs={{0,8},{4,12},{1,9},{5,13},{2,10},{6,14},{3,11},{7,15},{16,24},{20,... | collective-permute-start | bytes 393224 | tf_op jit(solution)/shard_map/ppermute | solution.py:66
  8.5 0.7 fusion.51
  10.1 0.5 convolution_convert_fusion
  10.9 0.8 pad_maximum_fusion.1
  11.7 1.3 %collective-permute-start.1 = (bf16[1040,128]{1,0:T(8,128)(2,1)}, bf16[1040,128]{1,0:T(8,128)(2,1)S(1)}, u32[]{:S(2)}, u32[]{:S(2)}) collective-permute-start(bf16[1040,128]{1,0:T(8,128)(2,1)} %pad_maximum_fusion.1), channel_id=1, source_target_pairs={{0,8},{4,12},{1,9},{5,13},{2,10},{6,14},{3,11},{7,15},{16,24},{20,... | collective-permute-start | bytes 798728 | tf_op jit(solution)/shard_map/ppermute | solution.py:66
  13.0 1.9 %collective-permute-start = (bf16[1040,128]{1,0:T(8,128)(2,1)}, bf16[1040,128]{1,0:T(8,128)(2,1)S(1)}, u32[]{:S(2)}, u32[]{:S(2)}) collective-permute-start(bf16[1040,128]{1,0:T(8,128)(2,1)} %pad_maximum_fusion.1), channel_id=1, source_target_pairs={{0,4},{4,8},{8,12},{1,5},{5,9},{9,13},{2,6},{6,10},{10,14},{3,7},{... | collective-permute-start | bytes 798728 | tf_op jit(solution)/shard_map/ppermute | solution.py:66
  15.2 0.3 bitcast_multiply_fusion.1
  15.6 2.3 %fusion.102 = f32[16,128,128]{1,2,0:T(8,128)} fusion(f32[16,128,128]{2,1,0:T(8,128)S(1)} %bitcast_multiply_fusion.1, bf16[16,128,128]{2,1,0:T(8,128)(2,1)S(1)} %copy-done.1), kind=kOutput, calls=%fused_computation.198 | convolution fusion | flops 402653184 | bytes 2621440 | tf_op jit(solution)/shard_map/hts,hsp->htp/dot_general | solution.py:161
  17.9 0.3 fusion.100
  18.7 0.7 collective-permute-start.2
  19.3 1.2 %fusion.101 = (f32[2,8,128]{2,1,0:T(8,128)S(1)}, f32[2,8,128,128]{2,3,1,0:T(8,128)S(1)}) fusion(bf16[2,8,128,128]{3,2,1,0:T(8,128)(2,1)S(1)} %bitcast.178, bf16[2,128,256]{2,1,0:T(8,128)(2,1)} %collective-permute-done.3, pred[]{:T(512)S(6)} %ge.51), kind=kOutput, calls=%fused_computation.197 | convolution fusion | flops 67893248 | bytes 1646593 | tf_op jit(solution)/shard_map/gptd,gkd->gptk/dot_general | solution.py:87
  20.5 1.1 %fusion.98 = (f32[2,8,128]{2,1,0:T(8,128)S(1)}, f32[2,8,128,128]{2,3,1,0:T(8,128)S(1)}) fusion(bf16[2,8,128,128]{3,2,1,0:T(8,128)(2,1)S(1)} %bitcast.180, bf16[2,128,256]{2,1,0:T(8,128)(2,1)} %collective-permute-done.5, pred[]{:T(512)S(6)} %ge.53), kind=kOutput, calls=%fused_computation.194 | convolution fusion | flops 67893248 | bytes 1646593 | tf_op jit(solution)/shard_map/gptd,gkd->gptk/dot_general | solution.py:87
  21.7 1.8 %collective-permute-done.4 = bf16[2,128,256]{2,1,0:T(8,128)(2,1)} collective-permute-done((bf16[2,128,256]{2,1,0:T(8,128)(2,1)}, bf16[2,128,256]{2,1,0:T(8,128)(2,1)}, u32[]{:S(2)}, u32[]{:S(2)}) %collective-permute-start.4) | collective-permute-done | bytes 131104 | tf_op jit(solution)/shard_map/ppermute | solution.py:66
  23.5 1.1 %fusion.99 = (f32[2,8,128]{2,1,0:T(8,128)S(1)}, f32[2,8,128,128]{2,3,1,0:T(8,128)S(1)}) fusion(bf16[2,8,128,128]{3,2,1,0:T(8,128)(2,1)S(1)} %bitcast.179, bf16[2,128,256]{2,1,0:T(8,128)(2,1)} %collective-permute-done.4, pred[]{:T(512)S(6)} %ge.52), kind=kOutput, calls=%fused_computation.195 | convolution fusion | flops 67893248 | bytes 1646593 | tf_op jit(solution)/shard_map/gptd,gkd->gptk/dot_general | solution.py:87
  24.7 0.3 fusion.32
  25.0 1.0 %fusion.16 = (f32[2,8,128]{2,1,0:T(8,128)S(1)}, f32[2,8,128]{2,1,0:T(8,128)S(1)}, f32[2,8,128]{2,1,0:T(8,128)S(1)}, f32[2,8,128]{2,1,0:T(8,128)S(1)}) fusion(f32[2,8,128,128]{2,3,1,0:T(8,128)S(1)} %get-tuple-element.49, f32[2,8,128]{2,1,0:T(8,128)S(1)} %maximum_maximum_fusion, f32[2,8,128,128]{2,3,1,0:T(8,128)S(1)} %get-tuple-element.47, ...), kind=kLoop, calls=%fused_computation.47 | loop fusion | flops 2088960 | bytes 4235264 | tf_op jit(solution)/shard_map/reduce_sum | solution.py:103
  26.0 1.2 %fusion.28 = f32[2,8,128,128]{2,3,1,0:T(8,128)S(1)} fusion(f32[2,8,128,128]{2,3,1,0:T(8,128)S(1)} %get-tuple-element.43, f32[2,8,128]{2,1,0:T(8,128)S(1)} %maximum_maximum_fusion, bf16[2,128,256]{2,1,0:T(8,128)(2,1)} %collective-permute-done.5), kind=kOutput, calls=%fused_computation.65 | convolution fusion | flops 67633152 | bytes 2170880 | tf_op jit(solution)/shard_map/gptk,gkd->gptd/dot_general | solution.py:104
  27.2 1.2 %convolution_add_fusion.2 = f32[2,8,128,128]{2,3,1,0:T(8,128)S(1)} fusion(f32[2,8,128,128]{2,3,1,0:T(8,128)S(1)} %fusion.32, f32[2,8,128,128]{2,3,1,0:T(8,128)S(1)} %get-tuple-element.49, f32[2,8,128]{2,1,0:T(8,128)S(1)} %maximum_maximum_fusion, bf16[2,128,256]{2,1,0:T(8,128)(2,1)} %collective-permute-done.3), kind=kOutput, calls=%fused_computation.8 | convolution fusion | flops 67895296 | bytes 3219456 | tf_op jit(solution)/shard_map/gptk,gkd->gptd/dot_general | solution.py:104
  28.4 1.4 %multiply_reduce_fusion.2 = (f32[2,8,128]{2,1,0:T(8,128)S(1)}, f32[2,8,128,128]{2,3,1,0:T(8,128)S(1)}) fusion(f32[2,8,128]{2,1,0:T(8,128)S(1)} %add_add_fusion, f32[2,8,128,128]{2,3,1,0:T(8,128)S(1)} %fusion.28, f32[2,8,128,128]{2,3,1,0:T(8,128)S(1)} %convolution_add_fusion.2, bf16[2,128,256]{2,1,0:T(8,128)(2,1)} %collective-permute-done.4, ...), kind=kOutput, calls=%fused_computation.38 | convolution fusion | flops 69466112 | bytes 4284416 | tf_op jit(solution)/shard_map/gptk,gkd->gptd/dot_general | solution.py:104
  29.8 5.2 %collective-permute-done.1 = bf16[1040,128]{1,0:T(8,128)(2,1)S(1)} collective-permute-done((bf16[1040,128]{1,0:T(8,128)(2,1)}, bf16[1040,128]{1,0:T(8,128)(2,1)S(1)}, u32[]{:S(2)}, u32[]{:S(2)}) %collective-permute-start.1) | collective-permute-done | bytes 266272 | tf_op jit(solution)/shard_map/ppermute | solution.py:66
  34.9 5.0 %collective-permute-done = bf16[1040,128]{1,0:T(8,128)(2,1)S(1)} collective-permute-done((bf16[1040,128]{1,0:T(8,128)(2,1)}, bf16[1040,128]{1,0:T(8,128)(2,1)S(1)}, u32[]{:S(2)}, u32[]{:S(2)}) %collective-permute-start) | collective-permute-done | bytes 266272 | tf_op jit(solution)/shard_map/ppermute | solution.py:66
  40.0 0.3 fusion.24
  40.4 0.8 %copy-done.8 = f32[16,128,128]{1,2,0:T(8,128)S(1)} copy-done((f32[16,128,128]{1,2,0:T(8,128)S(1)}, f32[16,128,128]{1,2,0:T(8,128)}, u32[]{:S(2)}) %copy-start.8) | copy-done | bytes 1048600
  41.3 2.0 %multiply_reduce_fusion.3 = (f32[16,128]{1,0:T(8,128)S(1)}, f32[16,128,128]{1,2,0:T(8,128)S(1)}) fusion(bf16[16,128,128]{1,2,0:T(8,128)(2,1)S(1)} %copy.48, f32[16]{0:T(128)S(1)} %copy-done.16, f32[16,128,128]{1,2,0:T(8,128)S(1)} %copy-done.8, f32[16,64,128]{2,1,0:T(8,128)S(1)} %fusion.24, f32[16,128,64]{1,2,0:T(8,128)S(1)} %bitcast.181, ...), kind=kOutput, calls=%fused_computation.43 | convolution fusion | flops 203159552 | bytes 3686464 | tf_op jit(solution)/shard_map/htn,hnp->htp/dot_general | solution.py:169
  43.3 0.4 multiply_reduce_fusion.1
  43.7 0.6 multiply_reduce_fusion
  44.3 2.1 %fusion.36 = f32[16,64,128]{2,1,0:T(8,128)S(1)} fusion(f32[16,128,128]{1,2,0:T(8,128)S(1)} %get-tuple-element.21, f32[16,128,64]{1,2,0:T(8,128)S(1)} %bitcast.182, f32[16,128]{1,0:T(8,128)S(1)} %get-tuple-element.31), kind=kOutput, calls=%fused_computation.73 | convolution fusion | flops 201457664 | bytes 2105344 | tf_op jit(solution)/shard_map/htn,htp->hnp/dot_general | solution.py:178
  46.5 0.9 %slice-done = bf16[1024,128]{1,0:T(8,128)(2,1)S(1)} async-done(((bf16[1040,128]{1,0:T(8,128)(2,1)}), bf16[1024,128]{1,0:T(8,128)(2,1)S(1)}, s32[]{:S(2)}) %slice-start) | async-done | bytes 262168 | tf_op jit(solution)/shard_map/slice | solution.py:38
  47.5 0.4 multiply_reduce_fusion.4
  48.1 0.7 collective-permute-start.8
  48.8 1.3 %collective-permute-start.7 = (bf16[1040,128]{1,0:T(8,128)(2,1)S(1)}, bf16[1040,128]{1,0:T(8,128)(2,1)S(1)}, u32[]{:S(2)}, u32[]{:S(2)}) collective-permute-start(bf16[1040,128]{1,0:T(8,128)(2,1)S(1)} %pad_maximum_fusion.2), channel_id=1, source_target_pairs={{8,0},{12,4},{9,1},{13,5},{10,2},{14,6},{11,3},{15,7},{24,16},{28,... | collective-permute-start | bytes 798728 | tf_op jit(solution)/shard_map/ppermute | solution.py:66
  50.1 2.1 %collective-permute-start.6 = (bf16[1040,128]{1,0:T(8,128)(2,1)S(1)}, bf16[1040,128]{1,0:T(8,128)(2,1)S(1)}, u32[]{:S(2)}, u32[]{:S(2)}) collective-permute-start(bf16[1040,128]{1,0:T(8,128)(2,1)S(1)} %pad_maximum_fusion.2), channel_id=1, source_target_pairs={{4,0},{8,4},{12,8},{5,1},{9,5},{13,9},{6,2},{10,6},{14,10},{7,3},{... | collective-permute-start | bytes 798728 | tf_op jit(solution)/shard_map/ppermute | solution.py:66
  52.2 2.3 %fusion.103 = f32[16,128,128]{1,2,0:T(8,128)S(1)} fusion(f32[16,128,128]{2,1,0:T(8,128)} %copy-done.2, f32[16,128,128]{1,2,0:T(8,128)S(1)} %get-tuple-element.21), kind=kOutput, calls=%fused_computation.199 | convolution fusion | flops 402653184 | bytes 3145728 | tf_op jit(solution)/shard_map/hts,htp->hsp/dot_general | solution.py:191
  54.5 1.2 %convolution_multiply_fusion = f32[16,128,128]{2,1,0:T(8,128)S(1)} fusion(f32[16,128,128]{1,2,0:T(8,128)S(1)} %get-tuple-element.21, bf16[16,128,128]{2,1,0:T(8,128)(2,1)S(1)} %copy-done.1, f32[16,128]{1,0:T(8,128)S(1)} %reduce_window_sum.21, pred[128,128]{1,0:T(8,128)(4,1)S(1)} %copy.44), kind=kOutput, calls=%fused_computation | convolution fusion | flops 403701760 | bytes 2646016 | tf_op jit(solution)/shard_map/htp,hsp->hts/dot_general | solution.py:193
  55.8 1.0 %convolution_multiply_fusion.6 = f32[16,128,64]{1,2,0:T(8,128)S(1)} fusion(f32[16,128,128]{1,2,0:T(8,128)S(1)} %get-tuple-element.21, f32[16,64,128]{2,1,0:T(8,128)S(1)} %copy-done.7, f32[16,128]{1,0:T(8,128)S(1)} %get-tuple-element.31), kind=kOutput, calls=%fused_computation.21 | convolution fusion | flops 201457664 | bytes 2105344 | tf_op jit(solution)/shard_map/hnp,htp->htn/dot_general | solution.py:197
  56.8 0.4 copy-done.5
  57.2 2.9 %convolution_add_fusion.3 = f32[16,128,64]{1,2,0:T(8,128)} fusion(f32[16,128,64]{1,2,0:T(8,128)S(1)} %convolution_multiply_fusion.6, f32[16,128,128]{2,1,0:T(8,128)S(1)} %convolution_multiply_fusion, f32[16,128,64]{1,2,0:T(8,128)S(1)} %bitcast.185), kind=kOutput, calls=%fused_computation.22 | convolution fusion | flops 201457664 | bytes 2621440 | tf_op jit(solution)/shard_map/hts,hsn->htn/dot_general | solution.py:196
  60.1 0.8 collective-permute-done.7
  60.9 9.3 %collective-permute-done.6 = bf16[1040,128]{1,0:T(8,128)(2,1)S(1)} collective-permute-done((bf16[1040,128]{1,0:T(8,128)(2,1)S(1)}, bf16[1040,128]{1,0:T(8,128)(2,1)S(1)}, u32[]{:S(2)}, u32[]{:S(2)}) %collective-permute-start.6) | collective-permute-done | bytes 266272 | tf_op jit(solution)/shard_map/ppermute | solution.py:66
  70.4 2.0 %fusion.10 = f32[16,128,64]{1,2,0:T(8,128)} fusion(bf16[16,128,128]{2,1,0:T(8,128)(2,1)S(1)} %copy-done.1, f32[16,128]{1,0:T(8,128)S(1)} %get-tuple-element.32, bf16[16,64,128]{2,1,0:T(8,128)(2,1)S(1)} %bitcast.191, f32[16,64,128]{2,1,0:T(8,128)S(1)} %bitcast.187, bf16[16,64,128]{2,1,0:T(8,128)(2,1)S(1)} %bitcast.189, f32[16]{0:T(128)S(1)} %get-tuple-element.34, ...), kind=kOutput, calls=%fused_computation.25 | convolution fusion | flops 202244096 | bytes 2105472 | tf_op jit(solution)/shard_map/hnp,hsp->hsn/dot_general | solution.py:228
  72.4 2.8 %fusion.12 = (f32[16,128]{1,0:T(8,128)S(1)}, bf16[16,128,128]{1,2,0:T(8,128)(2,1)}) fusion(bf16[16,128,128]{1,2,0:T(8,128)(2,1)S(1)} %copy.48, f32[16,128,128]{1,2,0:T(8,128)S(1)} %get-tuple-element.21, f32[16]{0:T(128)S(1)} %copy-done.16, f32[16,128,128]{1,2,0:T(8,128)S(1)} %fusion.103, bf16[16,64,128]{2,1,0:T(8,128)(2,1)S(1)} %bitcast.192, ...), kind=kOutput, calls=%fused_computation.28 | convolution fusion | flops 204077056 | bytes 4735168 | tf_op jit(solution)/shard_map/hsn,hnp->hsp/dot_general | solution.py:223
  75.2 1.2 %reduce_window_sum.22 = f32[16,128]{1,0:T(8,128)S(1)} reduce-window(f32[16,128]{1,0:T(8,128)S(1)} %sub.114, f32[]{:T(128)} %constant.12.clone.1), window={size=1x128 pad=0_0x0_127}, to_apply=%region_19.20 | reduce-window | flops 260096 | bytes 16388 | tf_op jit(solution)/shard_map/body/reduce_window_sum | solution.py:225
  76.5 2.4 %convolution_add_fusion.4 = f32[16,128,64]{1,2,0:T(8,128)S(1)} fusion(f32[16,128,64]{1,2,0:T(8,128)} %fusion.10, f32[16,128,128]{2,1,0:T(8,128)} %copy-done.3, f32[16,128,64]{1,2,0:T(8,128)S(1)} %bitcast.183), kind=kOutput, calls=%fused_computation.23 | convolution fusion | flops 201457664 | bytes 2621440 | tf_op jit(solution)/shard_map/hts,htn->hsn/dot_general | solution.py:195
  79.0 0.7 copy.61
  80.0 1.0 %copy.60 = bf16[16,128,128]{2,1,0:T(8,128)(2,1)} copy(bf16[16,128,128]{1,2,0:T(8,128)(2,1)S(1)} %copy-done.10) | data formatting | bytes 1048576
  81.0 0.7 broadcast_add_fusion
  (85 shorter events, 2.8 us)
Async XLA Ops:
  0.6 17.3 %copy-start = (bf16[16,128,128]{2,1,0:T(8,128)(2,1)S(1)}, bf16[16,128,128]{2,1,0:T(8,128)(2,1)}, u32[]{:S(2)}) copy-start(bf16[16,128,128]{2,1,0:T(8,128)(2,1)} %param.7) | copy-start | bytes 1572868
  0.6 9.2 %copy-start.13 = (bf16[2,128,128]{2,1,0:T(8,128)(2,1)S(1)}, bf16[2,128,128]{2,1,0:T(8,128)(2,1)}, u32[]{:S(2)}) copy-start(bf16[2,128,128]{2,1,0:T(8,128)(2,1)} %param.10) | copy-start | bytes 196612
  0.7 9.5 %copy-start.1 = (bf16[16,128,128]{2,1,0:T(8,128)(2,1)S(1)}, bf16[16,128,128]{2,1,0:T(8,128)(2,1)}, u32[]{:S(2)}) copy-start(bf16[16,128,128]{2,1,0:T(8,128)(2,1)} %param.9) | copy-start | bytes 1572868
  0.7 19.8 %collective-permute-start.5 = (bf16[2,128,256]{2,1,0:T(8,128)(2,1)}, bf16[2,128,256]{2,1,0:T(8,128)(2,1)}, u32[]{:S(2)}, u32[]{:S(2)}) collective-permute-start(bf16[2,128,256]{2,1,0:T(8,128)(2,1)} %param.8), channel_id=1, source_target_pairs={{0,12},{1,13},{2,14},{3,15},{16,28},{17,29},{18,30},{19,31}} | collective-permute-start | bytes 393224 | tf_op jit(solution)/shard_map/ppermute | solution.py:66
  2.1 16.5 %collective-permute-start.3 = (bf16[2,128,256]{2,1,0:T(8,128)(2,1)}, bf16[2,128,256]{2,1,0:T(8,128)(2,1)}, u32[]{:S(2)}, u32[]{:S(2)}) collective-permute-start(bf16[2,128,256]{2,1,0:T(8,128)(2,1)} %param.8), channel_id=1, source_target_pairs={{0,4},{4,8},{8,12},{1,5},{5,9},{9,13},{2,6},{6,10},{10,14},{3,7},{... | collective-permute-start | bytes 393224 | tf_op jit(solution)/shard_map/ppermute | solution.py:66
  5.6 17.9 %collective-permute-start.4 = (bf16[2,128,256]{2,1,0:T(8,128)(2,1)}, bf16[2,128,256]{2,1,0:T(8,128)(2,1)}, u32[]{:S(2)}, u32[]{:S(2)}) collective-permute-start(bf16[2,128,256]{2,1,0:T(8,128)(2,1)} %param.8), channel_id=1, source_target_pairs={{0,8},{4,12},{1,9},{5,13},{2,10},{6,14},{3,11},{7,15},{16,24},{20,... | collective-permute-start | bytes 393224 | tf_op jit(solution)/shard_map/ppermute | solution.py:66
  10.1 0.8 copy-start.4
  11.7 23.2 %collective-permute-start.1 = (bf16[1040,128]{1,0:T(8,128)(2,1)}, bf16[1040,128]{1,0:T(8,128)(2,1)S(1)}, u32[]{:S(2)}, u32[]{:S(2)}) collective-permute-start(bf16[1040,128]{1,0:T(8,128)(2,1)} %pad_maximum_fusion.1), channel_id=1, source_target_pairs={{0,8},{4,12},{1,9},{5,13},{2,10},{6,14},{3,11},{7,15},{16,24},{20,... | collective-permute-start | bytes 798728 | tf_op jit(solution)/shard_map/ppermute | solution.py:66
  13.0 26.9 %collective-permute-start = (bf16[1040,128]{1,0:T(8,128)(2,1)}, bf16[1040,128]{1,0:T(8,128)(2,1)S(1)}, u32[]{:S(2)}, u32[]{:S(2)}) collective-permute-start(bf16[1040,128]{1,0:T(8,128)(2,1)} %pad_maximum_fusion.1), channel_id=1, source_target_pairs={{0,4},{4,8},{8,12},{1,5},{5,9},{9,13},{2,6},{6,10},{10,14},{3,7},{... | collective-permute-start | bytes 798728 | tf_op jit(solution)/shard_map/ppermute | solution.py:66
  15.6 2.3 %copy-start.2 = (f32[16,128,128]{2,1,0:T(8,128)}, f32[16,128,128]{2,1,0:T(8,128)S(1)}, u32[]{:S(2)}) copy-start(f32[16,128,128]{2,1,0:T(8,128)S(1)} %bitcast_multiply_fusion.1) | copy-start | bytes 3145732
  15.6 2.3 %copy-start.15 = (bf16[2,128,256]{2,1,0:T(8,128)(2,1)S(1)}, bf16[2,128,256]{2,1,0:T(8,128)(2,1)}, u32[]{:S(2)}) copy-start(bf16[2,128,256]{2,1,0:T(8,128)(2,1)} %param.8) | copy-start | bytes 393220
  18.7 21.3 %collective-permute-start.2 = (bf16[1040,128]{1,0:T(8,128)(2,1)}, bf16[1040,128]{1,0:T(8,128)(2,1)S(1)}, u32[]{:S(2)}, u32[]{:S(2)}) collective-permute-start(bf16[1040,128]{1,0:T(8,128)(2,1)} %pad_maximum_fusion.1), channel_id=1, source_target_pairs={{0,12},{1,13},{2,14},{3,15},{16,28},{17,29},{18,30},{19,31}} | collective-permute-start | bytes 798728 | tf_op jit(solution)/shard_map/ppermute | solution.py:66
  28.4 11.6 %copy-start.14 = (f32[16,64,128]{2,1,0:T(8,128)S(1)}, f32[16,64,128]{2,1,0:T(8,128)}, u32[]{:S(2)}) copy-start(f32[16,64,128]{2,1,0:T(8,128)} %param.13) | copy-start | bytes 1572868
  34.9 5.4 %copy-start.12 = (bf16[1040,128]{1,0:T(8,128)(2,1)}, bf16[1040,128]{1,0:T(8,128)(2,1)S(1)}, u32[]{:S(2)}) copy-start(bf16[1040,128]{1,0:T(8,128)(2,1)S(1)} %collective-permute-done.1) | copy-start | bytes 798724
  39.9 6.5 %copy-start.11 = (bf16[1040,128]{1,0:T(8,128)(2,1)}, bf16[1040,128]{1,0:T(8,128)(2,1)S(1)}, u32[]{:S(2)}) copy-start(bf16[1040,128]{1,0:T(8,128)(2,1)S(1)} %collective-permute-done) | copy-start | bytes 798724
  40.0 1.2 %copy-start.8 = (f32[16,128,128]{1,2,0:T(8,128)S(1)}, f32[16,128,128]{1,2,0:T(8,128)}, u32[]{:S(2)}) copy-start(f32[16,128,128]{1,2,0:T(8,128)} %fusion.102) | copy-start | bytes 3145732
  40.3 6.2 %copy-start.6 = (f32[16,64,128]{2,1,0:T(8,128)}, f32[16,64,128]{2,1,0:T(8,128)S(1)}, u32[]{:S(2)}) copy-start(f32[16,64,128]{2,1,0:T(8,128)S(1)} %fusion.24) | copy-start | bytes 1572868
  40.4 0.8 %copy-start.16 = (f32[16]{0:T(128)S(1)}, f32[16]{0:T(128)}, u32[]{:S(2)}) copy-start(f32[16]{0:T(128)} %param.12) | copy-start | bytes 196
  46.5 1.0 %slice-start = ((bf16[1040,128]{1,0:T(8,128)(2,1)}), bf16[1024,128]{1,0:T(8,128)(2,1)S(1)}, s32[]{:S(2)}) async-start(bf16[1040,128]{1,0:T(8,128)(2,1)} %copy-done.11), calls=%async_computation | async-start | bytes 524288 | tf_op jit(solution)/shard_map/slice | solution.py:38
  46.5 1.0 %slice-start.1 = ((bf16[1040,128]{1,0:T(8,128)(2,1)}), bf16[1024,128]{1,0:T(8,128)(2,1)S(1)}, s32[]{:S(2)}) async-start(bf16[1040,128]{1,0:T(8,128)(2,1)} %copy-done.12), calls=%async_computation.1 | async-start | bytes 524288 | tf_op jit(solution)/shard_map/slice | solution.py:38
  48.1 12.0 %collective-permute-start.8 = (bf16[1040,128]{1,0:T(8,128)(2,1)S(1)}, bf16[1040,128]{1,0:T(8,128)(2,1)S(1)}, u32[]{:S(2)}, u32[]{:S(2)}) collective-permute-start(bf16[1040,128]{1,0:T(8,128)(2,1)S(1)} %pad_maximum_fusion.2), channel_id=1, source_target_pairs={{12,0},{13,1},{14,2},{15,3},{28,16},{29,17},{30,18},{31,19}} | collective-permute-start | bytes 798728 | tf_op jit(solution)/shard_map/ppermute | solution.py:66
  48.8 12.1 %collective-permute-start.7 = (bf16[1040,128]{1,0:T(8,128)(2,1)S(1)}, bf16[1040,128]{1,0:T(8,128)(2,1)S(1)}, u32[]{:S(2)}, u32[]{:S(2)}) collective-permute-start(bf16[1040,128]{1,0:T(8,128)(2,1)S(1)} %pad_maximum_fusion.2), channel_id=1, source_target_pairs={{8,0},{12,4},{9,1},{13,5},{10,2},{14,6},{11,3},{15,7},{24,16},{28,... | collective-permute-start | bytes 798728 | tf_op jit(solution)/shard_map/ppermute | solution.py:66
  50.1 20.1 %collective-permute-start.6 = (bf16[1040,128]{1,0:T(8,128)(2,1)S(1)}, bf16[1040,128]{1,0:T(8,128)(2,1)S(1)}, u32[]{:S(2)}, u32[]{:S(2)}) collective-permute-start(bf16[1040,128]{1,0:T(8,128)(2,1)S(1)} %pad_maximum_fusion.2), channel_id=1, source_target_pairs={{4,0},{8,4},{12,8},{5,1},{9,5},{13,9},{6,2},{10,6},{14,10},{7,3},{... | collective-permute-start | bytes 798728 | tf_op jit(solution)/shard_map/ppermute | solution.py:66
  54.5 1.2 %copy-start.7 = (f32[16,64,128]{2,1,0:T(8,128)S(1)}, f32[16,64,128]{2,1,0:T(8,128)}, u32[]{:S(2)}) copy-start(f32[16,64,128]{2,1,0:T(8,128)} %copy-done.6) | copy-start | bytes 1572868
  55.7 1.1 %copy-start.3 = (f32[16,128,128]{2,1,0:T(8,128)}, f32[16,128,128]{2,1,0:T(8,128)S(1)}, u32[]{:S(2)}) copy-start(f32[16,128,128]{2,1,0:T(8,128)S(1)} %convolution_multiply_fusion) | copy-start | bytes 3145732
  55.8 1.4 %copy-start.5 = (f32[2,8,128,64]{2,3,1,0:T(8,128)S(1)}, f32[2,8,128,64]{2,3,1,0:T(8,128)}, u32[]{:S(2)}) copy-start(f32[2,8,128,64]{2,3,1,0:T(8,128)} %copy-done.4) | copy-start | bytes 1572868
  76.4 2.4 %copy-start.9 = (f32[16,128,64]{1,2,0:T(8,128)S(1)}, f32[16,128,64]{1,2,0:T(8,128)}, u32[]{:S(2)}) copy-start(f32[16,128,64]{1,2,0:T(8,128)} %convolution_add_fusion.3) | copy-start | bytes 1572868
  78.9 1.0 %copy-start.10 = (bf16[16,128,128]{1,2,0:T(8,128)(2,1)S(1)}, bf16[16,128,128]{1,2,0:T(8,128)(2,1)}, u32[]{:S(2)}) copy-start(bf16[16,128,128]{1,2,0:T(8,128)(2,1)} %get-tuple-element.27) | copy-start | bytes 1572868

commit v4 on v3

--- a/solution.py
+++ b/solution.py
@@ -198,11 +198,16 @@
         "hnp,htp->htn", entering, grad_out, precision=highest
     )
 
+    grad_x_local = local_dx + skip_gain[:, None, None] * grad_out
+    local_terms = forward_term - jnp.sum(inputs_wide * local_dx, axis=2)
+    local_tail = lax.cumsum(local_terms, axis=1, reverse=True)
+    maps_in_local = local_din.reshape(local_groups, per_group, tok_dev, state_size).sum(axis=1)
+    maps_out = grad_output_maps.reshape(local_groups, per_group, tok_dev, state_size).sum(axis=1)
+
     incoming = jnp.zeros_like(flow)
     later_sum = jnp.zeros_like(totals)
     gap = jnp.zeros_like(totals)
     through = []
-    dots_there = []
     for distance, received in enumerate(flow_later, start=1):
         flows, (totals_there, closing_there, dots) = unpack_rows(
             received, flow.shape, [totals.shape, closing.shape, ends_dot_flow.shape]
@@ -220,16 +225,17 @@
         gap = gap + totals_there
         through.append(gap)
 
-    state_dx = local_dx + jnp.einsum("hsn,hnp->hsp", weighted_in, incoming, precision=highest)
-    terms = forward_term - jnp.sum(inputs_wide * state_dx, axis=2)
-    grad_log_decay = later_sum[:, None] + lax.cumsum(terms, axis=1, reverse=True)
-    grad_input_maps = (
-        local_din
-        + jnp.einsum("hnp,hsp->hsn", incoming, inputs_wide, precision=highest) * to_end[..., None]
-    )
-    grad_maps = jnp.concatenate([grad_input_maps, grad_output_maps], axis=2)
-    grad_maps = grad_maps.reshape(local_groups, per_group, tok_dev, 2 * state_size).sum(axis=1)
-    grad_x = state_dx + skip_gain[:, None, None] * grad_out
+    state_extra = jnp.einsum("hsn,hnp->hsp", weighted_in, incoming, precision=highest)
+    maps_extra = jnp.einsum("hnp,hsp->hsn", incoming, inputs_wide, precision=highest)
+    grad_x = grad_x_local + state_extra
+    extra_terms = jnp.sum(weighted_in * maps_extra, axis=2)
+    upper = (order_ids[:, None] <= order_ids[None, :]).astype(jnp.float32)
+    extra_tail = jnp.einsum("hu,su->hs", extra_terms, upper, precision=highest)
+    grad_log_decay = later_sum[:, None] + local_tail - extra_tail
+    maps_in = maps_in_local + (maps_extra * to_end[..., None]).reshape(
+        local_groups, per_group, tok_dev, state_size
+    ).sum(axis=1)
+    grad_maps = jnp.concatenate([maps_in, maps_out], axis=2)
     return (grad_x.astype(jnp.bfloat16), grad_maps.astype(jnp.bfloat16), grad_log_decay)
 
 

time: 82.4 us -> 90.6 us (1.100)
  local copies, waits for them, and re-layouts: 5.56 us -> 10.9 us
  waiting for transfers between devices: 22.1 us -> 18.6 us
  other arithmetic: 7.18 us -> 10.6 us
  matrix products: 29.7 us -> 31.2 us
  starting transfers between devices: 15.8 us -> 16.9 us
    unnamed x40 -> x52, local copies, waits for them, and re-layouts: 4.04 us -> 7.57 us
    ppermute x9, waiting for transfers between devices: 22.1 us -> 18.6 us  [shifted(): moved.append(lax.ppermute(x, 'seq', pairs))]
    convert_element_type x6, other arithmetic: 0.02 us -> 2.05 us  [join_three(): wide = parts.astype(jnp.float32)]
    slice x7 -> x6, local copies, waits for them, and re-layouts: 1.04 us -> 2.88 us  [unpack_rows(): big = received[:big_rows].reshape(big_shape)]
    dot_general x4, matrix products: 3.75 us -> 5.47 us  [teacher_rows(): jnp.einsum('gptd,gkd->gptk', grouped, block[..., :head_width], preferred_...]
    dot_general x1, matrix products: 2.84 us -> 4.01 us  [body(): jnp.einsum('hsn,hnp->hsp', weighted_in, incoming, precision=highest)]
    ppermute x9, starting transfers between devices: 15.8 us -> 16.9 us  [shifted(): moved.append(lax.ppermute(x, 'seq', pairs))]
    mul x1, other arithmetic: 0.04 us -> 1.09 us  [body(): incoming = incoming + weight[:, None, None] * flows.astype(jnp.float32)]
  transfers between devices with their start and end apart: 9 -> 9, of which waited for: 5 -> 4; matrix products, arithmetic and copies ran while one was open for 28% -> 29% of each run, Pallas kernels for 0% -> 0%
where the time goes in v4:
time: 90.6 us; the launch traced here: 89.5 us
  matrix products  31.2 us (34%)
  waiting for transfers between devices  18.6 us (21%)
  starting transfers between devices  16.9 us (19%)
  local copies, waits for them, and re-layouts  10.9 us (12%)
  other arithmetic  10.6 us (12%)
  between operations  1.31 us (1%)
    ppermute x9, waiting for transfers between devices, shifted(): moved.append(lax.ppermute(x, 'seq', pairs))  18.6 us
    ppermute x9, starting transfers between devices, shifted(): moved.append(lax.ppermute(x, 'seq', pairs))  16.9 us
    unnamed x52, local copies, waits for them, and re-layouts  7.57 us
    dot_general x4, matrix products, teacher_rows(): jnp.einsum('gptd,gkd->gptk', grouped, block[..., :head_width], preferred_...  5.47 us
    dot_general x4, matrix products, teacher_rows(): jnp.einsum('gptk,gkd->gptd', exponentials.astype(jnp.bfloat16), block[......  4.02 us
    dot_general x1, matrix products, body(): jnp.einsum('hsn,hnp->hsp', weighted_in, incoming, precision=highest)  4.01 us
    slice x6, local copies, waits for them, and re-layouts, unpack_rows(): big = received[:big_rows].reshape(big_shape)  2.88 us
    dot_general x1, matrix products, body(): local_dx = jnp.einsum('hts,htp->hsp', mixing, grad_out, precision=highest)  2.73 us
  transfers between devices with their start and end apart: 9, of which 4 were waited for; matrix products, arithmetic and copies ran while one was open for 29% of the time, Pallas kernels for 0%

profile of v4, /device:TPU:8, one launch (start us, length us, event | category | flops | bytes accessed | tf_op | source)
XLA Modules:
  0.0 89.5 jit_solution(17773274082083936164)
XLA Ops:
  0.7 1.5 %collective-permute-start.5 = (bf16[2,128,256]{2,1,0:T(8,128)(2,1)}, bf16[2,128,256]{2,1,0:T(8,128)(2,1)}, u32[]{:S(2)}, u32[]{:S(2)}) collective-permute-start(bf16[2,128,256]{2,1,0:T(8,128)(2,1)} %param.8), channel_id=1, source_target_pairs={{0,12},{1,13},{2,14},{3,15},{16,28},{17,29},{18,30},{19,31}} | collective-permute-start | bytes 393224 | tf_op jit(solution)/shard_map/ppermute | solution.py:66
  2.1 3.5 %collective-permute-start.3 = (bf16[2,128,256]{2,1,0:T(8,128)(2,1)}, bf16[2,128,256]{2,1,0:T(8,128)(2,1)}, u32[]{:S(2)}, u32[]{:S(2)}) collective-permute-start(bf16[2,128,256]{2,1,0:T(8,128)(2,1)} %param.8), channel_id=1, source_target_pairs={{0,4},{4,8},{8,12},{1,5},{5,9},{9,13},{2,6},{6,10},{10,14},{3,7},{... | collective-permute-start | bytes 393224 | tf_op jit(solution)/shard_map/ppermute | solution.py:66
  5.6 2.9 %collective-permute-start.4 = (bf16[2,128,256]{2,1,0:T(8,128)(2,1)}, bf16[2,128,256]{2,1,0:T(8,128)(2,1)}, u32[]{:S(2)}, u32[]{:S(2)}) collective-permute-start(bf16[2,128,256]{2,1,0:T(8,128)(2,1)} %param.8), channel_id=1, source_target_pairs={{0,8},{4,12},{1,9},{5,13},{2,10},{6,14},{3,11},{7,15},{16,24},{20,... | collective-permute-start | bytes 393224 | tf_op jit(solution)/shard_map/ppermute | solution.py:66
  8.5 0.7 fusion.51
  9.8 0.7 fusion.96
  11.3 0.7 pad_maximum_fusion
  12.0 2.0 %collective-permute-start.1 = (bf16[1040,128]{1,0:T(8,128)(2,1)}, bf16[1040,128]{1,0:T(8,128)(2,1)}, u32[]{:S(2)}, u32[]{:S(2)}) collective-permute-start(bf16[1040,128]{1,0:T(8,128)(2,1)} %pad_maximum_fusion), channel_id=1, source_target_pairs={{0,8},{4,12},{1,9},{5,13},{2,10},{6,14},{3,11},{7,15},{16,24},{20,... | collective-permute-start | bytes 798728 | tf_op jit(solution)/shard_map/ppermute | solution.py:66
  14.0 1.9 %collective-permute-start = (bf16[1040,128]{1,0:T(8,128)(2,1)}, bf16[1040,128]{1,0:T(8,128)(2,1)S(1)}, u32[]{:S(2)}, u32[]{:S(2)}) collective-permute-start(bf16[1040,128]{1,0:T(8,128)(2,1)} %pad_maximum_fusion), channel_id=1, source_target_pairs={{0,4},{4,8},{8,12},{1,5},{5,9},{9,13},{2,6},{6,10},{10,14},{3,7},{... | collective-permute-start | bytes 798728 | tf_op jit(solution)/shard_map/ppermute | solution.py:66
  16.7 1.2 %fusion.102 = f32[16,128,128]{1,2,0:T(8,128)S(1)} fusion(f32[16,128,128]{2,1,0:T(8,128)S(1)} %bitcast_multiply_fusion.1, bf16[16,128,128]{2,1,0:T(8,128)(2,1)S(1)} %copy-done.1), kind=kOutput, calls=%fused_computation.202 | convolution fusion | flops 402653184 | bytes 2621440 | tf_op jit(solution)/shard_map/hts,hsp->htp/dot_general | solution.py:161
  17.9 1.9 %fusion.100 = (f32[2,8,128]{2,1,0:T(8,128)}, f32[2,8,128,128]{2,3,1,0:T(8,128)}) fusion(bf16[2,8,128,128]{3,2,1,0:T(8,128)(2,1)S(1)} %bitcast.183, bf16[2,128,256]{2,1,0:T(8,128)(2,1)S(1)} %copy-done.16, pred[128,128]{0,1:T(8,128)(4,1)S(1)} %iota_compare_fusion.1), kind=kOutput, calls=%fused_computation.200 | convolution fusion | flops 67893248 | bytes 1662976 | tf_op jit(solution)/shard_map/gptd,gkd->gptk/dot_general | solution.py:87
  20.2 1.5 %copy.88 = bf16[2,128,64]{1,2,0:T(8,128)(2,1)} copy(bf16[2,128,64]{2,1,0:T(8,128)(2,1)} %get-tuple-element.27) | data formatting | bytes 65536
  21.7 0.8 collective-permute-start.2
  22.6 1.1 %fusion.101 = (f32[2,8,128]{2,1,0:T(8,128)S(1)}, f32[2,8,128,128]{2,3,1,0:T(8,128)S(1)}) fusion(bf16[2,8,128,128]{3,2,1,0:T(8,128)(2,1)S(1)} %bitcast.184, bf16[2,128,256]{2,1,0:T(8,128)(2,1)} %collective-permute-done.3, pred[]{:T(512)S(6)} %ge.55), kind=kOutput, calls=%fused_computation.201 | convolution fusion | flops 67893248 | bytes 1646593 | tf_op jit(solution)/shard_map/gptd,gkd->gptk/dot_general | solution.py:87
  23.8 1.1 %fusion.98 = (f32[2,8,128]{2,1,0:T(8,128)S(1)}, f32[2,8,128,128]{2,3,1,0:T(8,128)S(1)}) fusion(bf16[2,8,128,128]{3,2,1,0:T(8,128)(2,1)S(1)} %bitcast.186, bf16[2,128,256]{2,1,0:T(8,128)(2,1)} %collective-permute-done.5, pred[]{:T(512)S(6)} %ge.57), kind=kOutput, calls=%fused_computation.198 | convolution fusion | flops 67893248 | bytes 1646593 | tf_op jit(solution)/shard_map/gptd,gkd->gptk/dot_general | solution.py:87
  24.9 1.2 %fusion.99 = (f32[2,8,128]{2,1,0:T(8,128)S(1)}, f32[2,8,128,128]{2,3,1,0:T(8,128)S(1)}) fusion(bf16[2,8,128,128]{3,2,1,0:T(8,128)(2,1)S(1)} %bitcast.185, bf16[2,128,256]{2,1,0:T(8,128)(2,1)} %collective-permute-done.4, pred[]{:T(512)S(6)} %ge.56), kind=kOutput, calls=%fused_computation.199 | convolution fusion | flops 67893248 | bytes 1646593 | tf_op jit(solution)/shard_map/gptd,gkd->gptk/dot_general | solution.py:87
  26.6 1.0 %fusion.16 = (f32[2,8,128]{2,1,0:T(8,128)S(1)}, f32[2,8,128]{2,1,0:T(8,128)S(1)}, f32[2,8,128]{2,1,0:T(8,128)S(1)}, f32[2,8,128]{2,1,0:T(8,128)S(1)}) fusion(f32[2,8,128,128]{2,3,1,0:T(8,128)S(1)} %get-tuple-element.47, f32[2,8,128]{2,1,0:T(8,128)S(1)} %maximum_maximum_fusion, f32[2,8,128,128]{2,3,1,0:T(8,128)S(1)} %copy-done.4, ...), kind=kLoop, calls=%fused_computation.44 | loop fusion | flops 2088960 | bytes 4235264 | tf_op jit(solution)/shard_map/reduce_sum | solution.py:103
  27.6 1.2 %fusion.28 = f32[2,8,128,128]{2,3,1,0:T(8,128)S(1)} fusion(f32[2,8,128,128]{2,3,1,0:T(8,128)S(1)} %get-tuple-element.41, f32[2,8,128]{2,1,0:T(8,128)S(1)} %maximum_maximum_fusion, bf16[2,128,256]{2,1,0:T(8,128)(2,1)} %collective-permute-done.5), kind=kOutput, calls=%fused_computation.62 | convolution fusion | flops 67633152 | bytes 2170880 | tf_op jit(solution)/shard_map/gptk,gkd->gptd/dot_general | solution.py:104
  28.8 1.2 %convolution_add_fusion.2 = f32[2,8,128,128]{2,3,1,0:T(8,128)S(1)} fusion(f32[2,8,128,128]{2,3,1,0:T(8,128)S(1)} %fusion.32, f32[2,8,128,128]{2,3,1,0:T(8,128)S(1)} %get-tuple-element.47, f32[2,8,128]{2,1,0:T(8,128)S(1)} %maximum_maximum_fusion, bf16[2,128,256]{2,1,0:T(8,128)(2,1)} %collective-permute-done.3), kind=kOutput, calls=%fused_computation.8 | convolution fusion | flops 67895296 | bytes 3219456 | tf_op jit(solution)/shard_map/gptk,gkd->gptd/dot_general | solution.py:104
  30.0 1.3 %multiply_reduce_fusion.2 = (f32[2,8,128]{2,1,0:T(8,128)S(1)}, f32[2,8,128,128]{2,3,1,0:T(8,128)S(1)}) fusion(f32[2,8,128]{2,1,0:T(8,128)S(1)} %add_add_fusion, f32[2,8,128,128]{2,3,1,0:T(8,128)S(1)} %fusion.28, f32[2,8,128,128]{2,3,1,0:T(8,128)S(1)} %convolution_add_fusion.2, bf16[2,128,256]{2,1,0:T(8,128)(2,1)} %collective-permute-done.4, ...), kind=kOutput, calls=%fused_computation.35 | convolution fusion | flops 69466112 | bytes 4284416 | tf_op jit(solution)/shard_map/gptk,gkd->gptd/dot_general | solution.py:104
  31.3 3.6 %collective-permute-done.1 = bf16[1040,128]{1,0:T(8,128)(2,1)} collective-permute-done((bf16[1040,128]{1,0:T(8,128)(2,1)}, bf16[1040,128]{1,0:T(8,128)(2,1)}, u32[]{:S(2)}, u32[]{:S(2)}) %collective-permute-start.1) | collective-permute-done | bytes 266272 | tf_op jit(solution)/shard_map/ppermute | solution.py:66
  34.9 0.7 slice_convert_fusion.4
  35.6 4.3 %collective-permute-done = bf16[1040,128]{1,0:T(8,128)(2,1)S(1)} collective-permute-done((bf16[1040,128]{1,0:T(8,128)(2,1)}, bf16[1040,128]{1,0:T(8,128)(2,1)S(1)}, u32[]{:S(2)}, u32[]{:S(2)}) %collective-permute-start) | collective-permute-done | bytes 266272 | tf_op jit(solution)/shard_map/ppermute | solution.py:66
  40.0 1.3 %fusion.24 = f32[16,64,128]{2,1,0:T(8,128)S(1)} fusion(f32[16,64,128]{2,1,0:T(8,128)S(1)} %copy-done.14, f32[16]{0:T(128)S(1)} %fusion.89, f32[16]{0:T(128)S(1)} %get-tuple-element.24, f32[16]{0:T(128)S(1)} %get-tuple-element.36, f32[]{:T(128)S(6)} %select_n.163, bf16[1040,128]{1,0:T(8,128)(2,1)S(1)} %collective-permute-done.2, ...), kind=kLoop, calls=%fused_computation.58 | loop fusion | flops 1310720 | bytes 1835204 | tf_op jit(solution)/shard_map/add | solution.py:151
  41.4 0.7 copy-done.21
  42.1 2.0 %multiply_reduce_fusion.3 = (f32[16,128]{1,0:T(8,128)S(1)}, f32[16,128,128]{1,2,0:T(8,128)S(1)}) fusion(bf16[16,128,128]{1,2,0:T(8,128)(2,1)S(1)} %copy.50, f32[16]{0:T(128)S(1)} %copy-done.21, f32[16,128,128]{1,2,0:T(8,128)S(1)} %fusion.102, f32[16,64,128]{2,1,0:T(8,128)S(1)} %fusion.24, f32[16,128,64]{1,2,0:T(8,128)S(1)} %bitcast.190, ...), kind=kOutput, calls=%fused_computation.40 | convolution fusion | flops 203159552 | bytes 3686464 | tf_op jit(solution)/shard_map/htn,hnp->htp/dot_general | solution.py:169
  45.8 2.7 %fusion.12 = (f32[16,128]{1,0:T(8,128)}, f32[16,128,128]{1,2,0:T(8,128)}) fusion(bf16[16,128,128]{1,2,0:T(8,128)(2,1)S(1)} %copy.50, f32[16,128,128]{2,1,0:T(8,128)S(1)} %copy-done.3, f32[16,128,128]{1,2,0:T(8,128)S(1)} %get-tuple-element.21), kind=kOutput, calls=%fused_computation.28 | convolution fusion | flops 403437568 | bytes 3678208 | tf_op jit(solution)/shard_map/hts,htp->hsp/dot_general | solution.py:191
  48.5 2.1 %fusion.36 = f32[16,64,128]{2,1,0:T(8,128)S(1)} fusion(f32[16,128,128]{1,2,0:T(8,128)S(1)} %get-tuple-element.21, f32[16,128,64]{1,2,0:T(8,128)S(1)} %bitcast.191, f32[16,128]{1,0:T(8,128)S(1)} %get-tuple-element.29), kind=kOutput, calls=%fused_computation.74 | convolution fusion | flops 201457664 | bytes 2105344 | tf_op jit(solution)/shard_map/htn,htp->hnp/dot_general | solution.py:178
  50.6 1.0 %slice.242 = bf16[1024,128]{1,0:T(8,128)(2,1)S(1)} slice(bf16[1040,128]{1,0:T(8,128)(2,1)} %collective-permute-done.1), slice={[0:1024], [0:128]} | slice | bytes 524288 | tf_op jit(solution)/shard_map/slice | solution.py:38
  51.6 0.9 %slice-done = bf16[1024,128]{1,0:T(8,128)(2,1)S(1)} async-done(((bf16[1040,128]{1,0:T(8,128)(2,1)}), bf16[1024,128]{1,0:T(8,128)(2,1)S(1)}, s32[]{:S(2)}) %slice-start) | async-done | bytes 262168 | tf_op jit(solution)/shard_map/slice | solution.py:38
  53.2 0.8 collective-permute-start.8
  54.0 1.3 %collective-permute-start.7 = (bf16[1040,128]{1,0:T(8,128)(2,1)S(1)}, bf16[1040,128]{1,0:T(8,128)(2,1)}, u32[]{:S(2)}, u32[]{:S(2)}) collective-permute-start(bf16[1040,128]{1,0:T(8,128)(2,1)S(1)} %pad_maximum_fusion.1), channel_id=1, source_target_pairs={{8,0},{12,4},{9,1},{13,5},{10,2},{14,6},{11,3},{15,7},{24,16},{28,... | collective-permute-start | bytes 798728 | tf_op jit(solution)/shard_map/ppermute | solution.py:66
  55.3 2.1 %collective-permute-start.6 = (bf16[1040,128]{1,0:T(8,128)(2,1)S(1)}, bf16[1040,128]{1,0:T(8,128)(2,1)}, u32[]{:S(2)}, u32[]{:S(2)}) collective-permute-start(bf16[1040,128]{1,0:T(8,128)(2,1)S(1)} %pad_maximum_fusion.1), channel_id=1, source_target_pairs={{4,0},{8,4},{12,8},{5,1},{9,5},{13,9},{6,2},{10,6},{14,10},{7,3},{... | collective-permute-start | bytes 798728 | tf_op jit(solution)/shard_map/ppermute | solution.py:66
  57.4 1.2 %convolution_multiply_fusion = f32[16,128,128]{2,1,0:T(8,128)S(1)} fusion(f32[16,128,128]{1,2,0:T(8,128)S(1)} %get-tuple-element.21, bf16[16,128,128]{2,1,0:T(8,128)(2,1)S(1)} %copy-done.1, f32[16,128]{1,0:T(8,128)S(1)} %reduce_window_sum.21, pred[128,128]{1,0:T(8,128)(4,1)S(1)} %copy.46), kind=kOutput, calls=%fused_computation | convolution fusion | flops 403701760 | bytes 2646016 | tf_op jit(solution)/shard_map/htp,hsp->hts/dot_general | solution.py:193
  58.7 1.0 %convolution_multiply_fusion.6 = f32[16,128,64]{1,2,0:T(8,128)S(1)} fusion(f32[16,128,128]{1,2,0:T(8,128)S(1)} %get-tuple-element.21, f32[16,64,128]{2,1,0:T(8,128)S(1)} %copy-done.8, f32[16,128]{1,0:T(8,128)S(1)} %get-tuple-element.29), kind=kOutput, calls=%fused_computation.22 | convolution fusion | flops 201457664 | bytes 2105344 | tf_op jit(solution)/shard_map/hnp,htp->htn/dot_general | solution.py:197
  59.7 2.1 %bitcast_reduce_fusion = bf16[2,128,64]{1,2,0:T(8,128)(2,1)S(1)} fusion(f32[16,128,64]{1,2,0:T(8,128)S(1)} %convolution_multiply_fusion.6, f32[16,128,128]{2,1,0:T(8,128)S(1)} %convolution_multiply_fusion, f32[16,128,64]{1,2,0:T(8,128)S(1)} %bitcast.188), kind=kOutput, calls=%fused_computation.68 | convolution fusion | flops 201572352 | bytes 2129920 | tf_op jit(solution)/shard_map/hts,hsn->htn/dot_general | solution.py:196
  61.9 1.7 %bitcast_reduce_fusion.2 = f32[2,128,64]{1,2,0:T(8,128)} fusion(f32[16,128,128]{2,1,0:T(8,128)S(1)} %convolution_multiply_fusion, f32[16,128,64]{1,2,0:T(8,128)S(1)} %bitcast.192), kind=kOutput, calls=%fused_computation.70 | convolution fusion | flops 201441280 | bytes 1638400 | tf_op jit(solution)/shard_map/hts,htn->hsn/dot_general | solution.py:195
  63.5 1.2 %reduce_window_sum.22 = f32[16,128]{1,0:T(8,128)S(1)} reduce-window(f32[16,128]{1,0:T(8,128)S(1)} %sub.117, f32[]{:T(128)} %constant.12.clone.1), window={size=1x128 pad=0_0x0_127}, to_apply=%region_21.22 | reduce-window | flops 260096 | bytes 16388 | tf_op jit(solution)/shard_map/body/reduce_window_sum | solution.py:203
  64.8 1.4 %collective-permute-done.7 = bf16[1040,128]{1,0:T(8,128)(2,1)} collective-permute-done((bf16[1040,128]{1,0:T(8,128)(2,1)S(1)}, bf16[1040,128]{1,0:T(8,128)(2,1)}, u32[]{:S(2)}, u32[]{:S(2)}) %collective-permute-start.7) | collective-permute-done | bytes 266272 | tf_op jit(solution)/shard_map/ppermute | solution.py:66
  66.2 0.7 slice_convert_fusion.1
  66.9 9.2 %collective-permute-done.6 = bf16[1040,128]{1,0:T(8,128)(2,1)} collective-permute-done((bf16[1040,128]{1,0:T(8,128)(2,1)S(1)}, bf16[1040,128]{1,0:T(8,128)(2,1)}, u32[]{:S(2)}, u32[]{:S(2)}) %collective-permute-start.6) | collective-permute-done | bytes 266272 | tf_op jit(solution)/shard_map/ppermute | solution.py:66
  76.1 0.7 slice_convert_fusion.2
  76.9 1.0 %slice.254 = bf16[1024,128]{1,0:T(8,128)(2,1)S(1)} slice(bf16[1040,128]{1,0:T(8,128)(2,1)} %collective-permute-done.7), slice={[0:1024], [0:128]} | slice | bytes 524288 | tf_op jit(solution)/shard_map/slice | solution.py:38
  77.9 1.1 %convert_multiply_fusion.10 = f32[1024,128]{1,0:T(8,128)S(1)} fusion(bf16[1040,128]{1,0:T(8,128)(2,1)} %collective-permute-done.6, f32[]{:T(128)S(6)} %select_n.182), kind=kLoop, calls=%fused_computation.72 | loop fusion | flops 262144 | bytes 786436 | tf_op jit(solution)/shard_map/mul | solution.py:218
  79.0 2.0 %bitcast_reduce_fusion.1 = (f32[2,128,64]{1,2,0:T(8,128)S(1)}, f32[16,128,64]{1,2,0:T(8,128)}) fusion(f32[16,128]{1,0:T(8,128)S(1)} %get-tuple-element.30, bf16[16,128,128]{2,1,0:T(8,128)(2,1)S(1)} %copy-done.1, bf16[16,64,128]{2,1,0:T(8,128)(2,1)S(1)} %bitcast.197, f32[16,64,128]{2,1,0:T(8,128)S(1)} %bitcast.193, bf16[16,64,128]{2,1,0:T(8,128)(2,1)S(1)} %bitcast.195, ...), kind=kOutput, calls=%fused_computation.69 | convolution fusion | flops 202358784 | bytes 2171008 | tf_op jit(solution)/shard_map/hnp,hsp->hsn/dot_general | solution.py:229
  81.1 0.7 copy.64
  82.5 4.0 %fusion.10 = bf16[16,128,128]{1,2,0:T(8,128)(2,1)} fusion(f32[16,128,128]{1,2,0:T(8,128)} %get-tuple-element.55, f32[16,128,128]{1,2,0:T(8,128)S(1)} %get-tuple-element.21, f32[16]{0:T(128)S(1)} %copy-done.22, f32[16,128,64]{1,2,0:T(8,128)S(1)} %bitcast.189, f32[16,128]{1,0:T(8,128)S(1)} %get-tuple-element.30, bf16[16,64,128]{2,1,0:T(8,128)(2,1)S(1)} %bitcast.198, ...), kind=kOutput, calls=%fused_computation.21 | convolution fusion | flops 203292672 | bytes 4202688 | tf_op jit(solution)/shard_map/hsn,hnp->hsp/dot_general | solution.py:228
  86.5 2.1 %copy.63 = bf16[16,128,128]{2,1,0:T(8,128)(2,1)} copy(bf16[16,128,128]{1,2,0:T(8,128)(2,1)} %fusion.10) | data formatting | bytes 1048576
  88.7 0.8 convolution_subtract_fusion
  (99 shorter events, 5.9 us)
Async XLA Ops:
  0.6 17.3 %copy-start = (bf16[16,128,128]{2,1,0:T(8,128)(2,1)S(1)}, bf16[16,128,128]{2,1,0:T(8,128)(2,1)}, u32[]{:S(2)}) copy-start(bf16[16,128,128]{2,1,0:T(8,128)(2,1)} %param.7) | copy-start | bytes 1572868
  0.6 9.2 %copy-start.13 = (bf16[2,128,128]{2,1,0:T(8,128)(2,1)S(1)}, bf16[2,128,128]{2,1,0:T(8,128)(2,1)}, u32[]{:S(2)}) copy-start(bf16[2,128,128]{2,1,0:T(8,128)(2,1)} %param.10) | copy-start | bytes 196612
  0.7 10.1 %copy-start.1 = (bf16[16,128,128]{2,1,0:T(8,128)(2,1)S(1)}, bf16[16,128,128]{2,1,0:T(8,128)(2,1)}, u32[]{:S(2)}) copy-start(bf16[16,128,128]{2,1,0:T(8,128)(2,1)} %param.9) | copy-start | bytes 1572868
  0.7 23.1 %collective-permute-start.5 = (bf16[2,128,256]{2,1,0:T(8,128)(2,1)}, bf16[2,128,256]{2,1,0:T(8,128)(2,1)}, u32[]{:S(2)}, u32[]{:S(2)}) collective-permute-start(bf16[2,128,256]{2,1,0:T(8,128)(2,1)} %param.8), channel_id=1, source_target_pairs={{0,12},{1,13},{2,14},{3,15},{16,28},{17,29},{18,30},{19,31}} | collective-permute-start | bytes 393224 | tf_op jit(solution)/shard_map/ppermute | solution.py:66
  2.1 19.6 %collective-permute-start.3 = (bf16[2,128,256]{2,1,0:T(8,128)(2,1)}, bf16[2,128,256]{2,1,0:T(8,128)(2,1)}, u32[]{:S(2)}, u32[]{:S(2)}) collective-permute-start(bf16[2,128,256]{2,1,0:T(8,128)(2,1)} %param.8), channel_id=1, source_target_pairs={{0,4},{4,8},{8,12},{1,5},{5,9},{9,13},{2,6},{6,10},{10,14},{3,7},{... | collective-permute-start | bytes 393224 | tf_op jit(solution)/shard_map/ppermute | solution.py:66
  5.6 19.3 %collective-permute-start.4 = (bf16[2,128,256]{2,1,0:T(8,128)(2,1)}, bf16[2,128,256]{2,1,0:T(8,128)(2,1)}, u32[]{:S(2)}, u32[]{:S(2)}) collective-permute-start(bf16[2,128,256]{2,1,0:T(8,128)(2,1)} %param.8), channel_id=1, source_target_pairs={{0,8},{4,12},{1,9},{5,13},{2,10},{6,14},{3,11},{7,15},{16,24},{20,... | collective-permute-start | bytes 393224 | tf_op jit(solution)/shard_map/ppermute | solution.py:66
  12.0 22.9 %collective-permute-start.1 = (bf16[1040,128]{1,0:T(8,128)(2,1)}, bf16[1040,128]{1,0:T(8,128)(2,1)}, u32[]{:S(2)}, u32[]{:S(2)}) collective-permute-start(bf16[1040,128]{1,0:T(8,128)(2,1)} %pad_maximum_fusion), channel_id=1, source_target_pairs={{0,8},{4,12},{1,9},{5,13},{2,10},{6,14},{3,11},{7,15},{16,24},{20,... | collective-permute-start | bytes 798728 | tf_op jit(solution)/shard_map/ppermute | solution.py:66
  14.0 25.9 %collective-permute-start = (bf16[1040,128]{1,0:T(8,128)(2,1)}, bf16[1040,128]{1,0:T(8,128)(2,1)S(1)}, u32[]{:S(2)}, u32[]{:S(2)}) collective-permute-start(bf16[1040,128]{1,0:T(8,128)(2,1)} %pad_maximum_fusion), channel_id=1, source_target_pairs={{0,4},{4,8},{8,12},{1,5},{5,9},{9,13},{2,6},{6,10},{10,14},{3,7},{... | collective-permute-start | bytes 798728 | tf_op jit(solution)/shard_map/ppermute | solution.py:66
  16.7 1.2 %copy-start.2 = (f32[16,128,128]{2,1,0:T(8,128)}, f32[16,128,128]{2,1,0:T(8,128)S(1)}, u32[]{:S(2)}) copy-start(f32[16,128,128]{2,1,0:T(8,128)S(1)} %bitcast_multiply_fusion.1) | copy-start | bytes 3145732
  16.7 1.2 %copy-start.16 = (bf16[2,128,256]{2,1,0:T(8,128)(2,1)S(1)}, bf16[2,128,256]{2,1,0:T(8,128)(2,1)}, u32[]{:S(2)}) copy-start(bf16[2,128,256]{2,1,0:T(8,128)(2,1)} %param.8) | copy-start | bytes 393220
  21.7 18.2 %collective-permute-start.2 = (bf16[1040,128]{1,0:T(8,128)(2,1)}, bf16[1040,128]{1,0:T(8,128)(2,1)S(1)}, u32[]{:S(2)}, u32[]{:S(2)}) collective-permute-start(bf16[1040,128]{1,0:T(8,128)(2,1)} %pad_maximum_fusion), channel_id=1, source_target_pairs={{0,12},{1,13},{2,14},{3,15},{16,28},{17,29},{18,30},{19,31}} | collective-permute-start | bytes 798728 | tf_op jit(solution)/shard_map/ppermute | solution.py:66
  24.9 1.3 %copy-start.4 = (f32[2,8,128,128]{2,3,1,0:T(8,128)S(1)}, f32[2,8,128,128]{2,3,1,0:T(8,128)}, u32[]{:S(2)}) copy-start(f32[2,8,128,128]{2,3,1,0:T(8,128)} %get-tuple-element.45) | copy-start | bytes 3145732
  24.9 1.3 %copy-start.17 = (bf16[2,128,256]{2,1,0:T(8,128)(2,1)S(1)}, bf16[2,128,256]{2,1,0:T(8,128)(2,1)}, u32[]{:S(2)}) copy-start(bf16[2,128,256]{2,1,0:T(8,128)(2,1)} %param.8) | copy-start | bytes 393220
  24.9 1.3 %copy-start.20 = (f32[2,8,128]{2,1,0:T(8,128)S(1)}, f32[2,8,128]{2,1,0:T(8,128)}, u32[]{:S(2)}) copy-start(f32[2,8,128]{2,1,0:T(8,128)} %get-tuple-element.44) | copy-start | bytes 24580
  30.0 10.0 %copy-start.14 = (f32[16,64,128]{2,1,0:T(8,128)S(1)}, f32[16,64,128]{2,1,0:T(8,128)}, u32[]{:S(2)}) copy-start(f32[16,64,128]{2,1,0:T(8,128)} %param.13) | copy-start | bytes 1572868
  39.9 10.7 %copy-start.12 = (bf16[1040,128]{1,0:T(8,128)(2,1)}, bf16[1040,128]{1,0:T(8,128)(2,1)S(1)}, u32[]{:S(2)}) copy-start(bf16[1040,128]{1,0:T(8,128)(2,1)S(1)} %collective-permute-done) | copy-start | bytes 798724
  40.0 1.3 %copy-start.18 = (bf16[2,128,64]{1,2,0:T(8,128)(2,1)S(1)}, bf16[2,128,64]{1,2,0:T(8,128)(2,1)}, u32[]{:S(2)}) copy-start(bf16[2,128,64]{1,2,0:T(8,128)(2,1)} %copy.88) | copy-start | bytes 98308
  41.3 10.4 %copy-start.7 = (f32[16,64,128]{2,1,0:T(8,128)}, f32[16,64,128]{2,1,0:T(8,128)S(1)}, u32[]{:S(2)}) copy-start(f32[16,64,128]{2,1,0:T(8,128)S(1)} %fusion.24) | copy-start | bytes 1572868
  41.4 7.1 %copy-start.5 = (f32[2,8,128,64]{2,3,1,0:T(8,128)}, f32[2,8,128,64]{2,3,1,0:T(8,128)S(1)}, u32[]{:S(2)}) copy-start(f32[2,8,128,64]{2,3,1,0:T(8,128)S(1)} %broadcast_in_dim.102) | copy-start | bytes 1572868
  41.4 0.7 copy-start.21
  44.5 1.2 %copy-start.3 = (f32[16,128,128]{2,1,0:T(8,128)S(1)}, f32[16,128,128]{2,1,0:T(8,128)}, u32[]{:S(2)}) copy-start(f32[16,128,128]{2,1,0:T(8,128)} %copy-done.2) | copy-start | bytes 3145732
  51.6 1.0 %slice-start = ((bf16[1040,128]{1,0:T(8,128)(2,1)}), bf16[1024,128]{1,0:T(8,128)(2,1)S(1)}, s32[]{:S(2)}) async-start(bf16[1040,128]{1,0:T(8,128)(2,1)} %copy-done.12), calls=%async_computation | async-start | bytes 524288 | tf_op jit(solution)/shard_map/slice | solution.py:38
  53.2 5.5 %copy-start.8 = (f32[16,64,128]{2,1,0:T(8,128)S(1)}, f32[16,64,128]{2,1,0:T(8,128)}, u32[]{:S(2)}) copy-start(f32[16,64,128]{2,1,0:T(8,128)} %copy-done.7) | copy-start | bytes 1572868
  53.2 11.6 %collective-permute-start.8 = (bf16[1040,128]{1,0:T(8,128)(2,1)S(1)}, bf16[1040,128]{1,0:T(8,128)(2,1)S(1)}, u32[]{:S(2)}, u32[]{:S(2)}) collective-permute-start(bf16[1040,128]{1,0:T(8,128)(2,1)S(1)} %pad_maximum_fusion.1), channel_id=1, source_target_pairs={{12,0},{13,1},{14,2},{15,3},{28,16},{29,17},{30,18},{31,19}} | collective-permute-start | bytes 798728 | tf_op jit(solution)/shard_map/ppermute | solution.py:66
  54.0 12.2 %collective-permute-start.7 = (bf16[1040,128]{1,0:T(8,128)(2,1)S(1)}, bf16[1040,128]{1,0:T(8,128)(2,1)}, u32[]{:S(2)}, u32[]{:S(2)}) collective-permute-start(bf16[1040,128]{1,0:T(8,128)(2,1)S(1)} %pad_maximum_fusion.1), channel_id=1, source_target_pairs={{8,0},{12,4},{9,1},{13,5},{10,2},{14,6},{11,3},{15,7},{24,16},{28,... | collective-permute-start | bytes 798728 | tf_op jit(solution)/shard_map/ppermute | solution.py:66
  55.3 20.8 %collective-permute-start.6 = (bf16[1040,128]{1,0:T(8,128)(2,1)S(1)}, bf16[1040,128]{1,0:T(8,128)(2,1)}, u32[]{:S(2)}, u32[]{:S(2)}) collective-permute-start(bf16[1040,128]{1,0:T(8,128)(2,1)S(1)} %pad_maximum_fusion.1), channel_id=1, source_target_pairs={{4,0},{8,4},{12,8},{5,1},{9,5},{13,9},{6,2},{10,6},{14,10},{7,3},{... | collective-permute-start | bytes 798728 | tf_op jit(solution)/shard_map/ppermute | solution.py:66
  59.7 2.1 %copy-start.6 = (f32[2,8,128,64]{2,3,1,0:T(8,128)S(1)}, f32[2,8,128,64]{2,3,1,0:T(8,128)}, u32[]{:S(2)}) copy-start(f32[2,8,128,64]{2,3,1,0:T(8,128)} %copy-done.5) | copy-start | bytes 1572868
  61.9 1.7 %copy-start.19 = (f32[16,128]{1,0:T(8,128)S(1)}, f32[16,128]{1,0:T(8,128)}, u32[]{:S(2)}) copy-start(f32[16,128]{1,0:T(8,128)} %get-tuple-element.54) | copy-start | bytes 24580
  77.9 1.1 %copy-start.9 = (bf16[1024,128]{1,0:T(8,128)(2,1)}, bf16[1024,128]{1,0:T(8,128)(2,1)S(1)}, u32[]{:S(2)}) copy-start(bf16[1024,128]{1,0:T(8,128)(2,1)S(1)} %slice.256) | copy-start | bytes 786436
  79.0 2.0 %copy-start.15 = (f32[2,128,64]{1,2,0:T(8,128)S(1)}, f32[2,128,64]{1,2,0:T(8,128)}, u32[]{:S(2)}) copy-start(f32[2,128,64]{1,2,0:T(8,128)} %bitcast_reduce_fusion.2) | copy-start | bytes 196612
  81.0 0.9 %copy-start.10 = (bf16[1024,128]{1,0:T(8,128)(2,1)S(1)}, bf16[1024,128]{1,0:T(8,128)(2,1)}, u32[]{:S(2)}) copy-start(bf16[1024,128]{1,0:T(8,128)(2,1)} %copy-done.9) | copy-start | bytes 786436
  81.8 0.7 copy-start.22
  86.5 2.1 %copy-start.11 = (f32[16,128,64]{1,2,0:T(8,128)S(1)}, f32[16,128,64]{1,2,0:T(8,128)}, u32[]{:S(2)}) copy-start(f32[16,128,64]{1,2,0:T(8,128)} %get-tuple-element.53) | copy-start | bytes 1572868

commit v5 on v3

--- a/solution.py
+++ b/solution.py
@@ -137,7 +137,6 @@
     end_state = jnp.einsum("hsn,hsp->hnp", weighted_in, inputs_wide, precision=highest)
 
     state_earlier = shifted(pack_rows(end_state, [totals]), 1)
-    ends_earlier = []
     prefix_state = jnp.zeros_like(end_state)
     gap = jnp.zeros_like(totals)
     for distance, received in enumerate(state_earlier, start=1):
@@ -145,7 +144,6 @@
         valid = distance <= seq_rank
         totals_there = jnp.where(valid, totals_there, 0.0)
         weight = jnp.where(valid, jnp.exp(gap), 0.0)
-        ends_earlier.append(ends)
         prefix_state = prefix_state + weight[:, None, None] * ends.astype(jnp.float32)
         gap = gap + totals_there
     entering = prefix_state + jnp.exp(gap)[:, None, None] * init_state
@@ -178,15 +176,7 @@
     flow = jnp.einsum(
         "htn,htp->hnp", out_heads * from_start[..., None], grad_out, precision=highest
     )
-    closing = jnp.sum(flow * entering, axis=(1, 2))
-    if ends_earlier:
-        ends_dot_flow = jnp.stack(
-            [jnp.sum(ends.astype(jnp.float32) * flow, axis=(1, 2)) for ends in ends_earlier]
-        )
-    else:
-        ends_dot_flow = jnp.zeros((1,) + totals.shape, jnp.float32)
-
-    flow_later = shifted(pack_rows(flow, [totals, closing, ends_dot_flow]), -1)
+    flow_later = shifted(pack_rows(flow, [totals]), -1)
 
     local_dx = jnp.einsum("hts,htp->hsp", mixing, grad_out, precision=highest)
 
@@ -199,26 +189,16 @@
     )
 
     incoming = jnp.zeros_like(flow)
-    later_sum = jnp.zeros_like(totals)
     gap = jnp.zeros_like(totals)
-    through = []
-    dots_there = []
     for distance, received in enumerate(flow_later, start=1):
-        flows, (totals_there, closing_there, dots) = unpack_rows(
-            received, flow.shape, [totals.shape, closing.shape, ends_dot_flow.shape]
-        )
+        flows, (totals_there,) = unpack_rows(received, flow.shape, [totals.shape])
         valid = seq_rank + distance < seq_count
         totals_there = jnp.where(valid, totals_there, 0.0)
         weight = jnp.where(valid, jnp.exp(gap), 0.0)
         incoming = incoming + weight[:, None, None] * flows.astype(jnp.float32)
-        later_sum = later_sum + jnp.where(valid, closing_there, 0.0)
-        for early in range(1, distance):
-            pair_gap = gap - through[early - 1]
-            later_sum = later_sum - jnp.where(
-                valid, jnp.exp(jnp.where(valid, pair_gap, 0.0)) * dots[distance - early - 1], 0.0
-            )
         gap = gap + totals_there
-        through.append(gap)
+    leaving = jnp.exp(totals)[:, None, None] * entering + end_state
+    later_sum = jnp.sum(incoming * leaving, axis=(1, 2))
 
     state_dx = local_dx + jnp.einsum("hsn,hnp->hsp", weighted_in, incoming, precision=highest)
     terms = forward_term - jnp.sum(inputs_wide * state_dx, axis=2)

time: 82.4 us -> 89 us (1.080)
  waiting for transfers between devices: 22.1 us -> 25.7 us
  other arithmetic: 7.18 us -> 8.69 us
    ppermute x9, waiting for transfers between devices: 22.1 us -> 25.7 us  [shifted(): moved.append(lax.ppermute(x, 'seq', pairs))]
    dot_general x4, matrix products: 3.75 us -> 5.47 us  [teacher_rows(): jnp.einsum('gptd,gkd->gptk', grouped, block[..., :head_width], preferred_...]
    dot_general x1, matrix products: 2.31 us -> 1.14 us  [body(): local_dx = jnp.einsum('hts,htp->hsp', mixing, grad_out, precision=highest)]
    unnamed x40 -> x44, local copies, waits for them, and re-layouts: 4.04 us -> 5.14 us
    mul x0 -> x1, other arithmetic: none -> 1.07 us  [body(): weight[:, None, None] * ends.astype(jnp.float32)]
  transfers between devices with their start and end apart: 9 -> 9, of which waited for: 5 -> 4; matrix products, arithmetic and copies ran while one was open for 28% -> 28% of each run, Pallas kernels for 0% -> 0%
where the time goes in v5:
time: 89 us; the launch traced here: 88.3 us
  matrix products  30.5 us (34%)
  waiting for transfers between devices  25.7 us (29%)
  starting transfers between devices  15.8 us (18%)
  other arithmetic  8.69 us (10%)
  local copies, waits for them, and re-layouts  6.3 us (7%)
  between operations  1.24 us (1%)
    ppermute x9, waiting for transfers between devices, shifted(): moved.append(lax.ppermute(x, 'seq', pairs))  25.7 us
    ppermute x9, starting transfers between devices, shifted(): moved.append(lax.ppermute(x, 'seq', pairs))  15.8 us
    dot_general x4, matrix products, teacher_rows(): jnp.einsum('gptd,gkd->gptk', grouped, block[..., :head_width], preferred_...  5.47 us
    unnamed x44, local copies, waits for them, and re-layouts  5.14 us
    dot_general x4, matrix products, teacher_rows(): jnp.einsum('gptk,gkd->gptd', exponentials.astype(jnp.bfloat16), block[......  3.97 us
    dot_general x1, matrix products, body(): jnp.einsum('hts,hsn->htn', paired, in_heads, precision=highest)  2.91 us
    dot_general x1, matrix products, body(): jnp.einsum('hsn,hnp->hsp', weighted_in, incoming, precision=highest)  2.8 us
    dot_general x1, matrix products, body(): jnp.einsum('hts,hsp->htp', mixing, inputs_wide, precision=highest)  2.21 us
  transfers between devices with their start and end apart: 9, of which 4 were waited for; matrix products, arithmetic and copies ran while one was open for 28% of the time, Pallas kernels for 0%

profile of v5, /device:TPU:8, one launch (start us, length us, event | category | flops | bytes accessed | tf_op | source)
XLA Modules:
  0.0 88.3 jit_solution(11932093189978270233)
XLA Ops:
  0.7 1.5 %collective-permute-start.5 = (bf16[2,128,256]{2,1,0:T(8,128)(2,1)}, bf16[2,128,256]{2,1,0:T(8,128)(2,1)}, u32[]{:S(2)}, u32[]{:S(2)}) collective-permute-start(bf16[2,128,256]{2,1,0:T(8,128)(2,1)} %param.8), channel_id=1, source_target_pairs={{0,12},{1,13},{2,14},{3,15},{16,28},{17,29},{18,30},{19,31}} | collective-permute-start | bytes 393224 | tf_op jit(solution)/shard_map/ppermute | solution.py:66
  2.1 3.5 %collective-permute-start.3 = (bf16[2,128,256]{2,1,0:T(8,128)(2,1)}, bf16[2,128,256]{2,1,0:T(8,128)(2,1)}, u32[]{:S(2)}, u32[]{:S(2)}) collective-permute-start(bf16[2,128,256]{2,1,0:T(8,128)(2,1)} %param.8), channel_id=1, source_target_pairs={{0,4},{4,8},{8,12},{1,5},{5,9},{9,13},{2,6},{6,10},{10,14},{3,7},{... | collective-permute-start | bytes 393224 | tf_op jit(solution)/shard_map/ppermute | solution.py:66
  5.6 2.9 %collective-permute-start.4 = (bf16[2,128,256]{2,1,0:T(8,128)(2,1)}, bf16[2,128,256]{2,1,0:T(8,128)(2,1)}, u32[]{:S(2)}, u32[]{:S(2)}) collective-permute-start(bf16[2,128,256]{2,1,0:T(8,128)(2,1)} %param.8), channel_id=1, source_target_pairs={{0,8},{4,12},{1,9},{5,13},{2,10},{6,14},{3,11},{7,15},{16,24},{20,... | collective-permute-start | bytes 393224 | tf_op jit(solution)/shard_map/ppermute | solution.py:66
  8.6 0.7 fusion.48
  10.1 1.3 %fusion.75 = (bf16[16,64,128]{2,1,0:T(8,128)(2,1)S(1)}, f32[16,64,128]{2,1,0:T(8,128)}) fusion(bf16[16,128,128]{2,1,0:T(8,128)(2,1)S(1)} %copy-done.1, f32[16,128,64]{1,2,0:T(8,128)S(1)} %bitcast.130, f32[16,128]{1,0:T(8,128)S(1)} %get-tuple-element.27), kind=kOutput, calls=%fused_computation.149 | convolution fusion | flops 201588736 | bytes 1843200 | tf_op jit(solution)/shard_map/hsn,hsp->hnp/dot_general | solution.py:137
  11.4 0.7 pad_maximum_fusion.2
  12.2 1.3 %collective-permute-start.1 = (bf16[1040,128]{1,0:T(8,128)(2,1)}, bf16[1040,128]{1,0:T(8,128)(2,1)S(1)}, u32[]{:S(2)}, u32[]{:S(2)}) collective-permute-start(bf16[1040,128]{1,0:T(8,128)(2,1)} %pad_maximum_fusion.2), channel_id=1, source_target_pairs={{0,8},{4,12},{1,9},{5,13},{2,10},{6,14},{3,11},{7,15},{16,24},{20,... | collective-permute-start | bytes 798728 | tf_op jit(solution)/shard_map/ppermute | solution.py:66
  13.5 1.9 %collective-permute-start = (bf16[1040,128]{1,0:T(8,128)(2,1)}, bf16[1040,128]{1,0:T(8,128)(2,1)}, u32[]{:S(2)}, u32[]{:S(2)}) collective-permute-start(bf16[1040,128]{1,0:T(8,128)(2,1)} %pad_maximum_fusion.2), channel_id=1, source_target_pairs={{0,4},{4,8},{8,12},{1,5},{5,9},{9,13},{2,6},{6,10},{10,14},{3,7},{... | collective-permute-start | bytes 798728 | tf_op jit(solution)/shard_map/ppermute | solution.py:66
  15.8 0.4 bitcast_multiply_fusion.1
  16.1 2.2 %fusion.80 = f32[16,128,128]{1,2,0:T(8,128)} fusion(f32[16,128,128]{2,1,0:T(8,128)S(1)} %bitcast_multiply_fusion.1, bf16[16,128,128]{2,1,0:T(8,128)(2,1)S(1)} %copy-done.1), kind=kOutput, calls=%fused_computation.154 | convolution fusion | flops 402653184 | bytes 2621440 | tf_op jit(solution)/shard_map/hts,hsp->htp/dot_general | solution.py:159
  18.4 1.9 %fusion.78 = (f32[2,8,128]{2,1,0:T(8,128)}, f32[2,8,128,128]{2,3,1,0:T(8,128)}) fusion(bf16[2,8,128,128]{3,2,1,0:T(8,128)(2,1)S(1)} %bitcast.126, bf16[2,128,256]{2,1,0:T(8,128)(2,1)S(1)} %copy-done.14, pred[128,128]{0,1:T(8,128)(4,1)S(1)} %iota_compare_fusion), kind=kOutput, calls=%fused_computation.152 | convolution fusion | flops 67893248 | bytes 1662976 | tf_op jit(solution)/shard_map/gptd,gkd->gptk/dot_general | solution.py:87
  20.6 0.5 exp.79
  21.2 0.7 collective-permute-start.2
  21.9 1.1 %fusion.79 = (f32[2,8,128]{2,1,0:T(8,128)S(1)}, f32[2,8,128,128]{2,3,1,0:T(8,128)S(1)}) fusion(bf16[2,8,128,128]{3,2,1,0:T(8,128)(2,1)S(1)} %bitcast.127, bf16[2,128,256]{2,1,0:T(8,128)(2,1)} %collective-permute-done.3, pred[]{:T(512)S(6)} %ge.51), kind=kOutput, calls=%fused_computation.153 | convolution fusion | flops 67893248 | bytes 1646593 | tf_op jit(solution)/shard_map/gptd,gkd->gptk/dot_general | solution.py:87
  23.1 1.1 %fusion.76 = (f32[2,8,128]{2,1,0:T(8,128)S(1)}, f32[2,8,128,128]{2,3,1,0:T(8,128)S(1)}) fusion(bf16[2,8,128,128]{3,2,1,0:T(8,128)(2,1)S(1)} %bitcast.129, bf16[2,128,256]{2,1,0:T(8,128)(2,1)} %collective-permute-done.5, pred[]{:T(512)S(6)} %ge.53), kind=kOutput, calls=%fused_computation.150 | convolution fusion | flops 67893248 | bytes 1646593 | tf_op jit(solution)/shard_map/gptd,gkd->gptk/dot_general | solution.py:87
  24.3 1.2 %fusion.77 = (f32[2,8,128]{2,1,0:T(8,128)S(1)}, f32[2,8,128,128]{2,3,1,0:T(8,128)S(1)}) fusion(bf16[2,8,128,128]{3,2,1,0:T(8,128)(2,1)S(1)} %bitcast.128, bf16[2,128,256]{2,1,0:T(8,128)(2,1)} %collective-permute-done.4, pred[]{:T(512)S(6)} %ge.52), kind=kOutput, calls=%fused_computation.151 | convolution fusion | flops 67893248 | bytes 1646593 | tf_op jit(solution)/shard_map/gptd,gkd->gptk/dot_general | solution.py:87
  25.9 1.0 %fusion.16 = (f32[2,8,128]{2,1,0:T(8,128)S(1)}, f32[2,8,128]{2,1,0:T(8,128)S(1)}, f32[2,8,128]{2,1,0:T(8,128)S(1)}, f32[2,8,128]{2,1,0:T(8,128)S(1)}) fusion(f32[2,8,128,128]{2,3,1,0:T(8,128)S(1)} %get-tuple-element.43, f32[2,8,128]{2,1,0:T(8,128)S(1)} %maximum_maximum_fusion, f32[2,8,128,128]{2,3,1,0:T(8,128)S(1)} %copy-done.2, ...), kind=kLoop, calls=%fused_computation.47 | loop fusion | flops 2088960 | bytes 4235264 | tf_op jit(solution)/shard_map/reduce_sum | solution.py:103
  26.9 1.2 %fusion.22 = f32[2,8,128,128]{2,3,1,0:T(8,128)S(1)} fusion(f32[2,8,128,128]{2,3,1,0:T(8,128)S(1)} %get-tuple-element.37, f32[2,8,128]{2,1,0:T(8,128)S(1)} %maximum_maximum_fusion, bf16[2,128,256]{2,1,0:T(8,128)(2,1)} %collective-permute-done.5), kind=kOutput, calls=%fused_computation.53 | convolution fusion | flops 67633152 | bytes 2170880 | tf_op jit(solution)/shard_map/gptk,gkd->gptd/dot_general | solution.py:104
  28.1 1.2 %convolution_add_fusion.2 = f32[2,8,128,128]{2,3,1,0:T(8,128)S(1)} fusion(f32[2,8,128,128]{2,3,1,0:T(8,128)S(1)} %fusion.26, f32[2,8,128,128]{2,3,1,0:T(8,128)S(1)} %get-tuple-element.43, f32[2,8,128]{2,1,0:T(8,128)S(1)} %maximum_maximum_fusion, bf16[2,128,256]{2,1,0:T(8,128)(2,1)} %collective-permute-done.3), kind=kOutput, calls=%fused_computation.8 | convolution fusion | flops 67895296 | bytes 3219456 | tf_op jit(solution)/shard_map/gptk,gkd->gptd/dot_general | solution.py:104
  29.3 1.3 %multiply_reduce_fusion.2 = (f32[2,8,128]{2,1,0:T(8,128)S(1)}, f32[2,8,128,128]{2,3,1,0:T(8,128)S(1)}) fusion(f32[2,8,128]{2,1,0:T(8,128)S(1)} %add_add_fusion, f32[2,8,128,128]{2,3,1,0:T(8,128)S(1)} %fusion.22, f32[2,8,128,128]{2,3,1,0:T(8,128)S(1)} %convolution_add_fusion.2, bf16[2,128,256]{2,1,0:T(8,128)(2,1)} %collective-permute-done.4, ...), kind=kOutput, calls=%fused_computation.38 | convolution fusion | flops 69466112 | bytes 4284416 | tf_op jit(solution)/shard_map/gptk,gkd->gptd/dot_general | solution.py:104
  30.6 4.3 %collective-permute-done.1 = bf16[1040,128]{1,0:T(8,128)(2,1)S(1)} collective-permute-done((bf16[1040,128]{1,0:T(8,128)(2,1)}, bf16[1040,128]{1,0:T(8,128)(2,1)S(1)}, u32[]{:S(2)}, u32[]{:S(2)}) %collective-permute-start.1) | collective-permute-done | bytes 266272 | tf_op jit(solution)/shard_map/ppermute | solution.py:66
  34.9 5.0 %collective-permute-done = bf16[1040,128]{1,0:T(8,128)(2,1)} collective-permute-done((bf16[1040,128]{1,0:T(8,128)(2,1)}, bf16[1040,128]{1,0:T(8,128)(2,1)}, u32[]{:S(2)}, u32[]{:S(2)}) %collective-permute-start) | collective-permute-done | bytes 266272 | tf_op jit(solution)/shard_map/ppermute | solution.py:66
  39.9 0.7 slice_convert_fusion.4
  40.7 0.7 copy-done.11
  41.3 1.1 %convert_multiply_fusion.7 = f32[1024,128]{1,0:T(8,128)S(1)} fusion(bf16[1040,128]{1,0:T(8,128)(2,1)} %collective-permute-done, f32[]{:T(128)S(6)} %select_n.116), kind=kLoop, calls=%fused_computation.71 | loop fusion | flops 262144 | bytes 786436 | tf_op jit(solution)/shard_map/mul | solution.py:147
  42.9 0.9 %copy-done.5 = f32[16,128,128]{1,2,0:T(8,128)S(1)} copy-done((f32[16,128,128]{1,2,0:T(8,128)S(1)}, f32[16,128,128]{1,2,0:T(8,128)}, u32[]{:S(2)}) %copy-start.5) | copy-done | bytes 1048600
  43.8 2.0 %multiply_reduce_fusion.3 = (f32[16,128]{1,0:T(8,128)S(1)}, f32[16,128,128]{1,2,0:T(8,128)S(1)}) fusion(bf16[16,128,128]{1,2,0:T(8,128)(2,1)S(1)} %copy.48, f32[16]{0:T(128)S(1)} %copy-done.17, f32[16,128,128]{1,2,0:T(8,128)S(1)} %copy-done.5, f32[16,64,128]{2,1,0:T(8,128)S(1)} %fusion.31, f32[16,128,64]{1,2,0:T(8,128)S(1)} %bitcast.133, ...), kind=kOutput, calls=%fused_computation.43 | convolution fusion | flops 203159552 | bytes 3686464 | tf_op jit(solution)/shard_map/htn,hnp->htp/dot_general | solution.py:167
  45.9 0.4 multiply_reduce_fusion.1
  46.3 0.6 multiply_reduce_fusion
  46.9 2.1 %convolution_convert_fusion = bf16[16,64,128]{2,1,0:T(8,128)(2,1)S(1)} fusion(f32[16,128,128]{1,2,0:T(8,128)S(1)} %get-tuple-element.19, f32[16,128,64]{1,2,0:T(8,128)S(1)} %bitcast.134, f32[16,128]{1,0:T(8,128)S(1)} %get-tuple-element.26), kind=kOutput, calls=%fused_computation.26 | convolution fusion | flops 201588736 | bytes 1843200 | tf_op jit(solution)/shard_map/htn,htp->hnp/dot_general | solution.py:176
  49.1 1.3 %collective-permute-start.7 = (bf16[1040,128]{1,0:T(8,128)(2,1)S(1)}, bf16[1040,128]{1,0:T(8,128)(2,1)S(1)}, u32[]{:S(2)}, u32[]{:S(2)}) collective-permute-start(bf16[1040,128]{1,0:T(8,128)(2,1)S(1)} %pad_maximum_fusion.1), channel_id=1, source_target_pairs={{8,0},{12,4},{9,1},{13,5},{10,2},{14,6},{11,3},{15,7},{24,16},{28,... | collective-permute-start | bytes 798728 | tf_op jit(solution)/shard_map/ppermute | solution.py:66
  50.4 1.9 %collective-permute-start.6 = (bf16[1040,128]{1,0:T(8,128)(2,1)S(1)}, bf16[1040,128]{1,0:T(8,128)(2,1)S(1)}, u32[]{:S(2)}, u32[]{:S(2)}) collective-permute-start(bf16[1040,128]{1,0:T(8,128)(2,1)S(1)} %pad_maximum_fusion.1), channel_id=1, source_target_pairs={{4,0},{8,4},{12,8},{5,1},{9,5},{13,9},{6,2},{10,6},{14,10},{7,3},{... | collective-permute-start | bytes 798728 | tf_op jit(solution)/shard_map/ppermute | solution.py:66
  52.3 0.9 collective-permute-start.8
  53.2 1.1 %fusion.81 = f32[16,128,128]{1,2,0:T(8,128)S(1)} fusion(f32[16,128,128]{2,1,0:T(8,128)S(1)} %bitcast_multiply_fusion.1, f32[16,128,128]{1,2,0:T(8,128)S(1)} %get-tuple-element.19), kind=kOutput, calls=%fused_computation.155 | convolution fusion | flops 402653184 | bytes 3145728 | tf_op jit(solution)/shard_map/hts,htp->hsp/dot_general | solution.py:181
  54.3 1.2 %convolution_multiply_fusion = f32[16,128,128]{2,1,0:T(8,128)S(1)} fusion(f32[16,128,128]{1,2,0:T(8,128)S(1)} %get-tuple-element.19, bf16[16,128,128]{2,1,0:T(8,128)(2,1)S(1)} %copy-done.1, f32[16,128]{1,0:T(8,128)S(1)} %reduce_window_sum.21, pred[128,128]{1,0:T(8,128)(4,1)S(1)} %copy.44), kind=kOutput, calls=%fused_computation | convolution fusion | flops 403701760 | bytes 2646016 | tf_op jit(solution)/shard_map/htp,hsp->hts/dot_general | solution.py:183
  55.6 1.0 %convolution_multiply_fusion.6 = f32[16,128,64]{1,2,0:T(8,128)S(1)} fusion(f32[16,128,128]{1,2,0:T(8,128)S(1)} %get-tuple-element.19, f32[16,64,128]{2,1,0:T(8,128)S(1)} %fusion.31, f32[16,128]{1,0:T(8,128)S(1)} %get-tuple-element.26), kind=kOutput, calls=%fused_computation.21 | convolution fusion | flops 201457664 | bytes 2105344 | tf_op jit(solution)/shard_map/hnp,htp->htn/dot_general | solution.py:187
  56.6 2.9 %convolution_add_fusion.3 = f32[16,128,64]{1,2,0:T(8,128)} fusion(f32[16,128,64]{1,2,0:T(8,128)S(1)} %convolution_multiply_fusion.6, f32[16,128,128]{2,1,0:T(8,128)S(1)} %convolution_multiply_fusion, f32[16,128,64]{1,2,0:T(8,128)S(1)} %bitcast.131), kind=kOutput, calls=%fused_computation.22 | convolution fusion | flops 201457664 | bytes 2621440 | tf_op jit(solution)/shard_map/hts,hsn->htn/dot_general | solution.py:186
  59.5 1.7 %collective-permute-done.7 = bf16[1040,128]{1,0:T(8,128)(2,1)S(1)} collective-permute-done((bf16[1040,128]{1,0:T(8,128)(2,1)S(1)}, bf16[1040,128]{1,0:T(8,128)(2,1)S(1)}, u32[]{:S(2)}, u32[]{:S(2)}) %collective-permute-start.7) | collective-permute-done | bytes 266272 | tf_op jit(solution)/shard_map/ppermute | solution.py:66
  61.2 14.7 %collective-permute-done.6 = bf16[1040,128]{1,0:T(8,128)(2,1)S(1)} collective-permute-done((bf16[1040,128]{1,0:T(8,128)(2,1)S(1)}, bf16[1040,128]{1,0:T(8,128)(2,1)S(1)}, u32[]{:S(2)}, u32[]{:S(2)}) %collective-permute-start.6) | collective-permute-done | bytes 266272 | tf_op jit(solution)/shard_map/ppermute | solution.py:66
  76.1 0.9 %copy-done.8 = f32[16,64,128]{2,1,0:T(8,128)S(1)} copy-done((f32[16,64,128]{2,1,0:T(8,128)S(1)}, f32[16,64,128]{2,1,0:T(8,128)}, u32[]{:S(2)}) %copy-start.8) | copy-done | bytes 524312
  77.1 0.4 multiply_reduce_fusion.4
  77.5 1.9 %fusion.10 = f32[16,128,64]{1,2,0:T(8,128)} fusion(f32[16,64,128]{2,1,0:T(8,128)S(1)} %get-tuple-element.17, bf16[16,128,128]{2,1,0:T(8,128)(2,1)S(1)} %copy-done.1, f32[16,128]{1,0:T(8,128)S(1)} %get-tuple-element.27), kind=kOutput, calls=%fused_computation.25 | convolution fusion | flops 201457664 | bytes 1581056 | tf_op jit(solution)/shard_map/hnp,hsp->hsn/dot_general | solution.py:208
  79.4 2.8 %fusion.12 = (f32[16,128]{1,0:T(8,128)S(1)}, bf16[16,128,128]{1,2,0:T(8,128)(2,1)}) fusion(bf16[16,128,128]{1,2,0:T(8,128)(2,1)S(1)} %copy.48, f32[16,128,128]{1,2,0:T(8,128)S(1)} %get-tuple-element.19, f32[16]{0:T(128)S(1)} %copy-done.17, f32[16,128,128]{1,2,0:T(8,128)S(1)} %fusion.81, f32[16,64,128]{2,1,0:T(8,128)S(1)} %get-tuple-element.17, ...), kind=kOutput, calls=%fused_computation.28 | convolution fusion | flops 203290624 | bytes 4210752 | tf_op jit(solution)/shard_map/hsn,hnp->hsp/dot_general | solution.py:203
  82.2 1.2 %reduce_window_sum.22 = f32[16,128]{1,0:T(8,128)S(1)} reduce-window(f32[16,128]{1,0:T(8,128)S(1)} %sub.84, f32[]{:T(128)} %constant.12.clone.1), window={size=1x128 pad=0_0x0_127}, to_apply=%region_16.17 | reduce-window | flops 260096 | bytes 16388 | tf_op jit(solution)/shard_map/body/reduce_window_sum | solution.py:205
  83.4 2.1 %convolution_add_fusion.4 = f32[16,128,64]{1,2,0:T(8,128)S(1)} fusion(f32[16,128,64]{1,2,0:T(8,128)} %fusion.10, f32[16,128,128]{2,1,0:T(8,128)S(1)} %convolution_multiply_fusion, f32[16,128,64]{1,2,0:T(8,128)S(1)} %bitcast.135), kind=kOutput, calls=%fused_computation.23 | convolution fusion | flops 201457664 | bytes 2621440 | tf_op jit(solution)/shard_map/hts,htn->hsn/dot_general | solution.py:185
  85.7 0.7 copy.61
  86.6 1.0 %copy.60 = bf16[16,128,128]{2,1,0:T(8,128)(2,1)} copy(bf16[16,128,128]{1,2,0:T(8,128)(2,1)S(1)} %copy-done.7) | data formatting | bytes 1048576
  87.6 0.7 broadcast_add_fusion
  (84 shorter events, 3.0 us)
Async XLA Ops:
  0.6 17.7 %copy-start = (bf16[16,128,128]{2,1,0:T(8,128)(2,1)S(1)}, bf16[16,128,128]{2,1,0:T(8,128)(2,1)}, u32[]{:S(2)}) copy-start(bf16[16,128,128]{2,1,0:T(8,128)(2,1)} %param.7) | copy-start | bytes 1572868
  0.6 9.2 %copy-start.12 = (bf16[2,128,128]{2,1,0:T(8,128)(2,1)S(1)}, bf16[2,128,128]{2,1,0:T(8,128)(2,1)}, u32[]{:S(2)}) copy-start(bf16[2,128,128]{2,1,0:T(8,128)(2,1)} %param.10) | copy-start | bytes 196612
  0.7 9.5 %copy-start.1 = (bf16[16,128,128]{2,1,0:T(8,128)(2,1)S(1)}, bf16[16,128,128]{2,1,0:T(8,128)(2,1)}, u32[]{:S(2)}) copy-start(bf16[16,128,128]{2,1,0:T(8,128)(2,1)} %param.9) | copy-start | bytes 1572868
  0.7 22.4 %collective-permute-start.5 = (bf16[2,128,256]{2,1,0:T(8,128)(2,1)}, bf16[2,128,256]{2,1,0:T(8,128)(2,1)}, u32[]{:S(2)}, u32[]{:S(2)}) collective-permute-start(bf16[2,128,256]{2,1,0:T(8,128)(2,1)} %param.8), channel_id=1, source_target_pairs={{0,12},{1,13},{2,14},{3,15},{16,28},{17,29},{18,30},{19,31}} | collective-permute-start | bytes 393224 | tf_op jit(solution)/shard_map/ppermute | solution.py:66
  2.1 19.1 %collective-permute-start.3 = (bf16[2,128,256]{2,1,0:T(8,128)(2,1)}, bf16[2,128,256]{2,1,0:T(8,128)(2,1)}, u32[]{:S(2)}, u32[]{:S(2)}) collective-permute-start(bf16[2,128,256]{2,1,0:T(8,128)(2,1)} %param.8), channel_id=1, source_target_pairs={{0,4},{4,8},{8,12},{1,5},{5,9},{9,13},{2,6},{6,10},{10,14},{3,7},{... | collective-permute-start | bytes 393224 | tf_op jit(solution)/shard_map/ppermute | solution.py:66
  5.6 18.7 %collective-permute-start.4 = (bf16[2,128,256]{2,1,0:T(8,128)(2,1)}, bf16[2,128,256]{2,1,0:T(8,128)(2,1)}, u32[]{:S(2)}, u32[]{:S(2)}) collective-permute-start(bf16[2,128,256]{2,1,0:T(8,128)(2,1)} %param.8), channel_id=1, source_target_pairs={{0,8},{4,12},{1,9},{5,13},{2,10},{6,14},{3,11},{7,15},{16,24},{20,... | collective-permute-start | bytes 393224 | tf_op jit(solution)/shard_map/ppermute | solution.py:66
  12.2 22.7 %collective-permute-start.1 = (bf16[1040,128]{1,0:T(8,128)(2,1)}, bf16[1040,128]{1,0:T(8,128)(2,1)S(1)}, u32[]{:S(2)}, u32[]{:S(2)}) collective-permute-start(bf16[1040,128]{1,0:T(8,128)(2,1)} %pad_maximum_fusion.2), channel_id=1, source_target_pairs={{0,8},{4,12},{1,9},{5,13},{2,10},{6,14},{3,11},{7,15},{16,24},{20,... | collective-permute-start | bytes 798728 | tf_op jit(solution)/shard_map/ppermute | solution.py:66
  13.5 26.4 %collective-permute-start = (bf16[1040,128]{1,0:T(8,128)(2,1)}, bf16[1040,128]{1,0:T(8,128)(2,1)}, u32[]{:S(2)}, u32[]{:S(2)}) collective-permute-start(bf16[1040,128]{1,0:T(8,128)(2,1)} %pad_maximum_fusion.2), channel_id=1, source_target_pairs={{0,4},{4,8},{8,12},{1,5},{5,9},{9,13},{2,6},{6,10},{10,14},{3,7},{... | collective-permute-start | bytes 798728 | tf_op jit(solution)/shard_map/ppermute | solution.py:66
  16.1 2.2 %copy-start.14 = (bf16[2,128,256]{2,1,0:T(8,128)(2,1)S(1)}, bf16[2,128,256]{2,1,0:T(8,128)(2,1)}, u32[]{:S(2)}) copy-start(bf16[2,128,256]{2,1,0:T(8,128)(2,1)} %param.8) | copy-start | bytes 393220
  21.2 19.4 %collective-permute-start.2 = (bf16[1040,128]{1,0:T(8,128)(2,1)}, bf16[1040,128]{1,0:T(8,128)(2,1)S(1)}, u32[]{:S(2)}, u32[]{:S(2)}) collective-permute-start(bf16[1040,128]{1,0:T(8,128)(2,1)} %pad_maximum_fusion.2), channel_id=1, source_target_pairs={{0,12},{1,13},{2,14},{3,15},{16,28},{17,29},{18,30},{19,31}} | collective-permute-start | bytes 798728 | tf_op jit(solution)/shard_map/ppermute | solution.py:66
  24.2 1.3 %copy-start.2 = (f32[2,8,128,128]{2,3,1,0:T(8,128)S(1)}, f32[2,8,128,128]{2,3,1,0:T(8,128)}, u32[]{:S(2)}) copy-start(f32[2,8,128,128]{2,3,1,0:T(8,128)} %get-tuple-element.41) | copy-start | bytes 3145732
  24.3 1.3 %copy-start.15 = (bf16[2,128,256]{2,1,0:T(8,128)(2,1)S(1)}, bf16[2,128,256]{2,1,0:T(8,128)(2,1)}, u32[]{:S(2)}) copy-start(bf16[2,128,256]{2,1,0:T(8,128)(2,1)} %param.8) | copy-start | bytes 393220
  24.3 1.3 %copy-start.16 = (f32[2,8,128]{2,1,0:T(8,128)S(1)}, f32[2,8,128]{2,1,0:T(8,128)}, u32[]{:S(2)}) copy-start(f32[2,8,128]{2,1,0:T(8,128)} %get-tuple-element.40) | copy-start | bytes 24580
  34.9 5.8 %copy-start.10 = (bf16[1040,128]{1,0:T(8,128)(2,1)}, bf16[1040,128]{1,0:T(8,128)(2,1)S(1)}, u32[]{:S(2)}) copy-start(bf16[1040,128]{1,0:T(8,128)(2,1)S(1)} %collective-permute-done.1) | copy-start | bytes 798724
  40.6 0.7 copy-start.11
  41.3 1.1 %copy-start.13 = (f32[16,64,128]{2,1,0:T(8,128)S(1)}, f32[16,64,128]{2,1,0:T(8,128)}, u32[]{:S(2)}) copy-start(f32[16,64,128]{2,1,0:T(8,128)} %param.13) | copy-start | bytes 1572868
  41.3 1.2 %slice-start.1 = ((bf16[1040,128]{1,0:T(8,128)(2,1)}), bf16[1024,128]{1,0:T(8,128)(2,1)S(1)}, s32[]{:S(2)}) async-start(bf16[1040,128]{1,0:T(8,128)(2,1)} %copy-done.10), calls=%async_computation.1 | async-start | bytes 524288 | tf_op jit(solution)/shard_map/slice | solution.py:38
  41.3 1.3 %slice-start.2 = ((bf16[1040,128]{1,0:T(8,128)(2,1)}), bf16[1024,128]{1,0:T(8,128)(2,1)S(1)}, s32[]{:S(2)}) async-start(bf16[1040,128]{1,0:T(8,128)(2,1)} %copy-done.11), calls=%async_computation.2 | async-start | bytes 524288 | tf_op jit(solution)/shard_map/slice | solution.py:38
  42.6 1.2 %copy-start.5 = (f32[16,128,128]{1,2,0:T(8,128)S(1)}, f32[16,128,128]{1,2,0:T(8,128)}, u32[]{:S(2)}) copy-start(f32[16,128,128]{1,2,0:T(8,128)} %fusion.80) | copy-start | bytes 3145732
  42.9 4.0 %copy-start.3 = (f32[2,8,128,64]{2,3,1,0:T(8,128)}, f32[2,8,128,64]{2,3,1,0:T(8,128)S(1)}, u32[]{:S(2)}) copy-start(f32[2,8,128,64]{2,3,1,0:T(8,128)S(1)} %broadcast_in_dim.92) | copy-start | bytes 1572868
  42.9 0.9 %copy-start.17 = (f32[16]{0:T(128)S(1)}, f32[16]{0:T(128)}, u32[]{:S(2)}) copy-start(f32[16]{0:T(128)} %param.12) | copy-start | bytes 196
  49.1 12.1 %collective-permute-start.7 = (bf16[1040,128]{1,0:T(8,128)(2,1)S(1)}, bf16[1040,128]{1,0:T(8,128)(2,1)S(1)}, u32[]{:S(2)}, u32[]{:S(2)}) collective-permute-start(bf16[1040,128]{1,0:T(8,128)(2,1)S(1)} %pad_maximum_fusion.1), channel_id=1, source_target_pairs={{8,0},{12,4},{9,1},{13,5},{10,2},{14,6},{11,3},{15,7},{24,16},{28,... | collective-permute-start | bytes 798728 | tf_op jit(solution)/shard_map/ppermute | solution.py:66
  50.4 25.5 %collective-permute-start.6 = (bf16[1040,128]{1,0:T(8,128)(2,1)S(1)}, bf16[1040,128]{1,0:T(8,128)(2,1)S(1)}, u32[]{:S(2)}, u32[]{:S(2)}) collective-permute-start(bf16[1040,128]{1,0:T(8,128)(2,1)S(1)} %pad_maximum_fusion.1), channel_id=1, source_target_pairs={{4,0},{8,4},{12,8},{5,1},{9,5},{13,9},{6,2},{10,6},{14,10},{7,3},{... | collective-permute-start | bytes 798728 | tf_op jit(solution)/shard_map/ppermute | solution.py:66
  52.3 23.7 %collective-permute-start.8 = (bf16[1040,128]{1,0:T(8,128)(2,1)S(1)}, bf16[1040,128]{1,0:T(8,128)(2,1)S(1)}, u32[]{:S(2)}, u32[]{:S(2)}) collective-permute-start(bf16[1040,128]{1,0:T(8,128)(2,1)S(1)} %pad_maximum_fusion.1), channel_id=1, source_target_pairs={{12,0},{13,1},{14,2},{15,3},{28,16},{29,17},{30,18},{31,19}} | collective-permute-start | bytes 798728 | tf_op jit(solution)/shard_map/ppermute | solution.py:66
  61.2 14.7 %copy-start.9 = (bf16[1040,128]{1,0:T(8,128)(2,1)}, bf16[1040,128]{1,0:T(8,128)(2,1)S(1)}, u32[]{:S(2)}) copy-start(bf16[1040,128]{1,0:T(8,128)(2,1)S(1)} %collective-permute-done.7) | copy-start | bytes 798724
  76.0 1.0 %copy-start.8 = (f32[16,64,128]{2,1,0:T(8,128)S(1)}, f32[16,64,128]{2,1,0:T(8,128)}, u32[]{:S(2)}) copy-start(f32[16,64,128]{2,1,0:T(8,128)} %get-tuple-element.35) | copy-start | bytes 1572868
  76.0 1.1 %slice-start = ((bf16[1040,128]{1,0:T(8,128)(2,1)}), bf16[1024,128]{1,0:T(8,128)(2,1)S(1)}, s32[]{:S(2)}) async-start(bf16[1040,128]{1,0:T(8,128)(2,1)} %copy-done.9), calls=%async_computation | async-start | bytes 524288 | tf_op jit(solution)/shard_map/slice | solution.py:38
  76.1 1.0 %copy-start.18 = (f32[16]{0:T(128)S(1)}, f32[16]{0:T(128)}, u32[]{:S(2)}) copy-start(f32[16]{0:T(128)} %exp.79) | copy-start | bytes 196
  79.4 4.0 %copy-start.4 = (f32[2,8,128,64]{2,3,1,0:T(8,128)S(1)}, f32[2,8,128,64]{2,3,1,0:T(8,128)}, u32[]{:S(2)}) copy-start(f32[2,8,128,64]{2,3,1,0:T(8,128)} %copy-done.3) | copy-start | bytes 1572868
  83.4 2.1 %copy-start.6 = (f32[16,128,64]{1,2,0:T(8,128)S(1)}, f32[16,128,64]{1,2,0:T(8,128)}, u32[]{:S(2)}) copy-start(f32[16,128,64]{1,2,0:T(8,128)} %convolution_add_fusion.3) | copy-start | bytes 1572868
  85.6 1.0 %copy-start.7 = (bf16[16,128,128]{1,2,0:T(8,128)(2,1)S(1)}, bf16[16,128,128]{1,2,0:T(8,128)(2,1)}, u32[]{:S(2)}) copy-start(bf16[16,128,128]{1,2,0:T(8,128)(2,1)} %get-tuple-element.23) | copy-start | bytes 1572868

commit v6 on v5

--- a/solution.py
+++ b/solution.py
@@ -176,7 +176,12 @@
     flow = jnp.einsum(
         "htn,htp->hnp", out_heads * from_start[..., None], grad_out, precision=highest
     )
-    flow_later = shifted(pack_rows(flow, [totals]), -1)
+    if seq_count == 4:
+        payload = pack_rows(flow, [totals])
+        next_one = lax.ppermute(payload, "seq", [(3, 2), (2, 1)])
+        next_two = lax.ppermute(payload, "seq", [(3, 1)])
+    else:
+        flow_later = shifted(pack_rows(flow, [totals]), -1)
 
     local_dx = jnp.einsum("hts,htp->hsp", mixing, grad_out, precision=highest)
 
@@ -188,15 +193,27 @@
         "hnp,htp->htn", entering, grad_out, precision=highest
     )
 
-    incoming = jnp.zeros_like(flow)
-    gap = jnp.zeros_like(totals)
-    for distance, received in enumerate(flow_later, start=1):
-        flows, (totals_there,) = unpack_rows(received, flow.shape, [totals.shape])
-        valid = seq_rank + distance < seq_count
-        totals_there = jnp.where(valid, totals_there, 0.0)
-        weight = jnp.where(valid, jnp.exp(gap), 0.0)
-        incoming = incoming + weight[:, None, None] * flows.astype(jnp.float32)
-        gap = gap + totals_there
+    if seq_count == 4:
+        flow_one, (totals_one,) = unpack_rows(next_one, flow.shape, [totals.shape])
+        flow_two, _ = unpack_rows(next_two, flow.shape, [totals.shape])
+        has_one = (seq_rank == 1) | (seq_rank == 2)
+        has_two = seq_rank == 1
+        incoming = jnp.where(has_one, flow_one.astype(jnp.float32), 0.0) + jnp.where(
+            has_two, jnp.exp(totals_one)[:, None, None] * flow_two.astype(jnp.float32), 0.0
+        )
+        handoff = flow + jnp.exp(totals)[:, None, None] * incoming
+        first_incoming = lax.ppermute(handoff.astype(jnp.bfloat16), "seq", [(1, 0)])
+        incoming = jnp.where(seq_rank == 0, first_incoming.astype(jnp.float32), incoming)
+    else:
+        incoming = jnp.zeros_like(flow)
+        gap = jnp.zeros_like(totals)
+        for distance, received in enumerate(flow_later, start=1):
+            flows, (totals_there,) = unpack_rows(received, flow.shape, [totals.shape])
+            valid = seq_rank + distance < seq_count
+            totals_there = jnp.where(valid, totals_there, 0.0)
+            weight = jnp.where(valid, jnp.exp(gap), 0.0)
+            incoming = incoming + weight[:, None, None] * flows.astype(jnp.float32)
+            gap = gap + totals_there
     leaving = jnp.exp(totals)[:, None, None] * entering + end_state
     later_sum = jnp.sum(incoming * leaving, axis=(1, 2))
 

time: 89 us -> 85.8 us (0.964)
  the two profiles are of different devices: /device:TPU:8 before, /device:TPU:0 now
where the time goes in v6:
time: 85.8 us; the launch traced here: 85.1 us
  matrix products  29.7 us (35%)
  waiting for transfers between devices  20.3 us (24%)
  starting transfers between devices  19.1 us (22%)
  other arithmetic  8.91 us (10%)
  local copies, waits for them, and re-layouts  5.91 us (7%)
  between operations  1.23 us (1%)
    ppermute x1, waiting for transfers between devices, body(): first_incoming = lax.ppermute(handoff.astype(jnp.bfloat16), 'seq', [(1, 0)])  20.2 us
    ppermute x6, starting transfers between devices, shifted(): moved.append(lax.ppermute(x, 'seq', pairs))  16.3 us
    dot_general x4, matrix products, teacher_rows(): jnp.einsum('gptd,gkd->gptk', grouped, block[..., :head_width], preferred_...  5.47 us
    unnamed x38, local copies, waits for them, and re-layouts  4.84 us
    dot_general x4, matrix products, teacher_rows(): jnp.einsum('gptk,gkd->gptd', exponentials.astype(jnp.bfloat16), block[......  3.97 us
    dot_general x1, matrix products, body(): jnp.einsum('hsn,hnp->hsp', weighted_in, incoming, precision=highest)  2.79 us
    dot_general x1, matrix products, body(): jnp.einsum('hts,hsp->htp', mixing, inputs_wide, precision=highest)  2.21 us
    dot_general x1, matrix products, body(): jnp.einsum('hnp,hsp->hsn', incoming, inputs_wide, precision=highest)  2.16 us
  transfers between devices with their start and end apart: 9, of which 1 were waited for; matrix products, arithmetic and copies ran while one was open for 30% of the time, Pallas kernels for 0%

profile of v6, /device:TPU:0, one launch (start us, length us, event | category | flops | bytes accessed | tf_op | source)
XLA Modules:
  0.0 85.1 jit_solution(8522579692039765496)
XLA Ops:
  0.7 7.8 %collective-permute-start.5 = (bf16[2,128,256]{2,1,0:T(8,128)(2,1)}, bf16[2,128,256]{2,1,0:T(8,128)(2,1)}, u32[]{:S(2)}, u32[]{:S(2)}) collective-permute-start(bf16[2,128,256]{2,1,0:T(8,128)(2,1)} %param.8), channel_id=1, source_target_pairs={{0,12},{1,13},{2,14},{3,15},{16,28},{17,29},{18,30},{19,31}} | collective-permute-start | bytes 393224 | tf_op jit(solution)/shard_map/ppermute | solution.py:66
  8.4 1.9 %collective-permute-start.3 = (bf16[2,128,256]{2,1,0:T(8,128)(2,1)}, bf16[2,128,256]{2,1,0:T(8,128)(2,1)}, u32[]{:S(2)}, u32[]{:S(2)}) collective-permute-start(bf16[2,128,256]{2,1,0:T(8,128)(2,1)} %param.8), channel_id=1, source_target_pairs={{0,4},{4,8},{8,12},{1,5},{5,9},{9,13},{2,6},{6,10},{10,14},{3,7},{... | collective-permute-start | bytes 393224 | tf_op jit(solution)/shard_map/ppermute | solution.py:66
  10.4 1.9 %collective-permute-start.4 = (bf16[2,128,256]{2,1,0:T(8,128)(2,1)}, bf16[2,128,256]{2,1,0:T(8,128)(2,1)}, u32[]{:S(2)}, u32[]{:S(2)}) collective-permute-start(bf16[2,128,256]{2,1,0:T(8,128)(2,1)} %param.8), channel_id=1, source_target_pairs={{0,8},{4,12},{1,9},{5,13},{2,10},{6,14},{3,11},{7,15},{16,24},{20,... | collective-permute-start | bytes 393224 | tf_op jit(solution)/shard_map/ppermute | solution.py:66
  12.3 0.7 fusion.50
  13.0 0.3 reduce_window_sum.21
  13.9 1.3 %fusion.72 = (bf16[16,64,128]{2,1,0:T(8,128)(2,1)S(1)}, f32[16,64,128]{2,1,0:T(8,128)}) fusion(bf16[16,128,128]{2,1,0:T(8,128)(2,1)S(1)} %copy-done.1, f32[16,128,64]{1,2,0:T(8,128)S(1)} %bitcast.130, f32[16,128]{1,0:T(8,128)S(1)} %get-tuple-element.27), kind=kOutput, calls=%fused_computation.141 | convolution fusion | flops 201588736 | bytes 1843200 | tf_op jit(solution)/shard_map/hsn,hsp->hnp/dot_general | solution.py:137
  15.2 0.7 pad_maximum_fusion.2
  15.9 1.3 %collective-permute-start.1 = (bf16[1040,128]{1,0:T(8,128)(2,1)}, bf16[1040,128]{1,0:T(8,128)(2,1)S(1)}, u32[]{:S(2)}, u32[]{:S(2)}) collective-permute-start(bf16[1040,128]{1,0:T(8,128)(2,1)} %pad_maximum_fusion.2), channel_id=1, source_target_pairs={{0,8},{4,12},{1,9},{5,13},{2,10},{6,14},{3,11},{7,15},{16,24},{20,... | collective-permute-start | bytes 798728 | tf_op jit(solution)/shard_map/ppermute | solution.py:66
  17.2 2.0 %collective-permute-start = (bf16[1040,128]{1,0:T(8,128)(2,1)}, bf16[1040,128]{1,0:T(8,128)(2,1)}, u32[]{:S(2)}, u32[]{:S(2)}) collective-permute-start(bf16[1040,128]{1,0:T(8,128)(2,1)} %pad_maximum_fusion.2), channel_id=1, source_target_pairs={{0,4},{4,8},{8,12},{1,5},{5,9},{9,13},{2,6},{6,10},{10,14},{3,7},{... | collective-permute-start | bytes 798728 | tf_op jit(solution)/shard_map/ppermute | solution.py:66
  19.6 0.4 bitcast_multiply_fusion.1
  20.0 2.2 %fusion.78 = f32[16,128,128]{1,2,0:T(8,128)} fusion(f32[16,128,128]{2,1,0:T(8,128)S(1)} %bitcast_multiply_fusion.1, bf16[16,128,128]{2,1,0:T(8,128)(2,1)S(1)} %copy-done.1), kind=kOutput, calls=%fused_computation.147 | convolution fusion | flops 402653184 | bytes 2621440 | tf_op jit(solution)/shard_map/hts,hsp->htp/dot_general | solution.py:159
  22.2 1.9 %fusion.75 = (f32[2,8,128]{2,1,0:T(8,128)}, f32[2,8,128,128]{2,3,1,0:T(8,128)}) fusion(bf16[2,8,128,128]{3,2,1,0:T(8,128)(2,1)S(1)} %bitcast.126, bf16[2,128,256]{2,1,0:T(8,128)(2,1)S(1)} %copy-done.11, pred[128,128]{0,1:T(8,128)(4,1)S(1)} %iota_compare_fusion), kind=kOutput, calls=%fused_computation.144 | convolution fusion | flops 67893248 | bytes 1662976 | tf_op jit(solution)/shard_map/gptd,gkd->gptk/dot_general | solution.py:87
  24.1 0.3 copy.48
  24.4 0.5 exp.74
  25.1 1.3 %collective-permute-start.2 = (bf16[1040,128]{1,0:T(8,128)(2,1)}, bf16[1040,128]{1,0:T(8,128)(2,1)S(1)}, u32[]{:S(2)}, u32[]{:S(2)}) collective-permute-start(bf16[1040,128]{1,0:T(8,128)(2,1)} %pad_maximum_fusion.2), channel_id=1, source_target_pairs={{0,12},{1,13},{2,14},{3,15},{16,28},{17,29},{18,30},{19,31}} | collective-permute-start | bytes 798728 | tf_op jit(solution)/shard_map/ppermute | solution.py:66
  26.4 1.1 %fusion.76 = (f32[2,8,128]{2,1,0:T(8,128)S(1)}, f32[2,8,128,128]{2,3,1,0:T(8,128)S(1)}) fusion(bf16[2,8,128,128]{3,2,1,0:T(8,128)(2,1)S(1)} %bitcast.127, bf16[2,128,256]{2,1,0:T(8,128)(2,1)} %collective-permute-done.3, pred[]{:T(512)S(6)} %ge.51), kind=kOutput, calls=%fused_computation.145 | convolution fusion | flops 67893248 | bytes 1646593 | tf_op jit(solution)/shard_map/gptd,gkd->gptk/dot_general | solution.py:87
  27.6 1.2 %fusion.73 = (f32[2,8,128]{2,1,0:T(8,128)S(1)}, f32[2,8,128,128]{2,3,1,0:T(8,128)S(1)}) fusion(bf16[2,8,128,128]{3,2,1,0:T(8,128)(2,1)S(1)} %bitcast.129, bf16[2,128,256]{2,1,0:T(8,128)(2,1)} %collective-permute-done.5, pred[]{:T(512)S(6)} %ge.53), kind=kOutput, calls=%fused_computation.142 | convolution fusion | flops 67893248 | bytes 1646593 | tf_op jit(solution)/shard_map/gptd,gkd->gptk/dot_general | solution.py:87
  28.8 1.2 %fusion.74 = (f32[2,8,128]{2,1,0:T(8,128)S(1)}, f32[2,8,128,128]{2,3,1,0:T(8,128)S(1)}) fusion(bf16[2,8,128,128]{3,2,1,0:T(8,128)(2,1)S(1)} %bitcast.128, bf16[2,128,256]{2,1,0:T(8,128)(2,1)} %collective-permute-done.4, pred[]{:T(512)S(6)} %ge.52), kind=kOutput, calls=%fused_computation.143 | convolution fusion | flops 67893248 | bytes 1646593 | tf_op jit(solution)/shard_map/gptd,gkd->gptk/dot_general | solution.py:87
  30.1 0.3 fusion.27
  30.4 1.0 %fusion.17 = (f32[2,8,128]{2,1,0:T(8,128)S(1)}, f32[2,8,128]{2,1,0:T(8,128)S(1)}, f32[2,8,128]{2,1,0:T(8,128)S(1)}, f32[2,8,128]{2,1,0:T(8,128)S(1)}) fusion(f32[2,8,128,128]{2,3,1,0:T(8,128)S(1)} %get-tuple-element.41, f32[2,8,128]{2,1,0:T(8,128)S(1)} %maximum_maximum_fusion, f32[2,8,128,128]{2,3,1,0:T(8,128)S(1)} %copy-done.2, ...), kind=kLoop, calls=%fused_computation.46 | loop fusion | flops 2088960 | bytes 4235264 | tf_op jit(solution)/shard_map/reduce_sum | solution.py:103
  31.4 1.2 %fusion.23 = f32[2,8,128,128]{2,3,1,0:T(8,128)S(1)} fusion(f32[2,8,128,128]{2,3,1,0:T(8,128)S(1)} %get-tuple-element.35, f32[2,8,128]{2,1,0:T(8,128)S(1)} %maximum_maximum_fusion, bf16[2,128,256]{2,1,0:T(8,128)(2,1)} %collective-permute-done.5), kind=kOutput, calls=%fused_computation.52 | convolution fusion | flops 67633152 | bytes 2170880 | tf_op jit(solution)/shard_map/gptk,gkd->gptd/dot_general | solution.py:104
  32.6 1.2 %convolution_add_fusion.2 = f32[2,8,128,128]{2,3,1,0:T(8,128)S(1)} fusion(f32[2,8,128,128]{2,3,1,0:T(8,128)S(1)} %fusion.27, f32[2,8,128,128]{2,3,1,0:T(8,128)S(1)} %get-tuple-element.41, f32[2,8,128]{2,1,0:T(8,128)S(1)} %maximum_maximum_fusion, bf16[2,128,256]{2,1,0:T(8,128)(2,1)} %collective-permute-done.3), kind=kOutput, calls=%fused_computation.8 | convolution fusion | flops 67895296 | bytes 3219456 | tf_op jit(solution)/shard_map/gptk,gkd->gptd/dot_general | solution.py:104
  33.8 1.3 %multiply_reduce_fusion.2 = (f32[2,8,128]{2,1,0:T(8,128)S(1)}, f32[2,8,128,128]{2,3,1,0:T(8,128)S(1)}) fusion(f32[2,8,128]{2,1,0:T(8,128)S(1)} %add_add_fusion, f32[2,8,128,128]{2,3,1,0:T(8,128)S(1)} %fusion.23, f32[2,8,128,128]{2,3,1,0:T(8,128)S(1)} %convolution_add_fusion.2, bf16[2,128,256]{2,1,0:T(8,128)(2,1)} %collective-permute-done.4, ...), kind=kOutput, calls=%fused_computation.37 | convolution fusion | flops 69466112 | bytes 4284416 | tf_op jit(solution)/shard_map/gptk,gkd->gptd/dot_general | solution.py:104
  35.1 0.7 slice_convert_fusion.3
  35.9 0.7 copy-done.8
  36.6 1.1 %convert_multiply_fusion.5 = f32[1024,128]{1,0:T(8,128)S(1)} fusion(bf16[1040,128]{1,0:T(8,128)(2,1)} %collective-permute-done, f32[]{:T(128)S(6)} %select_n.110), kind=kLoop, calls=%fused_computation.72 | loop fusion | flops 262144 | bytes 786436 | tf_op jit(solution)/shard_map/mul | solution.py:147
  38.1 0.9 %copy-done.3 = f32[16,128,128]{1,2,0:T(8,128)S(1)} copy-done((f32[16,128,128]{1,2,0:T(8,128)S(1)}, f32[16,128,128]{1,2,0:T(8,128)}, u32[]{:S(2)}) %copy-start.3) | copy-done | bytes 1048600
  39.1 2.0 %multiply_reduce_fusion.3 = (f32[16,128]{1,0:T(8,128)S(1)}, f32[16,128,128]{1,2,0:T(8,128)S(1)}) fusion(bf16[16,128,128]{1,2,0:T(8,128)(2,1)S(1)} %copy.48, f32[16]{0:T(128)S(1)} %copy-done.14, f32[16,128,128]{1,2,0:T(8,128)S(1)} %copy-done.3, f32[16,64,128]{2,1,0:T(8,128)S(1)} %fusion.32, f32[16,128,64]{1,2,0:T(8,128)S(1)} %bitcast.133, ...), kind=kOutput, calls=%fused_computation.42 | convolution fusion | flops 203159552 | bytes 3686464 | tf_op jit(solution)/shard_map/htn,hnp->htp/dot_general | solution.py:167
  41.1 0.4 multiply_reduce_fusion.1
  41.5 0.6 multiply_reduce_fusion
  42.1 2.1 %fusion.77 = (bf16[16,64,128]{2,1,0:T(8,128)(2,1)S(1)}, f32[16,64,128]{2,1,0:T(8,128)S(1)}) fusion(f32[16,128,128]{1,2,0:T(8,128)S(1)} %get-tuple-element.19, f32[16,128,64]{1,2,0:T(8,128)S(1)} %bitcast.134, f32[16,128]{1,0:T(8,128)S(1)} %get-tuple-element.26), kind=kOutput, calls=%fused_computation.146 | convolution fusion | flops 201588736 | bytes 2367488 | tf_op jit(solution)/shard_map/htn,htp->hnp/dot_general | solution.py:176
  44.3 0.7 collective-permute-start.6
  45.0 0.9 %collective-permute-start.7 = (bf16[1040,128]{1,0:T(8,128)(2,1)S(1)}, bf16[1040,128]{1,0:T(8,128)(2,1)S(1)}, u32[]{:S(2)}, u32[]{:S(2)}) collective-permute-start(bf16[1040,128]{1,0:T(8,128)(2,1)S(1)} %pad_maximum_fusion.1), channel_id=1, source_target_pairs={{12,4},{13,5},{14,6},{15,7},{28,20},{29,21},{30,22},{31,23}} | collective-permute-start | bytes 798728 | tf_op jit(solution)/shard_map/ppermute | solution.py:182
  45.9 1.1 %fusion.79 = f32[16,128,128]{1,2,0:T(8,128)S(1)} fusion(f32[16,128,128]{2,1,0:T(8,128)S(1)} %bitcast_multiply_fusion.1, f32[16,128,128]{1,2,0:T(8,128)S(1)} %get-tuple-element.19), kind=kOutput, calls=%fused_computation.148 | convolution fusion | flops 402653184 | bytes 3145728 | tf_op jit(solution)/shard_map/hts,htp->hsp/dot_general | solution.py:186
  47.0 1.2 %convolution_multiply_fusion = f32[16,128,128]{2,1,0:T(8,128)S(1)} fusion(f32[16,128,128]{1,2,0:T(8,128)S(1)} %get-tuple-element.19, bf16[16,128,128]{2,1,0:T(8,128)(2,1)S(1)} %copy-done.1, f32[16,128]{1,0:T(8,128)S(1)} %reduce_window_sum.21, pred[128,128]{1,0:T(8,128)(4,1)S(1)} %copy.44), kind=kOutput, calls=%fused_computation | convolution fusion | flops 403701760 | bytes 2646016 | tf_op jit(solution)/shard_map/htp,hsp->hts/dot_general | solution.py:188
  48.2 1.0 %convolution_multiply_fusion.6 = f32[16,128,64]{1,2,0:T(8,128)S(1)} fusion(f32[16,128,128]{1,2,0:T(8,128)S(1)} %get-tuple-element.19, f32[16,64,128]{2,1,0:T(8,128)S(1)} %fusion.32, f32[16,128]{1,0:T(8,128)S(1)} %get-tuple-element.26), kind=kOutput, calls=%fused_computation.21 | convolution fusion | flops 201457664 | bytes 2105344 | tf_op jit(solution)/shard_map/hnp,htp->htn/dot_general | solution.py:192
  49.3 2.1 %convolution_add_fusion.3 = f32[16,128,64]{1,2,0:T(8,128)S(1)} fusion(f32[16,128,64]{1,2,0:T(8,128)S(1)} %convolution_multiply_fusion.6, f32[16,128,128]{2,1,0:T(8,128)S(1)} %convolution_multiply_fusion, f32[16,128,64]{1,2,0:T(8,128)S(1)} %bitcast.131), kind=kOutput, calls=%fused_computation.22 | convolution fusion | flops 201457664 | bytes 2621440 | tf_op jit(solution)/shard_map/hts,hsn->htn/dot_general | solution.py:191
  51.5 0.6 copy-done.15
  52.4 1.3 %collective-permute-start.8 = (bf16[16,64,128]{2,1,0:T(8,128)(2,1)S(1)}, bf16[16,64,128]{2,1,0:T(8,128)(2,1)S(1)}, u32[]{:S(2)}, u32[]{:S(2)}) collective-permute-start(bf16[16,64,128]{2,1,0:T(8,128)(2,1)S(1)} %add_convert_fusion.1), channel_id=1, source_target_pairs={{4,0},{5,1},{6,2},{7,3},{20,16},{21,17},{22,18},{23,19}} | collective-permute-start | bytes 786440 | tf_op jit(solution)/shard_map/ppermute | solution.py:205
  53.7 1.8 %fusion.80 = f32[16,128,64]{1,2,0:T(8,128)} fusion(f32[16,128,128]{2,1,0:T(8,128)S(1)} %convolution_multiply_fusion, f32[16,128,64]{1,2,0:T(8,128)S(1)} %bitcast.135), kind=kOutput, calls=%fused_computation.149 | convolution fusion | flops 201326592 | bytes 2097152 | tf_op jit(solution)/shard_map/hts,htn->hsn/dot_general | solution.py:190
  55.5 20.2 %collective-permute-done.8 = bf16[16,64,128]{2,1,0:T(8,128)(2,1)S(1)} collective-permute-done((bf16[16,64,128]{2,1,0:T(8,128)(2,1)S(1)}, bf16[16,64,128]{2,1,0:T(8,128)(2,1)S(1)}, u32[]{:S(2)}, u32[]{:S(2)}) %collective-permute-start.8) | collective-permute-done | bytes 262176 | tf_op jit(solution)/shard_map/ppermute | solution.py:205
  75.8 0.4 multiply_reduce_fusion.4
  76.2 2.8 %fusion.13 = (f32[16,128]{1,0:T(8,128)S(1)}, bf16[16,128,128]{1,2,0:T(8,128)(2,1)}) fusion(bf16[16,128,128]{1,2,0:T(8,128)(2,1)S(1)} %copy.48, f32[16,128,128]{1,2,0:T(8,128)S(1)} %get-tuple-element.19, f32[16]{0:T(128)S(1)} %copy-done.14, f32[16,128,128]{1,2,0:T(8,128)S(1)} %fusion.79, f32[16,64,128]{2,1,0:T(8,128)S(1)} %get-tuple-element.17, ...), kind=kOutput, calls=%fused_computation.27 | convolution fusion | flops 203290624 | bytes 4210752 | tf_op jit(solution)/shard_map/hsn,hnp->hsp/dot_general | solution.py:220
  79.0 1.2 %reduce_window_sum.22 = f32[16,128]{1,0:T(8,128)S(1)} reduce-window(f32[16,128]{1,0:T(8,128)S(1)} %sub.84, f32[]{:T(128)} %constant.13.clone.1), window={size=1x128 pad=0_0x0_127}, to_apply=%region_16.17 | reduce-window | flops 260096 | bytes 16388 | tf_op jit(solution)/shard_map/body/reduce_window_sum | solution.py:222
  80.2 2.2 %fusion.11 = f32[16,128,64]{1,2,0:T(8,128)S(1)} fusion(f32[16,128,64]{1,2,0:T(8,128)} %fusion.80, f32[16,64,128]{2,1,0:T(8,128)S(1)} %get-tuple-element.17, bf16[16,128,128]{2,1,0:T(8,128)(2,1)S(1)} %copy-done.1, f32[16,128]{1,0:T(8,128)S(1)} %get-tuple-element.27), kind=kOutput, calls=%fused_computation.25 | convolution fusion | flops 201588736 | bytes 2105344 | tf_op jit(solution)/shard_map/hnp,hsp->hsn/dot_general | solution.py:225
  82.4 0.7 copy.61
  83.4 1.0 %copy.60 = bf16[16,128,128]{2,1,0:T(8,128)(2,1)} copy(bf16[16,128,128]{1,2,0:T(8,128)(2,1)S(1)} %copy-done.5) | data formatting | bytes 1048576
  84.4 0.7 broadcast_add_fusion
  (76 shorter events, 2.2 us)
Async XLA Ops:
  0.6 21.6 %copy-start = (bf16[16,128,128]{2,1,0:T(8,128)(2,1)S(1)}, bf16[16,128,128]{2,1,0:T(8,128)(2,1)}, u32[]{:S(2)}) copy-start(bf16[16,128,128]{2,1,0:T(8,128)(2,1)} %param.7) | copy-start | bytes 1572868
  0.6 12.9 %copy-start.9 = (bf16[2,128,128]{2,1,0:T(8,128)(2,1)S(1)}, bf16[2,128,128]{2,1,0:T(8,128)(2,1)}, u32[]{:S(2)}) copy-start(bf16[2,128,128]{2,1,0:T(8,128)(2,1)} %param.10) | copy-start | bytes 196612
  0.7 13.2 %copy-start.1 = (bf16[16,128,128]{2,1,0:T(8,128)(2,1)S(1)}, bf16[16,128,128]{2,1,0:T(8,128)(2,1)}, u32[]{:S(2)}) copy-start(bf16[16,128,128]{2,1,0:T(8,128)(2,1)} %param.9) | copy-start | bytes 1572868
  0.7 26.9 %collective-permute-start.5 = (bf16[2,128,256]{2,1,0:T(8,128)(2,1)}, bf16[2,128,256]{2,1,0:T(8,128)(2,1)}, u32[]{:S(2)}, u32[]{:S(2)}) collective-permute-start(bf16[2,128,256]{2,1,0:T(8,128)(2,1)} %param.8), channel_id=1, source_target_pairs={{0,12},{1,13},{2,14},{3,15},{16,28},{17,29},{18,30},{19,31}} | collective-permute-start | bytes 393224 | tf_op jit(solution)/shard_map/ppermute | solution.py:66
  8.4 16.7 %collective-permute-start.3 = (bf16[2,128,256]{2,1,0:T(8,128)(2,1)}, bf16[2,128,256]{2,1,0:T(8,128)(2,1)}, u32[]{:S(2)}, u32[]{:S(2)}) collective-permute-start(bf16[2,128,256]{2,1,0:T(8,128)(2,1)} %param.8), channel_id=1, source_target_pairs={{0,4},{4,8},{8,12},{1,5},{5,9},{9,13},{2,6},{6,10},{10,14},{3,7},{... | collective-permute-start | bytes 393224 | tf_op jit(solution)/shard_map/ppermute | solution.py:66
  10.4 18.4 %collective-permute-start.4 = (bf16[2,128,256]{2,1,0:T(8,128)(2,1)}, bf16[2,128,256]{2,1,0:T(8,128)(2,1)}, u32[]{:S(2)}, u32[]{:S(2)}) collective-permute-start(bf16[2,128,256]{2,1,0:T(8,128)(2,1)} %param.8), channel_id=1, source_target_pairs={{0,8},{4,12},{1,9},{5,13},{2,10},{6,14},{3,11},{7,15},{16,24},{20,... | collective-permute-start | bytes 393224 | tf_op jit(solution)/shard_map/ppermute | solution.py:66
  15.9 19.2 %collective-permute-start.1 = (bf16[1040,128]{1,0:T(8,128)(2,1)}, bf16[1040,128]{1,0:T(8,128)(2,1)S(1)}, u32[]{:S(2)}, u32[]{:S(2)}) collective-permute-start(bf16[1040,128]{1,0:T(8,128)(2,1)} %pad_maximum_fusion.2), channel_id=1, source_target_pairs={{0,8},{4,12},{1,9},{5,13},{2,10},{6,14},{3,11},{7,15},{16,24},{20,... | collective-permute-start | bytes 798728 | tf_op jit(solution)/shard_map/ppermute | solution.py:66
  17.2 17.9 %collective-permute-start = (bf16[1040,128]{1,0:T(8,128)(2,1)}, bf16[1040,128]{1,0:T(8,128)(2,1)}, u32[]{:S(2)}, u32[]{:S(2)}) collective-permute-start(bf16[1040,128]{1,0:T(8,128)(2,1)} %pad_maximum_fusion.2), channel_id=1, source_target_pairs={{0,4},{4,8},{8,12},{1,5},{5,9},{9,13},{2,6},{6,10},{10,14},{3,7},{... | collective-permute-start | bytes 798728 | tf_op jit(solution)/shard_map/ppermute | solution.py:66
  20.0 2.2 %copy-start.11 = (bf16[2,128,256]{2,1,0:T(8,128)(2,1)S(1)}, bf16[2,128,256]{2,1,0:T(8,128)(2,1)}, u32[]{:S(2)}) copy-start(bf16[2,128,256]{2,1,0:T(8,128)(2,1)} %param.8) | copy-start | bytes 393220
  25.1 10.7 %collective-permute-start.2 = (bf16[1040,128]{1,0:T(8,128)(2,1)}, bf16[1040,128]{1,0:T(8,128)(2,1)S(1)}, u32[]{:S(2)}, u32[]{:S(2)}) collective-permute-start(bf16[1040,128]{1,0:T(8,128)(2,1)} %pad_maximum_fusion.2), channel_id=1, source_target_pairs={{0,12},{1,13},{2,14},{3,15},{16,28},{17,29},{18,30},{19,31}} | collective-permute-start | bytes 798728 | tf_op jit(solution)/shard_map/ppermute | solution.py:66
  28.7 1.3 %copy-start.2 = (f32[2,8,128,128]{2,3,1,0:T(8,128)S(1)}, f32[2,8,128,128]{2,3,1,0:T(8,128)}, u32[]{:S(2)}) copy-start(f32[2,8,128,128]{2,3,1,0:T(8,128)} %get-tuple-element.39) | copy-start | bytes 3145732
  28.7 1.3 %copy-start.12 = (bf16[2,128,256]{2,1,0:T(8,128)(2,1)S(1)}, bf16[2,128,256]{2,1,0:T(8,128)(2,1)}, u32[]{:S(2)}) copy-start(bf16[2,128,256]{2,1,0:T(8,128)(2,1)} %param.8) | copy-start | bytes 393220
  28.8 1.3 %copy-start.13 = (f32[2,8,128]{2,1,0:T(8,128)S(1)}, f32[2,8,128]{2,1,0:T(8,128)}, u32[]{:S(2)}) copy-start(f32[2,8,128]{2,1,0:T(8,128)} %get-tuple-element.38) | copy-start | bytes 24580
  35.1 0.8 copy-start.7
  35.8 0.7 copy-start.8
  36.6 1.1 %copy-start.10 = (f32[16,64,128]{2,1,0:T(8,128)S(1)}, f32[16,64,128]{2,1,0:T(8,128)}, u32[]{:S(2)}) copy-start(f32[16,64,128]{2,1,0:T(8,128)} %param.13) | copy-start | bytes 1572868
  36.6 1.2 %slice-start.1 = ((bf16[1040,128]{1,0:T(8,128)(2,1)}), bf16[1024,128]{1,0:T(8,128)(2,1)S(1)}, s32[]{:S(2)}) async-start(bf16[1040,128]{1,0:T(8,128)(2,1)} %copy-done.7), calls=%async_computation.1 | async-start | bytes 524288 | tf_op jit(solution)/shard_map/slice | solution.py:38
  36.6 1.3 %slice-start.2 = ((bf16[1040,128]{1,0:T(8,128)(2,1)}), bf16[1024,128]{1,0:T(8,128)(2,1)S(1)}, s32[]{:S(2)}) async-start(bf16[1040,128]{1,0:T(8,128)(2,1)} %copy-done.8), calls=%async_computation.2 | async-start | bytes 524288 | tf_op jit(solution)/shard_map/slice | solution.py:38
  37.8 1.2 %copy-start.3 = (f32[16,128,128]{1,2,0:T(8,128)S(1)}, f32[16,128,128]{1,2,0:T(8,128)}, u32[]{:S(2)}) copy-start(f32[16,128,128]{1,2,0:T(8,128)} %fusion.78) | copy-start | bytes 3145732
  38.1 0.9 %copy-start.14 = (f32[16]{0:T(128)S(1)}, f32[16]{0:T(128)}, u32[]{:S(2)}) copy-start(f32[16]{0:T(128)} %param.12) | copy-start | bytes 196
  44.3 7.1 %collective-permute-start.6 = (bf16[1040,128]{1,0:T(8,128)(2,1)S(1)}, bf16[1040,128]{1,0:T(8,128)(2,1)S(1)}, u32[]{:S(2)}, u32[]{:S(2)}) collective-permute-start(bf16[1040,128]{1,0:T(8,128)(2,1)S(1)} %pad_maximum_fusion.1), channel_id=1, source_target_pairs={{12,8},{8,4},{13,9},{9,5},{14,10},{10,6},{15,11},{11,7},{28,24},{2... | collective-permute-start | bytes 798728 | tf_op jit(solution)/shard_map/ppermute | solution.py:181
  45.0 6.5 %collective-permute-start.7 = (bf16[1040,128]{1,0:T(8,128)(2,1)S(1)}, bf16[1040,128]{1,0:T(8,128)(2,1)S(1)}, u32[]{:S(2)}, u32[]{:S(2)}) collective-permute-start(bf16[1040,128]{1,0:T(8,128)(2,1)S(1)} %pad_maximum_fusion.1), channel_id=1, source_target_pairs={{12,4},{13,5},{14,6},{15,7},{28,20},{29,21},{30,22},{31,23}} | collective-permute-start | bytes 798728 | tf_op jit(solution)/shard_map/ppermute | solution.py:182
  51.5 0.7 copy-start.15
  51.5 4.0 %copy-start.6 = (bf16[1040,128]{1,0:T(8,128)(2,1)}, bf16[1040,128]{1,0:T(8,128)(2,1)S(1)}, u32[]{:S(2)}) copy-start(bf16[1040,128]{1,0:T(8,128)(2,1)S(1)} %collective-permute-done.7) | copy-start | bytes 798724
  52.4 23.4 %collective-permute-start.8 = (bf16[16,64,128]{2,1,0:T(8,128)(2,1)S(1)}, bf16[16,64,128]{2,1,0:T(8,128)(2,1)S(1)}, u32[]{:S(2)}, u32[]{:S(2)}) collective-permute-start(bf16[16,64,128]{2,1,0:T(8,128)(2,1)S(1)} %add_convert_fusion.1), channel_id=1, source_target_pairs={{4,0},{5,1},{6,2},{7,3},{20,16},{21,17},{22,18},{23,19}} | collective-permute-start | bytes 786440 | tf_op jit(solution)/shard_map/ppermute | solution.py:205
  55.5 20.3 %copy-start.4 = (f32[16,64,128]{2,1,0:T(8,128)S(1)}, f32[16,64,128]{2,1,0:T(8,128)}, u32[]{:S(2)}) copy-start(f32[16,64,128]{2,1,0:T(8,128)} %get-tuple-element.33) | copy-start | bytes 1572868
  55.5 20.3 %slice-start = ((bf16[1040,128]{1,0:T(8,128)(2,1)}), bf16[1024,128]{1,0:T(8,128)(2,1)S(1)}, s32[]{:S(2)}) async-start(bf16[1040,128]{1,0:T(8,128)(2,1)} %copy-done.6), calls=%async_computation | async-start | bytes 524288 | tf_op jit(solution)/shard_map/slice | solution.py:38
  82.4 1.0 %copy-start.5 = (bf16[16,128,128]{1,2,0:T(8,128)(2,1)S(1)}, bf16[16,128,128]{1,2,0:T(8,128)(2,1)}, u32[]{:S(2)}) copy-start(bf16[16,128,128]{1,2,0:T(8,128)(2,1)} %get-tuple-element.23) | copy-start | bytes 1572868

commit v7 on v3

--- a/solution.py
+++ b/solution.py
@@ -121,8 +121,6 @@
     seq_count = lax.axis_size("seq")
     seq_rank = lax.axis_index("seq")
 
-    kv_earlier = shifted(keys_values, 1)
-
     log_decay = jax.nn.log_sigmoid(decay_logit)
     cumulative = jnp.cumsum(log_decay, axis=1)
     totals = cumulative[:, -1]
@@ -136,7 +134,9 @@
     weighted_in = in_heads * to_end[..., None]
     end_state = jnp.einsum("hsn,hsp->hnp", weighted_in, inputs_wide, precision=highest)
 
-    state_earlier = shifted(pack_rows(end_state, [totals]), 1)
+    kv_ready, state_ready = lax.optimization_barrier((keys_values, pack_rows(end_state, [totals])))
+    kv_earlier = shifted(kv_ready, 1)
+    state_earlier = shifted(state_ready, 1)
     ends_earlier = []
     prefix_state = jnp.zeros_like(end_state)
     gap = jnp.zeros_like(totals)

time: 82.4 us -> 85.5 us (1.038)
  matrix products: 29.7 us -> 31.4 us
  waiting for transfers between devices: 22.1 us -> 23.5 us
    ppermute x9, waiting for transfers between devices: 22.1 us -> 23.5 us  [shifted(): moved.append(lax.ppermute(x, 'seq', pairs))]
    unnamed x40 -> x38, local copies, waits for them, and re-layouts: 4.04 us -> 4.04 us
  transfers between devices with their start and end apart: 9 -> 9, of which waited for: 5 -> 5; matrix products, arithmetic and copies ran while one was open for 28% -> 25% of each run, Pallas kernels for 0% -> 0%
where the time goes in v7:
time: 85.5 us; the launch traced here: 84.7 us
  matrix products  31.4 us (37%)
  waiting for transfers between devices  23.5 us (27%)
  starting transfers between devices  15.7 us (18%)
  other arithmetic  7.27 us (9%)
  local copies, waits for them, and re-layouts  5.55 us (6%)
  between operations  1.27 us (1%)
    ppermute x9, waiting for transfers between devices, shifted(): moved.append(lax.ppermute(x, 'seq', pairs))  23.5 us
    ppermute x9, starting transfers between devices, shifted(): moved.append(lax.ppermute(x, 'seq', pairs))  15.7 us
    dot_general x4, matrix products, teacher_rows(): jnp.einsum('gptk,gkd->gptd', exponentials.astype(jnp.bfloat16), block[......  4.91 us
    dot_general x4, matrix products, teacher_rows(): jnp.einsum('gptd,gkd->gptk', grouped, block[..., :head_width], preferred_...  4.59 us
    unnamed x38, local copies, waits for them, and re-layouts  4.04 us
    dot_general x1, matrix products, body(): jnp.einsum('hts,hsn->htn', paired, in_heads, precision=highest)  2.94 us
    dot_general x1, matrix products, body(): jnp.einsum('hsn,hnp->hsp', weighted_in, incoming, precision=highest)  2.84 us
    dot_general x1, matrix products, body(): local_din = jnp.einsum('hts,htn->hsn', paired, out_heads, precision=highest)  2.44 us
  transfers between devices with their start and end apart: 9, of which 5 were waited for; matrix products, arithmetic and copies ran while one was open for 25% of the time, Pallas kernels for 0%

profile of v7, /device:TPU:8, one launch (start us, length us, event | category | flops | bytes accessed | tf_op | source)
XLA Modules:
  0.0 84.7 jit_solution(5259942811946966410)
XLA Ops:
  0.7 0.8 fusion.54
  2.3 0.5 convolution_convert_fusion
  3.1 0.8 pad_maximum_fusion.1
  3.9 1.3 %collective-permute-start.5 = (bf16[2,128,256]{2,1,0:T(8,128)(2,1)}, bf16[2,128,256]{2,1,0:T(8,128)(2,1)}, u32[]{:S(2)}, u32[]{:S(2)}) collective-permute-start(bf16[2,128,256]{2,1,0:T(8,128)(2,1)} %param.8), channel_id=1, source_target_pairs={{0,12},{1,13},{2,14},{3,15},{16,28},{17,29},{18,30},{19,31}} | collective-permute-start | bytes 393224 | tf_op jit(solution)/shard_map/ppermute | solution.py:66
  5.2 3.5 %collective-permute-start.3 = (bf16[2,128,256]{2,1,0:T(8,128)(2,1)}, bf16[2,128,256]{2,1,0:T(8,128)(2,1)}, u32[]{:S(2)}, u32[]{:S(2)}) collective-permute-start(bf16[2,128,256]{2,1,0:T(8,128)(2,1)} %param.8), channel_id=1, source_target_pairs={{0,4},{4,8},{8,12},{1,5},{5,9},{9,13},{2,6},{6,10},{10,14},{3,7},{... | collective-permute-start | bytes 393224 | tf_op jit(solution)/shard_map/ppermute | solution.py:66
  8.7 2.9 %collective-permute-start.4 = (bf16[2,128,256]{2,1,0:T(8,128)(2,1)}, bf16[2,128,256]{2,1,0:T(8,128)(2,1)}, u32[]{:S(2)}, u32[]{:S(2)}) collective-permute-start(bf16[2,128,256]{2,1,0:T(8,128)(2,1)} %param.8), channel_id=1, source_target_pairs={{0,8},{4,12},{1,9},{5,13},{2,10},{6,14},{3,11},{7,15},{16,24},{20,... | collective-permute-start | bytes 393224 | tf_op jit(solution)/shard_map/ppermute | solution.py:66
  11.6 1.3 %collective-permute-start.1 = (bf16[1040,128]{1,0:T(8,128)(2,1)}, bf16[1040,128]{1,0:T(8,128)(2,1)S(1)}, u32[]{:S(2)}, u32[]{:S(2)}) collective-permute-start(bf16[1040,128]{1,0:T(8,128)(2,1)} %pad_maximum_fusion.1), channel_id=1, source_target_pairs={{0,8},{4,12},{1,9},{5,13},{2,10},{6,14},{3,11},{7,15},{16,24},{20,... | collective-permute-start | bytes 798728 | tf_op jit(solution)/shard_map/ppermute | solution.py:66
  12.9 1.9 %collective-permute-start = (bf16[1040,128]{1,0:T(8,128)(2,1)}, bf16[1040,128]{1,0:T(8,128)(2,1)S(1)}, u32[]{:S(2)}, u32[]{:S(2)}) collective-permute-start(bf16[1040,128]{1,0:T(8,128)(2,1)} %pad_maximum_fusion.1), channel_id=1, source_target_pairs={{0,4},{4,8},{8,12},{1,5},{5,9},{9,13},{2,6},{6,10},{10,14},{3,7},{... | collective-permute-start | bytes 798728 | tf_op jit(solution)/shard_map/ppermute | solution.py:66
  15.2 0.3 bitcast_multiply_fusion.1
  15.6 2.3 %fusion.105 = f32[16,128,128]{1,2,0:T(8,128)} fusion(f32[16,128,128]{2,1,0:T(8,128)S(1)} %bitcast_multiply_fusion.1, bf16[16,128,128]{2,1,0:T(8,128)(2,1)S(1)} %copy-done.1), kind=kOutput, calls=%fused_computation.201 | convolution fusion | flops 402653184 | bytes 2621440 | tf_op jit(solution)/shard_map/hts,hsp->htp/dot_general | solution.py:161
  17.8 1.1 %fusion.103 = (f32[2,8,128]{2,1,0:T(8,128)S(1)}, f32[2,8,128,128]{2,3,1,0:T(8,128)S(1)}) fusion(bf16[2,8,128,128]{3,2,1,0:T(8,128)(2,1)S(1)} %bitcast.183, bf16[2,128,256]{2,1,0:T(8,128)(2,1)} %param.8, pred[128,128]{0,1:T(8,128)(4,1)S(1)} %iota_compare_fusion), kind=kOutput, calls=%fused_computation.199 | convolution fusion | flops 67893248 | bytes 1662976 | tf_op jit(solution)/shard_map/gptd,gkd->gptk/dot_general | solution.py:87
  19.4 0.7 collective-permute-start.2
  20.1 1.2 %fusion.104 = (f32[2,8,128]{2,1,0:T(8,128)S(1)}, f32[2,8,128,128]{2,3,1,0:T(8,128)S(1)}) fusion(bf16[2,8,128,128]{3,2,1,0:T(8,128)(2,1)S(1)} %bitcast.184, bf16[2,128,256]{2,1,0:T(8,128)(2,1)} %collective-permute-done.3, pred[]{:T(512)S(6)} %ge.51), kind=kOutput, calls=%fused_computation.200 | convolution fusion | flops 67893248 | bytes 1646593 | tf_op jit(solution)/shard_map/gptd,gkd->gptk/dot_general | solution.py:87
  21.3 1.1 %fusion.101 = (f32[2,8,128]{2,1,0:T(8,128)S(1)}, f32[2,8,128,128]{2,3,1,0:T(8,128)S(1)}) fusion(bf16[2,8,128,128]{3,2,1,0:T(8,128)(2,1)S(1)} %bitcast.186, bf16[2,128,256]{2,1,0:T(8,128)(2,1)} %collective-permute-done.5, pred[]{:T(512)S(6)} %ge.53), kind=kOutput, calls=%fused_computation.197 | convolution fusion | flops 67893248 | bytes 1646593 | tf_op jit(solution)/shard_map/gptd,gkd->gptk/dot_general | solution.py:87
  22.4 4.1 %collective-permute-done.4 = bf16[2,128,256]{2,1,0:T(8,128)(2,1)} collective-permute-done((bf16[2,128,256]{2,1,0:T(8,128)(2,1)}, bf16[2,128,256]{2,1,0:T(8,128)(2,1)}, u32[]{:S(2)}, u32[]{:S(2)}) %collective-permute-start.4) | collective-permute-done | bytes 131104 | tf_op jit(solution)/shard_map/ppermute | solution.py:66
  26.6 1.1 %fusion.102 = (f32[2,8,128]{2,1,0:T(8,128)S(1)}, f32[2,8,128,128]{2,3,1,0:T(8,128)S(1)}) fusion(bf16[2,8,128,128]{3,2,1,0:T(8,128)(2,1)S(1)} %bitcast.185, bf16[2,128,256]{2,1,0:T(8,128)(2,1)} %collective-permute-done.4, pred[]{:T(512)S(6)} %ge.52), kind=kOutput, calls=%fused_computation.198 | convolution fusion | flops 67893248 | bytes 1646593 | tf_op jit(solution)/shard_map/gptd,gkd->gptk/dot_general | solution.py:87
  27.7 1.2 %fusion.35 = f32[2,8,128,128]{2,3,1,0:T(8,128)S(1)} fusion(f32[2,8,128,128]{2,3,1,0:T(8,128)S(1)} %get-tuple-element.51, f32[2,8,128]{2,1,0:T(8,128)S(1)} %maximum_maximum_fusion, bf16[2,128,256]{2,1,0:T(8,128)(2,1)} %param.8), kind=kOutput, calls=%fused_computation.69 | convolution fusion | flops 67633152 | bytes 2170880 | tf_op jit(solution)/shard_map/gptk,gkd->gptd/dot_general | solution.py:104
  28.9 1.0 %fusion.19 = (f32[2,8,128]{2,1,0:T(8,128)S(1)}, f32[2,8,128]{2,1,0:T(8,128)S(1)}, f32[2,8,128]{2,1,0:T(8,128)S(1)}, f32[2,8,128]{2,1,0:T(8,128)S(1)}) fusion(f32[2,8,128,128]{2,3,1,0:T(8,128)S(1)} %get-tuple-element.53, f32[2,8,128]{2,1,0:T(8,128)S(1)} %maximum_maximum_fusion, f32[2,8,128,128]{2,3,1,0:T(8,128)S(1)} %get-tuple-element.51, ...), kind=kLoop, calls=%fused_computation.50 | loop fusion | flops 2088960 | bytes 4235264 | tf_op jit(solution)/shard_map/reduce_sum | solution.py:103
  29.9 1.2 %fusion.31 = f32[2,8,128,128]{2,3,1,0:T(8,128)S(1)} fusion(f32[2,8,128,128]{2,3,1,0:T(8,128)S(1)} %get-tuple-element.47, f32[2,8,128]{2,1,0:T(8,128)S(1)} %maximum_maximum_fusion, bf16[2,128,256]{2,1,0:T(8,128)(2,1)} %collective-permute-done.5), kind=kOutput, calls=%fused_computation.68 | convolution fusion | flops 67633152 | bytes 2170880 | tf_op jit(solution)/shard_map/gptk,gkd->gptd/dot_general | solution.py:104
  31.1 1.2 %convolution_add_fusion.2 = f32[2,8,128,128]{2,3,1,0:T(8,128)S(1)} fusion(f32[2,8,128,128]{2,3,1,0:T(8,128)S(1)} %fusion.35, f32[2,8,128,128]{2,3,1,0:T(8,128)S(1)} %get-tuple-element.53, f32[2,8,128]{2,1,0:T(8,128)S(1)} %maximum_maximum_fusion, bf16[2,128,256]{2,1,0:T(8,128)(2,1)} %collective-permute-done.3), kind=kOutput, calls=%fused_computation.8 | convolution fusion | flops 67895296 | bytes 3219456 | tf_op jit(solution)/shard_map/gptk,gkd->gptd/dot_general | solution.py:104
  32.3 1.4 %multiply_reduce_fusion.2 = (f32[2,8,128]{2,1,0:T(8,128)S(1)}, f32[2,8,128,128]{2,3,1,0:T(8,128)S(1)}) fusion(f32[2,8,128]{2,1,0:T(8,128)S(1)} %add_add_fusion, f32[2,8,128,128]{2,3,1,0:T(8,128)S(1)} %fusion.31, f32[2,8,128,128]{2,3,1,0:T(8,128)S(1)} %convolution_add_fusion.2, bf16[2,128,256]{2,1,0:T(8,128)(2,1)} %collective-permute-done.4, ...), kind=kOutput, calls=%fused_computation.41 | convolution fusion | flops 69466112 | bytes 4284416 | tf_op jit(solution)/shard_map/gptk,gkd->gptd/dot_general | solution.py:104
  33.7 4.3 %collective-permute-done.1 = bf16[1040,128]{1,0:T(8,128)(2,1)S(1)} collective-permute-done((bf16[1040,128]{1,0:T(8,128)(2,1)}, bf16[1040,128]{1,0:T(8,128)(2,1)S(1)}, u32[]{:S(2)}, u32[]{:S(2)}) %collective-permute-start.1) | collective-permute-done | bytes 266272 | tf_op jit(solution)/shard_map/ppermute | solution.py:66
  38.0 5.0 %collective-permute-done = bf16[1040,128]{1,0:T(8,128)(2,1)S(1)} collective-permute-done((bf16[1040,128]{1,0:T(8,128)(2,1)}, bf16[1040,128]{1,0:T(8,128)(2,1)S(1)}, u32[]{:S(2)}, u32[]{:S(2)}) %collective-permute-start) | collective-permute-done | bytes 266272 | tf_op jit(solution)/shard_map/ppermute | solution.py:66
  43.1 0.3 fusion.27
  43.5 0.8 copy-done.8
  44.3 2.0 %multiply_reduce_fusion.3 = (f32[16,128]{1,0:T(8,128)S(1)}, f32[16,128,128]{1,2,0:T(8,128)S(1)}) fusion(bf16[16,128,128]{1,2,0:T(8,128)(2,1)S(1)} %copy.48, f32[16]{0:T(128)S(1)} %copy-done.15, f32[16,128,128]{1,2,0:T(8,128)S(1)} %copy-done.8, f32[16,64,128]{2,1,0:T(8,128)S(1)} %fusion.27, f32[16,128,64]{1,2,0:T(8,128)S(1)} %bitcast.187, ...), kind=kOutput, calls=%fused_computation.46 | convolution fusion | flops 203159552 | bytes 3686464 | tf_op jit(solution)/shard_map/htn,hnp->htp/dot_general | solution.py:169
  46.3 0.4 multiply_reduce_fusion.1
  46.8 0.6 multiply_reduce_fusion
  47.4 2.1 %fusion.39 = f32[16,64,128]{2,1,0:T(8,128)S(1)} fusion(f32[16,128,128]{1,2,0:T(8,128)S(1)} %get-tuple-element.25, f32[16,128,64]{1,2,0:T(8,128)S(1)} %bitcast.188, f32[16,128]{1,0:T(8,128)S(1)} %get-tuple-element.35), kind=kOutput, calls=%fused_computation.76 | convolution fusion | flops 201457664 | bytes 2105344 | tf_op jit(solution)/shard_map/htn,htp->hnp/dot_general | solution.py:178
  49.6 0.9 %slice-done = bf16[1024,128]{1,0:T(8,128)(2,1)S(1)} async-done(((bf16[1040,128]{1,0:T(8,128)(2,1)}), bf16[1024,128]{1,0:T(8,128)(2,1)S(1)}, s32[]{:S(2)}) %slice-start) | async-done | bytes 262168 | tf_op jit(solution)/shard_map/slice | solution.py:38
  50.5 0.4 multiply_reduce_fusion.4
  51.1 0.7 collective-permute-start.8
  51.8 1.3 %collective-permute-start.7 = (bf16[1040,128]{1,0:T(8,128)(2,1)S(1)}, bf16[1040,128]{1,0:T(8,128)(2,1)S(1)}, u32[]{:S(2)}, u32[]{:S(2)}) collective-permute-start(bf16[1040,128]{1,0:T(8,128)(2,1)S(1)} %pad_maximum_fusion.2), channel_id=1, source_target_pairs={{8,0},{12,4},{9,1},{13,5},{10,2},{14,6},{11,3},{15,7},{24,16},{28,... | collective-permute-start | bytes 798728 | tf_op jit(solution)/shard_map/ppermute | solution.py:66
  53.1 2.1 %collective-permute-start.6 = (bf16[1040,128]{1,0:T(8,128)(2,1)S(1)}, bf16[1040,128]{1,0:T(8,128)(2,1)S(1)}, u32[]{:S(2)}, u32[]{:S(2)}) collective-permute-start(bf16[1040,128]{1,0:T(8,128)(2,1)S(1)} %pad_maximum_fusion.2), channel_id=1, source_target_pairs={{4,0},{8,4},{12,8},{5,1},{9,5},{13,9},{6,2},{10,6},{14,10},{7,3},{... | collective-permute-start | bytes 798728 | tf_op jit(solution)/shard_map/ppermute | solution.py:66
  55.2 2.3 %fusion.106 = f32[16,128,128]{1,2,0:T(8,128)S(1)} fusion(f32[16,128,128]{2,1,0:T(8,128)} %copy-done.2, f32[16,128,128]{1,2,0:T(8,128)S(1)} %get-tuple-element.25), kind=kOutput, calls=%fused_computation.202 | convolution fusion | flops 402653184 | bytes 3145728 | tf_op jit(solution)/shard_map/hts,htp->hsp/dot_general | solution.py:191
  57.6 1.2 %convolution_multiply_fusion = f32[16,128,128]{2,1,0:T(8,128)S(1)} fusion(f32[16,128,128]{1,2,0:T(8,128)S(1)} %get-tuple-element.25, bf16[16,128,128]{2,1,0:T(8,128)(2,1)S(1)} %copy-done.1, f32[16,128]{1,0:T(8,128)S(1)} %reduce_window_sum.21, pred[128,128]{1,0:T(8,128)(4,1)S(1)} %copy.44), kind=kOutput, calls=%fused_computation | convolution fusion | flops 403701760 | bytes 2646016 | tf_op jit(solution)/shard_map/htp,hsp->hts/dot_general | solution.py:193
  58.8 1.0 %convolution_multiply_fusion.6 = f32[16,128,64]{1,2,0:T(8,128)S(1)} fusion(f32[16,128,128]{1,2,0:T(8,128)S(1)} %get-tuple-element.25, f32[16,64,128]{2,1,0:T(8,128)S(1)} %copy-done.7, f32[16,128]{1,0:T(8,128)S(1)} %get-tuple-element.35), kind=kOutput, calls=%fused_computation.24 | convolution fusion | flops 201457664 | bytes 2105344 | tf_op jit(solution)/shard_map/hnp,htp->htn/dot_general | solution.py:197
  59.9 0.4 copy-done.5
  60.2 2.9 %convolution_add_fusion.3 = f32[16,128,64]{1,2,0:T(8,128)} fusion(f32[16,128,64]{1,2,0:T(8,128)S(1)} %convolution_multiply_fusion.6, f32[16,128,128]{2,1,0:T(8,128)S(1)} %convolution_multiply_fusion, f32[16,128,64]{1,2,0:T(8,128)S(1)} %bitcast.191), kind=kOutput, calls=%fused_computation.25 | convolution fusion | flops 201457664 | bytes 2621440 | tf_op jit(solution)/shard_map/hts,hsn->htn/dot_general | solution.py:196
  63.2 0.8 collective-permute-done.7
  64.0 9.3 %collective-permute-done.6 = bf16[1040,128]{1,0:T(8,128)(2,1)S(1)} collective-permute-done((bf16[1040,128]{1,0:T(8,128)(2,1)S(1)}, bf16[1040,128]{1,0:T(8,128)(2,1)S(1)}, u32[]{:S(2)}, u32[]{:S(2)}) %collective-permute-start.6) | collective-permute-done | bytes 266272 | tf_op jit(solution)/shard_map/ppermute | solution.py:66
  73.4 2.0 %fusion.13 = f32[16,128,64]{1,2,0:T(8,128)} fusion(bf16[16,128,128]{2,1,0:T(8,128)(2,1)S(1)} %copy-done.1, f32[16,128]{1,0:T(8,128)S(1)} %get-tuple-element.36, bf16[16,64,128]{2,1,0:T(8,128)(2,1)S(1)} %bitcast.197, f32[16,64,128]{2,1,0:T(8,128)S(1)} %bitcast.193, bf16[16,64,128]{2,1,0:T(8,128)(2,1)S(1)} %bitcast.195, f32[16]{0:T(128)S(1)} %get-tuple-element.38, ...), kind=kOutput, calls=%fused_computation.28 | convolution fusion | flops 202244096 | bytes 2105472 | tf_op jit(solution)/shard_map/hnp,hsp->hsn/dot_general | solution.py:228
  75.4 2.8 %fusion.15 = (f32[16,128]{1,0:T(8,128)S(1)}, bf16[16,128,128]{1,2,0:T(8,128)(2,1)}) fusion(bf16[16,128,128]{1,2,0:T(8,128)(2,1)S(1)} %copy.48, f32[16,128,128]{1,2,0:T(8,128)S(1)} %get-tuple-element.25, f32[16]{0:T(128)S(1)} %copy-done.15, f32[16,128,128]{1,2,0:T(8,128)S(1)} %fusion.106, bf16[16,64,128]{2,1,0:T(8,128)(2,1)S(1)} %bitcast.198, ...), kind=kOutput, calls=%fused_computation.31 | convolution fusion | flops 204077056 | bytes 4735168 | tf_op jit(solution)/shard_map/hsn,hnp->hsp/dot_general | solution.py:223
  78.3 1.2 %reduce_window_sum.22 = f32[16,128]{1,0:T(8,128)S(1)} reduce-window(f32[16,128]{1,0:T(8,128)S(1)} %sub.114, f32[]{:T(128)} %constant.12.clone.1), window={size=1x128 pad=0_0x0_127}, to_apply=%region_19.20 | reduce-window | flops 260096 | bytes 16388 | tf_op jit(solution)/shard_map/body/reduce_window_sum | solution.py:225
  79.5 2.4 %convolution_add_fusion.4 = f32[16,128,64]{1,2,0:T(8,128)S(1)} fusion(f32[16,128,64]{1,2,0:T(8,128)} %fusion.13, f32[16,128,128]{2,1,0:T(8,128)} %copy-done.3, f32[16,128,64]{1,2,0:T(8,128)S(1)} %bitcast.189), kind=kOutput, calls=%fused_computation.26 | convolution fusion | flops 201457664 | bytes 2621440 | tf_op jit(solution)/shard_map/hts,htn->hsn/dot_general | solution.py:195
  82.0 0.7 copy.61
  83.0 1.0 %copy.60 = bf16[16,128,128]{2,1,0:T(8,128)(2,1)} copy(bf16[16,128,128]{1,2,0:T(8,128)(2,1)S(1)} %copy-done.10) | data formatting | bytes 1048576
  84.0 0.7 broadcast_add_fusion
  (83 shorter events, 2.8 us)
Async XLA Ops:
  0.6 17.2 %copy-start = (bf16[16,128,128]{2,1,0:T(8,128)(2,1)S(1)}, bf16[16,128,128]{2,1,0:T(8,128)(2,1)}, u32[]{:S(2)}) copy-start(bf16[16,128,128]{2,1,0:T(8,128)(2,1)} %param.7) | copy-start | bytes 1572868
  0.6 1.4 %copy-start.13 = (bf16[2,128,128]{2,1,0:T(8,128)(2,1)S(1)}, bf16[2,128,128]{2,1,0:T(8,128)(2,1)}, u32[]{:S(2)}) copy-start(bf16[2,128,128]{2,1,0:T(8,128)(2,1)} %param.10) | copy-start | bytes 196612
  0.7 1.7 %copy-start.1 = (bf16[16,128,128]{2,1,0:T(8,128)(2,1)S(1)}, bf16[16,128,128]{2,1,0:T(8,128)(2,1)}, u32[]{:S(2)}) copy-start(bf16[16,128,128]{2,1,0:T(8,128)(2,1)} %param.9) | copy-start | bytes 1572868
  2.3 0.8 copy-start.4
  3.9 17.4 %collective-permute-start.5 = (bf16[2,128,256]{2,1,0:T(8,128)(2,1)}, bf16[2,128,256]{2,1,0:T(8,128)(2,1)}, u32[]{:S(2)}, u32[]{:S(2)}) collective-permute-start(bf16[2,128,256]{2,1,0:T(8,128)(2,1)} %param.8), channel_id=1, source_target_pairs={{0,12},{1,13},{2,14},{3,15},{16,28},{17,29},{18,30},{19,31}} | collective-permute-start | bytes 393224 | tf_op jit(solution)/shard_map/ppermute | solution.py:66
  5.2 14.2 %collective-permute-start.3 = (bf16[2,128,256]{2,1,0:T(8,128)(2,1)}, bf16[2,128,256]{2,1,0:T(8,128)(2,1)}, u32[]{:S(2)}, u32[]{:S(2)}) collective-permute-start(bf16[2,128,256]{2,1,0:T(8,128)(2,1)} %param.8), channel_id=1, source_target_pairs={{0,4},{4,8},{8,12},{1,5},{5,9},{9,13},{2,6},{6,10},{10,14},{3,7},{... | collective-permute-start | bytes 393224 | tf_op jit(solution)/shard_map/ppermute | solution.py:66
  8.7 17.9 %collective-permute-start.4 = (bf16[2,128,256]{2,1,0:T(8,128)(2,1)}, bf16[2,128,256]{2,1,0:T(8,128)(2,1)}, u32[]{:S(2)}, u32[]{:S(2)}) collective-permute-start(bf16[2,128,256]{2,1,0:T(8,128)(2,1)} %param.8), channel_id=1, source_target_pairs={{0,8},{4,12},{1,9},{5,13},{2,10},{6,14},{3,11},{7,15},{16,24},{20,... | collective-permute-start | bytes 393224 | tf_op jit(solution)/shard_map/ppermute | solution.py:66
  11.6 26.4 %collective-permute-start.1 = (bf16[1040,128]{1,0:T(8,128)(2,1)}, bf16[1040,128]{1,0:T(8,128)(2,1)S(1)}, u32[]{:S(2)}, u32[]{:S(2)}) collective-permute-start(bf16[1040,128]{1,0:T(8,128)(2,1)} %pad_maximum_fusion.1), channel_id=1, source_target_pairs={{0,8},{4,12},{1,9},{5,13},{2,10},{6,14},{3,11},{7,15},{16,24},{20,... | collective-permute-start | bytes 798728 | tf_op jit(solution)/shard_map/ppermute | solution.py:66
  12.9 30.1 %collective-permute-start = (bf16[1040,128]{1,0:T(8,128)(2,1)}, bf16[1040,128]{1,0:T(8,128)(2,1)S(1)}, u32[]{:S(2)}, u32[]{:S(2)}) collective-permute-start(bf16[1040,128]{1,0:T(8,128)(2,1)} %pad_maximum_fusion.1), channel_id=1, source_target_pairs={{0,4},{4,8},{8,12},{1,5},{5,9},{9,13},{2,6},{6,10},{10,14},{3,7},{... | collective-permute-start | bytes 798728 | tf_op jit(solution)/shard_map/ppermute | solution.py:66
  15.5 2.3 %copy-start.2 = (f32[16,128,128]{2,1,0:T(8,128)}, f32[16,128,128]{2,1,0:T(8,128)S(1)}, u32[]{:S(2)}) copy-start(f32[16,128,128]{2,1,0:T(8,128)S(1)} %bitcast_multiply_fusion.1) | copy-start | bytes 3145732
  19.4 23.6 %collective-permute-start.2 = (bf16[1040,128]{1,0:T(8,128)(2,1)}, bf16[1040,128]{1,0:T(8,128)(2,1)S(1)}, u32[]{:S(2)}, u32[]{:S(2)}) collective-permute-start(bf16[1040,128]{1,0:T(8,128)(2,1)} %pad_maximum_fusion.1), channel_id=1, source_target_pairs={{0,12},{1,13},{2,14},{3,15},{16,28},{17,29},{18,30},{19,31}} | collective-permute-start | bytes 798728 | tf_op jit(solution)/shard_map/ppermute | solution.py:66
  32.3 10.8 %copy-start.14 = (f32[16,64,128]{2,1,0:T(8,128)S(1)}, f32[16,64,128]{2,1,0:T(8,128)}, u32[]{:S(2)}) copy-start(f32[16,64,128]{2,1,0:T(8,128)} %param.13) | copy-start | bytes 1572868
  38.0 5.4 %copy-start.12 = (bf16[1040,128]{1,0:T(8,128)(2,1)}, bf16[1040,128]{1,0:T(8,128)(2,1)S(1)}, u32[]{:S(2)}) copy-start(bf16[1040,128]{1,0:T(8,128)(2,1)S(1)} %collective-permute-done.1) | copy-start | bytes 798724
  43.0 6.5 %copy-start.11 = (bf16[1040,128]{1,0:T(8,128)(2,1)}, bf16[1040,128]{1,0:T(8,128)(2,1)S(1)}, u32[]{:S(2)}) copy-start(bf16[1040,128]{1,0:T(8,128)(2,1)S(1)} %collective-permute-done) | copy-start | bytes 798724
  43.1 1.2 %copy-start.8 = (f32[16,128,128]{1,2,0:T(8,128)S(1)}, f32[16,128,128]{1,2,0:T(8,128)}, u32[]{:S(2)}) copy-start(f32[16,128,128]{1,2,0:T(8,128)} %fusion.105) | copy-start | bytes 3145732
  43.4 6.2 %copy-start.6 = (f32[16,64,128]{2,1,0:T(8,128)}, f32[16,64,128]{2,1,0:T(8,128)S(1)}, u32[]{:S(2)}) copy-start(f32[16,64,128]{2,1,0:T(8,128)S(1)} %fusion.27) | copy-start | bytes 1572868
  43.5 0.8 copy-start.15
  49.5 1.0 %slice-start = ((bf16[1040,128]{1,0:T(8,128)(2,1)}), bf16[1024,128]{1,0:T(8,128)(2,1)S(1)}, s32[]{:S(2)}) async-start(bf16[1040,128]{1,0:T(8,128)(2,1)} %copy-done.11), calls=%async_computation | async-start | bytes 524288 | tf_op jit(solution)/shard_map/slice | solution.py:38
  49.5 1.0 %slice-start.1 = ((bf16[1040,128]{1,0:T(8,128)(2,1)}), bf16[1024,128]{1,0:T(8,128)(2,1)S(1)}, s32[]{:S(2)}) async-start(bf16[1040,128]{1,0:T(8,128)(2,1)} %copy-done.12), calls=%async_computation.1 | async-start | bytes 524288 | tf_op jit(solution)/shard_map/slice | solution.py:38
  51.1 12.0 %collective-permute-start.8 = (bf16[1040,128]{1,0:T(8,128)(2,1)S(1)}, bf16[1040,128]{1,0:T(8,128)(2,1)S(1)}, u32[]{:S(2)}, u32[]{:S(2)}) collective-permute-start(bf16[1040,128]{1,0:T(8,128)(2,1)S(1)} %pad_maximum_fusion.2), channel_id=1, source_target_pairs={{12,0},{13,1},{14,2},{15,3},{28,16},{29,17},{30,18},{31,19}} | collective-permute-start | bytes 798728 | tf_op jit(solution)/shard_map/ppermute | solution.py:66
  51.8 12.1 %collective-permute-start.7 = (bf16[1040,128]{1,0:T(8,128)(2,1)S(1)}, bf16[1040,128]{1,0:T(8,128)(2,1)S(1)}, u32[]{:S(2)}, u32[]{:S(2)}) collective-permute-start(bf16[1040,128]{1,0:T(8,128)(2,1)S(1)} %pad_maximum_fusion.2), channel_id=1, source_target_pairs={{8,0},{12,4},{9,1},{13,5},{10,2},{14,6},{11,3},{15,7},{24,16},{28,... | collective-permute-start | bytes 798728 | tf_op jit(solution)/shard_map/ppermute | solution.py:66
  53.1 20.1 %collective-permute-start.6 = (bf16[1040,128]{1,0:T(8,128)(2,1)S(1)}, bf16[1040,128]{1,0:T(8,128)(2,1)S(1)}, u32[]{:S(2)}, u32[]{:S(2)}) collective-permute-start(bf16[1040,128]{1,0:T(8,128)(2,1)S(1)} %pad_maximum_fusion.2), channel_id=1, source_target_pairs={{4,0},{8,4},{12,8},{5,1},{9,5},{13,9},{6,2},{10,6},{14,10},{7,3},{... | collective-permute-start | bytes 798728 | tf_op jit(solution)/shard_map/ppermute | solution.py:66
  57.6 1.2 %copy-start.7 = (f32[16,64,128]{2,1,0:T(8,128)S(1)}, f32[16,64,128]{2,1,0:T(8,128)}, u32[]{:S(2)}) copy-start(f32[16,64,128]{2,1,0:T(8,128)} %copy-done.6) | copy-start | bytes 1572868
  58.8 1.1 %copy-start.3 = (f32[16,128,128]{2,1,0:T(8,128)}, f32[16,128,128]{2,1,0:T(8,128)S(1)}, u32[]{:S(2)}) copy-start(f32[16,128,128]{2,1,0:T(8,128)S(1)} %convolution_multiply_fusion) | copy-start | bytes 3145732
  58.8 1.4 %copy-start.5 = (f32[2,8,128,64]{2,3,1,0:T(8,128)S(1)}, f32[2,8,128,64]{2,3,1,0:T(8,128)}, u32[]{:S(2)}) copy-start(f32[2,8,128,64]{2,3,1,0:T(8,128)} %copy-done.4) | copy-start | bytes 1572868
  79.5 2.4 %copy-start.9 = (f32[16,128,64]{1,2,0:T(8,128)S(1)}, f32[16,128,64]{1,2,0:T(8,128)}, u32[]{:S(2)}) copy-start(f32[16,128,64]{1,2,0:T(8,128)} %convolution_add_fusion.3) | copy-start | bytes 1572868
  82.0 1.0 %copy-start.10 = (bf16[16,128,128]{1,2,0:T(8,128)(2,1)S(1)}, bf16[16,128,128]{1,2,0:T(8,128)(2,1)}, u32[]{:S(2)}) copy-start(bf16[16,128,128]{1,2,0:T(8,128)(2,1)} %get-tuple-element.31) | copy-start | bytes 1572868

commit v8 on v3

--- a/solution.py
+++ b/solution.py
@@ -192,7 +192,9 @@
 
     cross = jnp.einsum("htp,hsp->hts", grad_out, inputs_wide, precision=highest)
     paired = decayed * cross
-    local_din = jnp.einsum("hts,htn->hsn", paired, out_heads, precision=highest)
+    local_din = lax.optimization_barrier(
+        jnp.einsum("hts,htn->hsn", paired, out_heads, precision=highest)
+    )
     grad_output_maps = jnp.einsum("hts,hsn->htn", paired, in_heads, precision=highest)
     grad_output_maps = grad_output_maps + from_start[..., None] * jnp.einsum(
         "hnp,htp->htn", entering, grad_out, precision=highest

time: 82.4 us -> 83.7 us (1.016)
  waiting for transfers between devices: 22.1 us -> 19.5 us
  other arithmetic: 7.18 us -> 8.84 us
    ppermute x9, waiting for transfers between devices: 22.1 us -> 19.5 us  [shifted(): moved.append(lax.ppermute(x, 'seq', pairs))]
    add x1, other arithmetic: 0.3 us -> 1.33 us  [body(): entering = prefix_state + jnp.exp(gap)[:, None, None] * init_state]
    slice x7 -> x6, local copies, waits for them, and re-layouts: 1.04 us -> 1.93 us  [unpack_rows(): big = received[:big_rows].reshape(big_shape)]
    unnamed x40 -> x44, local copies, waits for them, and re-layouts: 4.04 us -> 3.94 us
  transfers between devices with their start and end apart: 9 -> 9, of which waited for: 5 -> 4; matrix products, arithmetic and copies ran while one was open for 28% -> 31% of each run, Pallas kernels for 0% -> 0%
where the time goes in v8:
time: 83.7 us; the launch traced here: 82.7 us
  matrix products  30.2 us (36%)
  waiting for transfers between devices  19.5 us (23%)
  starting transfers between devices  16.5 us (20%)
  other arithmetic  8.84 us (11%)
  local copies, waits for them, and re-layouts  6.36 us (8%)
  between operations  1.31 us (2%)
    ppermute x9, waiting for transfers between devices, shifted(): moved.append(lax.ppermute(x, 'seq', pairs))  19.5 us
    ppermute x9, starting transfers between devices, shifted(): moved.append(lax.ppermute(x, 'seq', pairs))  16.5 us
    dot_general x4, matrix products, teacher_rows(): jnp.einsum('gptd,gkd->gptk', grouped, block[..., :head_width], preferred_...  4.36 us
    dot_general x4, matrix products, teacher_rows(): jnp.einsum('gptk,gkd->gptd', exponentials.astype(jnp.bfloat16), block[......  4.06 us
    unnamed x44, local copies, waits for them, and re-layouts  3.94 us
    dot_general x1, matrix products, body(): jnp.einsum('hts,hsn->htn', paired, in_heads, precision=highest)  2.91 us
    dot_general x1, matrix products, body(): jnp.einsum('hsn,hnp->hsp', weighted_in, incoming, precision=highest)  2.85 us
    dot_general x1, matrix products, body(): jnp.einsum('hnp,hsp->hsn', incoming, inputs_wide, precision=highest)  2.46 us
  transfers between devices with their start and end apart: 9, of which 4 were waited for; matrix products, arithmetic and copies ran while one was open for 31% of the time, Pallas kernels for 0%

profile of v8, /device:TPU:8, one launch (start us, length us, event | category | flops | bytes accessed | tf_op | source)
XLA Modules:
  0.0 82.7 jit_solution(8732963379767344797)
XLA Ops:
  0.7 1.4 %collective-permute-start.5 = (bf16[2,128,256]{2,1,0:T(8,128)(2,1)}, bf16[2,128,256]{2,1,0:T(8,128)(2,1)}, u32[]{:S(2)}, u32[]{:S(2)}) collective-permute-start(bf16[2,128,256]{2,1,0:T(8,128)(2,1)} %param.8), channel_id=1, source_target_pairs={{0,12},{1,13},{2,14},{3,15},{16,28},{17,29},{18,30},{19,31}} | collective-permute-start | bytes 393224 | tf_op jit(solution)/shard_map/ppermute | solution.py:66
  2.1 3.5 %collective-permute-start.3 = (bf16[2,128,256]{2,1,0:T(8,128)(2,1)}, bf16[2,128,256]{2,1,0:T(8,128)(2,1)}, u32[]{:S(2)}, u32[]{:S(2)}) collective-permute-start(bf16[2,128,256]{2,1,0:T(8,128)(2,1)} %param.8), channel_id=1, source_target_pairs={{0,4},{4,8},{8,12},{1,5},{5,9},{9,13},{2,6},{6,10},{10,14},{3,7},{... | collective-permute-start | bytes 393224 | tf_op jit(solution)/shard_map/ppermute | solution.py:66
  5.6 2.9 %collective-permute-start.4 = (bf16[2,128,256]{2,1,0:T(8,128)(2,1)}, bf16[2,128,256]{2,1,0:T(8,128)(2,1)}, u32[]{:S(2)}, u32[]{:S(2)}) collective-permute-start(bf16[2,128,256]{2,1,0:T(8,128)(2,1)} %param.8), channel_id=1, source_target_pairs={{0,8},{4,12},{1,9},{5,13},{2,10},{6,14},{3,11},{7,15},{16,24},{20,... | collective-permute-start | bytes 393224 | tf_op jit(solution)/shard_map/ppermute | solution.py:66
  8.5 0.7 fusion.52
  10.1 0.5 convolution_convert_fusion
  10.6 0.7 pad_maximum_fusion.1
  11.4 2.0 %collective-permute-start.1 = (bf16[1040,128]{1,0:T(8,128)(2,1)}, bf16[1040,128]{1,0:T(8,128)(2,1)}, u32[]{:S(2)}, u32[]{:S(2)}) collective-permute-start(bf16[1040,128]{1,0:T(8,128)(2,1)} %pad_maximum_fusion.1), channel_id=1, source_target_pairs={{0,8},{4,12},{1,9},{5,13},{2,10},{6,14},{3,11},{7,15},{16,24},{20,... | collective-permute-start | bytes 798728 | tf_op jit(solution)/shard_map/ppermute | solution.py:66
  13.4 1.9 %collective-permute-start = (bf16[1040,128]{1,0:T(8,128)(2,1)}, bf16[1040,128]{1,0:T(8,128)(2,1)S(1)}, u32[]{:S(2)}, u32[]{:S(2)}) collective-permute-start(bf16[1040,128]{1,0:T(8,128)(2,1)} %pad_maximum_fusion.1), channel_id=1, source_target_pairs={{0,4},{4,8},{8,12},{1,5},{5,9},{9,13},{2,6},{6,10},{10,14},{3,7},{... | collective-permute-start | bytes 798728 | tf_op jit(solution)/shard_map/ppermute | solution.py:66
  15.6 0.4 bitcast_multiply_fusion.1
  16.0 2.3 %fusion.103 = f32[16,128,128]{1,2,0:T(8,128)} fusion(f32[16,128,128]{2,1,0:T(8,128)S(1)} %bitcast_multiply_fusion.1, bf16[16,128,128]{2,1,0:T(8,128)(2,1)S(1)} %copy-done.1), kind=kOutput, calls=%fused_computation.198 | convolution fusion | flops 402653184 | bytes 2621440 | tf_op jit(solution)/shard_map/hts,hsp->htp/dot_general | solution.py:161
  18.3 0.9 %fusion.101 = (f32[2,8,128]{2,1,0:T(8,128)}, f32[2,8,128,128]{2,3,1,0:T(8,128)S(1)}) fusion(bf16[2,8,128,128]{3,2,1,0:T(8,128)(2,1)S(1)} %bitcast.179, bf16[2,128,256]{2,1,0:T(8,128)(2,1)S(1)} %copy-done.15, pred[128,128]{0,1:T(8,128)(4,1)S(1)} %iota_compare_fusion), kind=kOutput, calls=%fused_computation.196 | convolution fusion | flops 67893248 | bytes 1662976 | tf_op jit(solution)/shard_map/gptd,gkd->gptk/dot_general | solution.py:87
  19.6 0.7 collective-permute-start.2
  20.3 1.1 %fusion.102 = (f32[2,8,128]{2,1,0:T(8,128)S(1)}, f32[2,8,128,128]{2,3,1,0:T(8,128)S(1)}) fusion(bf16[2,8,128,128]{3,2,1,0:T(8,128)(2,1)S(1)} %bitcast.180, bf16[2,128,256]{2,1,0:T(8,128)(2,1)} %collective-permute-done.3, pred[]{:T(512)S(6)} %ge.51), kind=kOutput, calls=%fused_computation.197 | convolution fusion | flops 67893248 | bytes 1646593 | tf_op jit(solution)/shard_map/gptd,gkd->gptk/dot_general | solution.py:87
  21.5 1.1 %fusion.99 = (f32[2,8,128]{2,1,0:T(8,128)S(1)}, f32[2,8,128,128]{2,3,1,0:T(8,128)S(1)}) fusion(bf16[2,8,128,128]{3,2,1,0:T(8,128)(2,1)S(1)} %bitcast.182, bf16[2,128,256]{2,1,0:T(8,128)(2,1)} %collective-permute-done.5, pred[]{:T(512)S(6)} %ge.53), kind=kOutput, calls=%fused_computation.194 | convolution fusion | flops 67893248 | bytes 1646593 | tf_op jit(solution)/shard_map/gptd,gkd->gptk/dot_general | solution.py:87
  22.6 0.8 %collective-permute-done.4 = bf16[2,128,256]{2,1,0:T(8,128)(2,1)} collective-permute-done((bf16[2,128,256]{2,1,0:T(8,128)(2,1)}, bf16[2,128,256]{2,1,0:T(8,128)(2,1)}, u32[]{:S(2)}, u32[]{:S(2)}) %collective-permute-start.4) | collective-permute-done | bytes 131104 | tf_op jit(solution)/shard_map/ppermute | solution.py:66
  23.5 1.2 %fusion.100 = (f32[2,8,128]{2,1,0:T(8,128)S(1)}, f32[2,8,128,128]{2,3,1,0:T(8,128)S(1)}) fusion(bf16[2,8,128,128]{3,2,1,0:T(8,128)(2,1)S(1)} %bitcast.181, bf16[2,128,256]{2,1,0:T(8,128)(2,1)} %collective-permute-done.4, pred[]{:T(512)S(6)} %ge.52), kind=kOutput, calls=%fused_computation.195 | convolution fusion | flops 67893248 | bytes 1646593 | tf_op jit(solution)/shard_map/gptd,gkd->gptk/dot_general | solution.py:87
  25.0 1.0 %fusion.17 = (f32[2,8,128]{2,1,0:T(8,128)S(1)}, f32[2,8,128]{2,1,0:T(8,128)S(1)}, f32[2,8,128]{2,1,0:T(8,128)S(1)}, f32[2,8,128]{2,1,0:T(8,128)S(1)}) fusion(f32[2,8,128,128]{2,3,1,0:T(8,128)S(1)} %get-tuple-element.49, f32[2,8,128]{2,1,0:T(8,128)S(1)} %maximum_maximum_fusion, f32[2,8,128,128]{2,3,1,0:T(8,128)S(1)} %get-tuple-element.47, ...), kind=kLoop, calls=%fused_computation.47 | loop fusion | flops 2088960 | bytes 4235264 | tf_op jit(solution)/shard_map/reduce_sum | solution.py:103
  26.0 1.2 %fusion.29 = f32[2,8,128,128]{2,3,1,0:T(8,128)S(1)} fusion(f32[2,8,128,128]{2,3,1,0:T(8,128)S(1)} %get-tuple-element.43, f32[2,8,128]{2,1,0:T(8,128)S(1)} %maximum_maximum_fusion, bf16[2,128,256]{2,1,0:T(8,128)(2,1)} %collective-permute-done.5), kind=kOutput, calls=%fused_computation.65 | convolution fusion | flops 67633152 | bytes 2170880 | tf_op jit(solution)/shard_map/gptk,gkd->gptd/dot_general | solution.py:104
  27.2 1.2 %convolution_add_fusion.2 = f32[2,8,128,128]{2,3,1,0:T(8,128)S(1)} fusion(f32[2,8,128,128]{2,3,1,0:T(8,128)S(1)} %fusion.33, f32[2,8,128,128]{2,3,1,0:T(8,128)S(1)} %get-tuple-element.49, f32[2,8,128]{2,1,0:T(8,128)S(1)} %maximum_maximum_fusion, bf16[2,128,256]{2,1,0:T(8,128)(2,1)} %collective-permute-done.3), kind=kOutput, calls=%fused_computation.8 | convolution fusion | flops 67895296 | bytes 3219456 | tf_op jit(solution)/shard_map/gptk,gkd->gptd/dot_general | solution.py:104
  28.4 1.4 %multiply_reduce_fusion.2 = (f32[2,8,128]{2,1,0:T(8,128)S(1)}, f32[2,8,128,128]{2,3,1,0:T(8,128)S(1)}) fusion(f32[2,8,128]{2,1,0:T(8,128)S(1)} %add_add_fusion, f32[2,8,128,128]{2,3,1,0:T(8,128)S(1)} %fusion.29, f32[2,8,128,128]{2,3,1,0:T(8,128)S(1)} %convolution_add_fusion.2, bf16[2,128,256]{2,1,0:T(8,128)(2,1)} %collective-permute-done.4, ...), kind=kOutput, calls=%fused_computation.38 | convolution fusion | flops 69466112 | bytes 4284416 | tf_op jit(solution)/shard_map/gptk,gkd->gptd/dot_general | solution.py:104
  29.8 5.1 %collective-permute-done.1 = bf16[1040,128]{1,0:T(8,128)(2,1)} collective-permute-done((bf16[1040,128]{1,0:T(8,128)(2,1)}, bf16[1040,128]{1,0:T(8,128)(2,1)}, u32[]{:S(2)}, u32[]{:S(2)}) %collective-permute-start.1) | collective-permute-done | bytes 266272 | tf_op jit(solution)/shard_map/ppermute | solution.py:66
  34.9 0.7 slice_convert_fusion.4
  35.6 4.3 %collective-permute-done = bf16[1040,128]{1,0:T(8,128)(2,1)S(1)} collective-permute-done((bf16[1040,128]{1,0:T(8,128)(2,1)}, bf16[1040,128]{1,0:T(8,128)(2,1)S(1)}, u32[]{:S(2)}, u32[]{:S(2)}) %collective-permute-start) | collective-permute-done | bytes 266272 | tf_op jit(solution)/shard_map/ppermute | solution.py:66
  40.0 1.3 %fusion.25 = f32[16,64,128]{2,1,0:T(8,128)S(1)} fusion(f32[16,64,128]{2,1,0:T(8,128)S(1)} %copy-done.14, f32[16]{0:T(128)S(1)} %fusion.90, f32[16]{0:T(128)S(1)} %get-tuple-element.24, f32[16]{0:T(128)S(1)} %get-tuple-element.38, f32[]{:T(128)S(6)} %select_n.163, bf16[1040,128]{1,0:T(8,128)(2,1)S(1)} %collective-permute-done.2, ...), kind=kLoop, calls=%fused_computation.61 | loop fusion | flops 1310720 | bytes 1835204 | tf_op jit(solution)/shard_map/add | solution.py:151
  41.4 0.7 copy-done.18
  42.1 2.0 %multiply_reduce_fusion.3 = (f32[16,128]{1,0:T(8,128)S(1)}, f32[16,128,128]{1,2,0:T(8,128)S(1)}) fusion(bf16[16,128,128]{1,2,0:T(8,128)(2,1)S(1)} %copy.48, f32[16]{0:T(128)S(1)} %copy-done.18, f32[16,128,128]{1,2,0:T(8,128)S(1)} %copy-done.8, f32[16,64,128]{2,1,0:T(8,128)S(1)} %fusion.25, f32[16,128,64]{1,2,0:T(8,128)S(1)} %bitcast.186, ...), kind=kOutput, calls=%fused_computation.43 | convolution fusion | flops 203159552 | bytes 3686464 | tf_op jit(solution)/shard_map/htn,hnp->htp/dot_general | solution.py:169
  44.1 0.4 multiply_reduce_fusion.1
  44.6 0.6 multiply_reduce_fusion
  45.2 2.1 %fusion.37 = f32[16,64,128]{2,1,0:T(8,128)S(1)} fusion(f32[16,128,128]{1,2,0:T(8,128)S(1)} %get-tuple-element.21, f32[16,128,64]{1,2,0:T(8,128)S(1)} %bitcast.187, f32[16,128]{1,0:T(8,128)S(1)} %get-tuple-element.31), kind=kOutput, calls=%fused_computation.73 | convolution fusion | flops 201457664 | bytes 2105344 | tf_op jit(solution)/shard_map/htn,htp->hnp/dot_general | solution.py:178
  47.3 1.0 %slice.242 = bf16[1024,128]{1,0:T(8,128)(2,1)S(1)} slice(bf16[1040,128]{1,0:T(8,128)(2,1)} %collective-permute-done.1), slice={[0:1024], [0:128]} | slice | bytes 524288 | tf_op jit(solution)/shard_map/slice | solution.py:38
  48.3 0.9 %slice-done = bf16[1024,128]{1,0:T(8,128)(2,1)S(1)} async-done(((bf16[1040,128]{1,0:T(8,128)(2,1)}), bf16[1024,128]{1,0:T(8,128)(2,1)S(1)}, s32[]{:S(2)}) %slice-start) | async-done | bytes 262168 | tf_op jit(solution)/shard_map/slice | solution.py:38
  49.3 0.4 multiply_reduce_fusion.4
  49.9 0.7 collective-permute-start.8
  50.5 1.5 %collective-permute-start.7 = (bf16[1040,128]{1,0:T(8,128)(2,1)S(1)}, bf16[1040,128]{1,0:T(8,128)(2,1)S(1)}, u32[]{:S(2)}, u32[]{:S(2)}) collective-permute-start(bf16[1040,128]{1,0:T(8,128)(2,1)S(1)} %pad_maximum_fusion.2), channel_id=1, source_target_pairs={{8,0},{12,4},{9,1},{13,5},{10,2},{14,6},{11,3},{15,7},{24,16},{28,... | collective-permute-start | bytes 798728 | tf_op jit(solution)/shard_map/ppermute | solution.py:66
  52.0 1.9 %collective-permute-start.6 = (bf16[1040,128]{1,0:T(8,128)(2,1)S(1)}, bf16[1040,128]{1,0:T(8,128)(2,1)S(1)}, u32[]{:S(2)}, u32[]{:S(2)}) collective-permute-start(bf16[1040,128]{1,0:T(8,128)(2,1)S(1)} %pad_maximum_fusion.2), channel_id=1, source_target_pairs={{4,0},{8,4},{12,8},{5,1},{9,5},{13,9},{6,2},{10,6},{14,10},{7,3},{... | collective-permute-start | bytes 798728 | tf_op jit(solution)/shard_map/ppermute | solution.py:66
  54.0 2.3 %fusion.104 = f32[16,128,128]{1,2,0:T(8,128)S(1)} fusion(f32[16,128,128]{2,1,0:T(8,128)} %copy-done.2, f32[16,128,128]{1,2,0:T(8,128)S(1)} %get-tuple-element.21), kind=kOutput, calls=%fused_computation.199 | convolution fusion | flops 402653184 | bytes 3145728 | tf_op jit(solution)/shard_map/hts,htp->hsp/dot_general | solution.py:191
  56.3 1.2 %convolution_multiply_fusion = f32[16,128,128]{2,1,0:T(8,128)S(1)} fusion(f32[16,128,128]{1,2,0:T(8,128)S(1)} %get-tuple-element.21, bf16[16,128,128]{2,1,0:T(8,128)(2,1)S(1)} %copy-done.1, f32[16,128]{1,0:T(8,128)S(1)} %reduce_window_sum.21, pred[128,128]{1,0:T(8,128)(4,1)S(1)} %copy.44), kind=kOutput, calls=%fused_computation | convolution fusion | flops 403701760 | bytes 2646016 | tf_op jit(solution)/shard_map/htp,hsp->hts/dot_general | solution.py:193
  57.5 1.0 %convolution_multiply_fusion.6 = f32[16,128,64]{1,2,0:T(8,128)S(1)} fusion(f32[16,128,128]{1,2,0:T(8,128)S(1)} %get-tuple-element.21, f32[16,64,128]{2,1,0:T(8,128)S(1)} %copy-done.4, f32[16,128]{1,0:T(8,128)S(1)} %get-tuple-element.31), kind=kOutput, calls=%fused_computation.21 | convolution fusion | flops 201457664 | bytes 2105344 | tf_op jit(solution)/shard_map/hnp,htp->htn/dot_general | solution.py:199
  58.6 2.9 %convolution_add_fusion.3 = f32[16,128,64]{1,2,0:T(8,128)} fusion(f32[16,128,64]{1,2,0:T(8,128)S(1)} %convolution_multiply_fusion.6, f32[16,128,128]{2,1,0:T(8,128)S(1)} %convolution_multiply_fusion, f32[16,128,64]{1,2,0:T(8,128)S(1)} %bitcast.184), kind=kOutput, calls=%fused_computation.22 | convolution fusion | flops 201457664 | bytes 2621440 | tf_op jit(solution)/shard_map/hts,hsn->htn/dot_general | solution.py:198
  61.5 1.8 %fusion.105 = f32[16,128,64]{1,2,0:T(8,128)} fusion(f32[16,128,128]{2,1,0:T(8,128)S(1)} %convolution_multiply_fusion, f32[16,128,64]{1,2,0:T(8,128)S(1)} %bitcast.188), kind=kOutput, calls=%fused_computation.200 | convolution fusion | flops 201326592 | bytes 2097152 | tf_op jit(solution)/shard_map/hts,htn->hsn/dot_general | solution.py:196
  63.4 9.2 %collective-permute-done.6 = bf16[1040,128]{1,0:T(8,128)(2,1)S(1)} collective-permute-done((bf16[1040,128]{1,0:T(8,128)(2,1)S(1)}, bf16[1040,128]{1,0:T(8,128)(2,1)S(1)}, u32[]{:S(2)}, u32[]{:S(2)}) %collective-permute-start.6) | collective-permute-done | bytes 266272 | tf_op jit(solution)/shard_map/ppermute | solution.py:66
  72.8 0.6 copy-done.9
  73.4 2.9 %fusion.13 = (f32[16,128]{1,0:T(8,128)S(1)}, bf16[16,128,128]{1,2,0:T(8,128)(2,1)}) fusion(bf16[16,128,128]{1,2,0:T(8,128)(2,1)S(1)} %copy.48, f32[16,128,128]{1,2,0:T(8,128)S(1)} %get-tuple-element.21, f32[16]{0:T(128)S(1)} %copy-done.18, f32[16,128,128]{1,2,0:T(8,128)S(1)} %fusion.104, bf16[16,64,128]{2,1,0:T(8,128)(2,1)S(1)} %bitcast.193, ...), kind=kOutput, calls=%fused_computation.28 | convolution fusion | flops 204077056 | bytes 4735168 | tf_op jit(solution)/shard_map/hsn,hnp->hsp/dot_general | solution.py:225
  76.2 1.2 %reduce_window_sum.22 = f32[16,128]{1,0:T(8,128)S(1)} reduce-window(f32[16,128]{1,0:T(8,128)S(1)} %sub.114, f32[]{:T(128)} %constant.12.clone.1), window={size=1x128 pad=0_0x0_127}, to_apply=%region_19.20 | reduce-window | flops 260096 | bytes 16388 | tf_op jit(solution)/shard_map/body/reduce_window_sum | solution.py:227
  77.5 2.5 %fusion.11 = f32[16,128,64]{1,2,0:T(8,128)S(1)} fusion(f32[16,128,64]{1,2,0:T(8,128)} %fusion.105, bf16[16,128,128]{2,1,0:T(8,128)(2,1)S(1)} %copy-done.1, f32[16,128]{1,0:T(8,128)S(1)} %get-tuple-element.32, bf16[16,64,128]{2,1,0:T(8,128)(2,1)} %bitcast.194, f32[16,64,128]{2,1,0:T(8,128)} %bitcast.190, bf16[16,64,128]{2,1,0:T(8,128)(2,1)S(1)} %bitcast.192, ...), kind=kOutput, calls=%fused_computation.25 | convolution fusion | flops 202375168 | bytes 2629760 | tf_op jit(solution)/shard_map/hnp,hsp->hsn/dot_general | solution.py:230
  80.0 0.7 copy.61
  81.0 1.0 %copy.60 = bf16[16,128,128]{2,1,0:T(8,128)(2,1)} copy(bf16[16,128,128]{1,2,0:T(8,128)(2,1)S(1)} %copy-done.11) | data formatting | bytes 1048576
  82.0 0.7 broadcast_add_fusion
  (88 shorter events, 2.8 us)
Async XLA Ops:
  0.6 17.7 %copy-start = (bf16[16,128,128]{2,1,0:T(8,128)(2,1)S(1)}, bf16[16,128,128]{2,1,0:T(8,128)(2,1)}, u32[]{:S(2)}) copy-start(bf16[16,128,128]{2,1,0:T(8,128)(2,1)} %param.7) | copy-start | bytes 1572868
  0.6 9.2 %copy-start.13 = (bf16[2,128,128]{2,1,0:T(8,128)(2,1)S(1)}, bf16[2,128,128]{2,1,0:T(8,128)(2,1)}, u32[]{:S(2)}) copy-start(bf16[2,128,128]{2,1,0:T(8,128)(2,1)} %param.10) | copy-start | bytes 196612
  0.7 9.4 %copy-start.1 = (bf16[16,128,128]{2,1,0:T(8,128)(2,1)S(1)}, bf16[16,128,128]{2,1,0:T(8,128)(2,1)}, u32[]{:S(2)}) copy-start(bf16[16,128,128]{2,1,0:T(8,128)(2,1)} %param.9) | copy-start | bytes 1572868
  0.7 20.8 %collective-permute-start.5 = (bf16[2,128,256]{2,1,0:T(8,128)(2,1)}, bf16[2,128,256]{2,1,0:T(8,128)(2,1)}, u32[]{:S(2)}, u32[]{:S(2)}) collective-permute-start(bf16[2,128,256]{2,1,0:T(8,128)(2,1)} %param.8), channel_id=1, source_target_pairs={{0,12},{1,13},{2,14},{3,15},{16,28},{17,29},{18,30},{19,31}} | collective-permute-start | bytes 393224 | tf_op jit(solution)/shard_map/ppermute | solution.py:66
  2.1 17.5 %collective-permute-start.3 = (bf16[2,128,256]{2,1,0:T(8,128)(2,1)}, bf16[2,128,256]{2,1,0:T(8,128)(2,1)}, u32[]{:S(2)}, u32[]{:S(2)}) collective-permute-start(bf16[2,128,256]{2,1,0:T(8,128)(2,1)} %param.8), channel_id=1, source_target_pairs={{0,4},{4,8},{8,12},{1,5},{5,9},{9,13},{2,6},{6,10},{10,14},{3,7},{... | collective-permute-start | bytes 393224 | tf_op jit(solution)/shard_map/ppermute | solution.py:66
  5.6 17.9 %collective-permute-start.4 = (bf16[2,128,256]{2,1,0:T(8,128)(2,1)}, bf16[2,128,256]{2,1,0:T(8,128)(2,1)}, u32[]{:S(2)}, u32[]{:S(2)}) collective-permute-start(bf16[2,128,256]{2,1,0:T(8,128)(2,1)} %param.8), channel_id=1, source_target_pairs={{0,8},{4,12},{1,9},{5,13},{2,10},{6,14},{3,11},{7,15},{16,24},{20,... | collective-permute-start | bytes 393224 | tf_op jit(solution)/shard_map/ppermute | solution.py:66
  11.4 23.5 %collective-permute-start.1 = (bf16[1040,128]{1,0:T(8,128)(2,1)}, bf16[1040,128]{1,0:T(8,128)(2,1)}, u32[]{:S(2)}, u32[]{:S(2)}) collective-permute-start(bf16[1040,128]{1,0:T(8,128)(2,1)} %pad_maximum_fusion.1), channel_id=1, source_target_pairs={{0,8},{4,12},{1,9},{5,13},{2,10},{6,14},{3,11},{7,15},{16,24},{20,... | collective-permute-start | bytes 798728 | tf_op jit(solution)/shard_map/ppermute | solution.py:66
  13.4 26.5 %collective-permute-start = (bf16[1040,128]{1,0:T(8,128)(2,1)}, bf16[1040,128]{1,0:T(8,128)(2,1)S(1)}, u32[]{:S(2)}, u32[]{:S(2)}) collective-permute-start(bf16[1040,128]{1,0:T(8,128)(2,1)} %pad_maximum_fusion.1), channel_id=1, source_target_pairs={{0,4},{4,8},{8,12},{1,5},{5,9},{9,13},{2,6},{6,10},{10,14},{3,7},{... | collective-permute-start | bytes 798728 | tf_op jit(solution)/shard_map/ppermute | solution.py:66
  16.0 2.3 %copy-start.2 = (f32[16,128,128]{2,1,0:T(8,128)}, f32[16,128,128]{2,1,0:T(8,128)S(1)}, u32[]{:S(2)}) copy-start(f32[16,128,128]{2,1,0:T(8,128)S(1)} %bitcast_multiply_fusion.1) | copy-start | bytes 3145732
  16.0 2.3 %copy-start.15 = (bf16[2,128,256]{2,1,0:T(8,128)(2,1)S(1)}, bf16[2,128,256]{2,1,0:T(8,128)(2,1)}, u32[]{:S(2)}) copy-start(bf16[2,128,256]{2,1,0:T(8,128)(2,1)} %param.8) | copy-start | bytes 393220
  19.6 20.3 %collective-permute-start.2 = (bf16[1040,128]{1,0:T(8,128)(2,1)}, bf16[1040,128]{1,0:T(8,128)(2,1)S(1)}, u32[]{:S(2)}, u32[]{:S(2)}) collective-permute-start(bf16[1040,128]{1,0:T(8,128)(2,1)} %pad_maximum_fusion.1), channel_id=1, source_target_pairs={{0,12},{1,13},{2,14},{3,15},{16,28},{17,29},{18,30},{19,31}} | collective-permute-start | bytes 798728 | tf_op jit(solution)/shard_map/ppermute | solution.py:66
  22.6 2.1 %copy-start.16 = (bf16[2,128,256]{2,1,0:T(8,128)(2,1)S(1)}, bf16[2,128,256]{2,1,0:T(8,128)(2,1)}, u32[]{:S(2)}) copy-start(bf16[2,128,256]{2,1,0:T(8,128)(2,1)} %param.8) | copy-start | bytes 393220
  23.5 1.2 %copy-start.17 = (f32[2,8,128]{2,1,0:T(8,128)S(1)}, f32[2,8,128]{2,1,0:T(8,128)}, u32[]{:S(2)}) copy-start(f32[2,8,128]{2,1,0:T(8,128)} %get-tuple-element.46) | copy-start | bytes 24580
  28.4 11.6 %copy-start.14 = (f32[16,64,128]{2,1,0:T(8,128)S(1)}, f32[16,64,128]{2,1,0:T(8,128)}, u32[]{:S(2)}) copy-start(f32[16,64,128]{2,1,0:T(8,128)} %param.13) | copy-start | bytes 1572868
  39.9 7.4 %copy-start.12 = (bf16[1040,128]{1,0:T(8,128)(2,1)}, bf16[1040,128]{1,0:T(8,128)(2,1)S(1)}, u32[]{:S(2)}) copy-start(bf16[1040,128]{1,0:T(8,128)(2,1)S(1)} %collective-permute-done) | copy-start | bytes 798724
  40.0 1.4 %copy-start.8 = (f32[16,128,128]{1,2,0:T(8,128)S(1)}, f32[16,128,128]{1,2,0:T(8,128)}, u32[]{:S(2)}) copy-start(f32[16,128,128]{1,2,0:T(8,128)} %fusion.103) | copy-start | bytes 3145732
  41.3 7.0 %copy-start.3 = (f32[16,64,128]{2,1,0:T(8,128)}, f32[16,64,128]{2,1,0:T(8,128)S(1)}, u32[]{:S(2)}) copy-start(f32[16,64,128]{2,1,0:T(8,128)S(1)} %fusion.25) | copy-start | bytes 1572868
  41.4 3.8 %copy-start.5 = (f32[2,8,128,64]{2,3,1,0:T(8,128)}, f32[2,8,128,64]{2,3,1,0:T(8,128)S(1)}, u32[]{:S(2)}) copy-start(f32[2,8,128,64]{2,3,1,0:T(8,128)S(1)} %broadcast_in_dim.100) | copy-start | bytes 1572868
  41.4 0.7 copy-start.18
  48.3 1.0 %slice-start = ((bf16[1040,128]{1,0:T(8,128)(2,1)}), bf16[1024,128]{1,0:T(8,128)(2,1)S(1)}, s32[]{:S(2)}) async-start(bf16[1040,128]{1,0:T(8,128)(2,1)} %copy-done.12), calls=%async_computation | async-start | bytes 524288 | tf_op jit(solution)/shard_map/slice | solution.py:38
  49.9 13.5 %collective-permute-start.8 = (bf16[1040,128]{1,0:T(8,128)(2,1)S(1)}, bf16[1040,128]{1,0:T(8,128)(2,1)S(1)}, u32[]{:S(2)}, u32[]{:S(2)}) collective-permute-start(bf16[1040,128]{1,0:T(8,128)(2,1)S(1)} %pad_maximum_fusion.2), channel_id=1, source_target_pairs={{12,0},{13,1},{14,2},{15,3},{28,16},{29,17},{30,18},{31,19}} | collective-permute-start | bytes 798728 | tf_op jit(solution)/shard_map/ppermute | solution.py:66
  50.5 12.8 %collective-permute-start.7 = (bf16[1040,128]{1,0:T(8,128)(2,1)S(1)}, bf16[1040,128]{1,0:T(8,128)(2,1)S(1)}, u32[]{:S(2)}, u32[]{:S(2)}) collective-permute-start(bf16[1040,128]{1,0:T(8,128)(2,1)S(1)} %pad_maximum_fusion.2), channel_id=1, source_target_pairs={{8,0},{12,4},{9,1},{13,5},{10,2},{14,6},{11,3},{15,7},{24,16},{28,... | collective-permute-start | bytes 798728 | tf_op jit(solution)/shard_map/ppermute | solution.py:66
  52.0 20.5 %collective-permute-start.6 = (bf16[1040,128]{1,0:T(8,128)(2,1)S(1)}, bf16[1040,128]{1,0:T(8,128)(2,1)S(1)}, u32[]{:S(2)}, u32[]{:S(2)}) collective-permute-start(bf16[1040,128]{1,0:T(8,128)(2,1)S(1)} %pad_maximum_fusion.2), channel_id=1, source_target_pairs={{4,0},{8,4},{12,8},{5,1},{9,5},{13,9},{6,2},{10,6},{14,10},{7,3},{... | collective-permute-start | bytes 798728 | tf_op jit(solution)/shard_map/ppermute | solution.py:66
  56.3 1.2 %copy-start.4 = (f32[16,64,128]{2,1,0:T(8,128)S(1)}, f32[16,64,128]{2,1,0:T(8,128)}, u32[]{:S(2)}) copy-start(f32[16,64,128]{2,1,0:T(8,128)} %copy-done.3) | copy-start | bytes 1572868
  58.6 2.9 %copy-start.6 = (f32[2,8,128,64]{2,3,1,0:T(8,128)S(1)}, f32[2,8,128,64]{2,3,1,0:T(8,128)}, u32[]{:S(2)}) copy-start(f32[2,8,128,64]{2,3,1,0:T(8,128)} %copy-done.5) | copy-start | bytes 1572868
  72.7 0.7 copy-start.9
  72.7 3.5 %copy-start.7 = (f32[1024,128]{1,0:T(8,128)}, f32[1024,128]{1,0:T(8,128)S(1)}, u32[]{:S(2)}) copy-start(f32[1024,128]{1,0:T(8,128)S(1)} %convert_multiply_fusion.10) | copy-start | bytes 1572868
  77.5 2.5 %copy-start.10 = (f32[16,128,64]{1,2,0:T(8,128)S(1)}, f32[16,128,64]{1,2,0:T(8,128)}, u32[]{:S(2)}) copy-start(f32[16,128,64]{1,2,0:T(8,128)} %convolution_add_fusion.3) | copy-start | bytes 1572868
  80.0 1.0 %copy-start.11 = (bf16[16,128,128]{1,2,0:T(8,128)(2,1)S(1)}, bf16[16,128,128]{1,2,0:T(8,128)(2,1)}, u32[]{:S(2)}) copy-start(bf16[16,128,128]{1,2,0:T(8,128)(2,1)} %get-tuple-element.27) | copy-start | bytes 1572868

commit v9 on v3

--- a/solution.py
+++ b/solution.py
@@ -1,6 +1,7 @@
 import jax
 import jax.numpy as jnp
 from jax import lax
+from jax.experimental.layout import Layout, with_layout_constraint
 from jax.sharding import PartitionSpec as P
 
 epsilon = 1e-05
@@ -230,7 +231,9 @@
     grad_maps = jnp.concatenate([grad_input_maps, grad_output_maps], axis=2)
     grad_maps = grad_maps.reshape(local_groups, per_group, tok_dev, 2 * state_size).sum(axis=1)
     grad_x = state_dx + skip_gain[:, None, None] * grad_out
-    return (grad_x.astype(jnp.bfloat16), grad_maps.astype(jnp.bfloat16), grad_log_decay)
+    grad_x = with_layout_constraint(grad_x.astype(jnp.bfloat16), Layout((0, 1, 2)))
+    grad_maps = with_layout_constraint(grad_maps.astype(jnp.bfloat16), Layout((0, 1, 2)))
+    return (grad_x, grad_maps, grad_log_decay)
 
 
 def solution(mesh):

time: 82.4 us -> 85.2 us (1.034)
  other arithmetic: 7.18 us -> 12.4 us
  matrix products: 29.7 us -> 25.8 us
    unnamed x40 -> x33, local copies, waits for them, and re-layouts: 4.04 us -> 1.27 us
    reduce_sum x1, other arithmetic: 0.58 us -> 2.4 us  [body(): forward_term = jnp.sum(grad_out * state_out, axis=2)]
    dot_general x4, matrix products: 4.06 us -> 2.47 us  [teacher_rows(): jnp.einsum('gptk,gkd->gptd', exponentials.astype(jnp.bfloat16), block[......]
    convert_element_type x0 -> x1, local copies, waits for them, and re-layouts: none -> 1.56 us  [body(): teacher_wide = teacher.astype(jnp.float32)]
    dot_general x4, matrix products: 3.75 us -> 2.26 us  [teacher_rows(): jnp.einsum('gptd,gkd->gptk', grouped, block[..., :head_width], preferred_...]
    convert_element_type x6, other arithmetic: 0.02 us -> 1.38 us  [join_three(): wide = parts.astype(jnp.float32)]
    add x1, other arithmetic: 0.3 us -> 1.56 us  [body(): entering = prefix_state + jnp.exp(gap)[:, None, None] * init_state]
    dot_general x1, matrix products: 1.04 us -> 2.13 us  [body(): jnp.einsum('hnp,htp->htn', entering, grad_out, precision=highest)]
  transfers between devices with their start and end apart: 9 -> 9, of which waited for: 5 -> 5; matrix products, arithmetic and copies ran while one was open for 28% -> 25% of each run, Pallas kernels for 0% -> 0%
where the time goes in v9:
time: 85.2 us; the launch traced here: 84.4 us
  matrix products  25.8 us (30%)
  waiting for transfers between devices  22.4 us (26%)
  starting transfers between devices  16.6 us (19%)
  other arithmetic  12.4 us (15%)
  local copies, waits for them, and re-layouts  6.07 us (7%)
  between operations  1.23 us (1%)
    ppermute x9, waiting for transfers between devices, shifted(): moved.append(lax.ppermute(x, 'seq', pairs))  22.4 us
    ppermute x9, starting transfers between devices, shifted(): moved.append(lax.ppermute(x, 'seq', pairs))  16.6 us
    dot_general x1, matrix products, body(): jnp.einsum('hts,hsn->htn', paired, in_heads, precision=highest)  2.92 us
    dot_general x1, matrix products, body(): jnp.einsum('hsn,hnp->hsp', weighted_in, incoming, precision=highest)  2.82 us
    dot_general x4, matrix products, teacher_rows(): jnp.einsum('gptk,gkd->gptd', exponentials.astype(jnp.bfloat16), block[......  2.47 us
    dot_general x1, matrix products, body(): jnp.einsum('htn,hnp->htp', out_heads, entering, precision=highest)  2.46 us
    reduce_sum x1, other arithmetic, body(): forward_term = jnp.sum(grad_out * state_out, axis=2)  2.4 us
    dot_general x1, matrix products, body(): local_din = jnp.einsum('hts,htn->hsn', paired, out_heads, precision=highest)  2.28 us
  transfers between devices with their start and end apart: 9, of which 5 were waited for; matrix products, arithmetic and copies ran while one was open for 25% of the time, Pallas kernels for 0%

profile of v9, /device:TPU:8, one launch (start us, length us, event | category | flops | bytes accessed | tf_op | source)
XLA Modules:
  0.0 84.4 jit_solution(13987088383468045618)
XLA Ops:
  0.7 0.8 collective-permute-start.5
  1.5 3.5 %collective-permute-start.3 = (bf16[2,128,256]{2,1,0:T(8,128)(2,1)}, bf16[2,128,256]{2,1,0:T(8,128)(2,1)S(1)}, u32[]{:S(2)}, u32[]{:S(2)}) collective-permute-start(bf16[2,128,256]{2,1,0:T(8,128)(2,1)} %param.8), channel_id=1, source_target_pairs={{0,4},{4,8},{8,12},{1,5},{5,9},{9,13},{2,6},{6,10},{10,14},{3,7},{... | collective-permute-start | bytes 393224 | tf_op jit(solution)/shard_map/ppermute | solution.py:67
  5.0 2.9 %collective-permute-start.4 = (bf16[2,128,256]{2,1,0:T(8,128)(2,1)}, bf16[2,128,256]{2,1,0:T(8,128)(2,1)S(1)}, u32[]{:S(2)}, u32[]{:S(2)}) collective-permute-start(bf16[2,128,256]{2,1,0:T(8,128)(2,1)} %param.8), channel_id=1, source_target_pairs={{0,8},{4,12},{1,9},{5,13},{2,10},{6,14},{3,11},{7,15},{16,24},{20,... | collective-permute-start | bytes 393224 | tf_op jit(solution)/shard_map/ppermute | solution.py:67
  7.9 0.7 fusion.51
  9.5 0.5 convolution_convert_fusion
  10.3 0.8 pad_maximum_fusion.1
  11.0 2.0 %collective-permute-start.1 = (bf16[1040,128]{1,0:T(8,128)(2,1)}, bf16[1040,128]{1,0:T(8,128)(2,1)}, u32[]{:S(2)}, u32[]{:S(2)}) collective-permute-start(bf16[1040,128]{1,0:T(8,128)(2,1)} %pad_maximum_fusion.1), channel_id=1, source_target_pairs={{0,8},{4,12},{1,9},{5,13},{2,10},{6,14},{3,11},{7,15},{16,24},{20,... | collective-permute-start | bytes 798728 | tf_op jit(solution)/shard_map/ppermute | solution.py:67
  13.0 1.9 %collective-permute-start = (bf16[1040,128]{1,0:T(8,128)(2,1)}, bf16[1040,128]{1,0:T(8,128)(2,1)S(1)}, u32[]{:S(2)}, u32[]{:S(2)}) collective-permute-start(bf16[1040,128]{1,0:T(8,128)(2,1)} %pad_maximum_fusion.1), channel_id=1, source_target_pairs={{0,4},{4,8},{8,12},{1,5},{5,9},{9,13},{2,6},{6,10},{10,14},{3,7},{... | collective-permute-start | bytes 798728 | tf_op jit(solution)/shard_map/ppermute | solution.py:67
  15.3 0.4 bitcast_multiply_fusion.1
  15.7 1.6 %fusion.102 = f32[16,128,128]{2,1,0:T(8,128)} fusion(f32[16,128,128]{2,1,0:T(8,128)S(1)} %bitcast_multiply_fusion.1, bf16[16,128,128]{2,1,0:T(8,128)(2,1)S(1)} %copy-done.1), kind=kOutput, calls=%fused_computation.198 | convolution fusion | flops 402653184 | bytes 2621440 | tf_op jit(solution)/shard_map/hts,hsp->htp/dot_general | solution.py:162
  17.3 1.3 %fusion.100 = (f32[2,8,128]{2,1,0:T(8,128)S(1)}, f32[2,8,128,128]{2,3,1,0:T(8,128)}) fusion(bf16[2,8,128,128]{3,2,1,0:T(8,128)(2,1)S(1)} %bitcast.177, bf16[2,128,256]{2,1,0:T(8,128)(2,1)S(1)} %copy-done.13, pred[128,128]{0,1:T(8,128)(4,1)S(1)} %iota_compare_fusion), kind=kOutput, calls=%fused_computation.196 | convolution fusion | flops 67893248 | bytes 1662976 | tf_op jit(solution)/shard_map/gptd,gkd->gptk/dot_general | solution.py:88
  18.8 1.4 %collective-permute-start.2 = (bf16[1040,128]{1,0:T(8,128)(2,1)}, bf16[1040,128]{1,0:T(8,128)(2,1)}, u32[]{:S(2)}, u32[]{:S(2)}) collective-permute-start(bf16[1040,128]{1,0:T(8,128)(2,1)} %pad_maximum_fusion.1), channel_id=1, source_target_pairs={{0,12},{1,13},{2,14},{3,15},{16,28},{17,29},{18,30},{19,31}} | collective-permute-start | bytes 798728 | tf_op jit(solution)/shard_map/ppermute | solution.py:67
  20.5 0.3 fusion.98
  20.8 2.5 %collective-permute-done.4 = bf16[2,128,256]{2,1,0:T(8,128)(2,1)S(1)} collective-permute-done((bf16[2,128,256]{2,1,0:T(8,128)(2,1)}, bf16[2,128,256]{2,1,0:T(8,128)(2,1)S(1)}, u32[]{:S(2)}, u32[]{:S(2)}) %collective-permute-start.4) | collective-permute-done | bytes 131104 | tf_op jit(solution)/shard_map/ppermute | solution.py:67
  23.6 0.3 fusion.32
  24.0 1.0 %fusion.16 = (f32[2,8,128]{2,1,0:T(8,128)S(1)}, f32[2,8,128]{2,1,0:T(8,128)S(1)}, f32[2,8,128]{2,1,0:T(8,128)S(1)}, f32[2,8,128]{2,1,0:T(8,128)S(1)}) fusion(f32[2,8,128,128]{2,3,1,0:T(8,128)S(1)} %get-tuple-element.40, f32[2,8,128]{2,1,0:T(8,128)S(1)} %maximum_maximum_fusion, f32[2,8,128,128]{2,3,1,0:T(8,128)S(1)} %copy-done.2, ...), kind=kLoop, calls=%fused_computation.47 | loop fusion | flops 2088960 | bytes 4235264 | tf_op jit(solution)/shard_map/reduce_sum | solution.py:104
  25.0 0.3 fusion.28
  25.3 0.3 convolution_add_fusion.2
  25.7 1.5 %multiply_reduce_fusion.2 = (f32[2,8,128]{2,1,0:T(8,128)S(1)}, f32[2,8,128,128]{2,3,1,0:T(8,128)}) fusion(f32[2,8,128]{2,1,0:T(8,128)S(1)} %add_add_fusion, f32[2,8,128,128]{2,3,1,0:T(8,128)S(1)} %fusion.28, f32[2,8,128,128]{2,3,1,0:T(8,128)S(1)} %convolution_add_fusion.2, bf16[2,128,256]{2,1,0:T(8,128)(2,1)S(1)} %collective-permute-done.4, ...), kind=kOutput, calls=%fused_computation.38 | convolution fusion | flops 69466112 | bytes 4284416 | tf_op jit(solution)/shard_map/gptk,gkd->gptd/dot_general | solution.py:105
  27.1 1.6 %copy.60 = f32[2,8,128,128]{3,2,1,0:T(8,128)S(1)} copy(f32[2,8,128,128]{2,3,1,0:T(8,128)} %get-tuple-element.42) | data formatting | bytes 2097152 | tf_op jit(solution)/shard_map/convert_element_type | solution.py:165
  28.7 6.0 %collective-permute-done.1 = bf16[1040,128]{1,0:T(8,128)(2,1)} collective-permute-done((bf16[1040,128]{1,0:T(8,128)(2,1)}, bf16[1040,128]{1,0:T(8,128)(2,1)}, u32[]{:S(2)}, u32[]{:S(2)}) %collective-permute-start.1) | collective-permute-done | bytes 266272 | tf_op jit(solution)/shard_map/ppermute | solution.py:67
  34.7 0.7 slice_convert_fusion.4
  35.4 3.9 %collective-permute-done = bf16[1040,128]{1,0:T(8,128)(2,1)S(1)} collective-permute-done((bf16[1040,128]{1,0:T(8,128)(2,1)}, bf16[1040,128]{1,0:T(8,128)(2,1)S(1)}, u32[]{:S(2)}, u32[]{:S(2)}) %collective-permute-start) | collective-permute-done | bytes 266272 | tf_op jit(solution)/shard_map/ppermute | solution.py:67
  39.3 0.7 slice_convert_fusion.3
  40.0 1.6 %fusion.24 = f32[16,64,128]{2,1,0:T(8,128)S(1)} fusion(f32[16,64,128]{2,1,0:T(8,128)} %param.13, f32[16]{0:T(128)S(1)} %fusion.89, f32[16]{0:T(128)S(1)} %get-tuple-element.15, f32[16]{0:T(128)S(1)} %get-tuple-element.29, f32[]{:T(128)S(6)} %select_n.163, bf16[1040,128]{1,0:T(8,128)(2,1)} %collective-permute-done.2, ...), kind=kLoop, calls=%fused_computation.61 | loop fusion | flops 1310720 | bytes 1835204 | tf_op jit(solution)/shard_map/add | solution.py:152
  41.7 0.7 copy-done.14
  42.4 2.5 %multiply_reduce_fusion.3 = (f32[16,128]{1,0:T(8,128)S(1)}, f32[16,128,128]{2,1,0:T(8,128)S(1)}) fusion(bf16[16,128,128]{2,1,0:T(8,128)(2,1)S(1)} %copy-done.1, f32[16]{0:T(128)S(1)} %copy-done.14, f32[16,128,128]{2,1,0:T(8,128)S(1)} %copy-done.9, f32[16,64,128]{2,1,0:T(8,128)S(1)} %fusion.24, f32[16,128,64]{1,2,0:T(8,128)S(1)} %bitcast.181, ...), kind=kOutput, calls=%fused_computation.43 | convolution fusion | flops 203159552 | bytes 3686464 | tf_op jit(solution)/shard_map/htn,hnp->htp/dot_general | solution.py:170
  44.9 1.1 %multiply_reduce_fusion.1 = f32[16,128]{1,0:T(8,128)S(1)} fusion(f32[2,8,128,128]{3,2,1,0:T(8,128)S(1)} %copy.60, f32[16,128]{1,0:T(8,128)S(1)} %rsqrt_bitcast_fusion, f32[16,128]{1,0:T(8,128)S(1)} %add_rsqrt_fusion, f32[16,128,128]{2,1,0:T(8,128)S(1)} %get-tuple-element.44, bf16[16,128,128]{2,1,0:T(8,128)(2,1)S(1)} %copy-done.1, f32[16]{0:T(128)S(1)} %copy-done.14), kind=kLoop, calls=%fused_computation.37 | loop fusion | flops 2095104 | bytes 2646080 | tf_op jit(solution)/shard_map/reduce_sum | solution.py:177
  46.0 2.4 %multiply_reduce_fusion = (f32[16,128]{1,0:T(8,128)S(1)}, f32[16,128,128]{2,1,0:T(8,128)S(1)}) fusion(f32[16,128,128]{2,1,0:T(8,128)S(1)} %get-tuple-element.44, f32[16,128]{1,0:T(8,128)S(1)} %broadcast_multiply_fusion, f32[16,128]{1,0:T(8,128)S(1)} %rsqrt_bitcast_fusion, f32[2,8,128,128]{3,2,1,0:T(8,128)} %copy-done.3, f32[16,128]{1,0:T(8,128)S(1)} %add_rsqrt_fusion, ...), kind=kLoop, calls=%fused_computation.34 | loop fusion | flops 2881536 | bytes 3702848 | tf_op jit(solution)/shard_map/reduce_sum | solution.py:178
  48.4 1.1 %fusion.36 = f32[16,64,128]{2,1,0:T(8,128)S(1)} fusion(f32[16,128,128]{2,1,0:T(8,128)S(1)} %get-tuple-element.12, f32[16,128,64]{1,2,0:T(8,128)S(1)} %bitcast.182, f32[16,128]{1,0:T(8,128)S(1)} %get-tuple-element.22), kind=kOutput, calls=%fused_computation.73 | convolution fusion | flops 201457664 | bytes 2105344 | tf_op jit(solution)/shard_map/htn,htp->hnp/dot_general | solution.py:179
  49.5 1.0 %slice.242 = bf16[1024,128]{1,0:T(8,128)(2,1)S(1)} slice(bf16[1040,128]{1,0:T(8,128)(2,1)} %collective-permute-done.1), slice={[0:1024], [0:128]} | slice | bytes 524288 | tf_op jit(solution)/shard_map/slice | solution.py:39
  50.5 1.0 %slice.244 = bf16[1024,128]{1,0:T(8,128)(2,1)S(1)} slice(bf16[1040,128]{1,0:T(8,128)(2,1)} %collective-permute-done.2), slice={[0:1024], [0:128]} | slice | bytes 524288 | tf_op jit(solution)/shard_map/slice | solution.py:39
  51.5 0.4 multiply_reduce_fusion.4
  52.1 0.7 collective-permute-start.8
  52.8 1.3 %collective-permute-start.7 = (bf16[1040,128]{1,0:T(8,128)(2,1)S(1)}, bf16[1040,128]{1,0:T(8,128)(2,1)S(1)}, u32[]{:S(2)}, u32[]{:S(2)}) collective-permute-start(bf16[1040,128]{1,0:T(8,128)(2,1)S(1)} %pad_maximum_fusion.2), channel_id=1, source_target_pairs={{8,0},{12,4},{9,1},{13,5},{10,2},{14,6},{11,3},{15,7},{24,16},{28,... | collective-permute-start | bytes 798728 | tf_op jit(solution)/shard_map/ppermute | solution.py:67
  54.1 2.1 %collective-permute-start.6 = (bf16[1040,128]{1,0:T(8,128)(2,1)S(1)}, bf16[1040,128]{1,0:T(8,128)(2,1)S(1)}, u32[]{:S(2)}, u32[]{:S(2)}) collective-permute-start(bf16[1040,128]{1,0:T(8,128)(2,1)S(1)} %pad_maximum_fusion.2), channel_id=1, source_target_pairs={{4,0},{8,4},{12,8},{5,1},{9,5},{13,9},{6,2},{10,6},{14,10},{7,3},{... | collective-permute-start | bytes 798728 | tf_op jit(solution)/shard_map/ppermute | solution.py:67
  56.2 1.8 %fusion.103 = f32[16,128,128]{2,1,0:T(8,128)S(1)} fusion(f32[16,128,128]{2,1,0:T(8,128)S(1)} %bitcast_multiply_fusion.1, f32[16,128,128]{2,1,0:T(8,128)S(1)} %get-tuple-element.12), kind=kOutput, calls=%fused_computation.199 | convolution fusion | flops 402653184 | bytes 3145728 | tf_op jit(solution)/shard_map/hts,htp->hsp/dot_general | solution.py:192
  58.1 1.3 %convolution_multiply_fusion = f32[16,128,128]{2,1,0:T(8,128)S(1)} fusion(f32[16,128,128]{2,1,0:T(8,128)S(1)} %get-tuple-element.12, bf16[16,128,128]{2,1,0:T(8,128)(2,1)S(1)} %copy-done.1, f32[16,128]{1,0:T(8,128)S(1)} %reduce_window_sum.21, pred[128,128]{1,0:T(8,128)(4,1)S(1)} %copy.46), kind=kOutput, calls=%fused_computation | convolution fusion | flops 403701760 | bytes 2646016 | tf_op jit(solution)/shard_map/htp,hsp->hts/dot_general | solution.py:194
  59.4 2.1 %convolution_multiply_fusion.6 = f32[16,128,64]{1,2,0:T(8,128)S(1)} fusion(f32[16,128,128]{2,1,0:T(8,128)S(1)} %get-tuple-element.12, f32[16,64,128]{2,1,0:T(8,128)S(1)} %copy-done.8, f32[16,128]{1,0:T(8,128)S(1)} %get-tuple-element.22), kind=kOutput, calls=%fused_computation.21 | convolution fusion | flops 201457664 | bytes 2105344 | tf_op jit(solution)/shard_map/hnp,htp->htn/dot_general | solution.py:198
  61.5 2.9 %convolution_add_fusion.3 = f32[16,128,64]{1,2,0:T(8,128)} fusion(f32[16,128,64]{1,2,0:T(8,128)S(1)} %convolution_multiply_fusion.6, f32[16,128,128]{2,1,0:T(8,128)S(1)} %convolution_multiply_fusion, f32[16,128,64]{1,2,0:T(8,128)S(1)} %bitcast.185), kind=kOutput, calls=%fused_computation.22 | convolution fusion | flops 201457664 | bytes 2621440 | tf_op jit(solution)/shard_map/hts,hsn->htn/dot_general | solution.py:197
  64.5 0.5 collective-permute-done.7
  65.0 9.5 %collective-permute-done.6 = bf16[1040,128]{1,0:T(8,128)(2,1)S(1)} collective-permute-done((bf16[1040,128]{1,0:T(8,128)(2,1)S(1)}, bf16[1040,128]{1,0:T(8,128)(2,1)S(1)}, u32[]{:S(2)}, u32[]{:S(2)}) %collective-permute-start.6) | collective-permute-done | bytes 266272 | tf_op jit(solution)/shard_map/ppermute | solution.py:67
  74.6 2.0 %fusion.10 = f32[16,128,64]{1,2,0:T(8,128)} fusion(bf16[16,128,128]{2,1,0:T(8,128)(2,1)S(1)} %copy-done.1, f32[16,128]{1,0:T(8,128)S(1)} %get-tuple-element.23, bf16[16,64,128]{2,1,0:T(8,128)(2,1)S(1)} %bitcast.191, f32[16,64,128]{2,1,0:T(8,128)S(1)} %bitcast.187, bf16[16,64,128]{2,1,0:T(8,128)(2,1)S(1)} %bitcast.189, f32[16]{0:T(128)S(1)} %get-tuple-element.25, ...), kind=kOutput, calls=%fused_computation.25 | convolution fusion | flops 202244096 | bytes 2105472 | tf_op jit(solution)/shard_map/hnp,hsp->hsn/dot_general | solution.py:229
  76.6 2.8 %fusion.12 = (f32[16,128]{1,0:T(8,128)S(1)}, bf16[16,128,128]{2,1,0:T(8,128)(2,1)}) fusion(bf16[16,128,128]{2,1,0:T(8,128)(2,1)S(1)} %copy-done.1, f32[16,128,128]{2,1,0:T(8,128)S(1)} %get-tuple-element.12, f32[16]{0:T(128)S(1)} %copy-done.14, f32[16,128,128]{2,1,0:T(8,128)S(1)} %fusion.103, bf16[16,64,128]{2,1,0:T(8,128)(2,1)S(1)} %bitcast.192, ...), kind=kOutput, calls=%fused_computation.28 | convolution fusion | flops 204077056 | bytes 4735168 | tf_op jit(solution)/shard_map/hsn,hnp->hsp/dot_general | solution.py:224
  79.4 1.2 %reduce_window_sum.22 = f32[16,128]{1,0:T(8,128)S(1)} reduce-window(f32[16,128]{1,0:T(8,128)S(1)} %sub.114, f32[]{:T(128)} %constant.12.clone.1), window={size=1x128 pad=0_0x0_127}, to_apply=%region_19.20 | reduce-window | flops 260096 | bytes 16388 | tf_op jit(solution)/shard_map/body/reduce_window_sum | solution.py:226
  80.7 2.3 %convolution_add_fusion.4 = f32[16,128,64]{1,2,0:T(8,128)S(1)} fusion(f32[16,128,64]{1,2,0:T(8,128)} %fusion.10, f32[16,128,128]{2,1,0:T(8,128)S(1)} %convolution_multiply_fusion, f32[16,128,64]{1,2,0:T(8,128)} %bitcast.183), kind=kOutput, calls=%fused_computation.23 | convolution fusion | flops 201457664 | bytes 2621440 | tf_op jit(solution)/shard_map/hts,htn->hsn/dot_general | solution.py:196
  83.0 0.7 copy.64
  83.8 0.7 broadcast_add_fusion
  (79 shorter events, 2.8 us)
Async XLA Ops:
  0.6 16.6 %copy-start = (bf16[16,128,128]{2,1,0:T(8,128)(2,1)S(1)}, bf16[16,128,128]{2,1,0:T(8,128)(2,1)}, u32[]{:S(2)}) copy-start(bf16[16,128,128]{2,1,0:T(8,128)(2,1)} %param.7) | copy-start | bytes 1572868
  0.6 8.5 %copy-start.12 = (bf16[2,128,128]{2,1,0:T(8,128)(2,1)S(1)}, bf16[2,128,128]{2,1,0:T(8,128)(2,1)}, u32[]{:S(2)}) copy-start(bf16[2,128,128]{2,1,0:T(8,128)(2,1)} %param.10) | copy-start | bytes 196612
  0.7 8.8 %copy-start.1 = (bf16[16,128,128]{2,1,0:T(8,128)(2,1)S(1)}, bf16[16,128,128]{2,1,0:T(8,128)(2,1)}, u32[]{:S(2)}) copy-start(bf16[16,128,128]{2,1,0:T(8,128)(2,1)} %param.9) | copy-start | bytes 1572868
  0.7 19.8 %collective-permute-start.5 = (bf16[2,128,256]{2,1,0:T(8,128)(2,1)}, bf16[2,128,256]{2,1,0:T(8,128)(2,1)S(1)}, u32[]{:S(2)}, u32[]{:S(2)}) collective-permute-start(bf16[2,128,256]{2,1,0:T(8,128)(2,1)} %param.8), channel_id=1, source_target_pairs={{0,12},{1,13},{2,14},{3,15},{16,28},{17,29},{18,30},{19,31}} | collective-permute-start | bytes 393224 | tf_op jit(solution)/shard_map/ppermute | solution.py:67
  1.5 17.3 %collective-permute-start.3 = (bf16[2,128,256]{2,1,0:T(8,128)(2,1)}, bf16[2,128,256]{2,1,0:T(8,128)(2,1)S(1)}, u32[]{:S(2)}, u32[]{:S(2)}) collective-permute-start(bf16[2,128,256]{2,1,0:T(8,128)(2,1)} %param.8), channel_id=1, source_target_pairs={{0,4},{4,8},{8,12},{1,5},{5,9},{9,13},{2,6},{6,10},{10,14},{3,7},{... | collective-permute-start | bytes 393224 | tf_op jit(solution)/shard_map/ppermute | solution.py:67
  5.0 18.3 %collective-permute-start.4 = (bf16[2,128,256]{2,1,0:T(8,128)(2,1)}, bf16[2,128,256]{2,1,0:T(8,128)(2,1)S(1)}, u32[]{:S(2)}, u32[]{:S(2)}) collective-permute-start(bf16[2,128,256]{2,1,0:T(8,128)(2,1)} %param.8), channel_id=1, source_target_pairs={{0,8},{4,12},{1,9},{5,13},{2,10},{6,14},{3,11},{7,15},{16,24},{20,... | collective-permute-start | bytes 393224 | tf_op jit(solution)/shard_map/ppermute | solution.py:67
  9.5 0.8 copy-start.5
  11.0 23.7 %collective-permute-start.1 = (bf16[1040,128]{1,0:T(8,128)(2,1)}, bf16[1040,128]{1,0:T(8,128)(2,1)}, u32[]{:S(2)}, u32[]{:S(2)}) collective-permute-start(bf16[1040,128]{1,0:T(8,128)(2,1)} %pad_maximum_fusion.1), channel_id=1, source_target_pairs={{0,8},{4,12},{1,9},{5,13},{2,10},{6,14},{3,11},{7,15},{16,24},{20,... | collective-permute-start | bytes 798728 | tf_op jit(solution)/shard_map/ppermute | solution.py:67
  13.0 26.2 %collective-permute-start = (bf16[1040,128]{1,0:T(8,128)(2,1)}, bf16[1040,128]{1,0:T(8,128)(2,1)S(1)}, u32[]{:S(2)}, u32[]{:S(2)}) collective-permute-start(bf16[1040,128]{1,0:T(8,128)(2,1)} %pad_maximum_fusion.1), channel_id=1, source_target_pairs={{0,4},{4,8},{8,12},{1,5},{5,9},{9,13},{2,6},{6,10},{10,14},{3,7},{... | collective-permute-start | bytes 798728 | tf_op jit(solution)/shard_map/ppermute | solution.py:67
  15.7 1.6 %copy-start.13 = (bf16[2,128,256]{2,1,0:T(8,128)(2,1)S(1)}, bf16[2,128,256]{2,1,0:T(8,128)(2,1)}, u32[]{:S(2)}) copy-start(bf16[2,128,256]{2,1,0:T(8,128)(2,1)} %param.8) | copy-start | bytes 393220
  18.8 20.5 %collective-permute-start.2 = (bf16[1040,128]{1,0:T(8,128)(2,1)}, bf16[1040,128]{1,0:T(8,128)(2,1)}, u32[]{:S(2)}, u32[]{:S(2)}) collective-permute-start(bf16[1040,128]{1,0:T(8,128)(2,1)} %pad_maximum_fusion.1), channel_id=1, source_target_pairs={{0,12},{1,13},{2,14},{3,15},{16,28},{17,29},{18,30},{19,31}} | collective-permute-start | bytes 798728 | tf_op jit(solution)/shard_map/ppermute | solution.py:67
  20.8 2.8 %copy-start.2 = (f32[2,8,128,128]{2,3,1,0:T(8,128)S(1)}, f32[2,8,128,128]{2,3,1,0:T(8,128)}, u32[]{:S(2)}) copy-start(f32[2,8,128,128]{2,3,1,0:T(8,128)} %get-tuple-element.38) | copy-start | bytes 3145732
  28.7 16.2 %copy-start.3 = (f32[2,8,128,128]{3,2,1,0:T(8,128)}, f32[2,8,128,128]{3,2,1,0:T(8,128)S(1)}, u32[]{:S(2)}) copy-start(f32[2,8,128,128]{3,2,1,0:T(8,128)S(1)} %copy.60) | copy-start | bytes 3145732
  39.3 10.2 %copy-start.11 = (bf16[1040,128]{1,0:T(8,128)(2,1)}, bf16[1040,128]{1,0:T(8,128)(2,1)S(1)}, u32[]{:S(2)}) copy-start(bf16[1040,128]{1,0:T(8,128)(2,1)S(1)} %collective-permute-done) | copy-start | bytes 798724
  40.0 1.7 %copy-start.9 = (f32[16,128,128]{2,1,0:T(8,128)S(1)}, f32[16,128,128]{2,1,0:T(8,128)}, u32[]{:S(2)}) copy-start(f32[16,128,128]{2,1,0:T(8,128)} %fusion.102) | copy-start | bytes 3145732
  41.6 9.9 %copy-start.7 = (f32[16,64,128]{2,1,0:T(8,128)}, f32[16,64,128]{2,1,0:T(8,128)S(1)}, u32[]{:S(2)}) copy-start(f32[16,64,128]{2,1,0:T(8,128)S(1)} %fusion.24) | copy-start | bytes 1572868
  41.7 6.8 %copy-start.4 = (f32[2,8,128,64]{2,3,1,0:T(8,128)}, f32[2,8,128,64]{2,3,1,0:T(8,128)S(1)}, u32[]{:S(2)}) copy-start(f32[2,8,128,64]{2,3,1,0:T(8,128)S(1)} %broadcast_in_dim.100) | copy-start | bytes 1572868
  41.7 0.7 copy-start.14
  50.5 1.0 %slice-start = ((bf16[1040,128]{1,0:T(8,128)(2,1)}), bf16[1024,128]{1,0:T(8,128)(2,1)S(1)}, s32[]{:S(2)}) async-start(bf16[1040,128]{1,0:T(8,128)(2,1)} %copy-done.11), calls=%async_computation | async-start | bytes 524288 | tf_op jit(solution)/shard_map/slice | solution.py:39
  52.1 12.3 %collective-permute-start.8 = (bf16[1040,128]{1,0:T(8,128)(2,1)S(1)}, bf16[1040,128]{1,0:T(8,128)(2,1)S(1)}, u32[]{:S(2)}, u32[]{:S(2)}) collective-permute-start(bf16[1040,128]{1,0:T(8,128)(2,1)S(1)} %pad_maximum_fusion.2), channel_id=1, source_target_pairs={{12,0},{13,1},{14,2},{15,3},{28,16},{29,17},{30,18},{31,19}} | collective-permute-start | bytes 798728 | tf_op jit(solution)/shard_map/ppermute | solution.py:67
  52.8 12.1 %collective-permute-start.7 = (bf16[1040,128]{1,0:T(8,128)(2,1)S(1)}, bf16[1040,128]{1,0:T(8,128)(2,1)S(1)}, u32[]{:S(2)}, u32[]{:S(2)}) collective-permute-start(bf16[1040,128]{1,0:T(8,128)(2,1)S(1)} %pad_maximum_fusion.2), channel_id=1, source_target_pairs={{8,0},{12,4},{9,1},{13,5},{10,2},{14,6},{11,3},{15,7},{24,16},{28,... | collective-permute-start | bytes 798728 | tf_op jit(solution)/shard_map/ppermute | solution.py:67
  54.1 20.3 %collective-permute-start.6 = (bf16[1040,128]{1,0:T(8,128)(2,1)S(1)}, bf16[1040,128]{1,0:T(8,128)(2,1)S(1)}, u32[]{:S(2)}, u32[]{:S(2)}) collective-permute-start(bf16[1040,128]{1,0:T(8,128)(2,1)S(1)} %pad_maximum_fusion.2), channel_id=1, source_target_pairs={{4,0},{8,4},{12,8},{5,1},{9,5},{13,9},{6,2},{10,6},{14,10},{7,3},{... | collective-permute-start | bytes 798728 | tf_op jit(solution)/shard_map/ppermute | solution.py:67
  58.1 1.3 %copy-start.8 = (f32[16,64,128]{2,1,0:T(8,128)S(1)}, f32[16,64,128]{2,1,0:T(8,128)}, u32[]{:S(2)}) copy-start(f32[16,64,128]{2,1,0:T(8,128)} %copy-done.7) | copy-start | bytes 1572868
  59.4 2.2 %copy-start.6 = (f32[2,8,128,64]{2,3,1,0:T(8,128)S(1)}, f32[2,8,128,64]{2,3,1,0:T(8,128)}, u32[]{:S(2)}) copy-start(f32[2,8,128,64]{2,3,1,0:T(8,128)} %copy-done.5) | copy-start | bytes 1572868
  80.7 2.3 %copy-start.10 = (f32[16,128,64]{1,2,0:T(8,128)S(1)}, f32[16,128,64]{1,2,0:T(8,128)}, u32[]{:S(2)}) copy-start(f32[16,128,64]{1,2,0:T(8,128)} %convolution_add_fusion.3) | copy-start | bytes 1572868

commit v10 on v3

--- a/solution.py
+++ b/solution.py
@@ -77,16 +77,14 @@
 
 def teacher_rows(queries, kv_list, seq_rank):
     local_heads, tok_dev, head_width = queries.shape
-    local_groups = kv_list[0].shape[0]
+    local_groups = kv_list[0][0].shape[0]
     per_group = local_heads // local_groups
     grouped = queries.reshape(local_groups, per_group, tok_dev, head_width)
     rows = jnp.arange(tok_dev)
     within = rows[:, None] >= rows[None, :]
     block_scores = []
-    for distance, block in enumerate(kv_list):
-        scores = jnp.einsum(
-            "gptd,gkd->gptk", grouped, block[..., :head_width], preferred_element_type=jnp.float32
-        )
+    for distance, (keys, _) in enumerate(kv_list):
+        scores = jnp.einsum("gptd,gkd->gptk", grouped, keys, preferred_element_type=jnp.float32)
         scores = scores * head_width ** (-0.5)
         if distance == 0:
             allowed = within
@@ -98,13 +96,13 @@
         highest_score = jnp.maximum(highest_score, scores.max(axis=3, keepdims=True))
     row_sums = None
     mixed = None
-    for scores, block in zip(block_scores, kv_list):
+    for scores, (_, values) in zip(block_scores, kv_list):
         exponentials = jnp.exp(scores - highest_score)
         part_sum = jnp.sum(exponentials, axis=3, keepdims=True)
         part = jnp.einsum(
             "gptk,gkd->gptd",
             exponentials.astype(jnp.bfloat16),
-            block[..., head_width:],
+            values,
             preferred_element_type=jnp.float32,
         )
         row_sums = part_sum if row_sums is None else row_sums + part_sum
@@ -121,7 +119,15 @@
     seq_count = lax.axis_size("seq")
     seq_rank = lax.axis_index("seq")
 
-    kv_earlier = shifted(keys_values, 1)
+    seq_small = seq_count <= 8
+    if seq_small:
+        kv_earlier = [
+            lax.ppermute(keys_values, "seq", [(j, j + distance) for j in range(seq_count - distance)])
+            for distance in range(1, seq_count - 1)
+        ]
+    else:
+        kv_earlier = shifted(keys_values, 1)
+    kv_earlier = [(block[..., :head_width], block[..., head_width:]) for block in kv_earlier]
 
     log_decay = jax.nn.log_sigmoid(decay_logit)
     cumulative = jnp.cumsum(log_decay, axis=1)
@@ -136,7 +142,29 @@
     weighted_in = in_heads * to_end[..., None]
     end_state = jnp.einsum("hsn,hsp->hnp", weighted_in, inputs_wide, precision=highest)
 
-    state_earlier = shifted(pack_rows(end_state, [totals]), 1)
+    state_payload = pack_rows(end_state, [totals])
+    if seq_small and seq_count > 1:
+        far = seq_count - 1
+        state_earlier = [
+            lax.ppermute(state_payload, "seq", [(j, j + distance) for j in range(seq_count - distance)])
+            for distance in range(1, far)
+        ]
+        own_keys = keys_values[..., :head_width]
+        own_values = keys_values[..., head_width:]
+        key_rows = own_keys.size // 128
+        merged = jnp.concatenate(
+            [own_keys.reshape(-1, 128), own_values.reshape(-1, 128), state_payload], axis=0
+        )
+        merged = lax.ppermute(merged, "seq", [(0, far)])
+        kv_earlier.append(
+            (
+                merged[:key_rows].reshape(own_keys.shape),
+                merged[key_rows : 2 * key_rows].reshape(own_values.shape),
+            )
+        )
+        state_earlier.append(merged[2 * key_rows :])
+    else:
+        state_earlier = shifted(state_payload, 1)
     ends_earlier = []
     prefix_state = jnp.zeros_like(end_state)
     gap = jnp.zeros_like(totals)
@@ -160,7 +188,9 @@
     ).reshape(local_heads, tok_dev, tok_dev)
     local_out = jnp.einsum("hts,hsp->htp", mixing, inputs_wide, precision=highest)
 
-    teacher = teacher_rows(queries, [keys_values] + kv_earlier, seq_rank)
+    teacher = teacher_rows(
+        queries, [(keys_values[..., :head_width], keys_values[..., head_width:])] + kv_earlier, seq_rank
+    )
     teacher_wide = teacher.astype(jnp.float32)
     target = teacher_wide * lax.rsqrt(
         jnp.mean(teacher_wide * teacher_wide, axis=2, keepdims=True) + epsilon

time: 82.4 us -> 89 us (1.080)
  other arithmetic: 7.18 us -> 10.8 us
  local copies, waits for them, and re-layouts: 5.56 us -> 8.52 us
  waiting for transfers between devices: 22.1 us -> 24.1 us
  matrix products: 29.7 us -> 28 us
    ppermute x0 -> x5, waiting for transfers between devices: none -> 14.2 us  [the longest x2 14.2 us: body(): lax.ppermute(state_payload, 'seq', [(j, j + distance) for j in range(seq_...]
    ppermute x9 -> x3, waiting for transfers between devices: 22.1 us -> 9.9 us  [shifted(): moved.append(lax.ppermute(x, 'seq', pairs))]
    ppermute x9 -> x3, starting transfers between devices: 15.8 us -> 4.07 us  [shifted(): moved.append(lax.ppermute(x, 'seq', pairs))]
    ppermute x0 -> x5, starting transfers between devices: none -> 11.1 us  [the longest x2 6.57 us: body(): lax.ppermute(keys_values, 'seq', [(j, j + distance) for j in range(seq_co...]
    unnamed x40 -> x56, local copies, waits for them, and re-layouts: 4.04 us -> 5.98 us
    dot_general x8, matrix products: 7.82 us -> 6.11 us  [the longest x4 3.19 us: teacher_rows(): jnp.einsum('gptk,gkd->gptd', exponentials.astype(jnp.bfloat16), values, p...]
    add x1, other arithmetic: 0.3 us -> 1.33 us  [body(): entering = prefix_state + jnp.exp(gap)[:, None, None] * init_state]
    slice x7 -> x6, local copies, waits for them, and re-layouts: 1.04 us -> 2.03 us  [unpack_rows(): big = received[:big_rows].reshape(big_shape)]
  transfers between devices with their start and end apart: 9 -> 8, of which waited for: 5 -> 4; matrix products, arithmetic and copies ran while one was open for 28% -> 23% of each run, Pallas kernels for 0% -> 0%
where the time goes in v10:
time: 89 us; the launch traced here: 88 us
  matrix products  28 us (31%)
  waiting for transfers between devices  24.1 us (27%)
  starting transfers between devices  15.2 us (17%)
  other arithmetic  10.8 us (12%)
  local copies, waits for them, and re-layouts  8.52 us (10%)
  between operations  1.34 us (2%)
    ppermute x2, waiting for transfers between devices, body(): lax.ppermute(state_payload, 'seq', [(j, j + distance) for j in range(seq_...  14.2 us
    ppermute x3, waiting for transfers between devices, shifted(): moved.append(lax.ppermute(x, 'seq', pairs))  9.9 us
    ppermute x2, starting transfers between devices, body(): lax.ppermute(keys_values, 'seq', [(j, j + distance) for j in range(seq_co...  6.57 us
    unnamed x56, local copies, waits for them, and re-layouts  5.98 us
    ppermute x3, starting transfers between devices, shifted(): moved.append(lax.ppermute(x, 'seq', pairs))  4.07 us
    ppermute x2, starting transfers between devices, body(): lax.ppermute(state_payload, 'seq', [(j, j + distance) for j in range(seq_...  3.89 us
    dot_general x4, matrix products, teacher_rows(): jnp.einsum('gptk,gkd->gptd', exponentials.astype(jnp.bfloat16), values, p...  3.19 us
    dot_general x1, matrix products, body(): jnp.einsum('hts,hsn->htn', paired, in_heads, precision=highest)  2.94 us
  transfers between devices with their start and end apart: 8, of which 4 were waited for; matrix products, arithmetic and copies ran while one was open for 23% of the time, Pallas kernels for 0%

profile of v10, /device:TPU:8, one launch (start us, length us, event | category | flops | bytes accessed | tf_op | source)
XLA Modules:
  0.0 88.0 jit_solution(2542613262931469769)
XLA Ops:
  0.7 3.6 %collective-permute-start.3 = (bf16[2,128,256]{2,1,0:T(8,128)(2,1)}, bf16[2,128,256]{2,1,0:T(8,128)(2,1)}, u32[]{:S(2)}, u32[]{:S(2)}) collective-permute-start(bf16[2,128,256]{2,1,0:T(8,128)(2,1)} %param.8), channel_id=1, source_target_pairs={{0,4},{4,8},{8,12},{1,5},{5,9},{9,13},{2,6},{6,10},{10,14},{3,7},{... | collective-permute-start | bytes 393224 | tf_op jit(solution)/shard_map/ppermute | solution.py:125
  4.3 3.0 %collective-permute-start.4 = (bf16[2,128,256]{2,1,0:T(8,128)(2,1)}, bf16[2,128,256]{2,1,0:T(8,128)(2,1)}, u32[]{:S(2)}, u32[]{:S(2)}) collective-permute-start(bf16[2,128,256]{2,1,0:T(8,128)(2,1)} %param.8), channel_id=1, source_target_pairs={{0,8},{4,12},{1,9},{5,13},{2,10},{6,14},{3,11},{7,15},{16,24},{20,... | collective-permute-start | bytes 393224 | tf_op jit(solution)/shard_map/ppermute | solution.py:125
  7.2 0.7 fusion.50
  8.4 0.6 fusion.100
  9.1 0.7 fusion.99
  10.0 0.5 convolution_convert_fusion
  10.8 0.7 pad_maximum_fusion.2
  11.5 2.0 %collective-permute-start.1 = (bf16[1040,128]{1,0:T(8,128)(2,1)}, bf16[1040,128]{1,0:T(8,128)(2,1)}, u32[]{:S(2)}, u32[]{:S(2)}) collective-permute-start(bf16[1040,128]{1,0:T(8,128)(2,1)} %pad_maximum_fusion.2), channel_id=1, source_target_pairs={{0,8},{4,12},{1,9},{5,13},{2,10},{6,14},{3,11},{7,15},{16,24},{20,... | collective-permute-start | bytes 798728 | tf_op jit(solution)/shard_map/ppermute | solution.py:149
  13.5 1.9 %collective-permute-start = (bf16[1040,128]{1,0:T(8,128)(2,1)}, bf16[1040,128]{1,0:T(8,128)(2,1)S(1)}, u32[]{:S(2)}, u32[]{:S(2)}) collective-permute-start(bf16[1040,128]{1,0:T(8,128)(2,1)} %pad_maximum_fusion.2), channel_id=1, source_target_pairs={{0,4},{4,8},{8,12},{1,5},{5,9},{9,13},{2,6},{6,10},{10,14},{3,7},{... | collective-permute-start | bytes 798728 | tf_op jit(solution)/shard_map/ppermute | solution.py:149
  15.4 0.8 pad_maximum_fusion.1
  16.2 0.7 collective-permute-start.2
  17.9 2.3 %fusion.105 = f32[16,128,128]{1,2,0:T(8,128)} fusion(f32[16,128,128]{2,1,0:T(8,128)S(1)} %bitcast_multiply_fusion.1, bf16[16,128,128]{2,1,0:T(8,128)(2,1)S(1)} %copy-done.1), kind=kOutput, calls=%fused_computation.200 | convolution fusion | flops 402653184 | bytes 2621440 | tf_op jit(solution)/shard_map/hts,hsp->htp/dot_general | solution.py:189
  20.8 0.5 copy-done.15
  21.4 1.1 %fusion.104 = (f32[2,8,128]{2,1,0:T(8,128)S(1)}, f32[2,8,128,128]{2,3,1,0:T(8,128)S(1)}) fusion(bf16[2,8,128,128]{3,2,1,0:T(8,128)(2,1)S(1)} %bitcast.182, bf16[2,128,256]{2,1,0:T(8,128)(2,1)} %collective-permute-done.3, pred[]{:T(512)S(6)} %ge.51), kind=kOutput, calls=%fused_computation.199 | convolution fusion | flops 67893248 | bytes 1646593 | tf_op jit(solution)/shard_map/gptd,gkd->gptk/dot_general | solution.py:87
  22.6 1.1 %fusion.102 = (f32[2,8,128]{2,1,0:T(8,128)S(1)}, f32[2,8,128,128]{2,3,1,0:T(8,128)S(1)}) fusion(bf16[2,8,128,128]{3,2,1,0:T(8,128)(2,1)S(1)} %bitcast.183, bf16[2,128,256]{2,1,0:T(8,128)(2,1)} %collective-permute-done.4, pred[]{:T(512)S(6)} %ge.52), kind=kOutput, calls=%fused_computation.197 | convolution fusion | flops 67893248 | bytes 1646593 | tf_op jit(solution)/shard_map/gptd,gkd->gptk/dot_general | solution.py:87
  23.7 2.0 %collective-permute-done.1 = bf16[1040,128]{1,0:T(8,128)(2,1)} collective-permute-done((bf16[1040,128]{1,0:T(8,128)(2,1)}, bf16[1040,128]{1,0:T(8,128)(2,1)}, u32[]{:S(2)}, u32[]{:S(2)}) %collective-permute-start.1) | collective-permute-done | bytes 266272 | tf_op jit(solution)/shard_map/ppermute | solution.py:149
  25.8 0.7 slice_convert_fusion.4
  26.5 12.2 %collective-permute-done = bf16[1040,128]{1,0:T(8,128)(2,1)S(1)} collective-permute-done((bf16[1040,128]{1,0:T(8,128)(2,1)}, bf16[1040,128]{1,0:T(8,128)(2,1)S(1)}, u32[]{:S(2)}, u32[]{:S(2)}) %collective-permute-start) | collective-permute-done | bytes 266272 | tf_op jit(solution)/shard_map/ppermute | solution.py:149
  38.6 1.1 %slice.247 = bf16[1024,128]{1,0:T(8,128)(2,1)S(1)} slice(bf16[1040,128]{1,0:T(8,128)(2,1)} %collective-permute-done.1), slice={[0:1024], [0:128]} | slice | bytes 524288 | tf_op jit(solution)/shard_map/slice | solution.py:38
  40.8 1.0 %fusion.17 = (f32[2,8,128]{2,1,0:T(8,128)S(1)}, f32[2,8,128]{2,1,0:T(8,128)S(1)}, f32[2,8,128]{2,1,0:T(8,128)S(1)}, f32[2,8,128]{2,1,0:T(8,128)S(1)}) fusion(f32[2,8,128,128]{2,3,1,0:T(8,128)S(1)} %get-tuple-element.53, f32[2,8,128]{2,1,0:T(8,128)S(1)} %maximum_maximum_fusion, f32[2,8,128,128]{2,3,1,0:T(8,128)S(1)} %get-tuple-element.51, ...), kind=kLoop, calls=%fused_computation.48 | loop fusion | flops 2088960 | bytes 4235264 | tf_op jit(solution)/shard_map/reduce_sum | solution.py:101
  41.8 1.2 %convolution_add_fusion.2 = f32[2,8,128,128]{2,3,1,0:T(8,128)S(1)} fusion(f32[2,8,128,128]{2,3,1,0:T(8,128)S(1)} %fusion.33, f32[2,8,128,128]{2,3,1,0:T(8,128)S(1)} %get-tuple-element.53, f32[2,8,128]{2,1,0:T(8,128)S(1)} %maximum_maximum_fusion, bf16[2,128,256]{2,1,0:T(8,128)(2,1)} %collective-permute-done.3), kind=kOutput, calls=%fused_computation.8 | convolution fusion | flops 67895296 | bytes 3219456 | tf_op jit(solution)/shard_map/gptk,gkd->gptd/dot_general | solution.py:102
  43.0 1.3 %multiply_reduce_fusion.2 = (f32[2,8,128]{2,1,0:T(8,128)S(1)}, f32[2,8,128,128]{2,3,1,0:T(8,128)S(1)}) fusion(f32[2,8,128]{2,1,0:T(8,128)S(1)} %add_add_fusion, f32[2,8,128,128]{2,3,1,0:T(8,128)S(1)} %fusion.29, f32[2,8,128,128]{2,3,1,0:T(8,128)S(1)} %convolution_add_fusion.2, bf16[2,128,256]{2,1,0:T(8,128)(2,1)} %collective-permute-done.4, ...), kind=kOutput, calls=%fused_computation.39 | convolution fusion | flops 69466112 | bytes 4284416 | tf_op jit(solution)/shard_map/gptk,gkd->gptd/dot_general | solution.py:102
  44.4 1.3 %fusion.25 = f32[16,64,128]{2,1,0:T(8,128)S(1)} fusion(f32[16,64,128]{2,1,0:T(8,128)S(1)} %copy-done.14, f32[16]{0:T(128)S(1)} %fusion.88, f32[16]{0:T(128)S(1)} %get-tuple-element.24, f32[16]{0:T(128)S(1)} %get-tuple-element.42, f32[]{:T(128)S(6)} %select_n.166, bf16[1552,128]{1,0:T(8,128)(2,1)S(1)} %collective-permute-done.2, ...), kind=kLoop, calls=%fused_computation.62 | loop fusion | flops 1310720 | bytes 1835204 | tf_op jit(solution)/shard_map/add | solution.py:179
  45.8 0.6 copy-done.20
  46.5 2.0 %multiply_reduce_fusion.3 = (f32[16,128]{1,0:T(8,128)S(1)}, f32[16,128,128]{1,2,0:T(8,128)S(1)}) fusion(bf16[16,128,128]{1,2,0:T(8,128)(2,1)S(1)} %copy.50, f32[16]{0:T(128)S(1)} %copy-done.23, f32[16,128,128]{1,2,0:T(8,128)S(1)} %copy-done.8, f32[16,64,128]{2,1,0:T(8,128)S(1)} %fusion.25, f32[16,128,64]{1,2,0:T(8,128)S(1)} %bitcast.185, ...), kind=kOutput, calls=%fused_computation.44 | convolution fusion | flops 203159552 | bytes 3686464 | tf_op jit(solution)/shard_map/htn,hnp->htp/dot_general | solution.py:199
  48.5 0.4 multiply_reduce_fusion.1
  49.0 1.2 %multiply_reduce_fusion = (f32[16,128]{1,0:T(8,128)}, f32[16,128,128]{1,2,0:T(8,128)S(1)}) fusion(f32[16,128,128]{1,2,0:T(8,128)S(1)} %get-tuple-element.57, f32[16,128]{1,0:T(8,128)S(1)} %broadcast_multiply_fusion, f32[16,128]{1,0:T(8,128)S(1)} %rsqrt_bitcast_fusion, f32[2,8,128,128]{2,3,1,0:T(8,128)S(1)} %get-tuple-element.55, ...), kind=kLoop, calls=%fused_computation.35 | loop fusion | flops 2881536 | bytes 3702848 | tf_op jit(solution)/shard_map/reduce_sum | solution.py:207
  50.2 2.1 %fusion.37 = f32[16,64,128]{2,1,0:T(8,128)S(1)} fusion(f32[16,128,128]{1,2,0:T(8,128)S(1)} %get-tuple-element.21, f32[16,128,64]{1,2,0:T(8,128)S(1)} %bitcast.186, f32[16,128]{1,0:T(8,128)S(1)} %copy-done.20), kind=kOutput, calls=%fused_computation.74 | convolution fusion | flops 201457664 | bytes 2105344 | tf_op jit(solution)/shard_map/htn,htp->hnp/dot_general | solution.py:208
  52.4 0.9 %slice-done = bf16[1024,128]{1,0:T(8,128)(2,1)S(1)} async-done(((bf16[1040,128]{1,0:T(8,128)(2,1)}), bf16[1024,128]{1,0:T(8,128)(2,1)S(1)}, s32[]{:S(2)}) %slice-start) | async-done | bytes 262168 | tf_op jit(solution)/shard_map/slice | solution.py:38
  53.3 0.4 multiply_reduce_fusion.4
  53.9 0.7 collective-permute-start.7
  54.6 1.5 %collective-permute-start.6 = (bf16[1040,128]{1,0:T(8,128)(2,1)S(1)}, bf16[1040,128]{1,0:T(8,128)(2,1)S(1)}, u32[]{:S(2)}, u32[]{:S(2)}) collective-permute-start(bf16[1040,128]{1,0:T(8,128)(2,1)S(1)} %pad_maximum_fusion.3), channel_id=1, source_target_pairs={{8,0},{12,4},{9,1},{13,5},{10,2},{14,6},{11,3},{15,7},{24,16},{28,... | collective-permute-start | bytes 798728 | tf_op jit(solution)/shard_map/ppermute | solution.py:66
  56.0 1.9 %collective-permute-start.5 = (bf16[1040,128]{1,0:T(8,128)(2,1)S(1)}, bf16[1040,128]{1,0:T(8,128)(2,1)S(1)}, u32[]{:S(2)}, u32[]{:S(2)}) collective-permute-start(bf16[1040,128]{1,0:T(8,128)(2,1)S(1)} %pad_maximum_fusion.3), channel_id=1, source_target_pairs={{4,0},{8,4},{12,8},{5,1},{9,5},{13,9},{6,2},{10,6},{14,10},{7,3},{... | collective-permute-start | bytes 798728 | tf_op jit(solution)/shard_map/ppermute | solution.py:66
  58.0 2.3 %fusion.106 = f32[16,128,128]{1,2,0:T(8,128)S(1)} fusion(f32[16,128,128]{2,1,0:T(8,128)} %copy-done.2, f32[16,128,128]{1,2,0:T(8,128)S(1)} %get-tuple-element.21), kind=kOutput, calls=%fused_computation.201 | convolution fusion | flops 402653184 | bytes 3145728 | tf_op jit(solution)/shard_map/hts,htp->hsp/dot_general | solution.py:221
  60.3 1.2 %convolution_multiply_fusion = f32[16,128,128]{2,1,0:T(8,128)S(1)} fusion(f32[16,128,128]{1,2,0:T(8,128)S(1)} %get-tuple-element.21, bf16[16,128,128]{2,1,0:T(8,128)(2,1)S(1)} %copy-done.1, f32[16,128]{1,0:T(8,128)S(1)} %reduce_window_sum.21, pred[128,128]{1,0:T(8,128)(4,1)S(1)} %copy-done.17), kind=kOutput, calls=%fused_computation | convolution fusion | flops 403701760 | bytes 2646016 | tf_op jit(solution)/shard_map/htp,hsp->hts/dot_general | solution.py:223
  61.6 1.0 %convolution_multiply_fusion.6 = f32[16,128,64]{1,2,0:T(8,128)S(1)} fusion(f32[16,128,128]{1,2,0:T(8,128)S(1)} %get-tuple-element.21, f32[16,64,128]{2,1,0:T(8,128)S(1)} %copy-done.7, f32[16,128]{1,0:T(8,128)S(1)} %copy-done.21), kind=kOutput, calls=%fused_computation.22 | convolution fusion | flops 201457664 | bytes 2105344 | tf_op jit(solution)/shard_map/hnp,htp->htn/dot_general | solution.py:227
  62.6 0.4 copy-done.5
  63.0 2.9 %convolution_add_fusion.3 = f32[16,128,64]{1,2,0:T(8,128)} fusion(f32[16,128,64]{1,2,0:T(8,128)S(1)} %convolution_multiply_fusion.6, f32[16,128,128]{2,1,0:T(8,128)S(1)} %convolution_multiply_fusion, f32[16,128,64]{1,2,0:T(8,128)S(1)} %bitcast.189), kind=kOutput, calls=%fused_computation.23 | convolution fusion | flops 201457664 | bytes 2621440 | tf_op jit(solution)/shard_map/hts,hsn->htn/dot_general | solution.py:226
  65.9 0.7 collective-permute-done.6
  66.7 9.2 %collective-permute-done.5 = bf16[1040,128]{1,0:T(8,128)(2,1)S(1)} collective-permute-done((bf16[1040,128]{1,0:T(8,128)(2,1)S(1)}, bf16[1040,128]{1,0:T(8,128)(2,1)S(1)}, u32[]{:S(2)}, u32[]{:S(2)}) %collective-permute-start.5) | collective-permute-done | bytes 266272 | tf_op jit(solution)/shard_map/ppermute | solution.py:66
  76.1 0.7 copy-done.19
  76.7 2.0 %fusion.11 = f32[16,128,64]{1,2,0:T(8,128)} fusion(bf16[16,128,128]{2,1,0:T(8,128)(2,1)S(1)} %copy-done.1, f32[16,128]{1,0:T(8,128)S(1)} %copy-done.19, bf16[16,64,128]{2,1,0:T(8,128)(2,1)S(1)} %bitcast.197, f32[16,64,128]{2,1,0:T(8,128)S(1)} %bitcast.191, bf16[16,64,128]{2,1,0:T(8,128)(2,1)S(1)} %bitcast.195, f32[16]{0:T(128)S(1)} %get-tuple-element.38, ...), kind=kOutput, calls=%fused_computation.26 | convolution fusion | flops 202244096 | bytes 2105472 | tf_op jit(solution)/shard_map/hnp,hsp->hsn/dot_general | solution.py:258
  78.7 2.8 %fusion.13 = (f32[16,128]{1,0:T(8,128)S(1)}, bf16[16,128,128]{1,2,0:T(8,128)(2,1)}) fusion(bf16[16,128,128]{1,2,0:T(8,128)(2,1)S(1)} %copy.50, f32[16,128,128]{1,2,0:T(8,128)S(1)} %get-tuple-element.21, f32[16]{0:T(128)S(1)} %copy-done.24, f32[16,128,128]{1,2,0:T(8,128)S(1)} %fusion.106, bf16[16,64,128]{2,1,0:T(8,128)(2,1)S(1)} %bitcast.198, ...), kind=kOutput, calls=%fused_computation.29 | convolution fusion | flops 204077056 | bytes 4735168 | tf_op jit(solution)/shard_map/hsn,hnp->hsp/dot_general | solution.py:253
  81.6 1.2 %reduce_window_sum.22 = f32[16,128]{1,0:T(8,128)S(1)} reduce-window(f32[16,128]{1,0:T(8,128)S(1)} %sub.114, f32[]{:T(128)} %constant.12.clone.1), window={size=1x128 pad=0_0x0_127}, to_apply=%region_19.20 | reduce-window | flops 260096 | bytes 16388 | tf_op jit(solution)/shard_map/body/reduce_window_sum | solution.py:255
  82.8 2.4 %convolution_add_fusion.4 = f32[16,128,64]{1,2,0:T(8,128)S(1)} fusion(f32[16,128,64]{1,2,0:T(8,128)} %fusion.11, f32[16,128,128]{2,1,0:T(8,128)} %copy-done.3, f32[16,128,64]{1,2,0:T(8,128)S(1)} %bitcast.187), kind=kOutput, calls=%fused_computation.24 | convolution fusion | flops 201457664 | bytes 2621440 | tf_op jit(solution)/shard_map/hts,htn->hsn/dot_general | solution.py:225
  85.3 0.7 copy.62
  86.3 1.0 %copy.61 = bf16[16,128,128]{2,1,0:T(8,128)(2,1)} copy(bf16[16,128,128]{1,2,0:T(8,128)(2,1)S(1)} %copy-done.10) | data formatting | bytes 1048576
  87.3 0.7 broadcast_add_fusion
  (101 shorter events, 4.5 us)
Async XLA Ops:
  0.6 19.5 %copy-start = (bf16[16,128,128]{2,1,0:T(8,128)(2,1)S(1)}, bf16[16,128,128]{2,1,0:T(8,128)(2,1)}, u32[]{:S(2)}) copy-start(bf16[16,128,128]{2,1,0:T(8,128)(2,1)} %param.7) | copy-start | bytes 1572868
  0.6 8.4 %copy-start.12 = (bf16[2,128,128]{2,1,0:T(8,128)(2,1)S(1)}, bf16[2,128,128]{2,1,0:T(8,128)(2,1)}, u32[]{:S(2)}) copy-start(bf16[2,128,128]{2,1,0:T(8,128)(2,1)} %param.10) | copy-start | bytes 196612
  0.7 9.3 %copy-start.1 = (bf16[16,128,128]{2,1,0:T(8,128)(2,1)S(1)}, bf16[16,128,128]{2,1,0:T(8,128)(2,1)}, u32[]{:S(2)}) copy-start(bf16[16,128,128]{2,1,0:T(8,128)(2,1)} %param.9) | copy-start | bytes 1572868
  0.7 20.7 %collective-permute-start.3 = (bf16[2,128,256]{2,1,0:T(8,128)(2,1)}, bf16[2,128,256]{2,1,0:T(8,128)(2,1)}, u32[]{:S(2)}, u32[]{:S(2)}) collective-permute-start(bf16[2,128,256]{2,1,0:T(8,128)(2,1)} %param.8), channel_id=1, source_target_pairs={{0,4},{4,8},{8,12},{1,5},{5,9},{9,13},{2,6},{6,10},{10,14},{3,7},{... | collective-permute-start | bytes 393224 | tf_op jit(solution)/shard_map/ppermute | solution.py:125
  4.3 18.3 %collective-permute-start.4 = (bf16[2,128,256]{2,1,0:T(8,128)(2,1)}, bf16[2,128,256]{2,1,0:T(8,128)(2,1)}, u32[]{:S(2)}, u32[]{:S(2)}) collective-permute-start(bf16[2,128,256]{2,1,0:T(8,128)(2,1)} %param.8), channel_id=1, source_target_pairs={{0,8},{4,12},{1,9},{5,13},{2,10},{6,14},{3,11},{7,15},{16,24},{20,... | collective-permute-start | bytes 393224 | tf_op jit(solution)/shard_map/ppermute | solution.py:125
  9.1 0.9 %copy-start.18 = (f32[16,128]{1,0:T(8,128)}, f32[16,128]{1,0:T(8,128)S(1)}, u32[]{:S(2)}) copy-start(f32[16,128]{1,0:T(8,128)S(1)} %get-tuple-element.36) | copy-start | bytes 24580
  10.0 0.8 copy-start.4
  10.8 4.6 %copy-start.13 = (bf16[2,128,256]{2,1,0:T(8,128)(2,1)S(1)}, bf16[2,128,256]{2,1,0:T(8,128)(2,1)}, u32[]{:S(2)}) copy-start(bf16[2,128,256]{2,1,0:T(8,128)(2,1)} %param.8) | copy-start | bytes 393220
  11.5 14.3 %collective-permute-start.1 = (bf16[1040,128]{1,0:T(8,128)(2,1)}, bf16[1040,128]{1,0:T(8,128)(2,1)}, u32[]{:S(2)}, u32[]{:S(2)}) collective-permute-start(bf16[1040,128]{1,0:T(8,128)(2,1)} %pad_maximum_fusion.2), channel_id=1, source_target_pairs={{0,8},{4,12},{1,9},{5,13},{2,10},{6,14},{3,11},{7,15},{16,24},{20,... | collective-permute-start | bytes 798728 | tf_op jit(solution)/shard_map/ppermute | solution.py:149
  13.5 25.2 %collective-permute-start = (bf16[1040,128]{1,0:T(8,128)(2,1)}, bf16[1040,128]{1,0:T(8,128)(2,1)S(1)}, u32[]{:S(2)}, u32[]{:S(2)}) collective-permute-start(bf16[1040,128]{1,0:T(8,128)(2,1)} %pad_maximum_fusion.2), channel_id=1, source_target_pairs={{0,4},{4,8},{8,12},{1,5},{5,9},{9,13},{2,6},{6,10},{10,14},{3,7},{... | collective-permute-start | bytes 798728 | tf_op jit(solution)/shard_map/ppermute | solution.py:149
  16.2 23.5 %collective-permute-start.2 = (bf16[1552,128]{1,0:T(8,128)(2,1)}, bf16[1552,128]{1,0:T(8,128)(2,1)S(1)}, u32[]{:S(2)}, u32[]{:S(2)}) collective-permute-start(bf16[1552,128]{1,0:T(8,128)(2,1)} %pad_maximum_fusion.1), channel_id=1, source_target_pairs={{0,12},{1,13},{2,14},{3,15},{16,28},{17,29},{18,30},{19,31}} | collective-permute-start | bytes 1191944 | tf_op jit(solution)/shard_map/ppermute | solution.py:158
  17.3 0.6 copy-start.16
  17.9 2.3 %copy-start.2 = (f32[16,128,128]{2,1,0:T(8,128)}, f32[16,128,128]{2,1,0:T(8,128)S(1)}, u32[]{:S(2)}) copy-start(f32[16,128,128]{2,1,0:T(8,128)S(1)} %bitcast_multiply_fusion.1) | copy-start | bytes 3145732
  20.4 0.8 copy-start.15
  38.6 5.7 %copy-start.11 = (bf16[1040,128]{1,0:T(8,128)(2,1)}, bf16[1040,128]{1,0:T(8,128)(2,1)S(1)}, u32[]{:S(2)}) copy-start(bf16[1040,128]{1,0:T(8,128)(2,1)S(1)} %collective-permute-done) | copy-start | bytes 798724
  43.0 1.4 %copy-start.14 = (f32[16,64,128]{2,1,0:T(8,128)S(1)}, f32[16,64,128]{2,1,0:T(8,128)}, u32[]{:S(2)}) copy-start(f32[16,64,128]{2,1,0:T(8,128)} %param.13) | copy-start | bytes 1572868
  44.4 1.4 %copy-start.8 = (f32[16,128,128]{1,2,0:T(8,128)S(1)}, f32[16,128,128]{1,2,0:T(8,128)}, u32[]{:S(2)}) copy-start(f32[16,128,128]{1,2,0:T(8,128)} %fusion.105) | copy-start | bytes 3145732
  45.7 6.6 %copy-start.6 = (f32[16,64,128]{2,1,0:T(8,128)}, f32[16,64,128]{2,1,0:T(8,128)S(1)}, u32[]{:S(2)}) copy-start(f32[16,64,128]{2,1,0:T(8,128)S(1)} %fusion.25) | copy-start | bytes 1572868
  45.7 0.7 copy-start.20
  45.8 0.7 copy-start.23
  52.3 1.0 %slice-start = ((bf16[1040,128]{1,0:T(8,128)(2,1)}), bf16[1024,128]{1,0:T(8,128)(2,1)S(1)}, s32[]{:S(2)}) async-start(bf16[1040,128]{1,0:T(8,128)(2,1)} %copy-done.11), calls=%async_computation | async-start | bytes 524288 | tf_op jit(solution)/shard_map/slice | solution.py:38
  53.9 6.4 %copy-start.17 = (pred[128,128]{1,0:T(8,128)(4,1)S(1)}, pred[128,128]{1,0:T(8,128)(4,1)}, u32[]{:S(2)}) copy-start(pred[128,128]{1,0:T(8,128)(4,1)} %copy-done.16) | copy-start | bytes 49156
  53.9 12.1 %collective-permute-start.7 = (bf16[1040,128]{1,0:T(8,128)(2,1)S(1)}, bf16[1040,128]{1,0:T(8,128)(2,1)S(1)}, u32[]{:S(2)}, u32[]{:S(2)}) collective-permute-start(bf16[1040,128]{1,0:T(8,128)(2,1)S(1)} %pad_maximum_fusion.3), channel_id=1, source_target_pairs={{12,0},{13,1},{14,2},{15,3},{28,16},{29,17},{30,18},{31,19}} | collective-permute-start | bytes 798728 | tf_op jit(solution)/shard_map/ppermute | solution.py:66
  54.6 12.1 %collective-permute-start.6 = (bf16[1040,128]{1,0:T(8,128)(2,1)S(1)}, bf16[1040,128]{1,0:T(8,128)(2,1)S(1)}, u32[]{:S(2)}, u32[]{:S(2)}) collective-permute-start(bf16[1040,128]{1,0:T(8,128)(2,1)S(1)} %pad_maximum_fusion.3), channel_id=1, source_target_pairs={{8,0},{12,4},{9,1},{13,5},{10,2},{14,6},{11,3},{15,7},{24,16},{28,... | collective-permute-start | bytes 798728 | tf_op jit(solution)/shard_map/ppermute | solution.py:66
  56.0 19.8 %collective-permute-start.5 = (bf16[1040,128]{1,0:T(8,128)(2,1)S(1)}, bf16[1040,128]{1,0:T(8,128)(2,1)S(1)}, u32[]{:S(2)}, u32[]{:S(2)}) collective-permute-start(bf16[1040,128]{1,0:T(8,128)(2,1)S(1)} %pad_maximum_fusion.3), channel_id=1, source_target_pairs={{4,0},{8,4},{12,8},{5,1},{9,5},{13,9},{6,2},{10,6},{14,10},{7,3},{... | collective-permute-start | bytes 798728 | tf_op jit(solution)/shard_map/ppermute | solution.py:66
  60.3 1.2 %copy-start.7 = (f32[16,64,128]{2,1,0:T(8,128)S(1)}, f32[16,64,128]{2,1,0:T(8,128)}, u32[]{:S(2)}) copy-start(f32[16,64,128]{2,1,0:T(8,128)} %copy-done.6) | copy-start | bytes 1572868
  60.3 1.2 %copy-start.21 = (f32[16,128]{1,0:T(8,128)S(1)}, f32[16,128]{1,0:T(8,128)}, u32[]{:S(2)}) copy-start(f32[16,128]{1,0:T(8,128)} %get-tuple-element.35) | copy-start | bytes 24580
  61.6 1.1 %copy-start.3 = (f32[16,128,128]{2,1,0:T(8,128)}, f32[16,128,128]{2,1,0:T(8,128)S(1)}, u32[]{:S(2)}) copy-start(f32[16,128,128]{2,1,0:T(8,128)S(1)} %convolution_multiply_fusion) | copy-start | bytes 3145732
  61.6 1.4 %copy-start.5 = (f32[2,8,128,64]{2,3,1,0:T(8,128)S(1)}, f32[2,8,128,64]{2,3,1,0:T(8,128)}, u32[]{:S(2)}) copy-start(f32[2,8,128,64]{2,3,1,0:T(8,128)} %copy-done.4) | copy-start | bytes 1572868
  76.0 0.7 copy-start.19
  76.7 2.0 %copy-start.24 = (f32[16]{0:T(128)S(1)}, f32[16]{0:T(128)}, u32[]{:S(2)}) copy-start(f32[16]{0:T(128)} %param.12) | copy-start | bytes 196
  78.7 2.8 %copy-start.22 = (f32[16,128]{1,0:T(8,128)S(1)}, f32[16,128]{1,0:T(8,128)}, u32[]{:S(2)}) copy-start(f32[16,128]{1,0:T(8,128)} %get-tuple-element.20) | copy-start | bytes 24580
  82.8 2.4 %copy-start.9 = (f32[16,128,64]{1,2,0:T(8,128)S(1)}, f32[16,128,64]{1,2,0:T(8,128)}, u32[]{:S(2)}) copy-start(f32[16,128,64]{1,2,0:T(8,128)} %convolution_add_fusion.3) | copy-start | bytes 1572868
  85.3 1.0 %copy-start.10 = (bf16[16,128,128]{1,2,0:T(8,128)(2,1)S(1)}, bf16[16,128,128]{1,2,0:T(8,128)(2,1)}, u32[]{:S(2)}) copy-start(bf16[16,128,128]{1,2,0:T(8,128)(2,1)} %get-tuple-element.27) | copy-start | bytes 1572868

commit v11 on v3

--- a/solution.py
+++ b/solution.py
@@ -68,7 +68,7 @@
     gathered = lax.all_gather(x, "seq", axis=0)
     moved = []
     for distance in range(1, seq_count):
-        source = seq_rank + step * distance
+        source = seq_rank - step * distance
         valid = (source >= 0) & (source < seq_count)
         picked = lax.dynamic_index_in_dim(gathered, jnp.clip(source, 0, seq_count - 1), 0, False)
         moved.append(jnp.where(valid, picked, jnp.zeros_like(picked)))

time: 82.4 us -> 82.4 us (level)
  no operation moved by 1% of the time
where the time goes in v11:
time: 82.4 us; the launch traced here: 81.6 us
  matrix products  29.7 us (36%)
  waiting for transfers between devices  22.1 us (27%)
  starting transfers between devices  15.8 us (19%)
  other arithmetic  7.18 us (9%)
  local copies, waits for them, and re-layouts  5.56 us (7%)
  between operations  1.28 us (2%)
    ppermute x9, waiting for transfers between devices, shifted(): moved.append(lax.ppermute(x, 'seq', pairs))  22.1 us
    ppermute x9, starting transfers between devices, shifted(): moved.append(lax.ppermute(x, 'seq', pairs))  15.8 us
    dot_general x4, matrix products, teacher_rows(): jnp.einsum('gptk,gkd->gptd', exponentials.astype(jnp.bfloat16), block[......  4.06 us
    unnamed x40, local copies, waits for them, and re-layouts  4.04 us
    dot_general x4, matrix products, teacher_rows(): jnp.einsum('gptd,gkd->gptk', grouped, block[..., :head_width], preferred_...  3.75 us
    dot_general x1, matrix products, body(): jnp.einsum('hts,hsn->htn', paired, in_heads, precision=highest)  2.94 us
    dot_general x1, matrix products, body(): jnp.einsum('hsn,hnp->hsp', weighted_in, incoming, precision=highest)  2.84 us
    dot_general x1, matrix products, body(): local_din = jnp.einsum('hts,htn->hsn', paired, out_heads, precision=highest)  2.44 us
  transfers between devices with their start and end apart: 9, of which 5 were waited for; matrix products, arithmetic and copies ran while one was open for 28% of the time, Pallas kernels for 0%

profile of v11, /device:TPU:8, one launch (start us, length us, event | category | flops | bytes accessed | tf_op | source)
XLA Modules:
  0.0 81.6 jit_solution(6475823142860286927)
XLA Ops:
  0.7 1.5 %collective-permute-start.5 = (bf16[2,128,256]{2,1,0:T(8,128)(2,1)}, bf16[2,128,256]{2,1,0:T(8,128)(2,1)}, u32[]{:S(2)}, u32[]{:S(2)}) collective-permute-start(bf16[2,128,256]{2,1,0:T(8,128)(2,1)} %param.8), channel_id=1, source_target_pairs={{0,12},{1,13},{2,14},{3,15},{16,28},{17,29},{18,30},{19,31}} | collective-permute-start | bytes 393224 | tf_op jit(solution)/shard_map/ppermute | solution.py:66
  2.1 3.5 %collective-permute-start.3 = (bf16[2,128,256]{2,1,0:T(8,128)(2,1)}, bf16[2,128,256]{2,1,0:T(8,128)(2,1)}, u32[]{:S(2)}, u32[]{:S(2)}) collective-permute-start(bf16[2,128,256]{2,1,0:T(8,128)(2,1)} %param.8), channel_id=1, source_target_pairs={{0,4},{4,8},{8,12},{1,5},{5,9},{9,13},{2,6},{6,10},{10,14},{3,7},{... | collective-permute-start | bytes 393224 | tf_op jit(solution)/shard_map/ppermute | solution.py:66
  5.6 2.9 %collective-permute-start.4 = (bf16[2,128,256]{2,1,0:T(8,128)(2,1)}, bf16[2,128,256]{2,1,0:T(8,128)(2,1)}, u32[]{:S(2)}, u32[]{:S(2)}) collective-permute-start(bf16[2,128,256]{2,1,0:T(8,128)(2,1)} %param.8), channel_id=1, source_target_pairs={{0,8},{4,12},{1,9},{5,13},{2,10},{6,14},{3,11},{7,15},{16,24},{20,... | collective-permute-start | bytes 393224 | tf_op jit(solution)/shard_map/ppermute | solution.py:66
  8.5 0.7 fusion.51
  10.1 0.5 convolution_convert_fusion
  10.9 0.8 pad_maximum_fusion.1
  11.7 1.3 %collective-permute-start.1 = (bf16[1040,128]{1,0:T(8,128)(2,1)}, bf16[1040,128]{1,0:T(8,128)(2,1)S(1)}, u32[]{:S(2)}, u32[]{:S(2)}) collective-permute-start(bf16[1040,128]{1,0:T(8,128)(2,1)} %pad_maximum_fusion.1), channel_id=1, source_target_pairs={{0,8},{4,12},{1,9},{5,13},{2,10},{6,14},{3,11},{7,15},{16,24},{20,... | collective-permute-start | bytes 798728 | tf_op jit(solution)/shard_map/ppermute | solution.py:66
  13.0 1.9 %collective-permute-start = (bf16[1040,128]{1,0:T(8,128)(2,1)}, bf16[1040,128]{1,0:T(8,128)(2,1)S(1)}, u32[]{:S(2)}, u32[]{:S(2)}) collective-permute-start(bf16[1040,128]{1,0:T(8,128)(2,1)} %pad_maximum_fusion.1), channel_id=1, source_target_pairs={{0,4},{4,8},{8,12},{1,5},{5,9},{9,13},{2,6},{6,10},{10,14},{3,7},{... | collective-permute-start | bytes 798728 | tf_op jit(solution)/shard_map/ppermute | solution.py:66
  15.2 0.3 bitcast_multiply_fusion.1
  15.6 2.3 %fusion.102 = f32[16,128,128]{1,2,0:T(8,128)} fusion(f32[16,128,128]{2,1,0:T(8,128)S(1)} %bitcast_multiply_fusion.1, bf16[16,128,128]{2,1,0:T(8,128)(2,1)S(1)} %copy-done.1), kind=kOutput, calls=%fused_computation.198 | convolution fusion | flops 402653184 | bytes 2621440 | tf_op jit(solution)/shard_map/hts,hsp->htp/dot_general | solution.py:161
  17.9 0.3 fusion.100
  18.7 0.7 collective-permute-start.2
  19.3 1.2 %fusion.101 = (f32[2,8,128]{2,1,0:T(8,128)S(1)}, f32[2,8,128,128]{2,3,1,0:T(8,128)S(1)}) fusion(bf16[2,8,128,128]{3,2,1,0:T(8,128)(2,1)S(1)} %bitcast.178, bf16[2,128,256]{2,1,0:T(8,128)(2,1)} %collective-permute-done.3, pred[]{:T(512)S(6)} %ge.51), kind=kOutput, calls=%fused_computation.197 | convolution fusion | flops 67893248 | bytes 1646593 | tf_op jit(solution)/shard_map/gptd,gkd->gptk/dot_general | solution.py:87
  20.5 1.1 %fusion.98 = (f32[2,8,128]{2,1,0:T(8,128)S(1)}, f32[2,8,128,128]{2,3,1,0:T(8,128)S(1)}) fusion(bf16[2,8,128,128]{3,2,1,0:T(8,128)(2,1)S(1)} %bitcast.180, bf16[2,128,256]{2,1,0:T(8,128)(2,1)} %collective-permute-done.5, pred[]{:T(512)S(6)} %ge.53), kind=kOutput, calls=%fused_computation.194 | convolution fusion | flops 67893248 | bytes 1646593 | tf_op jit(solution)/shard_map/gptd,gkd->gptk/dot_general | solution.py:87
  21.7 1.8 %collective-permute-done.4 = bf16[2,128,256]{2,1,0:T(8,128)(2,1)} collective-permute-done((bf16[2,128,256]{2,1,0:T(8,128)(2,1)}, bf16[2,128,256]{2,1,0:T(8,128)(2,1)}, u32[]{:S(2)}, u32[]{:S(2)}) %collective-permute-start.4) | collective-permute-done | bytes 131104 | tf_op jit(solution)/shard_map/ppermute | solution.py:66
  23.5 1.1 %fusion.99 = (f32[2,8,128]{2,1,0:T(8,128)S(1)}, f32[2,8,128,128]{2,3,1,0:T(8,128)S(1)}) fusion(bf16[2,8,128,128]{3,2,1,0:T(8,128)(2,1)S(1)} %bitcast.179, bf16[2,128,256]{2,1,0:T(8,128)(2,1)} %collective-permute-done.4, pred[]{:T(512)S(6)} %ge.52), kind=kOutput, calls=%fused_computation.195 | convolution fusion | flops 67893248 | bytes 1646593 | tf_op jit(solution)/shard_map/gptd,gkd->gptk/dot_general | solution.py:87
  24.7 0.3 fusion.32
  25.0 1.0 %fusion.16 = (f32[2,8,128]{2,1,0:T(8,128)S(1)}, f32[2,8,128]{2,1,0:T(8,128)S(1)}, f32[2,8,128]{2,1,0:T(8,128)S(1)}, f32[2,8,128]{2,1,0:T(8,128)S(1)}) fusion(f32[2,8,128,128]{2,3,1,0:T(8,128)S(1)} %get-tuple-element.49, f32[2,8,128]{2,1,0:T(8,128)S(1)} %maximum_maximum_fusion, f32[2,8,128,128]{2,3,1,0:T(8,128)S(1)} %get-tuple-element.47, ...), kind=kLoop, calls=%fused_computation.47 | loop fusion | flops 2088960 | bytes 4235264 | tf_op jit(solution)/shard_map/reduce_sum | solution.py:103
  26.0 1.2 %fusion.28 = f32[2,8,128,128]{2,3,1,0:T(8,128)S(1)} fusion(f32[2,8,128,128]{2,3,1,0:T(8,128)S(1)} %get-tuple-element.43, f32[2,8,128]{2,1,0:T(8,128)S(1)} %maximum_maximum_fusion, bf16[2,128,256]{2,1,0:T(8,128)(2,1)} %collective-permute-done.5), kind=kOutput, calls=%fused_computation.65 | convolution fusion | flops 67633152 | bytes 2170880 | tf_op jit(solution)/shard_map/gptk,gkd->gptd/dot_general | solution.py:104
  27.2 1.2 %convolution_add_fusion.2 = f32[2,8,128,128]{2,3,1,0:T(8,128)S(1)} fusion(f32[2,8,128,128]{2,3,1,0:T(8,128)S(1)} %fusion.32, f32[2,8,128,128]{2,3,1,0:T(8,128)S(1)} %get-tuple-element.49, f32[2,8,128]{2,1,0:T(8,128)S(1)} %maximum_maximum_fusion, bf16[2,128,256]{2,1,0:T(8,128)(2,1)} %collective-permute-done.3), kind=kOutput, calls=%fused_computation.8 | convolution fusion | flops 67895296 | bytes 3219456 | tf_op jit(solution)/shard_map/gptk,gkd->gptd/dot_general | solution.py:104
  28.4 1.4 %multiply_reduce_fusion.2 = (f32[2,8,128]{2,1,0:T(8,128)S(1)}, f32[2,8,128,128]{2,3,1,0:T(8,128)S(1)}) fusion(f32[2,8,128]{2,1,0:T(8,128)S(1)} %add_add_fusion, f32[2,8,128,128]{2,3,1,0:T(8,128)S(1)} %fusion.28, f32[2,8,128,128]{2,3,1,0:T(8,128)S(1)} %convolution_add_fusion.2, bf16[2,128,256]{2,1,0:T(8,128)(2,1)} %collective-permute-done.4, ...), kind=kOutput, calls=%fused_computation.38 | convolution fusion | flops 69466112 | bytes 4284416 | tf_op jit(solution)/shard_map/gptk,gkd->gptd/dot_general | solution.py:104
  29.8 5.2 %collective-permute-done.1 = bf16[1040,128]{1,0:T(8,128)(2,1)S(1)} collective-permute-done((bf16[1040,128]{1,0:T(8,128)(2,1)}, bf16[1040,128]{1,0:T(8,128)(2,1)S(1)}, u32[]{:S(2)}, u32[]{:S(2)}) %collective-permute-start.1) | collective-permute-done | bytes 266272 | tf_op jit(solution)/shard_map/ppermute | solution.py:66
  34.9 5.0 %collective-permute-done = bf16[1040,128]{1,0:T(8,128)(2,1)S(1)} collective-permute-done((bf16[1040,128]{1,0:T(8,128)(2,1)}, bf16[1040,128]{1,0:T(8,128)(2,1)S(1)}, u32[]{:S(2)}, u32[]{:S(2)}) %collective-permute-start) | collective-permute-done | bytes 266272 | tf_op jit(solution)/shard_map/ppermute | solution.py:66
  40.0 0.3 fusion.24
  40.4 0.8 %copy-done.8 = f32[16,128,128]{1,2,0:T(8,128)S(1)} copy-done((f32[16,128,128]{1,2,0:T(8,128)S(1)}, f32[16,128,128]{1,2,0:T(8,128)}, u32[]{:S(2)}) %copy-start.8) | copy-done | bytes 1048600
  41.3 2.0 %multiply_reduce_fusion.3 = (f32[16,128]{1,0:T(8,128)S(1)}, f32[16,128,128]{1,2,0:T(8,128)S(1)}) fusion(bf16[16,128,128]{1,2,0:T(8,128)(2,1)S(1)} %copy.48, f32[16]{0:T(128)S(1)} %copy-done.16, f32[16,128,128]{1,2,0:T(8,128)S(1)} %copy-done.8, f32[16,64,128]{2,1,0:T(8,128)S(1)} %fusion.24, f32[16,128,64]{1,2,0:T(8,128)S(1)} %bitcast.181, ...), kind=kOutput, calls=%fused_computation.43 | convolution fusion | flops 203159552 | bytes 3686464 | tf_op jit(solution)/shard_map/htn,hnp->htp/dot_general | solution.py:169
  43.3 0.4 multiply_reduce_fusion.1
  43.7 0.6 multiply_reduce_fusion
  44.3 2.1 %fusion.36 = f32[16,64,128]{2,1,0:T(8,128)S(1)} fusion(f32[16,128,128]{1,2,0:T(8,128)S(1)} %get-tuple-element.21, f32[16,128,64]{1,2,0:T(8,128)S(1)} %bitcast.182, f32[16,128]{1,0:T(8,128)S(1)} %get-tuple-element.31), kind=kOutput, calls=%fused_computation.73 | convolution fusion | flops 201457664 | bytes 2105344 | tf_op jit(solution)/shard_map/htn,htp->hnp/dot_general | solution.py:178
  46.5 0.9 %slice-done = bf16[1024,128]{1,0:T(8,128)(2,1)S(1)} async-done(((bf16[1040,128]{1,0:T(8,128)(2,1)}), bf16[1024,128]{1,0:T(8,128)(2,1)S(1)}, s32[]{:S(2)}) %slice-start) | async-done | bytes 262168 | tf_op jit(solution)/shard_map/slice | solution.py:38
  47.5 0.4 multiply_reduce_fusion.4
  48.1 0.7 collective-permute-start.8
  48.8 1.3 %collective-permute-start.7 = (bf16[1040,128]{1,0:T(8,128)(2,1)S(1)}, bf16[1040,128]{1,0:T(8,128)(2,1)S(1)}, u32[]{:S(2)}, u32[]{:S(2)}) collective-permute-start(bf16[1040,128]{1,0:T(8,128)(2,1)S(1)} %pad_maximum_fusion.2), channel_id=1, source_target_pairs={{8,0},{12,4},{9,1},{13,5},{10,2},{14,6},{11,3},{15,7},{24,16},{28,... | collective-permute-start | bytes 798728 | tf_op jit(solution)/shard_map/ppermute | solution.py:66
  50.1 2.1 %collective-permute-start.6 = (bf16[1040,128]{1,0:T(8,128)(2,1)S(1)}, bf16[1040,128]{1,0:T(8,128)(2,1)S(1)}, u32[]{:S(2)}, u32[]{:S(2)}) collective-permute-start(bf16[1040,128]{1,0:T(8,128)(2,1)S(1)} %pad_maximum_fusion.2), channel_id=1, source_target_pairs={{4,0},{8,4},{12,8},{5,1},{9,5},{13,9},{6,2},{10,6},{14,10},{7,3},{... | collective-permute-start | bytes 798728 | tf_op jit(solution)/shard_map/ppermute | solution.py:66
  52.2 2.3 %fusion.103 = f32[16,128,128]{1,2,0:T(8,128)S(1)} fusion(f32[16,128,128]{2,1,0:T(8,128)} %copy-done.2, f32[16,128,128]{1,2,0:T(8,128)S(1)} %get-tuple-element.21), kind=kOutput, calls=%fused_computation.199 | convolution fusion | flops 402653184 | bytes 3145728 | tf_op jit(solution)/shard_map/hts,htp->hsp/dot_general | solution.py:191
  54.5 1.2 %convolution_multiply_fusion = f32[16,128,128]{2,1,0:T(8,128)S(1)} fusion(f32[16,128,128]{1,2,0:T(8,128)S(1)} %get-tuple-element.21, bf16[16,128,128]{2,1,0:T(8,128)(2,1)S(1)} %copy-done.1, f32[16,128]{1,0:T(8,128)S(1)} %reduce_window_sum.21, pred[128,128]{1,0:T(8,128)(4,1)S(1)} %copy.44), kind=kOutput, calls=%fused_computation | convolution fusion | flops 403701760 | bytes 2646016 | tf_op jit(solution)/shard_map/htp,hsp->hts/dot_general | solution.py:193
  55.8 1.0 %convolution_multiply_fusion.6 = f32[16,128,64]{1,2,0:T(8,128)S(1)} fusion(f32[16,128,128]{1,2,0:T(8,128)S(1)} %get-tuple-element.21, f32[16,64,128]{2,1,0:T(8,128)S(1)} %copy-done.7, f32[16,128]{1,0:T(8,128)S(1)} %get-tuple-element.31), kind=kOutput, calls=%fused_computation.21 | convolution fusion | flops 201457664 | bytes 2105344 | tf_op jit(solution)/shard_map/hnp,htp->htn/dot_general | solution.py:197
  56.8 0.4 copy-done.5
  57.2 2.9 %convolution_add_fusion.3 = f32[16,128,64]{1,2,0:T(8,128)} fusion(f32[16,128,64]{1,2,0:T(8,128)S(1)} %convolution_multiply_fusion.6, f32[16,128,128]{2,1,0:T(8,128)S(1)} %convolution_multiply_fusion, f32[16,128,64]{1,2,0:T(8,128)S(1)} %bitcast.185), kind=kOutput, calls=%fused_computation.22 | convolution fusion | flops 201457664 | bytes 2621440 | tf_op jit(solution)/shard_map/hts,hsn->htn/dot_general | solution.py:196
  60.1 0.8 collective-permute-done.7
  60.9 9.3 %collective-permute-done.6 = bf16[1040,128]{1,0:T(8,128)(2,1)S(1)} collective-permute-done((bf16[1040,128]{1,0:T(8,128)(2,1)S(1)}, bf16[1040,128]{1,0:T(8,128)(2,1)S(1)}, u32[]{:S(2)}, u32[]{:S(2)}) %collective-permute-start.6) | collective-permute-done | bytes 266272 | tf_op jit(solution)/shard_map/ppermute | solution.py:66
  70.4 2.0 %fusion.10 = f32[16,128,64]{1,2,0:T(8,128)} fusion(bf16[16,128,128]{2,1,0:T(8,128)(2,1)S(1)} %copy-done.1, f32[16,128]{1,0:T(8,128)S(1)} %get-tuple-element.32, bf16[16,64,128]{2,1,0:T(8,128)(2,1)S(1)} %bitcast.191, f32[16,64,128]{2,1,0:T(8,128)S(1)} %bitcast.187, bf16[16,64,128]{2,1,0:T(8,128)(2,1)S(1)} %bitcast.189, f32[16]{0:T(128)S(1)} %get-tuple-element.34, ...), kind=kOutput, calls=%fused_computation.25 | convolution fusion | flops 202244096 | bytes 2105472 | tf_op jit(solution)/shard_map/hnp,hsp->hsn/dot_general | solution.py:228
  72.4 2.8 %fusion.12 = (f32[16,128]{1,0:T(8,128)S(1)}, bf16[16,128,128]{1,2,0:T(8,128)(2,1)}) fusion(bf16[16,128,128]{1,2,0:T(8,128)(2,1)S(1)} %copy.48, f32[16,128,128]{1,2,0:T(8,128)S(1)} %get-tuple-element.21, f32[16]{0:T(128)S(1)} %copy-done.16, f32[16,128,128]{1,2,0:T(8,128)S(1)} %fusion.103, bf16[16,64,128]{2,1,0:T(8,128)(2,1)S(1)} %bitcast.192, ...), kind=kOutput, calls=%fused_computation.28 | convolution fusion | flops 204077056 | bytes 4735168 | tf_op jit(solution)/shard_map/hsn,hnp->hsp/dot_general | solution.py:223
  75.2 1.2 %reduce_window_sum.22 = f32[16,128]{1,0:T(8,128)S(1)} reduce-window(f32[16,128]{1,0:T(8,128)S(1)} %sub.114, f32[]{:T(128)} %constant.12.clone.1), window={size=1x128 pad=0_0x0_127}, to_apply=%region_19.20 | reduce-window | flops 260096 | bytes 16388 | tf_op jit(solution)/shard_map/body/reduce_window_sum | solution.py:225
  76.5 2.4 %convolution_add_fusion.4 = f32[16,128,64]{1,2,0:T(8,128)S(1)} fusion(f32[16,128,64]{1,2,0:T(8,128)} %fusion.10, f32[16,128,128]{2,1,0:T(8,128)} %copy-done.3, f32[16,128,64]{1,2,0:T(8,128)S(1)} %bitcast.183), kind=kOutput, calls=%fused_computation.23 | convolution fusion | flops 201457664 | bytes 2621440 | tf_op jit(solution)/shard_map/hts,htn->hsn/dot_general | solution.py:195
  79.0 0.7 copy.61
  80.0 1.0 %copy.60 = bf16[16,128,128]{2,1,0:T(8,128)(2,1)} copy(bf16[16,128,128]{1,2,0:T(8,128)(2,1)S(1)} %copy-done.10) | data formatting | bytes 1048576
  81.0 0.7 broadcast_add_fusion
  (85 shorter events, 2.8 us)
Async XLA Ops:
  0.6 17.3 %copy-start = (bf16[16,128,128]{2,1,0:T(8,128)(2,1)S(1)}, bf16[16,128,128]{2,1,0:T(8,128)(2,1)}, u32[]{:S(2)}) copy-start(bf16[16,128,128]{2,1,0:T(8,128)(2,1)} %param.7) | copy-start | bytes 1572868
  0.6 9.2 %copy-start.13 = (bf16[2,128,128]{2,1,0:T(8,128)(2,1)S(1)}, bf16[2,128,128]{2,1,0:T(8,128)(2,1)}, u32[]{:S(2)}) copy-start(bf16[2,128,128]{2,1,0:T(8,128)(2,1)} %param.10) | copy-start | bytes 196612
  0.7 9.5 %copy-start.1 = (bf16[16,128,128]{2,1,0:T(8,128)(2,1)S(1)}, bf16[16,128,128]{2,1,0:T(8,128)(2,1)}, u32[]{:S(2)}) copy-start(bf16[16,128,128]{2,1,0:T(8,128)(2,1)} %param.9) | copy-start | bytes 1572868
  0.7 19.8 %collective-permute-start.5 = (bf16[2,128,256]{2,1,0:T(8,128)(2,1)}, bf16[2,128,256]{2,1,0:T(8,128)(2,1)}, u32[]{:S(2)}, u32[]{:S(2)}) collective-permute-start(bf16[2,128,256]{2,1,0:T(8,128)(2,1)} %param.8), channel_id=1, source_target_pairs={{0,12},{1,13},{2,14},{3,15},{16,28},{17,29},{18,30},{19,31}} | collective-permute-start | bytes 393224 | tf_op jit(solution)/shard_map/ppermute | solution.py:66
  2.1 16.5 %collective-permute-start.3 = (bf16[2,128,256]{2,1,0:T(8,128)(2,1)}, bf16[2,128,256]{2,1,0:T(8,128)(2,1)}, u32[]{:S(2)}, u32[]{:S(2)}) collective-permute-start(bf16[2,128,256]{2,1,0:T(8,128)(2,1)} %param.8), channel_id=1, source_target_pairs={{0,4},{4,8},{8,12},{1,5},{5,9},{9,13},{2,6},{6,10},{10,14},{3,7},{... | collective-permute-start | bytes 393224 | tf_op jit(solution)/shard_map/ppermute | solution.py:66
  5.6 17.9 %collective-permute-start.4 = (bf16[2,128,256]{2,1,0:T(8,128)(2,1)}, bf16[2,128,256]{2,1,0:T(8,128)(2,1)}, u32[]{:S(2)}, u32[]{:S(2)}) collective-permute-start(bf16[2,128,256]{2,1,0:T(8,128)(2,1)} %param.8), channel_id=1, source_target_pairs={{0,8},{4,12},{1,9},{5,13},{2,10},{6,14},{3,11},{7,15},{16,24},{20,... | collective-permute-start | bytes 393224 | tf_op jit(solution)/shard_map/ppermute | solution.py:66
  10.1 0.8 copy-start.4
  11.7 23.2 %collective-permute-start.1 = (bf16[1040,128]{1,0:T(8,128)(2,1)}, bf16[1040,128]{1,0:T(8,128)(2,1)S(1)}, u32[]{:S(2)}, u32[]{:S(2)}) collective-permute-start(bf16[1040,128]{1,0:T(8,128)(2,1)} %pad_maximum_fusion.1), channel_id=1, source_target_pairs={{0,8},{4,12},{1,9},{5,13},{2,10},{6,14},{3,11},{7,15},{16,24},{20,... | collective-permute-start | bytes 798728 | tf_op jit(solution)/shard_map/ppermute | solution.py:66
  13.0 26.9 %collective-permute-start = (bf16[1040,128]{1,0:T(8,128)(2,1)}, bf16[1040,128]{1,0:T(8,128)(2,1)S(1)}, u32[]{:S(2)}, u32[]{:S(2)}) collective-permute-start(bf16[1040,128]{1,0:T(8,128)(2,1)} %pad_maximum_fusion.1), channel_id=1, source_target_pairs={{0,4},{4,8},{8,12},{1,5},{5,9},{9,13},{2,6},{6,10},{10,14},{3,7},{... | collective-permute-start | bytes 798728 | tf_op jit(solution)/shard_map/ppermute | solution.py:66
  15.6 2.3 %copy-start.2 = (f32[16,128,128]{2,1,0:T(8,128)}, f32[16,128,128]{2,1,0:T(8,128)S(1)}, u32[]{:S(2)}) copy-start(f32[16,128,128]{2,1,0:T(8,128)S(1)} %bitcast_multiply_fusion.1) | copy-start | bytes 3145732
  15.6 2.3 %copy-start.15 = (bf16[2,128,256]{2,1,0:T(8,128)(2,1)S(1)}, bf16[2,128,256]{2,1,0:T(8,128)(2,1)}, u32[]{:S(2)}) copy-start(bf16[2,128,256]{2,1,0:T(8,128)(2,1)} %param.8) | copy-start | bytes 393220
  18.7 21.3 %collective-permute-start.2 = (bf16[1040,128]{1,0:T(8,128)(2,1)}, bf16[1040,128]{1,0:T(8,128)(2,1)S(1)}, u32[]{:S(2)}, u32[]{:S(2)}) collective-permute-start(bf16[1040,128]{1,0:T(8,128)(2,1)} %pad_maximum_fusion.1), channel_id=1, source_target_pairs={{0,12},{1,13},{2,14},{3,15},{16,28},{17,29},{18,30},{19,31}} | collective-permute-start | bytes 798728 | tf_op jit(solution)/shard_map/ppermute | solution.py:66
  28.4 11.6 %copy-start.14 = (f32[16,64,128]{2,1,0:T(8,128)S(1)}, f32[16,64,128]{2,1,0:T(8,128)}, u32[]{:S(2)}) copy-start(f32[16,64,128]{2,1,0:T(8,128)} %param.13) | copy-start | bytes 1572868
  34.9 5.4 %copy-start.12 = (bf16[1040,128]{1,0:T(8,128)(2,1)}, bf16[1040,128]{1,0:T(8,128)(2,1)S(1)}, u32[]{:S(2)}) copy-start(bf16[1040,128]{1,0:T(8,128)(2,1)S(1)} %collective-permute-done.1) | copy-start | bytes 798724
  39.9 6.5 %copy-start.11 = (bf16[1040,128]{1,0:T(8,128)(2,1)}, bf16[1040,128]{1,0:T(8,128)(2,1)S(1)}, u32[]{:S(2)}) copy-start(bf16[1040,128]{1,0:T(8,128)(2,1)S(1)} %collective-permute-done) | copy-start | bytes 798724
  40.0 1.2 %copy-start.8 = (f32[16,128,128]{1,2,0:T(8,128)S(1)}, f32[16,128,128]{1,2,0:T(8,128)}, u32[]{:S(2)}) copy-start(f32[16,128,128]{1,2,0:T(8,128)} %fusion.102) | copy-start | bytes 3145732
  40.3 6.2 %copy-start.6 = (f32[16,64,128]{2,1,0:T(8,128)}, f32[16,64,128]{2,1,0:T(8,128)S(1)}, u32[]{:S(2)}) copy-start(f32[16,64,128]{2,1,0:T(8,128)S(1)} %fusion.24) | copy-start | bytes 1572868
  40.4 0.8 %copy-start.16 = (f32[16]{0:T(128)S(1)}, f32[16]{0:T(128)}, u32[]{:S(2)}) copy-start(f32[16]{0:T(128)} %param.12) | copy-start | bytes 196
  46.5 1.0 %slice-start = ((bf16[1040,128]{1,0:T(8,128)(2,1)}), bf16[1024,128]{1,0:T(8,128)(2,1)S(1)}, s32[]{:S(2)}) async-start(bf16[1040,128]{1,0:T(8,128)(2,1)} %copy-done.11), calls=%async_computation | async-start | bytes 524288 | tf_op jit(solution)/shard_map/slice | solution.py:38
  46.5 1.0 %slice-start.1 = ((bf16[1040,128]{1,0:T(8,128)(2,1)}), bf16[1024,128]{1,0:T(8,128)(2,1)S(1)}, s32[]{:S(2)}) async-start(bf16[1040,128]{1,0:T(8,128)(2,1)} %copy-done.12), calls=%async_computation.1 | async-start | bytes 524288 | tf_op jit(solution)/shard_map/slice | solution.py:38
  48.1 12.0 %collective-permute-start.8 = (bf16[1040,128]{1,0:T(8,128)(2,1)S(1)}, bf16[1040,128]{1,0:T(8,128)(2,1)S(1)}, u32[]{:S(2)}, u32[]{:S(2)}) collective-permute-start(bf16[1040,128]{1,0:T(8,128)(2,1)S(1)} %pad_maximum_fusion.2), channel_id=1, source_target_pairs={{12,0},{13,1},{14,2},{15,3},{28,16},{29,17},{30,18},{31,19}} | collective-permute-start | bytes 798728 | tf_op jit(solution)/shard_map/ppermute | solution.py:66
  48.8 12.1 %collective-permute-start.7 = (bf16[1040,128]{1,0:T(8,128)(2,1)S(1)}, bf16[1040,128]{1,0:T(8,128)(2,1)S(1)}, u32[]{:S(2)}, u32[]{:S(2)}) collective-permute-start(bf16[1040,128]{1,0:T(8,128)(2,1)S(1)} %pad_maximum_fusion.2), channel_id=1, source_target_pairs={{8,0},{12,4},{9,1},{13,5},{10,2},{14,6},{11,3},{15,7},{24,16},{28,... | collective-permute-start | bytes 798728 | tf_op jit(solution)/shard_map/ppermute | solution.py:66
  50.1 20.1 %collective-permute-start.6 = (bf16[1040,128]{1,0:T(8,128)(2,1)S(1)}, bf16[1040,128]{1,0:T(8,128)(2,1)S(1)}, u32[]{:S(2)}, u32[]{:S(2)}) collective-permute-start(bf16[1040,128]{1,0:T(8,128)(2,1)S(1)} %pad_maximum_fusion.2), channel_id=1, source_target_pairs={{4,0},{8,4},{12,8},{5,1},{9,5},{13,9},{6,2},{10,6},{14,10},{7,3},{... | collective-permute-start | bytes 798728 | tf_op jit(solution)/shard_map/ppermute | solution.py:66
  54.5 1.2 %copy-start.7 = (f32[16,64,128]{2,1,0:T(8,128)S(1)}, f32[16,64,128]{2,1,0:T(8,128)}, u32[]{:S(2)}) copy-start(f32[16,64,128]{2,1,0:T(8,128)} %copy-done.6) | copy-start | bytes 1572868
  55.7 1.1 %copy-start.3 = (f32[16,128,128]{2,1,0:T(8,128)}, f32[16,128,128]{2,1,0:T(8,128)S(1)}, u32[]{:S(2)}) copy-start(f32[16,128,128]{2,1,0:T(8,128)S(1)} %convolution_multiply_fusion) | copy-start | bytes 3145732
  55.8 1.4 %copy-start.5 = (f32[2,8,128,64]{2,3,1,0:T(8,128)S(1)}, f32[2,8,128,64]{2,3,1,0:T(8,128)}, u32[]{:S(2)}) copy-start(f32[2,8,128,64]{2,3,1,0:T(8,128)} %copy-done.4) | copy-start | bytes 1572868
  76.4 2.4 %copy-start.9 = (f32[16,128,64]{1,2,0:T(8,128)S(1)}, f32[16,128,64]{1,2,0:T(8,128)}, u32[]{:S(2)}) copy-start(f32[16,128,64]{1,2,0:T(8,128)} %convolution_add_fusion.3) | copy-start | bytes 1572868
  78.9 1.0 %copy-start.10 = (bf16[16,128,128]{1,2,0:T(8,128)(2,1)S(1)}, bf16[16,128,128]{1,2,0:T(8,128)(2,1)}, u32[]{:S(2)}) copy-start(bf16[16,128,128]{1,2,0:T(8,128)(2,1)} %get-tuple-element.27) | copy-start | bytes 1572868

commit v12 on v11

--- a/solution.py
+++ b/solution.py
@@ -222,7 +222,8 @@
 
     state_dx = local_dx + jnp.einsum("hsn,hnp->hsp", weighted_in, incoming, precision=highest)
     terms = forward_term - jnp.sum(inputs_wide * state_dx, axis=2)
-    grad_log_decay = later_sum[:, None] + lax.cumsum(terms, axis=1, reverse=True)
+    upper = (order_ids[:, None] <= order_ids[None, :]).astype(jnp.float32)
+    grad_log_decay = later_sum[:, None] + jnp.einsum("hu,su->hs", terms, upper, precision=highest)
     grad_input_maps = (
         local_din
         + jnp.einsum("hnp,hsp->hsn", incoming, inputs_wide, precision=highest) * to_end[..., None]

time: 82.4 us -> 79 us (0.959)
  matrix products: 29.7 us -> 27.5 us
  other arithmetic: 7.18 us -> 5.27 us
  waiting for transfers between devices: 22.1 us -> 23.2 us
    dot_general x1, matrix products: 2.44 us -> 1.03 us  [body(): local_din = jnp.einsum('hts,htn->hsn', paired, out_heads, precision=highest)]
    another operation x1 -> x0, other arithmetic: 1.24 us -> none  [body(): lax.cumsum(terms, axis=1, reverse=True)]
    ppermute x9, waiting for transfers between devices: 22.1 us -> 23.2 us  [shifted(): moved.append(lax.ppermute(x, 'seq', pairs))]
    unnamed x40 -> x36, local copies, waits for them, and re-layouts: 4.04 us -> 3.68 us
where the time goes in v12:
time: 79 us; the launch traced here: 78.3 us
  matrix products  27.5 us (35%)
  waiting for transfers between devices  23.2 us (29%)
  starting transfers between devices  15.8 us (20%)
  other arithmetic  5.27 us (7%)
  local copies, waits for them, and re-layouts  5.2 us (7%)
  between operations  1.29 us (2%)
    ppermute x9, waiting for transfers between devices, shifted(): moved.append(lax.ppermute(x, 'seq', pairs))  23.2 us
    ppermute x9, starting transfers between devices, shifted(): moved.append(lax.ppermute(x, 'seq', pairs))  15.8 us
    dot_general x4, matrix products, teacher_rows(): jnp.einsum('gptk,gkd->gptd', exponentials.astype(jnp.bfloat16), block[......  4.06 us
    dot_general x4, matrix products, teacher_rows(): jnp.einsum('gptd,gkd->gptk', grouped, block[..., :head_width], preferred_...  3.76 us
    unnamed x36, local copies, waits for them, and re-layouts  3.68 us
    dot_general x1, matrix products, body(): jnp.einsum('hsn,hnp->hsp', weighted_in, incoming, precision=highest)  2.84 us
    dot_general x1, matrix products, body(): local_dx = jnp.einsum('hts,htp->hsp', mixing, grad_out, precision=highest)  2.31 us
    dot_general x1, matrix products, body(): jnp.einsum('hts,hsp->htp', mixing, inputs_wide, precision=highest)  2.26 us
  transfers between devices with their start and end apart: 9, of which 5 were waited for; matrix products, arithmetic and copies ran while one was open for 28% of the time, Pallas kernels for 0%

profile of v12, /device:TPU:8, one launch (start us, length us, event | category | flops | bytes accessed | tf_op | source)
XLA Modules:
  0.0 78.3 jit_solution(6971752697493839449)
XLA Ops:
  0.7 1.5 %collective-permute-start.5 = (bf16[2,128,256]{2,1,0:T(8,128)(2,1)}, bf16[2,128,256]{2,1,0:T(8,128)(2,1)}, u32[]{:S(2)}, u32[]{:S(2)}) collective-permute-start(bf16[2,128,256]{2,1,0:T(8,128)(2,1)} %param.8), channel_id=1, source_target_pairs={{0,12},{1,13},{2,14},{3,15},{16,28},{17,29},{18,30},{19,31}} | collective-permute-start | bytes 393224 | tf_op jit(solution)/shard_map/ppermute | solution.py:66
  2.1 3.5 %collective-permute-start.3 = (bf16[2,128,256]{2,1,0:T(8,128)(2,1)}, bf16[2,128,256]{2,1,0:T(8,128)(2,1)}, u32[]{:S(2)}, u32[]{:S(2)}) collective-permute-start(bf16[2,128,256]{2,1,0:T(8,128)(2,1)} %param.8), channel_id=1, source_target_pairs={{0,4},{4,8},{8,12},{1,5},{5,9},{9,13},{2,6},{6,10},{10,14},{3,7},{... | collective-permute-start | bytes 393224 | tf_op jit(solution)/shard_map/ppermute | solution.py:66
  5.6 2.9 %collective-permute-start.4 = (bf16[2,128,256]{2,1,0:T(8,128)(2,1)}, bf16[2,128,256]{2,1,0:T(8,128)(2,1)}, u32[]{:S(2)}, u32[]{:S(2)}) collective-permute-start(bf16[2,128,256]{2,1,0:T(8,128)(2,1)} %param.8), channel_id=1, source_target_pairs={{0,8},{4,12},{1,9},{5,13},{2,10},{6,14},{3,11},{7,15},{16,24},{20,... | collective-permute-start | bytes 393224 | tf_op jit(solution)/shard_map/ppermute | solution.py:66
  8.5 0.7 fusion.51
  9.3 0.3 reduce_window_sum.11
  10.1 0.5 convolution_convert_fusion
  10.9 0.8 pad_maximum_fusion.1
  11.7 1.3 %collective-permute-start.1 = (bf16[1040,128]{1,0:T(8,128)(2,1)}, bf16[1040,128]{1,0:T(8,128)(2,1)S(1)}, u32[]{:S(2)}, u32[]{:S(2)}) collective-permute-start(bf16[1040,128]{1,0:T(8,128)(2,1)} %pad_maximum_fusion.1), channel_id=1, source_target_pairs={{0,8},{4,12},{1,9},{5,13},{2,10},{6,14},{3,11},{7,15},{16,24},{20,... | collective-permute-start | bytes 798728 | tf_op jit(solution)/shard_map/ppermute | solution.py:66
  13.0 1.9 %collective-permute-start = (bf16[1040,128]{1,0:T(8,128)(2,1)}, bf16[1040,128]{1,0:T(8,128)(2,1)S(1)}, u32[]{:S(2)}, u32[]{:S(2)}) collective-permute-start(bf16[1040,128]{1,0:T(8,128)(2,1)} %pad_maximum_fusion.1), channel_id=1, source_target_pairs={{0,4},{4,8},{8,12},{1,5},{5,9},{9,13},{2,6},{6,10},{10,14},{3,7},{... | collective-permute-start | bytes 798728 | tf_op jit(solution)/shard_map/ppermute | solution.py:66
  15.2 0.3 bitcast_multiply_fusion.1
  15.6 2.3 %fusion.103 = f32[16,128,128]{1,2,0:T(8,128)} fusion(f32[16,128,128]{2,1,0:T(8,128)S(1)} %bitcast_multiply_fusion.1, bf16[16,128,128]{2,1,0:T(8,128)(2,1)S(1)} %copy-done.1), kind=kOutput, calls=%fused_computation.200 | convolution fusion | flops 402653184 | bytes 2621440 | tf_op jit(solution)/shard_map/hts,hsp->htp/dot_general | solution.py:161
  17.9 0.3 fusion.101
  18.2 0.3 copy.48
  18.7 0.7 collective-permute-start.2
  19.3 1.1 %fusion.102 = (f32[2,8,128]{2,1,0:T(8,128)S(1)}, f32[2,8,128,128]{2,3,1,0:T(8,128)S(1)}) fusion(bf16[2,8,128,128]{3,2,1,0:T(8,128)(2,1)S(1)} %bitcast.178, bf16[2,128,256]{2,1,0:T(8,128)(2,1)} %collective-permute-done.3, pred[]{:T(512)S(6)} %ge.55), kind=kOutput, calls=%fused_computation.199 | convolution fusion | flops 67893248 | bytes 1646593 | tf_op jit(solution)/shard_map/gptd,gkd->gptk/dot_general | solution.py:87
  20.5 1.1 %fusion.99 = (f32[2,8,128]{2,1,0:T(8,128)S(1)}, f32[2,8,128,128]{2,3,1,0:T(8,128)S(1)}) fusion(bf16[2,8,128,128]{3,2,1,0:T(8,128)(2,1)S(1)} %bitcast.180, bf16[2,128,256]{2,1,0:T(8,128)(2,1)} %collective-permute-done.5, pred[]{:T(512)S(6)} %ge.57), kind=kOutput, calls=%fused_computation.196 | convolution fusion | flops 67893248 | bytes 1646593 | tf_op jit(solution)/shard_map/gptd,gkd->gptk/dot_general | solution.py:87
  21.7 1.8 %collective-permute-done.4 = bf16[2,128,256]{2,1,0:T(8,128)(2,1)} collective-permute-done((bf16[2,128,256]{2,1,0:T(8,128)(2,1)}, bf16[2,128,256]{2,1,0:T(8,128)(2,1)}, u32[]{:S(2)}, u32[]{:S(2)}) %collective-permute-start.4) | collective-permute-done | bytes 131104 | tf_op jit(solution)/shard_map/ppermute | solution.py:66
  23.5 1.1 %fusion.100 = (f32[2,8,128]{2,1,0:T(8,128)S(1)}, f32[2,8,128,128]{2,3,1,0:T(8,128)S(1)}) fusion(bf16[2,8,128,128]{3,2,1,0:T(8,128)(2,1)S(1)} %bitcast.179, bf16[2,128,256]{2,1,0:T(8,128)(2,1)} %collective-permute-done.4, pred[]{:T(512)S(6)} %ge.56), kind=kOutput, calls=%fused_computation.197 | convolution fusion | flops 67893248 | bytes 1646593 | tf_op jit(solution)/shard_map/gptd,gkd->gptk/dot_general | solution.py:87
  24.7 0.3 fusion.32
  25.0 1.0 %fusion.16 = (f32[2,8,128]{2,1,0:T(8,128)S(1)}, f32[2,8,128]{2,1,0:T(8,128)S(1)}, f32[2,8,128]{2,1,0:T(8,128)S(1)}, f32[2,8,128]{2,1,0:T(8,128)S(1)}) fusion(f32[2,8,128,128]{2,3,1,0:T(8,128)S(1)} %get-tuple-element.49, f32[2,8,128]{2,1,0:T(8,128)S(1)} %maximum_maximum_fusion, f32[2,8,128,128]{2,3,1,0:T(8,128)S(1)} %get-tuple-element.47, ...), kind=kLoop, calls=%fused_computation.48 | loop fusion | flops 2088960 | bytes 4235264 | tf_op jit(solution)/shard_map/reduce_sum | solution.py:103
  26.0 1.2 %fusion.28 = f32[2,8,128,128]{2,3,1,0:T(8,128)S(1)} fusion(f32[2,8,128,128]{2,3,1,0:T(8,128)S(1)} %get-tuple-element.43, f32[2,8,128]{2,1,0:T(8,128)S(1)} %maximum_maximum_fusion, bf16[2,128,256]{2,1,0:T(8,128)(2,1)} %collective-permute-done.5), kind=kOutput, calls=%fused_computation.66 | convolution fusion | flops 67633152 | bytes 2170880 | tf_op jit(solution)/shard_map/gptk,gkd->gptd/dot_general | solution.py:104
  27.2 1.2 %convolution_add_fusion.2 = f32[2,8,128,128]{2,3,1,0:T(8,128)S(1)} fusion(f32[2,8,128,128]{2,3,1,0:T(8,128)S(1)} %fusion.32, f32[2,8,128,128]{2,3,1,0:T(8,128)S(1)} %get-tuple-element.49, f32[2,8,128]{2,1,0:T(8,128)S(1)} %maximum_maximum_fusion, bf16[2,128,256]{2,1,0:T(8,128)(2,1)} %collective-permute-done.3), kind=kOutput, calls=%fused_computation.8 | convolution fusion | flops 67895296 | bytes 3219456 | tf_op jit(solution)/shard_map/gptk,gkd->gptd/dot_general | solution.py:104
  28.4 1.4 %multiply_reduce_fusion.2 = (f32[2,8,128]{2,1,0:T(8,128)S(1)}, f32[2,8,128,128]{2,3,1,0:T(8,128)S(1)}) fusion(f32[2,8,128]{2,1,0:T(8,128)S(1)} %add_add_fusion, f32[2,8,128,128]{2,3,1,0:T(8,128)S(1)} %fusion.28, f32[2,8,128,128]{2,3,1,0:T(8,128)S(1)} %convolution_add_fusion.2, bf16[2,128,256]{2,1,0:T(8,128)(2,1)} %collective-permute-done.4, ...), kind=kOutput, calls=%fused_computation.39 | convolution fusion | flops 69466112 | bytes 4284416 | tf_op jit(solution)/shard_map/gptk,gkd->gptd/dot_general | solution.py:104
  29.8 5.2 %collective-permute-done.1 = bf16[1040,128]{1,0:T(8,128)(2,1)S(1)} collective-permute-done((bf16[1040,128]{1,0:T(8,128)(2,1)}, bf16[1040,128]{1,0:T(8,128)(2,1)S(1)}, u32[]{:S(2)}, u32[]{:S(2)}) %collective-permute-start.1) | collective-permute-done | bytes 266272 | tf_op jit(solution)/shard_map/ppermute | solution.py:66
  34.9 5.0 %collective-permute-done = bf16[1040,128]{1,0:T(8,128)(2,1)S(1)} collective-permute-done((bf16[1040,128]{1,0:T(8,128)(2,1)}, bf16[1040,128]{1,0:T(8,128)(2,1)S(1)}, u32[]{:S(2)}, u32[]{:S(2)}) %collective-permute-start) | collective-permute-done | bytes 266272 | tf_op jit(solution)/shard_map/ppermute | solution.py:66
  40.0 0.3 fusion.24
  40.4 0.8 %copy-done.7 = f32[16,128,128]{1,2,0:T(8,128)S(1)} copy-done((f32[16,128,128]{1,2,0:T(8,128)S(1)}, f32[16,128,128]{1,2,0:T(8,128)}, u32[]{:S(2)}) %copy-start.7) | copy-done | bytes 1048600
  41.3 2.0 %multiply_reduce_fusion.3 = (f32[16,128]{1,0:T(8,128)S(1)}, f32[16,128,128]{1,2,0:T(8,128)S(1)}) fusion(bf16[16,128,128]{1,2,0:T(8,128)(2,1)S(1)} %copy.48, f32[16]{0:T(128)S(1)} %copy-done.14, f32[16,128,128]{1,2,0:T(8,128)S(1)} %copy-done.7, f32[16,64,128]{2,1,0:T(8,128)S(1)} %fusion.24, f32[16,128,64]{1,2,0:T(8,128)S(1)} %bitcast.181, ...), kind=kOutput, calls=%fused_computation.44 | convolution fusion | flops 203159552 | bytes 3686464 | tf_op jit(solution)/shard_map/htn,hnp->htp/dot_general | solution.py:169
  43.3 0.4 multiply_reduce_fusion.1
  43.7 0.6 multiply_reduce_fusion
  44.3 2.1 %fusion.36 = f32[16,64,128]{2,1,0:T(8,128)S(1)} fusion(f32[16,128,128]{1,2,0:T(8,128)S(1)} %get-tuple-element.21, f32[16,128,64]{1,2,0:T(8,128)S(1)} %bitcast.182, f32[16,128]{1,0:T(8,128)S(1)} %get-tuple-element.31), kind=kOutput, calls=%fused_computation.74 | convolution fusion | flops 201457664 | bytes 2105344 | tf_op jit(solution)/shard_map/htn,htp->hnp/dot_general | solution.py:178
  46.5 0.9 %slice-done = bf16[1024,128]{1,0:T(8,128)(2,1)S(1)} async-done(((bf16[1040,128]{1,0:T(8,128)(2,1)}), bf16[1024,128]{1,0:T(8,128)(2,1)S(1)}, s32[]{:S(2)}) %slice-start) | async-done | bytes 262168 | tf_op jit(solution)/shard_map/slice | solution.py:38
  47.5 0.4 multiply_reduce_fusion.4
  48.1 0.7 collective-permute-start.8
  48.8 1.3 %collective-permute-start.7 = (bf16[1040,128]{1,0:T(8,128)(2,1)S(1)}, bf16[1040,128]{1,0:T(8,128)(2,1)S(1)}, u32[]{:S(2)}, u32[]{:S(2)}) collective-permute-start(bf16[1040,128]{1,0:T(8,128)(2,1)S(1)} %pad_maximum_fusion.2), channel_id=1, source_target_pairs={{8,0},{12,4},{9,1},{13,5},{10,2},{14,6},{11,3},{15,7},{24,16},{28,... | collective-permute-start | bytes 798728 | tf_op jit(solution)/shard_map/ppermute | solution.py:66
  50.1 2.1 %collective-permute-start.6 = (bf16[1040,128]{1,0:T(8,128)(2,1)S(1)}, bf16[1040,128]{1,0:T(8,128)(2,1)S(1)}, u32[]{:S(2)}, u32[]{:S(2)}) collective-permute-start(bf16[1040,128]{1,0:T(8,128)(2,1)S(1)} %pad_maximum_fusion.2), channel_id=1, source_target_pairs={{4,0},{8,4},{12,8},{5,1},{9,5},{13,9},{6,2},{10,6},{14,10},{7,3},{... | collective-permute-start | bytes 798728 | tf_op jit(solution)/shard_map/ppermute | solution.py:66
  52.2 2.3 %fusion.104 = f32[16,128,128]{1,2,0:T(8,128)S(1)} fusion(f32[16,128,128]{2,1,0:T(8,128)} %copy-done.2, f32[16,128,128]{1,2,0:T(8,128)S(1)} %get-tuple-element.21), kind=kOutput, calls=%fused_computation.201 | convolution fusion | flops 402653184 | bytes 3145728 | tf_op jit(solution)/shard_map/hts,htp->hsp/dot_general | solution.py:191
  54.5 1.2 %convolution_multiply_fusion = f32[16,128,128]{2,1,0:T(8,128)S(1)} fusion(f32[16,128,128]{1,2,0:T(8,128)S(1)} %get-tuple-element.21, bf16[16,128,128]{2,1,0:T(8,128)(2,1)S(1)} %copy-done.1, f32[16,128]{1,0:T(8,128)S(1)} %reduce_window_sum.11, pred[128,128]{1,0:T(8,128)(4,1)S(1)} %copy.44), kind=kOutput, calls=%fused_computation | convolution fusion | flops 403701760 | bytes 2646016 | tf_op jit(solution)/shard_map/htp,hsp->hts/dot_general | solution.py:193
  55.7 1.0 %convolution_multiply_fusion.6 = f32[16,128,64]{1,2,0:T(8,128)S(1)} fusion(f32[16,128,128]{1,2,0:T(8,128)S(1)} %get-tuple-element.21, f32[16,64,128]{2,1,0:T(8,128)S(1)} %copy-done.6, f32[16,128]{1,0:T(8,128)S(1)} %get-tuple-element.31), kind=kOutput, calls=%fused_computation.21 | convolution fusion | flops 201457664 | bytes 2105344 | tf_op jit(solution)/shard_map/hnp,htp->htn/dot_general | solution.py:197
  56.8 2.1 %convolution_add_fusion.3 = f32[16,128,64]{1,2,0:T(8,128)S(1)} fusion(f32[16,128,64]{1,2,0:T(8,128)S(1)} %convolution_multiply_fusion.6, f32[16,128,128]{2,1,0:T(8,128)S(1)} %convolution_multiply_fusion, f32[16,128,64]{1,2,0:T(8,128)S(1)} %bitcast.185), kind=kOutput, calls=%fused_computation.22 | convolution fusion | flops 201457664 | bytes 2621440 | tf_op jit(solution)/shard_map/hts,hsn->htn/dot_general | solution.py:196
  59.0 1.9 %collective-permute-done.7 = bf16[1040,128]{1,0:T(8,128)(2,1)S(1)} collective-permute-done((bf16[1040,128]{1,0:T(8,128)(2,1)S(1)}, bf16[1040,128]{1,0:T(8,128)(2,1)S(1)}, u32[]{:S(2)}, u32[]{:S(2)}) %collective-permute-start.7) | collective-permute-done | bytes 266272 | tf_op jit(solution)/shard_map/ppermute | solution.py:66
  60.9 9.3 %collective-permute-done.6 = bf16[1040,128]{1,0:T(8,128)(2,1)S(1)} collective-permute-done((bf16[1040,128]{1,0:T(8,128)(2,1)S(1)}, bf16[1040,128]{1,0:T(8,128)(2,1)S(1)}, u32[]{:S(2)}, u32[]{:S(2)}) %collective-permute-start.6) | collective-permute-done | bytes 266272 | tf_op jit(solution)/shard_map/ppermute | solution.py:66
  70.4 1.2 %fusion.10 = f32[16,128,64]{1,2,0:T(8,128)S(1)} fusion(bf16[16,128,128]{2,1,0:T(8,128)(2,1)S(1)} %copy-done.1, f32[16,128]{1,0:T(8,128)S(1)} %get-tuple-element.32, bf16[16,64,128]{2,1,0:T(8,128)(2,1)S(1)} %bitcast.191, f32[16,64,128]{2,1,0:T(8,128)S(1)} %bitcast.187, bf16[16,64,128]{2,1,0:T(8,128)(2,1)S(1)} %bitcast.189, f32[16]{0:T(128)S(1)} %get-tuple-element.34, ...), kind=kOutput, calls=%fused_computation.25 | convolution fusion | flops 202244096 | bytes 2105472 | tf_op jit(solution)/shard_map/hnp,hsp->hsn/dot_general | solution.py:229
  71.6 2.8 %fusion.12 = (f32[16,128]{1,0:T(8,128)S(1)}, bf16[16,128,128]{1,2,0:T(8,128)(2,1)}) fusion(bf16[16,128,128]{1,2,0:T(8,128)(2,1)S(1)} %copy.48, f32[16,128,128]{1,2,0:T(8,128)S(1)} %get-tuple-element.21, f32[16]{0:T(128)S(1)} %copy-done.14, f32[16,128,128]{1,2,0:T(8,128)S(1)} %fusion.104, bf16[16,64,128]{2,1,0:T(8,128)(2,1)S(1)} %bitcast.192, ...), kind=kOutput, calls=%fused_computation.29 | convolution fusion | flops 204077056 | bytes 4735168 | tf_op jit(solution)/shard_map/hsn,hnp->hsp/dot_general | solution.py:223
  74.4 1.0 %convolution_add_fusion.4 = f32[16,128,64]{1,2,0:T(8,128)S(1)} fusion(f32[16,128,64]{1,2,0:T(8,128)S(1)} %fusion.10, f32[16,128,128]{2,1,0:T(8,128)S(1)} %convolution_multiply_fusion, f32[16,128,64]{1,2,0:T(8,128)S(1)} %bitcast.183), kind=kOutput, calls=%fused_computation.23 | convolution fusion | flops 201457664 | bytes 2621440 | tf_op jit(solution)/shard_map/hts,htn->hsn/dot_general | solution.py:195
  75.5 0.7 copy.61
  76.5 1.0 %copy.60 = bf16[16,128,128]{2,1,0:T(8,128)(2,1)} copy(bf16[16,128,128]{1,2,0:T(8,128)(2,1)S(1)} %copy-done.8) | data formatting | bytes 1048576
  77.5 0.8 %convolution_add_fusion.5 = f32[16,128]{1,0:T(8,128)} fusion(f32[16,128]{1,0:T(8,128)S(1)} %get-tuple-element.20, f32[16,128]{1,0:T(8,128)S(1)} %get-tuple-element.26, f32[16]{0:T(128)S(1)} %get-tuple-element.33), kind=kOutput, calls=%fused_computation.27 | convolution fusion | flops 3166208 | bytes 24640 | tf_op jit(solution)/shard_map/hu,su->hs/dot_general | solution.py:226
  (79 shorter events, 2.2 us)
Async XLA Ops:
  0.6 17.3 %copy-start = (bf16[16,128,128]{2,1,0:T(8,128)(2,1)S(1)}, bf16[16,128,128]{2,1,0:T(8,128)(2,1)}, u32[]{:S(2)}) copy-start(bf16[16,128,128]{2,1,0:T(8,128)(2,1)} %param.7) | copy-start | bytes 1572868
  0.6 9.2 %copy-start.11 = (bf16[2,128,128]{2,1,0:T(8,128)(2,1)S(1)}, bf16[2,128,128]{2,1,0:T(8,128)(2,1)}, u32[]{:S(2)}) copy-start(bf16[2,128,128]{2,1,0:T(8,128)(2,1)} %param.10) | copy-start | bytes 196612
  0.7 9.5 %copy-start.1 = (bf16[16,128,128]{2,1,0:T(8,128)(2,1)S(1)}, bf16[16,128,128]{2,1,0:T(8,128)(2,1)}, u32[]{:S(2)}) copy-start(bf16[16,128,128]{2,1,0:T(8,128)(2,1)} %param.9) | copy-start | bytes 1572868
  0.7 19.8 %collective-permute-start.5 = (bf16[2,128,256]{2,1,0:T(8,128)(2,1)}, bf16[2,128,256]{2,1,0:T(8,128)(2,1)}, u32[]{:S(2)}, u32[]{:S(2)}) collective-permute-start(bf16[2,128,256]{2,1,0:T(8,128)(2,1)} %param.8), channel_id=1, source_target_pairs={{0,12},{1,13},{2,14},{3,15},{16,28},{17,29},{18,30},{19,31}} | collective-permute-start | bytes 393224 | tf_op jit(solution)/shard_map/ppermute | solution.py:66
  2.1 16.5 %collective-permute-start.3 = (bf16[2,128,256]{2,1,0:T(8,128)(2,1)}, bf16[2,128,256]{2,1,0:T(8,128)(2,1)}, u32[]{:S(2)}, u32[]{:S(2)}) collective-permute-start(bf16[2,128,256]{2,1,0:T(8,128)(2,1)} %param.8), channel_id=1, source_target_pairs={{0,4},{4,8},{8,12},{1,5},{5,9},{9,13},{2,6},{6,10},{10,14},{3,7},{... | collective-permute-start | bytes 393224 | tf_op jit(solution)/shard_map/ppermute | solution.py:66
  5.6 17.9 %collective-permute-start.4 = (bf16[2,128,256]{2,1,0:T(8,128)(2,1)}, bf16[2,128,256]{2,1,0:T(8,128)(2,1)}, u32[]{:S(2)}, u32[]{:S(2)}) collective-permute-start(bf16[2,128,256]{2,1,0:T(8,128)(2,1)} %param.8), channel_id=1, source_target_pairs={{0,8},{4,12},{1,9},{5,13},{2,10},{6,14},{3,11},{7,15},{16,24},{20,... | collective-permute-start | bytes 393224 | tf_op jit(solution)/shard_map/ppermute | solution.py:66
  10.1 0.8 %copy-start.3 = (f32[2,8,128,64]{2,3,1,0:T(8,128)}, f32[2,8,128,64]{2,3,1,0:T(8,128)S(1)}, u32[]{:S(2)}) copy-start(f32[2,8,128,64]{2,3,1,0:T(8,128)S(1)} %broadcast_in_dim.99) | copy-start | bytes 1572868
  11.7 23.2 %collective-permute-start.1 = (bf16[1040,128]{1,0:T(8,128)(2,1)}, bf16[1040,128]{1,0:T(8,128)(2,1)S(1)}, u32[]{:S(2)}, u32[]{:S(2)}) collective-permute-start(bf16[1040,128]{1,0:T(8,128)(2,1)} %pad_maximum_fusion.1), channel_id=1, source_target_pairs={{0,8},{4,12},{1,9},{5,13},{2,10},{6,14},{3,11},{7,15},{16,24},{20,... | collective-permute-start | bytes 798728 | tf_op jit(solution)/shard_map/ppermute | solution.py:66
  13.0 26.9 %collective-permute-start = (bf16[1040,128]{1,0:T(8,128)(2,1)}, bf16[1040,128]{1,0:T(8,128)(2,1)S(1)}, u32[]{:S(2)}, u32[]{:S(2)}) collective-permute-start(bf16[1040,128]{1,0:T(8,128)(2,1)} %pad_maximum_fusion.1), channel_id=1, source_target_pairs={{0,4},{4,8},{8,12},{1,5},{5,9},{9,13},{2,6},{6,10},{10,14},{3,7},{... | collective-permute-start | bytes 798728 | tf_op jit(solution)/shard_map/ppermute | solution.py:66
  15.6 2.3 %copy-start.2 = (f32[16,128,128]{2,1,0:T(8,128)}, f32[16,128,128]{2,1,0:T(8,128)S(1)}, u32[]{:S(2)}) copy-start(f32[16,128,128]{2,1,0:T(8,128)S(1)} %bitcast_multiply_fusion.1) | copy-start | bytes 3145732
  15.6 2.3 %copy-start.13 = (bf16[2,128,256]{2,1,0:T(8,128)(2,1)S(1)}, bf16[2,128,256]{2,1,0:T(8,128)(2,1)}, u32[]{:S(2)}) copy-start(bf16[2,128,256]{2,1,0:T(8,128)(2,1)} %param.8) | copy-start | bytes 393220
  18.7 21.3 %collective-permute-start.2 = (bf16[1040,128]{1,0:T(8,128)(2,1)}, bf16[1040,128]{1,0:T(8,128)(2,1)S(1)}, u32[]{:S(2)}, u32[]{:S(2)}) collective-permute-start(bf16[1040,128]{1,0:T(8,128)(2,1)} %pad_maximum_fusion.1), channel_id=1, source_target_pairs={{0,12},{1,13},{2,14},{3,15},{16,28},{17,29},{18,30},{19,31}} | collective-permute-start | bytes 798728 | tf_op jit(solution)/shard_map/ppermute | solution.py:66
  28.4 11.6 %copy-start.12 = (f32[16,64,128]{2,1,0:T(8,128)S(1)}, f32[16,64,128]{2,1,0:T(8,128)}, u32[]{:S(2)}) copy-start(f32[16,64,128]{2,1,0:T(8,128)} %param.13) | copy-start | bytes 1572868
  34.9 5.4 %copy-start.10 = (bf16[1040,128]{1,0:T(8,128)(2,1)}, bf16[1040,128]{1,0:T(8,128)(2,1)S(1)}, u32[]{:S(2)}) copy-start(bf16[1040,128]{1,0:T(8,128)(2,1)S(1)} %collective-permute-done.1) | copy-start | bytes 798724
  39.9 6.5 %copy-start.9 = (bf16[1040,128]{1,0:T(8,128)(2,1)}, bf16[1040,128]{1,0:T(8,128)(2,1)S(1)}, u32[]{:S(2)}) copy-start(bf16[1040,128]{1,0:T(8,128)(2,1)S(1)} %collective-permute-done) | copy-start | bytes 798724
  40.0 1.2 %copy-start.7 = (f32[16,128,128]{1,2,0:T(8,128)S(1)}, f32[16,128,128]{1,2,0:T(8,128)}, u32[]{:S(2)}) copy-start(f32[16,128,128]{1,2,0:T(8,128)} %fusion.103) | copy-start | bytes 3145732
  40.3 6.2 %copy-start.5 = (f32[16,64,128]{2,1,0:T(8,128)}, f32[16,64,128]{2,1,0:T(8,128)S(1)}, u32[]{:S(2)}) copy-start(f32[16,64,128]{2,1,0:T(8,128)S(1)} %fusion.24) | copy-start | bytes 1572868
  40.4 0.8 %copy-start.14 = (f32[16]{0:T(128)S(1)}, f32[16]{0:T(128)}, u32[]{:S(2)}) copy-start(f32[16]{0:T(128)} %param.12) | copy-start | bytes 196
  46.4 1.0 %slice-start = ((bf16[1040,128]{1,0:T(8,128)(2,1)}), bf16[1024,128]{1,0:T(8,128)(2,1)S(1)}, s32[]{:S(2)}) async-start(bf16[1040,128]{1,0:T(8,128)(2,1)} %copy-done.9), calls=%async_computation | async-start | bytes 524288 | tf_op jit(solution)/shard_map/slice | solution.py:38
  46.5 1.0 %slice-start.1 = ((bf16[1040,128]{1,0:T(8,128)(2,1)}), bf16[1024,128]{1,0:T(8,128)(2,1)S(1)}, s32[]{:S(2)}) async-start(bf16[1040,128]{1,0:T(8,128)(2,1)} %copy-done.10), calls=%async_computation.1 | async-start | bytes 524288 | tf_op jit(solution)/shard_map/slice | solution.py:38
  48.1 10.9 %collective-permute-start.8 = (bf16[1040,128]{1,0:T(8,128)(2,1)S(1)}, bf16[1040,128]{1,0:T(8,128)(2,1)S(1)}, u32[]{:S(2)}, u32[]{:S(2)}) collective-permute-start(bf16[1040,128]{1,0:T(8,128)(2,1)S(1)} %pad_maximum_fusion.2), channel_id=1, source_target_pairs={{12,0},{13,1},{14,2},{15,3},{28,16},{29,17},{30,18},{31,19}} | collective-permute-start | bytes 798728 | tf_op jit(solution)/shard_map/ppermute | solution.py:66
  48.8 12.1 %collective-permute-start.7 = (bf16[1040,128]{1,0:T(8,128)(2,1)S(1)}, bf16[1040,128]{1,0:T(8,128)(2,1)S(1)}, u32[]{:S(2)}, u32[]{:S(2)}) collective-permute-start(bf16[1040,128]{1,0:T(8,128)(2,1)S(1)} %pad_maximum_fusion.2), channel_id=1, source_target_pairs={{8,0},{12,4},{9,1},{13,5},{10,2},{14,6},{11,3},{15,7},{24,16},{28,... | collective-permute-start | bytes 798728 | tf_op jit(solution)/shard_map/ppermute | solution.py:66
  50.1 20.1 %collective-permute-start.6 = (bf16[1040,128]{1,0:T(8,128)(2,1)S(1)}, bf16[1040,128]{1,0:T(8,128)(2,1)S(1)}, u32[]{:S(2)}, u32[]{:S(2)}) collective-permute-start(bf16[1040,128]{1,0:T(8,128)(2,1)S(1)} %pad_maximum_fusion.2), channel_id=1, source_target_pairs={{4,0},{8,4},{12,8},{5,1},{9,5},{13,9},{6,2},{10,6},{14,10},{7,3},{... | collective-permute-start | bytes 798728 | tf_op jit(solution)/shard_map/ppermute | solution.py:66
  54.5 1.2 %copy-start.6 = (f32[16,64,128]{2,1,0:T(8,128)S(1)}, f32[16,64,128]{2,1,0:T(8,128)}, u32[]{:S(2)}) copy-start(f32[16,64,128]{2,1,0:T(8,128)} %copy-done.5) | copy-start | bytes 1572868
  55.7 1.1 %copy-start.4 = (f32[2,8,128,64]{2,3,1,0:T(8,128)S(1)}, f32[2,8,128,64]{2,3,1,0:T(8,128)}, u32[]{:S(2)}) copy-start(f32[2,8,128,64]{2,3,1,0:T(8,128)} %copy-done.3) | copy-start | bytes 1572868
  75.4 1.0 %copy-start.8 = (bf16[16,128,128]{1,2,0:T(8,128)(2,1)S(1)}, bf16[16,128,128]{1,2,0:T(8,128)(2,1)}, u32[]{:S(2)}) copy-start(bf16[16,128,128]{1,2,0:T(8,128)(2,1)} %get-tuple-element.27) | copy-start | bytes 1572868

commit v13 on v12

--- a/solution.py
+++ b/solution.py
@@ -124,7 +124,9 @@
     kv_earlier = shifted(keys_values, 1)
 
     log_decay = jax.nn.log_sigmoid(decay_logit)
-    cumulative = jnp.cumsum(log_decay, axis=1)
+    token_ids = jnp.arange(tok_dev)
+    through = (token_ids[:, None] <= token_ids[None, :]).astype(jnp.float32)
+    cumulative = jnp.einsum("hu,ut->ht", log_decay, through, precision=highest)
     totals = cumulative[:, -1]
     to_end = jnp.exp(totals[:, None] - cumulative)
     from_start = jnp.exp(cumulative)

time: 79 us -> 79 us (level)
  other arithmetic: 5.27 us -> 4.27 us
  matrix products: 27.5 us -> 28.3 us
    dot_general x0 -> x1, matrix products: none -> 0.83 us  [body(): cumulative = jnp.einsum('hu,ut->ht', log_decay, through, precision=highest)]
  transfers between devices with their start and end apart: 9 -> 9, of which waited for: 5 -> 5; matrix products, arithmetic and copies ran while one was open for 28% -> 27% of each run, Pallas kernels for 0% -> 0%
where the time goes in v13:
time: 79 us; the launch traced here: 78.3 us
  matrix products  28.3 us (36%)
  waiting for transfers between devices  23.4 us (30%)
  starting transfers between devices  15.8 us (20%)
  local copies, waits for them, and re-layouts  5.22 us (7%)
  other arithmetic  4.27 us (5%)
  between operations  1.29 us (2%)
    ppermute x9, waiting for transfers between devices, shifted(): moved.append(lax.ppermute(x, 'seq', pairs))  23.4 us
    ppermute x9, starting transfers between devices, shifted(): moved.append(lax.ppermute(x, 'seq', pairs))  15.8 us
    dot_general x4, matrix products, teacher_rows(): jnp.einsum('gptk,gkd->gptd', exponentials.astype(jnp.bfloat16), block[......  4.06 us
    dot_general x4, matrix products, teacher_rows(): jnp.einsum('gptd,gkd->gptk', grouped, block[..., :head_width], preferred_...  3.75 us
    unnamed x36, local copies, waits for them, and re-layouts  3.68 us
    dot_general x1, matrix products, body(): jnp.einsum('hsn,hnp->hsp', weighted_in, incoming, precision=highest)  2.84 us
    dot_general x1, matrix products, body(): local_dx = jnp.einsum('hts,htp->hsp', mixing, grad_out, precision=highest)  2.31 us
    dot_general x1, matrix products, body(): jnp.einsum('hts,hsp->htp', mixing, inputs_wide, precision=highest)  2.26 us
  transfers between devices with their start and end apart: 9, of which 5 were waited for; matrix products, arithmetic and copies ran while one was open for 27% of the time, Pallas kernels for 0%

profile of v13, /device:TPU:8, one launch (start us, length us, event | category | flops | bytes accessed | tf_op | source)
XLA Modules:
  0.0 78.3 jit_solution(13737494779957357410)
XLA Ops:
  0.7 1.5 %collective-permute-start.5 = (bf16[2,128,256]{2,1,0:T(8,128)(2,1)}, bf16[2,128,256]{2,1,0:T(8,128)(2,1)}, u32[]{:S(2)}, u32[]{:S(2)}) collective-permute-start(bf16[2,128,256]{2,1,0:T(8,128)(2,1)} %param.8), channel_id=1, source_target_pairs={{0,12},{1,13},{2,14},{3,15},{16,28},{17,29},{18,30},{19,31}} | collective-permute-start | bytes 393224 | tf_op jit(solution)/shard_map/ppermute | solution.py:66
  2.1 3.5 %collective-permute-start.3 = (bf16[2,128,256]{2,1,0:T(8,128)(2,1)}, bf16[2,128,256]{2,1,0:T(8,128)(2,1)}, u32[]{:S(2)}, u32[]{:S(2)}) collective-permute-start(bf16[2,128,256]{2,1,0:T(8,128)(2,1)} %param.8), channel_id=1, source_target_pairs={{0,4},{4,8},{8,12},{1,5},{5,9},{9,13},{2,6},{6,10},{10,14},{3,7},{... | collective-permute-start | bytes 393224 | tf_op jit(solution)/shard_map/ppermute | solution.py:66
  5.6 2.9 %collective-permute-start.4 = (bf16[2,128,256]{2,1,0:T(8,128)(2,1)}, bf16[2,128,256]{2,1,0:T(8,128)(2,1)}, u32[]{:S(2)}, u32[]{:S(2)}) collective-permute-start(bf16[2,128,256]{2,1,0:T(8,128)(2,1)} %param.8), channel_id=1, source_target_pairs={{0,8},{4,12},{1,9},{5,13},{2,10},{6,14},{3,11},{7,15},{16,24},{20,... | collective-permute-start | bytes 393224 | tf_op jit(solution)/shard_map/ppermute | solution.py:66
  8.5 0.8 %fusion.51 = f32[16,128]{1,0:T(8,128)S(1)} fusion(f32[16,128]{1,0:T(8,128)} %param.11), kind=kOutput, calls=%fused_computation.98 | convolution fusion | flops 3178496 | bytes 16384 | tf_op jit(solution)/shard_map/hu,ut->ht/dot_general | solution.py:129
  10.0 0.5 convolution_convert_fusion
  10.5 0.2 copy-done.3
  10.8 0.8 pad_maximum_fusion.1
  11.5 1.3 %collective-permute-start.1 = (bf16[1040,128]{1,0:T(8,128)(2,1)}, bf16[1040,128]{1,0:T(8,128)(2,1)S(1)}, u32[]{:S(2)}, u32[]{:S(2)}) collective-permute-start(bf16[1040,128]{1,0:T(8,128)(2,1)} %pad_maximum_fusion.1), channel_id=1, source_target_pairs={{0,8},{4,12},{1,9},{5,13},{2,10},{6,14},{3,11},{7,15},{16,24},{20,... | collective-permute-start | bytes 798728 | tf_op jit(solution)/shard_map/ppermute | solution.py:66
  12.8 1.9 %collective-permute-start = (bf16[1040,128]{1,0:T(8,128)(2,1)}, bf16[1040,128]{1,0:T(8,128)(2,1)S(1)}, u32[]{:S(2)}, u32[]{:S(2)}) collective-permute-start(bf16[1040,128]{1,0:T(8,128)(2,1)} %pad_maximum_fusion.1), channel_id=1, source_target_pairs={{0,4},{4,8},{8,12},{1,5},{5,9},{9,13},{2,6},{6,10},{10,14},{3,7},{... | collective-permute-start | bytes 798728 | tf_op jit(solution)/shard_map/ppermute | solution.py:66
  15.1 0.3 bitcast_multiply_fusion.1
  15.5 2.3 %fusion.114 = f32[16,128,128]{1,2,0:T(8,128)} fusion(f32[16,128,128]{2,1,0:T(8,128)S(1)} %bitcast_multiply_fusion.1, bf16[16,128,128]{2,1,0:T(8,128)(2,1)S(1)} %copy-done.1), kind=kOutput, calls=%fused_computation.210 | convolution fusion | flops 402653184 | bytes 2621440 | tf_op jit(solution)/shard_map/hts,hsp->htp/dot_general | solution.py:163
  17.8 0.3 fusion.112
  18.1 0.3 copy.48
  18.5 0.7 collective-permute-start.2
  19.2 1.1 %fusion.113 = (f32[2,8,128]{2,1,0:T(8,128)S(1)}, f32[2,8,128,128]{2,3,1,0:T(8,128)S(1)}) fusion(bf16[2,8,128,128]{3,2,1,0:T(8,128)(2,1)S(1)} %bitcast.178, bf16[2,128,256]{2,1,0:T(8,128)(2,1)} %collective-permute-done.3, pred[]{:T(512)S(6)} %ge.61), kind=kOutput, calls=%fused_computation.209 | convolution fusion | flops 67893248 | bytes 1646593 | tf_op jit(solution)/shard_map/gptd,gkd->gptk/dot_general | solution.py:87
  20.4 1.1 %fusion.110 = (f32[2,8,128]{2,1,0:T(8,128)S(1)}, f32[2,8,128,128]{2,3,1,0:T(8,128)S(1)}) fusion(bf16[2,8,128,128]{3,2,1,0:T(8,128)(2,1)S(1)} %bitcast.180, bf16[2,128,256]{2,1,0:T(8,128)(2,1)} %collective-permute-done.5, pred[]{:T(512)S(6)} %ge.63), kind=kOutput, calls=%fused_computation.206 | convolution fusion | flops 67893248 | bytes 1646593 | tf_op jit(solution)/shard_map/gptd,gkd->gptk/dot_general | solution.py:87
  21.5 2.0 %collective-permute-done.4 = bf16[2,128,256]{2,1,0:T(8,128)(2,1)} collective-permute-done((bf16[2,128,256]{2,1,0:T(8,128)(2,1)}, bf16[2,128,256]{2,1,0:T(8,128)(2,1)}, u32[]{:S(2)}, u32[]{:S(2)}) %collective-permute-start.4) | collective-permute-done | bytes 131104 | tf_op jit(solution)/shard_map/ppermute | solution.py:66
  23.5 1.1 %fusion.111 = (f32[2,8,128]{2,1,0:T(8,128)S(1)}, f32[2,8,128,128]{2,3,1,0:T(8,128)S(1)}) fusion(bf16[2,8,128,128]{3,2,1,0:T(8,128)(2,1)S(1)} %bitcast.179, bf16[2,128,256]{2,1,0:T(8,128)(2,1)} %collective-permute-done.4, pred[]{:T(512)S(6)} %ge.62), kind=kOutput, calls=%fused_computation.207 | convolution fusion | flops 67893248 | bytes 1646593 | tf_op jit(solution)/shard_map/gptd,gkd->gptk/dot_general | solution.py:87
  24.7 0.3 fusion.32
  25.0 1.0 %fusion.16 = (f32[2,8,128]{2,1,0:T(8,128)S(1)}, f32[2,8,128]{2,1,0:T(8,128)S(1)}, f32[2,8,128]{2,1,0:T(8,128)S(1)}, f32[2,8,128]{2,1,0:T(8,128)S(1)}) fusion(f32[2,8,128,128]{2,3,1,0:T(8,128)S(1)} %get-tuple-element.49, f32[2,8,128]{2,1,0:T(8,128)S(1)} %maximum_maximum_fusion, f32[2,8,128,128]{2,3,1,0:T(8,128)S(1)} %get-tuple-element.47, ...), kind=kLoop, calls=%fused_computation.48 | loop fusion | flops 2088960 | bytes 4235264 | tf_op jit(solution)/shard_map/reduce_sum | solution.py:103
  26.0 1.2 %fusion.28 = f32[2,8,128,128]{2,3,1,0:T(8,128)S(1)} fusion(f32[2,8,128,128]{2,3,1,0:T(8,128)S(1)} %get-tuple-element.43, f32[2,8,128]{2,1,0:T(8,128)S(1)} %maximum_maximum_fusion, bf16[2,128,256]{2,1,0:T(8,128)(2,1)} %collective-permute-done.5), kind=kOutput, calls=%fused_computation.66 | convolution fusion | flops 67633152 | bytes 2170880 | tf_op jit(solution)/shard_map/gptk,gkd->gptd/dot_general | solution.py:104
  27.2 1.2 %convolution_add_fusion.2 = f32[2,8,128,128]{2,3,1,0:T(8,128)S(1)} fusion(f32[2,8,128,128]{2,3,1,0:T(8,128)S(1)} %fusion.32, f32[2,8,128,128]{2,3,1,0:T(8,128)S(1)} %get-tuple-element.49, f32[2,8,128]{2,1,0:T(8,128)S(1)} %maximum_maximum_fusion, bf16[2,128,256]{2,1,0:T(8,128)(2,1)} %collective-permute-done.3), kind=kOutput, calls=%fused_computation.8 | convolution fusion | flops 67895296 | bytes 3219456 | tf_op jit(solution)/shard_map/gptk,gkd->gptd/dot_general | solution.py:104
  28.4 1.4 %multiply_reduce_fusion.2 = (f32[2,8,128]{2,1,0:T(8,128)S(1)}, f32[2,8,128,128]{2,3,1,0:T(8,128)S(1)}) fusion(f32[2,8,128]{2,1,0:T(8,128)S(1)} %add_add_fusion, f32[2,8,128,128]{2,3,1,0:T(8,128)S(1)} %fusion.28, f32[2,8,128,128]{2,3,1,0:T(8,128)S(1)} %convolution_add_fusion.2, bf16[2,128,256]{2,1,0:T(8,128)(2,1)} %collective-permute-done.4, ...), kind=kOutput, calls=%fused_computation.39 | convolution fusion | flops 69466112 | bytes 4284416 | tf_op jit(solution)/shard_map/gptk,gkd->gptd/dot_general | solution.py:104
  29.8 5.2 %collective-permute-done.1 = bf16[1040,128]{1,0:T(8,128)(2,1)S(1)} collective-permute-done((bf16[1040,128]{1,0:T(8,128)(2,1)}, bf16[1040,128]{1,0:T(8,128)(2,1)S(1)}, u32[]{:S(2)}, u32[]{:S(2)}) %collective-permute-start.1) | collective-permute-done | bytes 266272 | tf_op jit(solution)/shard_map/ppermute | solution.py:66
  34.9 5.0 %collective-permute-done = bf16[1040,128]{1,0:T(8,128)(2,1)S(1)} collective-permute-done((bf16[1040,128]{1,0:T(8,128)(2,1)}, bf16[1040,128]{1,0:T(8,128)(2,1)S(1)}, u32[]{:S(2)}, u32[]{:S(2)}) %collective-permute-start) | collective-permute-done | bytes 266272 | tf_op jit(solution)/shard_map/ppermute | solution.py:66
  40.0 0.3 fusion.24
  40.4 0.8 %copy-done.7 = f32[16,128,128]{1,2,0:T(8,128)S(1)} copy-done((f32[16,128,128]{1,2,0:T(8,128)S(1)}, f32[16,128,128]{1,2,0:T(8,128)}, u32[]{:S(2)}) %copy-start.7) | copy-done | bytes 1048600
  41.3 2.0 %multiply_reduce_fusion.3 = (f32[16,128]{1,0:T(8,128)S(1)}, f32[16,128,128]{1,2,0:T(8,128)S(1)}) fusion(bf16[16,128,128]{1,2,0:T(8,128)(2,1)S(1)} %copy.48, f32[16]{0:T(128)S(1)} %copy-done.14, f32[16,128,128]{1,2,0:T(8,128)S(1)} %copy-done.7, f32[16,64,128]{2,1,0:T(8,128)S(1)} %fusion.24, f32[16,128,64]{1,2,0:T(8,128)S(1)} %bitcast.181, ...), kind=kOutput, calls=%fused_computation.44 | convolution fusion | flops 203159552 | bytes 3686464 | tf_op jit(solution)/shard_map/htn,hnp->htp/dot_general | solution.py:171
  43.3 0.4 multiply_reduce_fusion.1
  43.7 0.6 multiply_reduce_fusion
  44.3 2.1 %fusion.36 = f32[16,64,128]{2,1,0:T(8,128)S(1)} fusion(f32[16,128,128]{1,2,0:T(8,128)S(1)} %get-tuple-element.21, f32[16,128,64]{1,2,0:T(8,128)S(1)} %bitcast.182, f32[16,128]{1,0:T(8,128)S(1)} %get-tuple-element.31), kind=kOutput, calls=%fused_computation.74 | convolution fusion | flops 201457664 | bytes 2105344 | tf_op jit(solution)/shard_map/htn,htp->hnp/dot_general | solution.py:180
  46.5 0.9 %slice-done = bf16[1024,128]{1,0:T(8,128)(2,1)S(1)} async-done(((bf16[1040,128]{1,0:T(8,128)(2,1)}), bf16[1024,128]{1,0:T(8,128)(2,1)S(1)}, s32[]{:S(2)}) %slice-start) | async-done | bytes 262168 | tf_op jit(solution)/shard_map/slice | solution.py:38
  47.5 0.4 multiply_reduce_fusion.4
  48.1 0.7 collective-permute-start.8
  48.8 1.3 %collective-permute-start.7 = (bf16[1040,128]{1,0:T(8,128)(2,1)S(1)}, bf16[1040,128]{1,0:T(8,128)(2,1)S(1)}, u32[]{:S(2)}, u32[]{:S(2)}) collective-permute-start(bf16[1040,128]{1,0:T(8,128)(2,1)S(1)} %pad_maximum_fusion.2), channel_id=1, source_target_pairs={{8,0},{12,4},{9,1},{13,5},{10,2},{14,6},{11,3},{15,7},{24,16},{28,... | collective-permute-start | bytes 798728 | tf_op jit(solution)/shard_map/ppermute | solution.py:66
  50.1 2.1 %collective-permute-start.6 = (bf16[1040,128]{1,0:T(8,128)(2,1)S(1)}, bf16[1040,128]{1,0:T(8,128)(2,1)S(1)}, u32[]{:S(2)}, u32[]{:S(2)}) collective-permute-start(bf16[1040,128]{1,0:T(8,128)(2,1)S(1)} %pad_maximum_fusion.2), channel_id=1, source_target_pairs={{4,0},{8,4},{12,8},{5,1},{9,5},{13,9},{6,2},{10,6},{14,10},{7,3},{... | collective-permute-start | bytes 798728 | tf_op jit(solution)/shard_map/ppermute | solution.py:66
  52.2 2.3 %fusion.115 = f32[16,128,128]{1,2,0:T(8,128)S(1)} fusion(f32[16,128,128]{2,1,0:T(8,128)} %copy-done.2, f32[16,128,128]{1,2,0:T(8,128)S(1)} %get-tuple-element.21), kind=kOutput, calls=%fused_computation.211 | convolution fusion | flops 402653184 | bytes 3145728 | tf_op jit(solution)/shard_map/hts,htp->hsp/dot_general | solution.py:193
  54.5 1.2 %convolution_multiply_fusion = f32[16,128,128]{2,1,0:T(8,128)S(1)} fusion(f32[16,128,128]{1,2,0:T(8,128)S(1)} %get-tuple-element.21, bf16[16,128,128]{2,1,0:T(8,128)(2,1)S(1)} %copy-done.1, f32[16,128]{1,0:T(8,128)S(1)} %fusion.51, pred[128,128]{1,0:T(8,128)(4,1)S(1)} %copy.44), kind=kOutput, calls=%fused_computation | convolution fusion | flops 403701760 | bytes 2646016 | tf_op jit(solution)/shard_map/htp,hsp->hts/dot_general | solution.py:195
  55.7 1.0 %convolution_multiply_fusion.6 = f32[16,128,64]{1,2,0:T(8,128)S(1)} fusion(f32[16,128,128]{1,2,0:T(8,128)S(1)} %get-tuple-element.21, f32[16,64,128]{2,1,0:T(8,128)S(1)} %copy-done.6, f32[16,128]{1,0:T(8,128)S(1)} %get-tuple-element.31), kind=kOutput, calls=%fused_computation.21 | convolution fusion | flops 201457664 | bytes 2105344 | tf_op jit(solution)/shard_map/hnp,htp->htn/dot_general | solution.py:199
  56.8 2.1 %convolution_add_fusion.3 = f32[16,128,64]{1,2,0:T(8,128)S(1)} fusion(f32[16,128,64]{1,2,0:T(8,128)S(1)} %convolution_multiply_fusion.6, f32[16,128,128]{2,1,0:T(8,128)S(1)} %convolution_multiply_fusion, f32[16,128,64]{1,2,0:T(8,128)S(1)} %bitcast.185), kind=kOutput, calls=%fused_computation.22 | convolution fusion | flops 201457664 | bytes 2621440 | tf_op jit(solution)/shard_map/hts,hsn->htn/dot_general | solution.py:198
  59.0 1.9 %collective-permute-done.7 = bf16[1040,128]{1,0:T(8,128)(2,1)S(1)} collective-permute-done((bf16[1040,128]{1,0:T(8,128)(2,1)S(1)}, bf16[1040,128]{1,0:T(8,128)(2,1)S(1)}, u32[]{:S(2)}, u32[]{:S(2)}) %collective-permute-start.7) | collective-permute-done | bytes 266272 | tf_op jit(solution)/shard_map/ppermute | solution.py:66
  60.9 9.3 %collective-permute-done.6 = bf16[1040,128]{1,0:T(8,128)(2,1)S(1)} collective-permute-done((bf16[1040,128]{1,0:T(8,128)(2,1)S(1)}, bf16[1040,128]{1,0:T(8,128)(2,1)S(1)}, u32[]{:S(2)}, u32[]{:S(2)}) %collective-permute-start.6) | collective-permute-done | bytes 266272 | tf_op jit(solution)/shard_map/ppermute | solution.py:66
  70.4 1.2 %fusion.10 = f32[16,128,64]{1,2,0:T(8,128)S(1)} fusion(bf16[16,128,128]{2,1,0:T(8,128)(2,1)S(1)} %copy-done.1, f32[16,128]{1,0:T(8,128)S(1)} %get-tuple-element.32, bf16[16,64,128]{2,1,0:T(8,128)(2,1)S(1)} %bitcast.191, f32[16,64,128]{2,1,0:T(8,128)S(1)} %bitcast.187, bf16[16,64,128]{2,1,0:T(8,128)(2,1)S(1)} %bitcast.189, f32[16]{0:T(128)S(1)} %get-tuple-element.34, ...), kind=kOutput, calls=%fused_computation.25 | convolution fusion | flops 202244096 | bytes 2105472 | tf_op jit(solution)/shard_map/hnp,hsp->hsn/dot_general | solution.py:231
  71.6 2.8 %fusion.12 = (f32[16,128]{1,0:T(8,128)S(1)}, bf16[16,128,128]{1,2,0:T(8,128)(2,1)}) fusion(bf16[16,128,128]{1,2,0:T(8,128)(2,1)S(1)} %copy.48, f32[16,128,128]{1,2,0:T(8,128)S(1)} %get-tuple-element.21, f32[16]{0:T(128)S(1)} %copy-done.14, f32[16,128,128]{1,2,0:T(8,128)S(1)} %fusion.115, bf16[16,64,128]{2,1,0:T(8,128)(2,1)S(1)} %bitcast.192, ...), kind=kOutput, calls=%fused_computation.29 | convolution fusion | flops 204077056 | bytes 4735168 | tf_op jit(solution)/shard_map/hsn,hnp->hsp/dot_general | solution.py:225
  74.4 1.0 %convolution_add_fusion.4 = f32[16,128,64]{1,2,0:T(8,128)S(1)} fusion(f32[16,128,64]{1,2,0:T(8,128)S(1)} %fusion.10, f32[16,128,128]{2,1,0:T(8,128)S(1)} %convolution_multiply_fusion, f32[16,128,64]{1,2,0:T(8,128)S(1)} %bitcast.183), kind=kOutput, calls=%fused_computation.23 | convolution fusion | flops 201457664 | bytes 2621440 | tf_op jit(solution)/shard_map/hts,htn->hsn/dot_general | solution.py:197
  75.5 0.7 copy.61
  76.5 1.0 %copy.60 = bf16[16,128,128]{2,1,0:T(8,128)(2,1)} copy(bf16[16,128,128]{1,2,0:T(8,128)(2,1)S(1)} %copy-done.8) | data formatting | bytes 1048576
  77.5 0.8 %convolution_add_fusion.5 = f32[16,128]{1,0:T(8,128)} fusion(f32[16,128]{1,0:T(8,128)S(1)} %get-tuple-element.20, f32[16,128]{1,0:T(8,128)S(1)} %get-tuple-element.26, f32[16]{0:T(128)S(1)} %get-tuple-element.33), kind=kOutput, calls=%fused_computation.27 | convolution fusion | flops 3166208 | bytes 24640 | tf_op jit(solution)/shard_map/hu,su->hs/dot_general | solution.py:228
  (78 shorter events, 2.0 us)
Async XLA Ops:
  0.6 17.1 %copy-start = (bf16[16,128,128]{2,1,0:T(8,128)(2,1)S(1)}, bf16[16,128,128]{2,1,0:T(8,128)(2,1)}, u32[]{:S(2)}) copy-start(bf16[16,128,128]{2,1,0:T(8,128)(2,1)} %param.7) | copy-start | bytes 1572868
  0.6 9.0 %copy-start.11 = (bf16[2,128,128]{2,1,0:T(8,128)(2,1)S(1)}, bf16[2,128,128]{2,1,0:T(8,128)(2,1)}, u32[]{:S(2)}) copy-start(bf16[2,128,128]{2,1,0:T(8,128)(2,1)} %param.10) | copy-start | bytes 196612
  0.7 9.3 %copy-start.1 = (bf16[16,128,128]{2,1,0:T(8,128)(2,1)S(1)}, bf16[16,128,128]{2,1,0:T(8,128)(2,1)}, u32[]{:S(2)}) copy-start(bf16[16,128,128]{2,1,0:T(8,128)(2,1)} %param.9) | copy-start | bytes 1572868
  0.7 19.7 %collective-permute-start.5 = (bf16[2,128,256]{2,1,0:T(8,128)(2,1)}, bf16[2,128,256]{2,1,0:T(8,128)(2,1)}, u32[]{:S(2)}, u32[]{:S(2)}) collective-permute-start(bf16[2,128,256]{2,1,0:T(8,128)(2,1)} %param.8), channel_id=1, source_target_pairs={{0,12},{1,13},{2,14},{3,15},{16,28},{17,29},{18,30},{19,31}} | collective-permute-start | bytes 393224 | tf_op jit(solution)/shard_map/ppermute | solution.py:66
  2.1 16.4 %collective-permute-start.3 = (bf16[2,128,256]{2,1,0:T(8,128)(2,1)}, bf16[2,128,256]{2,1,0:T(8,128)(2,1)}, u32[]{:S(2)}, u32[]{:S(2)}) collective-permute-start(bf16[2,128,256]{2,1,0:T(8,128)(2,1)} %param.8), channel_id=1, source_target_pairs={{0,4},{4,8},{8,12},{1,5},{5,9},{9,13},{2,6},{6,10},{10,14},{3,7},{... | collective-permute-start | bytes 393224 | tf_op jit(solution)/shard_map/ppermute | solution.py:66
  5.6 17.9 %collective-permute-start.4 = (bf16[2,128,256]{2,1,0:T(8,128)(2,1)}, bf16[2,128,256]{2,1,0:T(8,128)(2,1)}, u32[]{:S(2)}, u32[]{:S(2)}) collective-permute-start(bf16[2,128,256]{2,1,0:T(8,128)(2,1)} %param.8), channel_id=1, source_target_pairs={{0,8},{4,12},{1,9},{5,13},{2,10},{6,14},{3,11},{7,15},{16,24},{20,... | collective-permute-start | bytes 393224 | tf_op jit(solution)/shard_map/ppermute | solution.py:66
  10.0 0.8 %copy-start.3 = (f32[2,8,128,64]{2,3,1,0:T(8,128)}, f32[2,8,128,64]{2,3,1,0:T(8,128)S(1)}, u32[]{:S(2)}) copy-start(f32[2,8,128,64]{2,3,1,0:T(8,128)S(1)} %broadcast_in_dim.101) | copy-start | bytes 1572868
  11.5 23.4 %collective-permute-start.1 = (bf16[1040,128]{1,0:T(8,128)(2,1)}, bf16[1040,128]{1,0:T(8,128)(2,1)S(1)}, u32[]{:S(2)}, u32[]{:S(2)}) collective-permute-start(bf16[1040,128]{1,0:T(8,128)(2,1)} %pad_maximum_fusion.1), channel_id=1, source_target_pairs={{0,8},{4,12},{1,9},{5,13},{2,10},{6,14},{3,11},{7,15},{16,24},{20,... | collective-permute-start | bytes 798728 | tf_op jit(solution)/shard_map/ppermute | solution.py:66
  12.8 27.1 %collective-permute-start = (bf16[1040,128]{1,0:T(8,128)(2,1)}, bf16[1040,128]{1,0:T(8,128)(2,1)S(1)}, u32[]{:S(2)}, u32[]{:S(2)}) collective-permute-start(bf16[1040,128]{1,0:T(8,128)(2,1)} %pad_maximum_fusion.1), channel_id=1, source_target_pairs={{0,4},{4,8},{8,12},{1,5},{5,9},{9,13},{2,6},{6,10},{10,14},{3,7},{... | collective-permute-start | bytes 798728 | tf_op jit(solution)/shard_map/ppermute | solution.py:66
  15.5 2.3 %copy-start.2 = (f32[16,128,128]{2,1,0:T(8,128)}, f32[16,128,128]{2,1,0:T(8,128)S(1)}, u32[]{:S(2)}) copy-start(f32[16,128,128]{2,1,0:T(8,128)S(1)} %bitcast_multiply_fusion.1) | copy-start | bytes 3145732
  15.5 2.3 %copy-start.13 = (bf16[2,128,256]{2,1,0:T(8,128)(2,1)S(1)}, bf16[2,128,256]{2,1,0:T(8,128)(2,1)}, u32[]{:S(2)}) copy-start(bf16[2,128,256]{2,1,0:T(8,128)(2,1)} %param.8) | copy-start | bytes 393220
  18.5 21.4 %collective-permute-start.2 = (bf16[1040,128]{1,0:T(8,128)(2,1)}, bf16[1040,128]{1,0:T(8,128)(2,1)S(1)}, u32[]{:S(2)}, u32[]{:S(2)}) collective-permute-start(bf16[1040,128]{1,0:T(8,128)(2,1)} %pad_maximum_fusion.1), channel_id=1, source_target_pairs={{0,12},{1,13},{2,14},{3,15},{16,28},{17,29},{18,30},{19,31}} | collective-permute-start | bytes 798728 | tf_op jit(solution)/shard_map/ppermute | solution.py:66
  28.4 11.6 %copy-start.12 = (f32[16,64,128]{2,1,0:T(8,128)S(1)}, f32[16,64,128]{2,1,0:T(8,128)}, u32[]{:S(2)}) copy-start(f32[16,64,128]{2,1,0:T(8,128)} %param.13) | copy-start | bytes 1572868
  34.9 5.4 %copy-start.10 = (bf16[1040,128]{1,0:T(8,128)(2,1)}, bf16[1040,128]{1,0:T(8,128)(2,1)S(1)}, u32[]{:S(2)}) copy-start(bf16[1040,128]{1,0:T(8,128)(2,1)S(1)} %collective-permute-done.1) | copy-start | bytes 798724
  39.9 6.5 %copy-start.9 = (bf16[1040,128]{1,0:T(8,128)(2,1)}, bf16[1040,128]{1,0:T(8,128)(2,1)S(1)}, u32[]{:S(2)}) copy-start(bf16[1040,128]{1,0:T(8,128)(2,1)S(1)} %collective-permute-done) | copy-start | bytes 798724
  40.0 1.2 %copy-start.7 = (f32[16,128,128]{1,2,0:T(8,128)S(1)}, f32[16,128,128]{1,2,0:T(8,128)}, u32[]{:S(2)}) copy-start(f32[16,128,128]{1,2,0:T(8,128)} %fusion.114) | copy-start | bytes 3145732
  40.3 6.2 %copy-start.5 = (f32[16,64,128]{2,1,0:T(8,128)}, f32[16,64,128]{2,1,0:T(8,128)S(1)}, u32[]{:S(2)}) copy-start(f32[16,64,128]{2,1,0:T(8,128)S(1)} %fusion.24) | copy-start | bytes 1572868
  40.4 0.8 %copy-start.14 = (f32[16]{0:T(128)S(1)}, f32[16]{0:T(128)}, u32[]{:S(2)}) copy-start(f32[16]{0:T(128)} %param.12) | copy-start | bytes 196
  46.4 1.0 %slice-start = ((bf16[1040,128]{1,0:T(8,128)(2,1)}), bf16[1024,128]{1,0:T(8,128)(2,1)S(1)}, s32[]{:S(2)}) async-start(bf16[1040,128]{1,0:T(8,128)(2,1)} %copy-done.9), calls=%async_computation | async-start | bytes 524288 | tf_op jit(solution)/shard_map/slice | solution.py:38
  46.5 1.0 %slice-start.1 = ((bf16[1040,128]{1,0:T(8,128)(2,1)}), bf16[1024,128]{1,0:T(8,128)(2,1)S(1)}, s32[]{:S(2)}) async-start(bf16[1040,128]{1,0:T(8,128)(2,1)} %copy-done.10), calls=%async_computation.1 | async-start | bytes 524288 | tf_op jit(solution)/shard_map/slice | solution.py:38
  48.1 10.9 %collective-permute-start.8 = (bf16[1040,128]{1,0:T(8,128)(2,1)S(1)}, bf16[1040,128]{1,0:T(8,128)(2,1)S(1)}, u32[]{:S(2)}, u32[]{:S(2)}) collective-permute-start(bf16[1040,128]{1,0:T(8,128)(2,1)S(1)} %pad_maximum_fusion.2), channel_id=1, source_target_pairs={{12,0},{13,1},{14,2},{15,3},{28,16},{29,17},{30,18},{31,19}} | collective-permute-start | bytes 798728 | tf_op jit(solution)/shard_map/ppermute | solution.py:66
  48.8 12.1 %collective-permute-start.7 = (bf16[1040,128]{1,0:T(8,128)(2,1)S(1)}, bf16[1040,128]{1,0:T(8,128)(2,1)S(1)}, u32[]{:S(2)}, u32[]{:S(2)}) collective-permute-start(bf16[1040,128]{1,0:T(8,128)(2,1)S(1)} %pad_maximum_fusion.2), channel_id=1, source_target_pairs={{8,0},{12,4},{9,1},{13,5},{10,2},{14,6},{11,3},{15,7},{24,16},{28,... | collective-permute-start | bytes 798728 | tf_op jit(solution)/shard_map/ppermute | solution.py:66
  50.1 20.1 %collective-permute-start.6 = (bf16[1040,128]{1,0:T(8,128)(2,1)S(1)}, bf16[1040,128]{1,0:T(8,128)(2,1)S(1)}, u32[]{:S(2)}, u32[]{:S(2)}) collective-permute-start(bf16[1040,128]{1,0:T(8,128)(2,1)S(1)} %pad_maximum_fusion.2), channel_id=1, source_target_pairs={{4,0},{8,4},{12,8},{5,1},{9,5},{13,9},{6,2},{10,6},{14,10},{7,3},{... | collective-permute-start | bytes 798728 | tf_op jit(solution)/shard_map/ppermute | solution.py:66
  54.5 1.2 %copy-start.6 = (f32[16,64,128]{2,1,0:T(8,128)S(1)}, f32[16,64,128]{2,1,0:T(8,128)}, u32[]{:S(2)}) copy-start(f32[16,64,128]{2,1,0:T(8,128)} %copy-done.5) | copy-start | bytes 1572868
  55.7 1.1 %copy-start.4 = (f32[2,8,128,64]{2,3,1,0:T(8,128)S(1)}, f32[2,8,128,64]{2,3,1,0:T(8,128)}, u32[]{:S(2)}) copy-start(f32[2,8,128,64]{2,3,1,0:T(8,128)} %copy-done.3) | copy-start | bytes 1572868
  75.4 1.0 %copy-start.8 = (bf16[16,128,128]{1,2,0:T(8,128)(2,1)S(1)}, bf16[16,128,128]{1,2,0:T(8,128)(2,1)}, u32[]{:S(2)}) copy-start(bf16[16,128,128]{1,2,0:T(8,128)(2,1)} %get-tuple-element.27) | copy-start | bytes 1572868

commit v14 on v12

--- a/solution.py
+++ b/solution.py
@@ -170,10 +170,14 @@
         "htn,hnp->htp", out_heads, entering, precision=highest
     )
     outputs = state_out + skip_gain[:, None, None] * inputs_wide
-    inverse = lax.rsqrt(jnp.mean(outputs * outputs, axis=2, keepdims=True) + epsilon)
+    lane_mean = jnp.full((head_width, 1), 1.0 / head_width, jnp.float32)
+    inverse = lax.rsqrt(
+        jnp.einsum("htp,pk->htk", outputs * outputs, lane_mean, precision=highest) + epsilon
+    )
     normed = outputs * inverse
     residual = normed - target
-    grad_out = (residual - normed * jnp.mean(residual * normed, axis=2, keepdims=True)) * inverse
+    projection = jnp.einsum("htp,pk->htk", residual * normed, lane_mean, precision=highest)
+    grad_out = (residual - normed * projection) * inverse
     forward_term = jnp.sum(grad_out * state_out, axis=2)
     flow = jnp.einsum(
         "htn,htp->hnp", out_heads * from_start[..., None], grad_out, precision=highest

time: 79 us -> 80.5 us (1.019)
  matrix products: 27.5 us -> 29.1 us
    dot_general x0 -> x2, matrix products: none -> 1.73 us  [the longest x1 0.89 us: body(): jnp.einsum('htp,pk->htk', residual * normed, lane_mean, precision=highest)]
  transfers between devices with their start and end apart: 9 -> 9, of which waited for: 5 -> 5; matrix products, arithmetic and copies ran while one was open for 28% -> 27% of each run, Pallas kernels for 0% -> 0%
where the time goes in v14:
time: 80.5 us; the launch traced here: 79.7 us
  matrix products  29.1 us (36%)
  waiting for transfers between devices  22.9 us (28%)
  starting transfers between devices  16.1 us (20%)
  local copies, waits for them, and re-layouts  5.21 us (6%)
  other arithmetic  5.2 us (6%)
  between operations  1.29 us (2%)
    ppermute x9, waiting for transfers between devices, shifted(): moved.append(lax.ppermute(x, 'seq', pairs))  22.9 us
    ppermute x9, starting transfers between devices, shifted(): moved.append(lax.ppermute(x, 'seq', pairs))  16.1 us
    dot_general x4, matrix products, teacher_rows(): jnp.einsum('gptk,gkd->gptd', exponentials.astype(jnp.bfloat16), block[......  4.06 us
    dot_general x4, matrix products, teacher_rows(): jnp.einsum('gptd,gkd->gptk', grouped, block[..., :head_width], preferred_...  3.75 us
    unnamed x36, local copies, waits for them, and re-layouts  3.69 us
    dot_general x1, matrix products, body(): jnp.einsum('hsn,hnp->hsp', weighted_in, incoming, precision=highest)  2.85 us
    dot_general x1, matrix products, body(): local_dx = jnp.einsum('hts,htp->hsp', mixing, grad_out, precision=highest)  2.31 us
    dot_general x1, matrix products, body(): jnp.einsum('hts,hsp->htp', mixing, inputs_wide, precision=highest)  2.26 us
  transfers between devices with their start and end apart: 9, of which 5 were waited for; matrix products, arithmetic and copies ran while one was open for 27% of the time, Pallas kernels for 0%

profile of v14, /device:TPU:8, one launch (start us, length us, event | category | flops | bytes accessed | tf_op | source)
XLA Modules:
  0.0 79.7 jit_solution(4588337702313223328)
XLA Ops:
  0.7 1.5 %collective-permute-start.5 = (bf16[2,128,256]{2,1,0:T(8,128)(2,1)}, bf16[2,128,256]{2,1,0:T(8,128)(2,1)}, u32[]{:S(2)}, u32[]{:S(2)}) collective-permute-start(bf16[2,128,256]{2,1,0:T(8,128)(2,1)} %param.8), channel_id=1, source_target_pairs={{0,12},{1,13},{2,14},{3,15},{16,28},{17,29},{18,30},{19,31}} | collective-permute-start | bytes 393224 | tf_op jit(solution)/shard_map/ppermute | solution.py:66
  2.1 3.5 %collective-permute-start.3 = (bf16[2,128,256]{2,1,0:T(8,128)(2,1)}, bf16[2,128,256]{2,1,0:T(8,128)(2,1)}, u32[]{:S(2)}, u32[]{:S(2)}) collective-permute-start(bf16[2,128,256]{2,1,0:T(8,128)(2,1)} %param.8), channel_id=1, source_target_pairs={{0,4},{4,8},{8,12},{1,5},{5,9},{9,13},{2,6},{6,10},{10,14},{3,7},{... | collective-permute-start | bytes 393224 | tf_op jit(solution)/shard_map/ppermute | solution.py:66
  5.6 2.9 %collective-permute-start.4 = (bf16[2,128,256]{2,1,0:T(8,128)(2,1)}, bf16[2,128,256]{2,1,0:T(8,128)(2,1)}, u32[]{:S(2)}, u32[]{:S(2)}) collective-permute-start(bf16[2,128,256]{2,1,0:T(8,128)(2,1)} %param.8), channel_id=1, source_target_pairs={{0,8},{4,12},{1,9},{5,13},{2,10},{6,14},{3,11},{7,15},{16,24},{20,... | collective-permute-start | bytes 393224 | tf_op jit(solution)/shard_map/ppermute | solution.py:66
  8.5 0.7 fusion.57
  10.1 0.5 convolution_convert_fusion
  10.9 0.8 pad_maximum_fusion.1
  11.7 1.3 %collective-permute-start.1 = (bf16[1040,128]{1,0:T(8,128)(2,1)}, bf16[1040,128]{1,0:T(8,128)(2,1)S(1)}, u32[]{:S(2)}, u32[]{:S(2)}) collective-permute-start(bf16[1040,128]{1,0:T(8,128)(2,1)} %pad_maximum_fusion.1), channel_id=1, source_target_pairs={{0,8},{4,12},{1,9},{5,13},{2,10},{6,14},{3,11},{7,15},{16,24},{20,... | collective-permute-start | bytes 798728 | tf_op jit(solution)/shard_map/ppermute | solution.py:66
  13.0 1.9 %collective-permute-start = (bf16[1040,128]{1,0:T(8,128)(2,1)}, bf16[1040,128]{1,0:T(8,128)(2,1)S(1)}, u32[]{:S(2)}, u32[]{:S(2)}) collective-permute-start(bf16[1040,128]{1,0:T(8,128)(2,1)} %pad_maximum_fusion.1), channel_id=1, source_target_pairs={{0,4},{4,8},{8,12},{1,5},{5,9},{9,13},{2,6},{6,10},{10,14},{3,7},{... | collective-permute-start | bytes 798728 | tf_op jit(solution)/shard_map/ppermute | solution.py:66
  15.2 0.3 bitcast_multiply_fusion.1
  15.6 2.3 %fusion.115 = f32[16,128,128]{1,2,0:T(8,128)} fusion(f32[16,128,128]{2,1,0:T(8,128)S(1)} %bitcast_multiply_fusion.1, bf16[16,128,128]{2,1,0:T(8,128)(2,1)S(1)} %copy-done.1), kind=kOutput, calls=%fused_computation.207 | convolution fusion | flops 402653184 | bytes 2621440 | tf_op jit(solution)/shard_map/hts,hsp->htp/dot_general | solution.py:161
  17.9 0.3 fusion.113
  18.7 0.9 %collective-permute-start.2 = (bf16[1040,128]{1,0:T(8,128)(2,1)}, bf16[1040,128]{1,0:T(8,128)(2,1)S(1)}, u32[]{:S(2)}, u32[]{:S(2)}) collective-permute-start(bf16[1040,128]{1,0:T(8,128)(2,1)} %pad_maximum_fusion.1), channel_id=1, source_target_pairs={{0,12},{1,13},{2,14},{3,15},{16,28},{17,29},{18,30},{19,31}} | collective-permute-start | bytes 798728 | tf_op jit(solution)/shard_map/ppermute | solution.py:66
  19.5 1.1 %fusion.114 = (f32[2,8,128]{2,1,0:T(8,128)S(1)}, f32[2,8,128,128]{2,3,1,0:T(8,128)S(1)}) fusion(bf16[2,8,128,128]{3,2,1,0:T(8,128)(2,1)S(1)} %bitcast.180, bf16[2,128,256]{2,1,0:T(8,128)(2,1)} %collective-permute-done.3, pred[]{:T(512)S(6)} %ge.55), kind=kOutput, calls=%fused_computation.206 | convolution fusion | flops 67893248 | bytes 1646593 | tf_op jit(solution)/shard_map/gptd,gkd->gptk/dot_general | solution.py:87
  20.7 1.1 %fusion.111 = (f32[2,8,128]{2,1,0:T(8,128)S(1)}, f32[2,8,128,128]{2,3,1,0:T(8,128)S(1)}) fusion(bf16[2,8,128,128]{3,2,1,0:T(8,128)(2,1)S(1)} %bitcast.182, bf16[2,128,256]{2,1,0:T(8,128)(2,1)} %collective-permute-done.5, pred[]{:T(512)S(6)} %ge.57), kind=kOutput, calls=%fused_computation.203 | convolution fusion | flops 67893248 | bytes 1646593 | tf_op jit(solution)/shard_map/gptd,gkd->gptk/dot_general | solution.py:87
  21.8 1.7 %collective-permute-done.4 = bf16[2,128,256]{2,1,0:T(8,128)(2,1)} collective-permute-done((bf16[2,128,256]{2,1,0:T(8,128)(2,1)}, bf16[2,128,256]{2,1,0:T(8,128)(2,1)}, u32[]{:S(2)}, u32[]{:S(2)}) %collective-permute-start.4) | collective-permute-done | bytes 131104 | tf_op jit(solution)/shard_map/ppermute | solution.py:66
  23.5 1.1 %fusion.112 = (f32[2,8,128]{2,1,0:T(8,128)S(1)}, f32[2,8,128,128]{2,3,1,0:T(8,128)S(1)}) fusion(bf16[2,8,128,128]{3,2,1,0:T(8,128)(2,1)S(1)} %bitcast.181, bf16[2,128,256]{2,1,0:T(8,128)(2,1)} %collective-permute-done.4, pred[]{:T(512)S(6)} %ge.56), kind=kOutput, calls=%fused_computation.204 | convolution fusion | flops 67893248 | bytes 1646593 | tf_op jit(solution)/shard_map/gptd,gkd->gptk/dot_general | solution.py:87
  24.7 0.3 fusion.37
  25.0 1.0 %fusion.20 = (f32[2,8,128]{2,1,0:T(8,128)S(1)}, f32[2,8,128]{2,1,0:T(8,128)S(1)}, f32[2,8,128]{2,1,0:T(8,128)S(1)}, f32[2,8,128]{2,1,0:T(8,128)S(1)}) fusion(f32[2,8,128,128]{2,3,1,0:T(8,128)S(1)} %get-tuple-element.49, f32[2,8,128]{2,1,0:T(8,128)S(1)} %maximum_maximum_fusion, f32[2,8,128,128]{2,3,1,0:T(8,128)S(1)} %get-tuple-element.47, ...), kind=kLoop, calls=%fused_computation.50 | loop fusion | flops 2088960 | bytes 4235264 | tf_op jit(solution)/shard_map/reduce_sum | solution.py:103
  26.0 1.2 %fusion.33 = f32[2,8,128,128]{2,3,1,0:T(8,128)S(1)} fusion(f32[2,8,128,128]{2,3,1,0:T(8,128)S(1)} %get-tuple-element.43, f32[2,8,128]{2,1,0:T(8,128)S(1)} %maximum_maximum_fusion, bf16[2,128,256]{2,1,0:T(8,128)(2,1)} %collective-permute-done.5), kind=kOutput, calls=%fused_computation.69 | convolution fusion | flops 67633152 | bytes 2170880 | tf_op jit(solution)/shard_map/gptk,gkd->gptd/dot_general | solution.py:104
  27.2 1.2 %convolution_add_fusion.2 = f32[2,8,128,128]{2,3,1,0:T(8,128)S(1)} fusion(f32[2,8,128,128]{2,3,1,0:T(8,128)S(1)} %fusion.37, f32[2,8,128,128]{2,3,1,0:T(8,128)S(1)} %get-tuple-element.49, f32[2,8,128]{2,1,0:T(8,128)S(1)} %maximum_maximum_fusion, bf16[2,128,256]{2,1,0:T(8,128)(2,1)} %collective-permute-done.3), kind=kOutput, calls=%fused_computation.8 | convolution fusion | flops 67895296 | bytes 3219456 | tf_op jit(solution)/shard_map/gptk,gkd->gptd/dot_general | solution.py:104
  28.4 1.4 %multiply_reduce_fusion.1 = (f32[2,8,128]{2,1,0:T(8,128)S(1)}, f32[2,8,128,128]{2,3,1,0:T(8,128)S(1)}) fusion(f32[2,8,128]{2,1,0:T(8,128)S(1)} %add_add_fusion, f32[2,8,128,128]{2,3,1,0:T(8,128)S(1)} %fusion.33, f32[2,8,128,128]{2,3,1,0:T(8,128)S(1)} %convolution_add_fusion.2, bf16[2,128,256]{2,1,0:T(8,128)(2,1)} %collective-permute-done.4, ...), kind=kOutput, calls=%fused_computation.40 | convolution fusion | flops 69466112 | bytes 4284416 | tf_op jit(solution)/shard_map/gptk,gkd->gptd/dot_general | solution.py:104
  29.8 5.2 %collective-permute-done.1 = bf16[1040,128]{1,0:T(8,128)(2,1)S(1)} collective-permute-done((bf16[1040,128]{1,0:T(8,128)(2,1)}, bf16[1040,128]{1,0:T(8,128)(2,1)S(1)}, u32[]{:S(2)}, u32[]{:S(2)}) %collective-permute-start.1) | collective-permute-done | bytes 266272 | tf_op jit(solution)/shard_map/ppermute | solution.py:66
  34.9 5.0 %collective-permute-done = bf16[1040,128]{1,0:T(8,128)(2,1)S(1)} collective-permute-done((bf16[1040,128]{1,0:T(8,128)(2,1)}, bf16[1040,128]{1,0:T(8,128)(2,1)S(1)}, u32[]{:S(2)}, u32[]{:S(2)}) %collective-permute-start) | collective-permute-done | bytes 266272 | tf_op jit(solution)/shard_map/ppermute | solution.py:66
  40.0 0.3 fusion.29
  40.4 0.8 %copy-done.7 = f32[16,128,128]{1,2,0:T(8,128)S(1)} copy-done((f32[16,128,128]{1,2,0:T(8,128)S(1)}, f32[16,128,128]{1,2,0:T(8,128)}, u32[]{:S(2)}) %copy-start.7) | copy-done | bytes 1048600
  41.3 1.9 %fusion.1 = f32[16,128,128]{1,2,0:T(8,128)S(1)} fusion(f32[16,128,128]{1,2,0:T(8,128)S(1)} %copy-done.7, f32[16,64,128]{2,1,0:T(8,128)S(1)} %fusion.29, f32[16,128,64]{1,2,0:T(8,128)S(1)} %bitcast.183, f32[16,128]{1,0:T(8,128)S(1)} %get-tuple-element.31), kind=kOutput, calls=%fused_computation.4 | convolution fusion | flops 201850880 | bytes 3153920 | tf_op jit(solution)/shard_map/htn,hnp->htp/dot_general | solution.py:169
  43.1 0.8 %fusion.16 = f32[1,16,128]{2,0,1:T(1,128)S(1)} fusion(f32[16,128,128]{1,2,0:T(8,128)S(1)} %fusion.1, bf16[16,128,128]{1,2,0:T(8,128)(2,1)S(1)} %copy.48, f32[16]{0:T(128)S(1)} %copy-done.14), kind=kOutput, calls=%fused_computation.45 | convolution fusion | flops 4194304 | bytes 1581120 | tf_op jit(solution)/shard_map/htp,pk->htk/dot_general | solution.py:175
  44.0 0.4 fusion.13
  44.4 0.9 %fusion.14 = f32[1,16,128]{2,0,1:T(1,128)S(1)} fusion(f32[16,128,128]{1,2,0:T(8,128)S(1)} %fusion.13, f32[16,128]{1,0:T(8,128)S(1)} %add_rsqrt_fusion, f32[16,128,128]{1,2,0:T(8,128)S(1)} %fusion.1, bf16[16,128,128]{1,2,0:T(8,128)(2,1)S(1)} %copy.48, f32[16]{0:T(128)S(1)} %copy-done.14), kind=kOutput, calls=%fused_computation.38 | convolution fusion | flops 4456448 | bytes 2637888 | tf_op jit(solution)/shard_map/htp,pk->htk/dot_general | solution.py:179
  45.2 0.6 multiply_reduce_fusion
  45.8 2.1 %fusion.41 = f32[16,64,128]{2,1,0:T(8,128)S(1)} fusion(f32[16,128,128]{1,2,0:T(8,128)S(1)} %get-tuple-element.21, f32[16,128,64]{1,2,0:T(8,128)S(1)} %bitcast.184, f32[16,128]{1,0:T(8,128)S(1)} %get-tuple-element.31), kind=kOutput, calls=%fused_computation.77 | convolution fusion | flops 201457664 | bytes 2105344 | tf_op jit(solution)/shard_map/htn,htp->hnp/dot_general | solution.py:182
  48.0 0.9 %slice-done = bf16[1024,128]{1,0:T(8,128)(2,1)S(1)} async-done(((bf16[1040,128]{1,0:T(8,128)(2,1)}), bf16[1024,128]{1,0:T(8,128)(2,1)S(1)}, s32[]{:S(2)}) %slice-start) | async-done | bytes 262168 | tf_op jit(solution)/shard_map/slice | solution.py:38
  49.0 0.4 multiply_reduce_fusion.2
  49.6 0.7 collective-permute-start.8
  50.3 1.3 %collective-permute-start.7 = (bf16[1040,128]{1,0:T(8,128)(2,1)S(1)}, bf16[1040,128]{1,0:T(8,128)(2,1)S(1)}, u32[]{:S(2)}, u32[]{:S(2)}) collective-permute-start(bf16[1040,128]{1,0:T(8,128)(2,1)S(1)} %pad_maximum_fusion.2), channel_id=1, source_target_pairs={{8,0},{12,4},{9,1},{13,5},{10,2},{14,6},{11,3},{15,7},{24,16},{28,... | collective-permute-start | bytes 798728 | tf_op jit(solution)/shard_map/ppermute | solution.py:66
  51.6 2.1 %collective-permute-start.6 = (bf16[1040,128]{1,0:T(8,128)(2,1)S(1)}, bf16[1040,128]{1,0:T(8,128)(2,1)S(1)}, u32[]{:S(2)}, u32[]{:S(2)}) collective-permute-start(bf16[1040,128]{1,0:T(8,128)(2,1)S(1)} %pad_maximum_fusion.2), channel_id=1, source_target_pairs={{4,0},{8,4},{12,8},{5,1},{9,5},{13,9},{6,2},{10,6},{14,10},{7,3},{... | collective-permute-start | bytes 798728 | tf_op jit(solution)/shard_map/ppermute | solution.py:66
  53.7 2.3 %fusion.116 = f32[16,128,128]{1,2,0:T(8,128)S(1)} fusion(f32[16,128,128]{2,1,0:T(8,128)} %copy-done.2, f32[16,128,128]{1,2,0:T(8,128)S(1)} %get-tuple-element.21), kind=kOutput, calls=%fused_computation.208 | convolution fusion | flops 402653184 | bytes 3145728 | tf_op jit(solution)/shard_map/hts,htp->hsp/dot_general | solution.py:195
  56.1 1.2 %convolution_multiply_fusion = f32[16,128,128]{2,1,0:T(8,128)S(1)} fusion(f32[16,128,128]{1,2,0:T(8,128)S(1)} %get-tuple-element.21, bf16[16,128,128]{2,1,0:T(8,128)(2,1)S(1)} %copy-done.1, f32[16,128]{1,0:T(8,128)S(1)} %reduce_window_sum.11, pred[128,128]{1,0:T(8,128)(4,1)S(1)} %copy.44), kind=kOutput, calls=%fused_computation | convolution fusion | flops 403701760 | bytes 2646016 | tf_op jit(solution)/shard_map/htp,hsp->hts/dot_general | solution.py:197
  57.3 1.0 %convolution_multiply_fusion.6 = f32[16,128,64]{1,2,0:T(8,128)S(1)} fusion(f32[16,128,128]{1,2,0:T(8,128)S(1)} %get-tuple-element.21, f32[16,64,128]{2,1,0:T(8,128)S(1)} %copy-done.6, f32[16,128]{1,0:T(8,128)S(1)} %get-tuple-element.31), kind=kOutput, calls=%fused_computation.21 | convolution fusion | flops 201457664 | bytes 2105344 | tf_op jit(solution)/shard_map/hnp,htp->htn/dot_general | solution.py:201
  58.4 2.1 %convolution_add_fusion.3 = f32[16,128,64]{1,2,0:T(8,128)S(1)} fusion(f32[16,128,64]{1,2,0:T(8,128)S(1)} %convolution_multiply_fusion.6, f32[16,128,128]{2,1,0:T(8,128)S(1)} %convolution_multiply_fusion, f32[16,128,64]{1,2,0:T(8,128)S(1)} %bitcast.187), kind=kOutput, calls=%fused_computation.22 | convolution fusion | flops 201457664 | bytes 2621440 | tf_op jit(solution)/shard_map/hts,hsn->htn/dot_general | solution.py:200
  60.5 1.9 %collective-permute-done.7 = bf16[1040,128]{1,0:T(8,128)(2,1)S(1)} collective-permute-done((bf16[1040,128]{1,0:T(8,128)(2,1)S(1)}, bf16[1040,128]{1,0:T(8,128)(2,1)S(1)}, u32[]{:S(2)}, u32[]{:S(2)}) %collective-permute-start.7) | collective-permute-done | bytes 266272 | tf_op jit(solution)/shard_map/ppermute | solution.py:66
  62.4 9.2 %collective-permute-done.6 = bf16[1040,128]{1,0:T(8,128)(2,1)S(1)} collective-permute-done((bf16[1040,128]{1,0:T(8,128)(2,1)S(1)}, bf16[1040,128]{1,0:T(8,128)(2,1)S(1)}, u32[]{:S(2)}, u32[]{:S(2)}) %collective-permute-start.6) | collective-permute-done | bytes 266272 | tf_op jit(solution)/shard_map/ppermute | solution.py:66
  71.8 1.2 %fusion.10 = f32[16,128,64]{1,2,0:T(8,128)S(1)} fusion(bf16[16,128,128]{2,1,0:T(8,128)(2,1)S(1)} %copy-done.1, f32[16,128]{1,0:T(8,128)S(1)} %get-tuple-element.32, bf16[16,64,128]{2,1,0:T(8,128)(2,1)S(1)} %bitcast.193, f32[16,64,128]{2,1,0:T(8,128)S(1)} %bitcast.189, bf16[16,64,128]{2,1,0:T(8,128)(2,1)S(1)} %bitcast.191, f32[16]{0:T(128)S(1)} %get-tuple-element.34, ...), kind=kOutput, calls=%fused_computation.25 | convolution fusion | flops 202244096 | bytes 2105472 | tf_op jit(solution)/shard_map/hnp,hsp->hsn/dot_general | solution.py:233
  73.0 2.8 %fusion.12 = (f32[16,128]{1,0:T(8,128)S(1)}, bf16[16,128,128]{1,2,0:T(8,128)(2,1)}) fusion(bf16[16,128,128]{1,2,0:T(8,128)(2,1)S(1)} %copy.48, f32[16,128,128]{1,2,0:T(8,128)S(1)} %get-tuple-element.21, f32[16]{0:T(128)S(1)} %copy-done.14, f32[16,128,128]{1,2,0:T(8,128)S(1)} %fusion.116, bf16[16,64,128]{2,1,0:T(8,128)(2,1)S(1)} %bitcast.194, ...), kind=kOutput, calls=%fused_computation.29 | convolution fusion | flops 204077056 | bytes 4735168 | tf_op jit(solution)/shard_map/hsn,hnp->hsp/dot_general | solution.py:227
  75.8 1.0 %convolution_add_fusion.4 = f32[16,128,64]{1,2,0:T(8,128)S(1)} fusion(f32[16,128,64]{1,2,0:T(8,128)S(1)} %fusion.10, f32[16,128,128]{2,1,0:T(8,128)S(1)} %convolution_multiply_fusion, f32[16,128,64]{1,2,0:T(8,128)S(1)} %bitcast.185), kind=kOutput, calls=%fused_computation.23 | convolution fusion | flops 201457664 | bytes 2621440 | tf_op jit(solution)/shard_map/hts,htn->hsn/dot_general | solution.py:199
  76.9 0.7 copy.61
  77.9 1.0 %copy.60 = bf16[16,128,128]{2,1,0:T(8,128)(2,1)} copy(bf16[16,128,128]{1,2,0:T(8,128)(2,1)S(1)} %copy-done.8) | data formatting | bytes 1048576
  78.9 0.8 convolution_add_fusion.5
  (80 shorter events, 2.8 us)
Async XLA Ops:
  0.6 17.3 %copy-start = (bf16[16,128,128]{2,1,0:T(8,128)(2,1)S(1)}, bf16[16,128,128]{2,1,0:T(8,128)(2,1)}, u32[]{:S(2)}) copy-start(bf16[16,128,128]{2,1,0:T(8,128)(2,1)} %param.7) | copy-start | bytes 1572868
  0.6 9.2 %copy-start.11 = (bf16[2,128,128]{2,1,0:T(8,128)(2,1)S(1)}, bf16[2,128,128]{2,1,0:T(8,128)(2,1)}, u32[]{:S(2)}) copy-start(bf16[2,128,128]{2,1,0:T(8,128)(2,1)} %param.10) | copy-start | bytes 196612
  0.7 9.5 %copy-start.1 = (bf16[16,128,128]{2,1,0:T(8,128)(2,1)S(1)}, bf16[16,128,128]{2,1,0:T(8,128)(2,1)}, u32[]{:S(2)}) copy-start(bf16[16,128,128]{2,1,0:T(8,128)(2,1)} %param.9) | copy-start | bytes 1572868
  0.7 20.0 %collective-permute-start.5 = (bf16[2,128,256]{2,1,0:T(8,128)(2,1)}, bf16[2,128,256]{2,1,0:T(8,128)(2,1)}, u32[]{:S(2)}, u32[]{:S(2)}) collective-permute-start(bf16[2,128,256]{2,1,0:T(8,128)(2,1)} %param.8), channel_id=1, source_target_pairs={{0,12},{1,13},{2,14},{3,15},{16,28},{17,29},{18,30},{19,31}} | collective-permute-start | bytes 393224 | tf_op jit(solution)/shard_map/ppermute | solution.py:66
  2.1 16.5 %collective-permute-start.3 = (bf16[2,128,256]{2,1,0:T(8,128)(2,1)}, bf16[2,128,256]{2,1,0:T(8,128)(2,1)}, u32[]{:S(2)}, u32[]{:S(2)}) collective-permute-start(bf16[2,128,256]{2,1,0:T(8,128)(2,1)} %param.8), channel_id=1, source_target_pairs={{0,4},{4,8},{8,12},{1,5},{5,9},{9,13},{2,6},{6,10},{10,14},{3,7},{... | collective-permute-start | bytes 393224 | tf_op jit(solution)/shard_map/ppermute | solution.py:66
  5.6 17.9 %collective-permute-start.4 = (bf16[2,128,256]{2,1,0:T(8,128)(2,1)}, bf16[2,128,256]{2,1,0:T(8,128)(2,1)}, u32[]{:S(2)}, u32[]{:S(2)}) collective-permute-start(bf16[2,128,256]{2,1,0:T(8,128)(2,1)} %param.8), channel_id=1, source_target_pairs={{0,8},{4,12},{1,9},{5,13},{2,10},{6,14},{3,11},{7,15},{16,24},{20,... | collective-permute-start | bytes 393224 | tf_op jit(solution)/shard_map/ppermute | solution.py:66
  10.1 0.8 copy-start.3
  11.7 23.2 %collective-permute-start.1 = (bf16[1040,128]{1,0:T(8,128)(2,1)}, bf16[1040,128]{1,0:T(8,128)(2,1)S(1)}, u32[]{:S(2)}, u32[]{:S(2)}) collective-permute-start(bf16[1040,128]{1,0:T(8,128)(2,1)} %pad_maximum_fusion.1), channel_id=1, source_target_pairs={{0,8},{4,12},{1,9},{5,13},{2,10},{6,14},{3,11},{7,15},{16,24},{20,... | collective-permute-start | bytes 798728 | tf_op jit(solution)/shard_map/ppermute | solution.py:66
  13.0 26.9 %collective-permute-start = (bf16[1040,128]{1,0:T(8,128)(2,1)}, bf16[1040,128]{1,0:T(8,128)(2,1)S(1)}, u32[]{:S(2)}, u32[]{:S(2)}) collective-permute-start(bf16[1040,128]{1,0:T(8,128)(2,1)} %pad_maximum_fusion.1), channel_id=1, source_target_pairs={{0,4},{4,8},{8,12},{1,5},{5,9},{9,13},{2,6},{6,10},{10,14},{3,7},{... | collective-permute-start | bytes 798728 | tf_op jit(solution)/shard_map/ppermute | solution.py:66
  15.6 2.3 %copy-start.2 = (f32[16,128,128]{2,1,0:T(8,128)}, f32[16,128,128]{2,1,0:T(8,128)S(1)}, u32[]{:S(2)}) copy-start(f32[16,128,128]{2,1,0:T(8,128)S(1)} %bitcast_multiply_fusion.1) | copy-start | bytes 3145732
  15.6 2.3 %copy-start.13 = (bf16[2,128,256]{2,1,0:T(8,128)(2,1)S(1)}, bf16[2,128,256]{2,1,0:T(8,128)(2,1)}, u32[]{:S(2)}) copy-start(bf16[2,128,256]{2,1,0:T(8,128)(2,1)} %param.8) | copy-start | bytes 393220
  18.7 21.3 %collective-permute-start.2 = (bf16[1040,128]{1,0:T(8,128)(2,1)}, bf16[1040,128]{1,0:T(8,128)(2,1)S(1)}, u32[]{:S(2)}, u32[]{:S(2)}) collective-permute-start(bf16[1040,128]{1,0:T(8,128)(2,1)} %pad_maximum_fusion.1), channel_id=1, source_target_pairs={{0,12},{1,13},{2,14},{3,15},{16,28},{17,29},{18,30},{19,31}} | collective-permute-start | bytes 798728 | tf_op jit(solution)/shard_map/ppermute | solution.py:66
  28.4 11.6 %copy-start.12 = (f32[16,64,128]{2,1,0:T(8,128)S(1)}, f32[16,64,128]{2,1,0:T(8,128)}, u32[]{:S(2)}) copy-start(f32[16,64,128]{2,1,0:T(8,128)} %param.13) | copy-start | bytes 1572868
  34.9 5.4 %copy-start.10 = (bf16[1040,128]{1,0:T(8,128)(2,1)}, bf16[1040,128]{1,0:T(8,128)(2,1)S(1)}, u32[]{:S(2)}) copy-start(bf16[1040,128]{1,0:T(8,128)(2,1)S(1)} %collective-permute-done.1) | copy-start | bytes 798724
  39.9 8.1 %copy-start.9 = (bf16[1040,128]{1,0:T(8,128)(2,1)}, bf16[1040,128]{1,0:T(8,128)(2,1)S(1)}, u32[]{:S(2)}) copy-start(bf16[1040,128]{1,0:T(8,128)(2,1)S(1)} %collective-permute-done) | copy-start | bytes 798724
  40.0 1.2 %copy-start.7 = (f32[16,128,128]{1,2,0:T(8,128)S(1)}, f32[16,128,128]{1,2,0:T(8,128)}, u32[]{:S(2)}) copy-start(f32[16,128,128]{1,2,0:T(8,128)} %fusion.115) | copy-start | bytes 3145732
  40.3 7.7 %copy-start.5 = (f32[16,64,128]{2,1,0:T(8,128)}, f32[16,64,128]{2,1,0:T(8,128)S(1)}, u32[]{:S(2)}) copy-start(f32[16,64,128]{2,1,0:T(8,128)S(1)} %fusion.29) | copy-start | bytes 1572868
  41.2 1.9 %copy-start.14 = (f32[16]{0:T(128)S(1)}, f32[16]{0:T(128)}, u32[]{:S(2)}) copy-start(f32[16]{0:T(128)} %param.12) | copy-start | bytes 196
  48.0 1.0 %slice-start = ((bf16[1040,128]{1,0:T(8,128)(2,1)}), bf16[1024,128]{1,0:T(8,128)(2,1)S(1)}, s32[]{:S(2)}) async-start(bf16[1040,128]{1,0:T(8,128)(2,1)} %copy-done.9), calls=%async_computation | async-start | bytes 524288 | tf_op jit(solution)/shard_map/slice | solution.py:38
  48.0 1.0 %slice-start.1 = ((bf16[1040,128]{1,0:T(8,128)(2,1)}), bf16[1024,128]{1,0:T(8,128)(2,1)S(1)}, s32[]{:S(2)}) async-start(bf16[1040,128]{1,0:T(8,128)(2,1)} %copy-done.10), calls=%async_computation.1 | async-start | bytes 524288 | tf_op jit(solution)/shard_map/slice | solution.py:38
  49.6 10.9 %collective-permute-start.8 = (bf16[1040,128]{1,0:T(8,128)(2,1)S(1)}, bf16[1040,128]{1,0:T(8,128)(2,1)S(1)}, u32[]{:S(2)}, u32[]{:S(2)}) collective-permute-start(bf16[1040,128]{1,0:T(8,128)(2,1)S(1)} %pad_maximum_fusion.2), channel_id=1, source_target_pairs={{12,0},{13,1},{14,2},{15,3},{28,16},{29,17},{30,18},{31,19}} | collective-permute-start | bytes 798728 | tf_op jit(solution)/shard_map/ppermute | solution.py:66
  50.3 12.1 %collective-permute-start.7 = (bf16[1040,128]{1,0:T(8,128)(2,1)S(1)}, bf16[1040,128]{1,0:T(8,128)(2,1)S(1)}, u32[]{:S(2)}, u32[]{:S(2)}) collective-permute-start(bf16[1040,128]{1,0:T(8,128)(2,1)S(1)} %pad_maximum_fusion.2), channel_id=1, source_target_pairs={{8,0},{12,4},{9,1},{13,5},{10,2},{14,6},{11,3},{15,7},{24,16},{28,... | collective-permute-start | bytes 798728 | tf_op jit(solution)/shard_map/ppermute | solution.py:66
  51.6 20.0 %collective-permute-start.6 = (bf16[1040,128]{1,0:T(8,128)(2,1)S(1)}, bf16[1040,128]{1,0:T(8,128)(2,1)S(1)}, u32[]{:S(2)}, u32[]{:S(2)}) collective-permute-start(bf16[1040,128]{1,0:T(8,128)(2,1)S(1)} %pad_maximum_fusion.2), channel_id=1, source_target_pairs={{4,0},{8,4},{12,8},{5,1},{9,5},{13,9},{6,2},{10,6},{14,10},{7,3},{... | collective-permute-start | bytes 798728 | tf_op jit(solution)/shard_map/ppermute | solution.py:66
  56.1 1.2 %copy-start.6 = (f32[16,64,128]{2,1,0:T(8,128)S(1)}, f32[16,64,128]{2,1,0:T(8,128)}, u32[]{:S(2)}) copy-start(f32[16,64,128]{2,1,0:T(8,128)} %copy-done.5) | copy-start | bytes 1572868
  57.3 1.1 %copy-start.4 = (f32[2,8,128,64]{2,3,1,0:T(8,128)S(1)}, f32[2,8,128,64]{2,3,1,0:T(8,128)}, u32[]{:S(2)}) copy-start(f32[2,8,128,64]{2,3,1,0:T(8,128)} %copy-done.3) | copy-start | bytes 1572868
  76.9 1.0 %copy-start.8 = (bf16[16,128,128]{1,2,0:T(8,128)(2,1)S(1)}, bf16[16,128,128]{1,2,0:T(8,128)(2,1)}, u32[]{:S(2)}) copy-start(bf16[16,128,128]{1,2,0:T(8,128)(2,1)} %get-tuple-element.27) | copy-start | bytes 1572868
